TPU v7x, 32 devices: a whole 2x2x4 slice. The times are simulated.
32 devices in a mesh: groups: 2 (over y), ctx: 4 (over z), tp: 2 (over x), dp: 2 (over core).
Axes of the slice: x: 2, y: 2, z: 4, core: 2. Of those that a mesh axis runs over, the one named last changes fastest.
Arguments:
- tokens: bfloat16 [1024, 5120], P(('groups', 'ctx'), ('tp', 'dp')), parts along dimension 0, may hold values from -6 to 6
- lengths: int32 [8], P('groups'), parts along dimension 0, may hold values from 1 to 256, 512 in all
- request_adapter_ids: int32 [8], P('groups'), parts along dimension 0, may hold values from 0 to 7
- adapter_store_slot: int32 [8], replicated, may hold values from 0 to 7, each once
- xchan_input_weight: bfloat16 [5120, 4096], P('ctx', ('tp', 'dp')), may hold values from -0.078125 to 0.078125
- bc_input_weight: bfloat16 [5120, 512], P('ctx', ('tp', 'dp')), may hold values from -0.078125 to 0.078125
- step_input_weight: bfloat16 [5120, 64], P('ctx', ('tp', 'dp')), may hold values from -0.078125 to 0.078125
- convolution_x_taps: float32 [4, 4096], P(None, ('tp', 'dp')), may hold values from -3 to 3
- convolution_bc_taps: float32 [4, 512], P(None, ('tp', 'dp')), may hold values from -3 to 3
- step_bias: float32 [64], P(('tp', 'dp')), may hold values from -2 to 1
- decay_log_rate: float32 [64], P(('tp', 'dp')), may hold values from -16 to -2
- head_skip_gain: float32 [64], P(('tp', 'dp')), may hold values from 0.5 to 1.5
- output_norm_gain: float32 [4096], P(('tp', 'dp')), may hold values from 0.1 to 1.9
- output_weight: bfloat16 [4096, 5120], P(('tp', 'dp'), 'ctx'), may hold values from -0.09375 to 0.09375
- adapter_down_input: bfloat16 [8, 5120, 64], P('ctx', ('tp', 'dp')), may hold values from -0.078125 to 0.078125
- adapter_up_xchan: bfloat16 [8, 64, 4096], P('ctx', None, ('tp', 'dp')), may hold values from -0.75 to 0.75
- adapter_up_bc: bfloat16 [8, 64, 512], P('ctx', None, ('tp', 'dp')), may hold values from -0.75 to 0.75
- adapter_down_output: bfloat16 [8, 4096, 64], P('ctx', ('tp', 'dp')), may hold values from -0.09375 to 0.09375
- adapter_up_output: bfloat16 [8, 64, 5120], P('ctx', None, ('tp', 'dp')), may hold values from -0.75 to 0.75
Outputs:
- mixed: bfloat16 [1024, 5120], P(('groups', 'ctx'), ('tp', 'dp')), parts along dimension 0
There are 2 independent parts, one for each index of `groups`. A program takes and returns all parts, laid end to end along the dimension named above; an argument that names none is the same for every part. Nothing has to cross between parts.
Inputs may be any that keep to these rules, and one draw needn't show every extreme that they name: The 4 lengths add up to 512; the longest is exactly 256. `adapter_store_slot`: each slot once; the adapter in slot k is stored on index k // 2 of ctx, at its place k % 2 there.
All inputs are finite; a program needn't handle non-finite values.
Results may differ from a plain program's by a relative error of at most 0.023.
Values may be sent and summed in bfloat16 or wider, within the bound.
No kernel may reach another device: no remote copies, remote signals or barrier semaphores. Data moves between devices by JAX's collectives and lax.ppermute only.
A program may use at most 64 MiB of HBM per device.

v0:
```python
import jax
import jax.numpy as jnp
from jax import lax
from jax.sharding import PartitionSpec as P

FULL_PRECISION = lax.Precision.HIGHEST
NORM_EPSILON = 1e-06


def from_root(block, axis, source):
    block = jnp.where(lax.axis_index(axis) == source, block, jnp.zeros_like(block))
    return lax.psum(block, axis)


def passed_along(shard, axis, by):
    size = lax.axis_size(axis)
    pairs = [(i, i + by) for i in range(size) if 0 <= i + by < size]
    return lax.ppermute(shard, axis, pairs)


def prefix(shard, axis, combine, identity):
    size, place = (lax.axis_size(axis), lax.axis_index(axis))
    everything = jax.tree.map(
        lambda part, kind: lax.all_gather(part.astype(kind), axis),
        shard,
        (jnp.bfloat16, jnp.bfloat16),
    )
    start = jax.tree.map(
        lambda part, zero: jnp.broadcast_to(jnp.asarray(zero, part.dtype), part.shape),
        shard,
        identity,
    )

    def lap(k, before):
        reached = k < place
        new = combine(
            before, jax.tree.map(lambda part, own: part[k].astype(own.dtype), everything, shard)
        )
        return jax.tree.map(lambda a, b: jnp.where(reached, a, b), new, before)

    return lax.fori_loop(0, size, lap, start)


def segment_of(positions, request_ends):
    inside = (positions[:, None] >= request_ends[None, :]).astype(jnp.int32)
    counted = jnp.sum(inside, axis=1, dtype=jnp.int32)
    return jnp.where(positions < 0, jnp.int32(-1), counted)


def span_parts(x_heads, b_proj, c_proj, step_size, log_decay, segment, previous):
    length = x_heads.shape[0]
    cumulative = jnp.cumsum(log_decay, axis=0)
    final_log = cumulative[length - 1]
    places = jnp.arange(length, dtype=jnp.int32)
    same_request = jnp.logical_and(
        segment[:, None] == segment[None, :], places[None, :] <= places[:, None]
    ).astype(jnp.float32)
    log_gap = cumulative.T[:, :, None] - cumulative.T[:, None, :]
    decay_table = jnp.exp(jnp.minimum(log_gap, 0.0)) * same_request[None]
    scores = lax.dot_general(
        c_proj, b_proj, (((1,), (1,)), ((), ())), preferred_element_type=jnp.float32
    )
    weights = scores[None] * decay_table * step_size.T[:, None, :]
    inner_out = jnp.einsum("hts,shd->thd", weights, x_heads, precision=FULL_PRECISION)
    at_end = (segment == segment[length - 1]).astype(jnp.float32)
    state_weight = jnp.exp(final_log[None, :] - cumulative) * at_end[:, None] * step_size
    local_state = jnp.einsum(
        "sh,shd,sn->hdn",
        state_weight,
        x_heads,
        b_proj.astype(jnp.float32),
        precision=FULL_PRECISION,
    )
    enter_weight = jnp.exp(cumulative) * (segment == previous).astype(jnp.float32)[:, None]
    carry_decay = jnp.exp(final_log) * (segment[length - 1] == previous).astype(jnp.float32)
    return (inner_out, local_state, enter_weight, carry_decay)


def select_rows(wide, adapter_picker_matrix):
    shaped = wide.reshape(wide.shape[0], adapter_picker_matrix.shape[1], -1)
    return jnp.sum(shaped * adapter_picker_matrix[:, :, None], axis=1)


def masked_wide(values, onehot_b):
    return (values[:, None, :] * onehot_b[:, :, None]).reshape(values.shape[0], -1)


def body(
    tokens,
    lengths,
    request_adapter_ids,
    adapter_store_slot,
    xchan_input_weight,
    bc_input_weight,
    step_input_weight,
    convolution_x_taps,
    convolution_bc_taps,
    step_bias,
    decay_log_rate,
    head_skip_gain,
    output_norm_gain,
    output_weight,
    adapter_down_input,
    adapter_up_xchan,
    adapter_up_bc,
    adapter_down_output,
    adapter_up_output,
):
    length = tokens.shape[0]
    request_list = lengths.shape[0]
    taps = convolution_x_taps.shape[0]
    bank_entries = adapter_down_input.shape[0]
    head_count = step_bias.shape[0]
    channels = xchan_input_weight.shape[1]
    start_pos = lax.axis_index("ctx") * length
    request_ends = jnp.cumsum(lengths, dtype=jnp.int32)
    positions = start_pos + jnp.arange(length, dtype=jnp.int32)
    segment = segment_of(positions, request_ends)
    previous = segment_of(jnp.reshape(start_pos - 1, (1,)), request_ends)[0]
    adapter_picker_matrix = (
        segment[:, None] == jnp.arange(request_list, dtype=jnp.int32)[None, :]
    ).astype(jnp.float32)
    onehot_b = adapter_picker_matrix.astype(jnp.bfloat16)
    slot_indices = adapter_store_slot[request_adapter_ids]
    initial_stacks = (
        jnp.zeros(
            (adapter_down_input.shape[1], request_list, adapter_down_input.shape[2]), jnp.bfloat16
        ),
        jnp.zeros((request_list,) + adapter_up_xchan.shape[1:], jnp.bfloat16),
        jnp.zeros((request_list,) + adapter_up_bc.shape[1:], jnp.bfloat16),
        jnp.zeros(
            (adapter_down_output.shape[1], request_list, adapter_down_output.shape[2]), jnp.bfloat16
        ),
        jnp.zeros((request_list,) + adapter_up_output.shape[1:], jnp.bfloat16),
    )
    stack_dims = (1, 0, 0, 1, 0)

    def fetch(request_item, current):
        slot = slot_indices[request_item]
        owner = slot // bank_entries
        within = slot % bank_entries
        a_in, b_x, b_bc, a_out, b_out = [
            lax.dynamic_index_in_dim(adapter_bank, within, 0, keepdims=False)
            for adapter_bank in (
                adapter_down_input,
                adapter_up_xchan,
                adapter_up_bc,
                adapter_down_output,
                adapter_up_output,
            )
        ]
        received = (
            from_root(a_in, "ctx", owner),
            from_root(b_x, "ctx", owner),
            from_root(b_bc, "ctx", owner),
            from_root(a_out, "ctx", owner),
            from_root(b_out, "ctx", owner),
        )
        return tuple(
            (
                lax.dynamic_update_index_in_dim(stack, panel, request_item, along)
                for stack, panel, along in zip(current, received, stack_dims)
            )
        )

    stacks = lax.fori_loop(0, request_list, fetch, initial_stacks)
    rank_value = adapter_down_input.shape[2]
    down_in = stacks[0].reshape(stacks[0].shape[0], request_list * rank_value)
    up_x = stacks[1].reshape(request_list * rank_value, -1)
    up_bc = stacks[2].reshape(request_list * rank_value, -1)
    down_out = stacks[3].reshape(stacks[3].shape[0], request_list * rank_value)
    up_out = stacks[4].reshape(request_list * rank_value, -1)
    lowrank_part = select_rows(
        jnp.dot(tokens, down_in, preferred_element_type=jnp.float32), adapter_picker_matrix
    )
    rank_hidden = lax.psum(lowrank_part.astype(jnp.bfloat16), ("tp", "dp"))
    lowrank_wide = masked_wide(rank_hidden, onehot_b)
    full_tokens = lax.all_gather(tokens, ("tp", "dp"), axis=1, tiled=True)
    pieces = (
        lax.all_gather(xchan_input_weight, "ctx", axis=0, tiled=True),
        lax.all_gather(bc_input_weight, "ctx", axis=0, tiled=True),
        lax.all_gather(step_input_weight, "ctx", axis=0, tiled=True),
    )
    xchan_values, bc_channel_values, step_raw = tuple(
        (jnp.dot(full_tokens, piece, preferred_element_type=jnp.float32) for piece in pieces)
    )
    xchan_values = xchan_values + jnp.dot(lowrank_wide, up_x, preferred_element_type=jnp.float32)
    bc_channel_values = bc_channel_values + jnp.dot(
        lowrank_wide, up_bc, preferred_element_type=jnp.float32
    )
    values = jnp.concatenate([xchan_values, bc_channel_values], axis=1)
    kernel = jnp.concatenate([convolution_x_taps, convolution_bc_taps], axis=1)
    tail_rows = passed_along(values[length - (taps - 1) :], "ctx", 1)
    extended = jnp.concatenate([tail_rows, values], axis=0)
    extended_segment = segment_of(
        start_pos - (taps - 1) + jnp.arange(length + taps - 1, dtype=jnp.int32), request_ends
    )
    convolved = jnp.zeros_like(values)
    for tap in range(taps):
        keep = (extended_segment[tap : tap + length] == segment).astype(jnp.float32)
        convolved = convolved + kernel[tap][None, :] * extended[tap : tap + length] * keep[:, None]
    act = jax.nn.silu(convolved)
    x_heads = act[:, :channels].reshape(length, head_count, -1)
    bc_local = act[:, channels:].astype(jnp.bfloat16)
    bc_all = lax.all_gather(bc_local, ("tp", "dp"), axis=1, tiled=True)
    state_width = bc_all.shape[1] // 2
    b_proj = bc_all[:, :state_width]
    c_proj = bc_all[:, state_width:]
    step_size = jax.nn.softplus(step_raw + step_bias[None, :])
    log_decay = -step_size * jnp.exp(decay_log_rate)[None, :]
    inner_out, local_state, enter_weight, carry_decay = span_parts(
        x_heads, b_proj, c_proj, step_size, log_decay, segment, previous
    )

    def compose(earlier, later):
        return (earlier[0] * later[0], later[0][:, None, None] * earlier[1] + later[1])

    carried = prefix(
        (carry_decay, local_state),
        "ctx",
        compose,
        (jnp.ones_like(carry_decay), jnp.zeros_like(local_state)),
    )
    entering = carried[1]
    entered = (
        jnp.einsum("tn,hdn->thd", c_proj.astype(jnp.float32), entering, precision=FULL_PRECISION)
        * enter_weight[:, :, None]
    )
    mixer_out = (inner_out + entered + head_skip_gain[None, :, None] * x_heads).reshape(
        length, channels
    )
    scale = lax.rsqrt(jnp.mean(mixer_out * mixer_out, axis=1, keepdims=True) + NORM_EPSILON)
    normalized_rows = (mixer_out * scale * output_norm_gain[None, :]).astype(jnp.bfloat16)
    term = jnp.dot(
        normalized_rows,
        lax.all_gather(output_weight, "ctx", axis=1, tiled=True),
        preferred_element_type=jnp.float32,
    )
    base = lax.psum_scatter(
        term.astype(jnp.bfloat16), ("tp", "dp"), scatter_dimension=1, tiled=True
    ).astype(jnp.float32)
    lowrank_out_part = select_rows(
        jnp.dot(normalized_rows, down_out, preferred_element_type=jnp.float32),
        adapter_picker_matrix,
    )
    rank_hidden_output = lax.psum(lowrank_out_part.astype(jnp.bfloat16), ("tp", "dp"))
    adapter_term = jnp.dot(
        masked_wide(rank_hidden_output, onehot_b), up_out, preferred_element_type=jnp.float32
    )
    return (base + adapter_term).astype(jnp.bfloat16)


def solution(mesh):
    placed = (
        P(("groups", "ctx"), ("tp", "dp")),
        P("groups"),
        P("groups"),
        P(),
        P("ctx", ("tp", "dp")),
        P("ctx", ("tp", "dp")),
        P("ctx", ("tp", "dp")),
        P(None, ("tp", "dp")),
        P(None, ("tp", "dp")),
        P(("tp", "dp")),
        P(("tp", "dp")),
        P(("tp", "dp")),
        P(("tp", "dp")),
        P(("tp", "dp"), "ctx"),
        P("ctx", ("tp", "dp"), None),
        P("ctx", None, ("tp", "dp")),
        P("ctx", None, ("tp", "dp")),
        P("ctx", ("tp", "dp"), None),
        P("ctx", None, ("tp", "dp")),
    )
    return jax.shard_map(
        body,
        mesh=mesh,
        in_specs=placed,
        out_specs=P(("groups", "ctx"), ("tp", "dp")),
        check_vma=False,
    )
```

profile of v0, /device:TPU:2, one launch (start us, length us, event | category | flops | bytes accessed | tf_op | source)
XLA Modules:
  0.0 749.4 jit_solution(9867855290832250756)
XLA Ops:
  8.7 216.4 %while.37 = (s32[]{:T(128)}, bf16[1280,4,64]{0,2,1:T(8,128)(2,1)S(1)}, bf16[4,64,1024]{2,1,0:T(8,128)(2,1)S(1)}, bf16[4,64,128]{2,1,0:T(8,128)(2,1)S(1)}, bf16[1...) while((s32[]{:T(128)}, ...), condition=%wide.region_6.7_spmd, body=%wide.region_0.6_spmd.sunk | while | flops 606236 | bytes 6128176 | solution.py:166
  11.9 1.6 dynamic-slice_select_fusion.7
  13.5 1.6 select_bitcast_fusion.4
  18.3 19.1 %psum.87 = bf16[1,64,128]{2,1,0:T(8,128)(2,1)S(1)} all-reduce(bf16[1,64,128]{2,1,0:T(8,128)(2,1)S(1)} %dynamic-slice_select_fusion.8), channel_id=1, replica_groups=mesh['groups'=2,'ctx'=4,'tp'=2,'dp'=2] {'ctx'}, use_global_device_ids=true, to_apply=%region_3.3 | all-reduce | flops 8192 | bytes 32768 | tf_op jit(solution)/shard_map/while/body/eval_jaxpr/psum | solution.py:12
  37.4 22.3 %all-reduce.5.cloned.1.call-done = (bf16[1280,1,64]{0,2,1:T(8,128)(2,1)}, bf16[1,64,1024]{2,1,0:T(8,128)(2,1)}, bf16[1024,1,64]{0,2,1:T(8,128)(2,1)}, bf16[1,64,1280]{2,1,0:T(8,128)(2,1)}) async-done(((bf16[1280,1,64]{0,2,1:T(8,128)(2,1)}, bf16[1,64,1024]{2,1,0:T(8,128)(2,1)}, bf16[1024,1,64]{0,2,1:T(8,128)(2,1)}, bf16[1,64,1280]{2,1,0:T(8,128)(2,1)}), (bf16[1280,1,64]{0,2,1:T(8,128)(2,1)}, ...) | async-done | bytes 589840 | tf_op jit(solution)/shard_map/while/body/eval_jaxpr/psum | solution.py:12
  67.3 1.6 dynamic-slice_select_fusion.7
  68.8 1.6 select_bitcast_fusion.4
  73.6 17.3 %psum.87 = bf16[1,64,128]{2,1,0:T(8,128)(2,1)S(1)} all-reduce(bf16[1,64,128]{2,1,0:T(8,128)(2,1)S(1)} %dynamic-slice_select_fusion.8), channel_id=1, replica_groups=mesh['groups'=2,'ctx'=4,'tp'=2,'dp'=2] {'ctx'}, use_global_device_ids=true, to_apply=%region_3.3 | all-reduce | flops 8192 | bytes 32768 | tf_op jit(solution)/shard_map/while/body/eval_jaxpr/psum | solution.py:12
  90.9 22.5 %all-reduce.5.cloned.1.call-done = (bf16[1280,1,64]{0,2,1:T(8,128)(2,1)}, bf16[1,64,1024]{2,1,0:T(8,128)(2,1)}, bf16[1024,1,64]{0,2,1:T(8,128)(2,1)}, bf16[1,64,1280]{2,1,0:T(8,128)(2,1)}) async-done(((bf16[1280,1,64]{0,2,1:T(8,128)(2,1)}, bf16[1,64,1024]{2,1,0:T(8,128)(2,1)}, bf16[1024,1,64]{0,2,1:T(8,128)(2,1)}, bf16[1,64,1280]{2,1,0:T(8,128)(2,1)}), (bf16[1280,1,64]{0,2,1:T(8,128)(2,1)}, ...) | async-done | bytes 589840 | tf_op jit(solution)/shard_map/while/body/eval_jaxpr/psum | solution.py:12
  122.5 1.6 select_bitcast_fusion.4
  127.3 17.3 %psum.87 = bf16[1,64,128]{2,1,0:T(8,128)(2,1)S(1)} all-reduce(bf16[1,64,128]{2,1,0:T(8,128)(2,1)S(1)} %dynamic-slice_select_fusion.8), channel_id=1, replica_groups=mesh['groups'=2,'ctx'=4,'tp'=2,'dp'=2] {'ctx'}, use_global_device_ids=true, to_apply=%region_3.3 | all-reduce | flops 8192 | bytes 32768 | tf_op jit(solution)/shard_map/while/body/eval_jaxpr/psum | solution.py:12
  144.6 22.5 %all-reduce.5.cloned.1.call-done = (bf16[1280,1,64]{0,2,1:T(8,128)(2,1)}, bf16[1,64,1024]{2,1,0:T(8,128)(2,1)}, bf16[1024,1,64]{0,2,1:T(8,128)(2,1)}, bf16[1,64,1280]{2,1,0:T(8,128)(2,1)}) async-done(((bf16[1280,1,64]{0,2,1:T(8,128)(2,1)}, bf16[1,64,1024]{2,1,0:T(8,128)(2,1)}, bf16[1024,1,64]{0,2,1:T(8,128)(2,1)}, bf16[1,64,1280]{2,1,0:T(8,128)(2,1)}), (bf16[1280,1,64]{0,2,1:T(8,128)(2,1)}, ...) | async-done | bytes 589840 | tf_op jit(solution)/shard_map/while/body/eval_jaxpr/psum | solution.py:12
  176.2 1.6 select_bitcast_fusion.4
  181.0 17.3 %psum.87 = bf16[1,64,128]{2,1,0:T(8,128)(2,1)S(1)} all-reduce(bf16[1,64,128]{2,1,0:T(8,128)(2,1)S(1)} %dynamic-slice_select_fusion.8), channel_id=1, replica_groups=mesh['groups'=2,'ctx'=4,'tp'=2,'dp'=2] {'ctx'}, use_global_device_ids=true, to_apply=%region_3.3 | all-reduce | flops 8192 | bytes 32768 | tf_op jit(solution)/shard_map/while/body/eval_jaxpr/psum | solution.py:12
  198.3 22.5 %all-reduce.5.cloned.1.call-done = (bf16[1280,1,64]{0,2,1:T(8,128)(2,1)}, bf16[1,64,1024]{2,1,0:T(8,128)(2,1)}, bf16[1024,1,64]{0,2,1:T(8,128)(2,1)}, bf16[1,64,1280]{2,1,0:T(8,128)(2,1)}) async-done(((bf16[1280,1,64]{0,2,1:T(8,128)(2,1)}, bf16[1,64,1024]{2,1,0:T(8,128)(2,1)}, bf16[1024,1,64]{0,2,1:T(8,128)(2,1)}, bf16[1,64,1280]{2,1,0:T(8,128)(2,1)}), (bf16[1280,1,64]{0,2,1:T(8,128)(2,1)}, ...) | async-done | bytes 589840 | tf_op jit(solution)/shard_map/while/body/eval_jaxpr/psum | solution.py:12
  230.0 10.8 %psum.84 = bf16[128,64]{0,1:T(8,128)(2,1)S(1)} all-reduce(bf16[128,64]{0,1:T(8,128)(2,1)S(1)} %multiply_reduce_fusion.1), channel_id=1, replica_groups=mesh['groups'=2,'ctx'=4,'tp'=2,'dp'=2] {'tp','dp'}, use_global_device_ids=true, to_apply=%region_10.11 | all-reduce | flops 8192 | bytes 32768 | tf_op jit(solution)/shard_map/psum | solution.py:176
  240.9 13.7 %all_gather.32 = bf16[5120,16]{0,1:T(8,128)(2,1)S(1)} all-gather(bf16[1280,16]{0,1:T(8,128)(2,1)S(1)} %copy-done.5), channel_id=1, replica_groups=mesh['groups'=2,'ctx'=4,'tp'=2,'dp'=2] {'ctx'}, dimensions={0}, use_global_device_ids=true | all-gather | bytes 204800 | tf_op jit(solution)/shard_map/all_gather | solution.py:182
  255.8 1.9 compare_select_fusion
  258.1 20.5 %all-gather.12.cloned.1.call-done = bf16[5120,128]{1,0:T(8,128)(2,1)} async-done(((bf16[1280,128]{1,0:T(8,128)(2,1)}), bf16[5120,128]{1,0:T(8,128)(2,1)}) %all-gather.12.cloned.1.call-update) | async-done | bytes 1310736 | tf_op jit(solution)/shard_map/all_gather | solution.py:181
  278.7 1.8 convolution_add_fusion.1
  280.5 182.5 %all-gather.10.cloned.1.call-done = bf16[5120,1024]{1,0:T(8,128)(2,1)} async-done(((bf16[1280,1024]{1,0:T(8,128)(2,1)}), bf16[5120,1024]{1,0:T(8,128)(2,1)}) %all-gather.10.cloned.1.call-update) | async-done | bytes 10485776 | tf_op jit(solution)/shard_map/all_gather | solution.py:180
  463.0 5.6 convolution_add_fusion
  472.2 5.4 all_gather.31
  479.9 10.9 %all-gather.1 = bf16[4,1,16]{2,1,0:T(2,128)(2,1)S(1)} all-gather(bf16[1,1,16]{2,1,0:T(2,128)(2,1)S(1)} %get-tuple-element.473), channel_id=1, replica_groups=mesh['groups'=2,'ctx'=4,'tp'=2,'dp'=2] {'ctx'}, dimensions={0}, use_global_device_ids=true | all-gather | bytes 160 | tf_op jit(solution)/shard_map/all_gather | solution.py:24
  491.2 2.3 convolution_bitcast_fusion.1
  493.5 32.3 %all-gather.16.cloned.1.call-done = bf16[64,64,256]{2,1,0:T(8,128)(2,1)} async-done(((bf16[16,64,256]{2,1,0:T(8,128)(2,1)}), bf16[64,64,256]{2,1,0:T(8,128)(2,1)}) %all-gather.16.cloned.1.call-update) | async-done | bytes 2097168 | tf_op jit(solution)/shard_map/all_gather | solution.py:24
  525.8 5.4 while.38
  532.1 177.9 %all-gather.14.cloned.1.call-done = bf16[1024,5120]{1,0:T(8,128)(2,1)} async-done(((bf16[1024,1280]{1,0:T(8,128)(2,1)}), bf16[1024,5120]{1,0:T(8,128)(2,1)}) %all-gather.14.cloned.1.call-update) | async-done | bytes 10485776 | tf_op jit(solution)/shard_map/all_gather | solution.py:236
  710.0 6.6 convolution_convert_fusion
  718.0 10.3 %psum.85 = bf16[128,64]{0,1:T(8,128)(2,1)S(1)} all-reduce(bf16[128,64]{0,1:T(8,128)(2,1)S(1)} %fusion.5), channel_id=1, replica_groups=mesh['groups'=2,'ctx'=4,'tp'=2,'dp'=2] {'tp','dp'}, use_global_device_ids=true, to_apply=%region_19.20 | all-reduce | flops 8192 | bytes 32768 | tf_op jit(solution)/shard_map/psum | solution.py:246
  728.2 12.0 %reduce-scatter.2.cloned.1.call-done = bf16[128,1280]{1,0:T(8,128)(2,1)} async-done(((bf16[128,5120]{1,0:T(8,128)(2,1)}), bf16[128,1280]{1,0:T(8,128)(2,1)}) %reduce-scatter.2.cloned.1.call-update) | async-done | bytes 327696 | tf_op jit(solution)/shard_map/reduce_scatter | solution.py:239
  740.3 2.0 fusion.2
  (154 shorter events, 55.8 us)
Async XLA Ops:
  7.4 0.7 copy-start
  8.7 9.6 %copy-start.4 = (bf16[2,64,128]{2,1,0:T(8,128)(2,1)S(1)}, bf16[2,64,128]{2,1,0:T(8,128)(2,1)}, u32[]{:S(2)}) copy-start(bf16[2,64,128]{2,1,0:T(8,128)(2,1)} %get-tuple-element.642) | copy-start | bytes 98308 | tf_op jit(solution)/shard_map/while
  8.7 51.0 %all-reduce.5.cloned.1.call-start = ((), (), s32[]{:S(2)}) async-start(), calls=%async_computation.7 | async-start | bytes 1179648 | tf_op jit(solution)/shard_map/while/body/eval_jaxpr/psum | solution.py:12
  64.0 9.5 %copy-start.4 = (bf16[2,64,128]{2,1,0:T(8,128)(2,1)S(1)}, bf16[2,64,128]{2,1,0:T(8,128)(2,1)}, u32[]{:S(2)}) copy-start(bf16[2,64,128]{2,1,0:T(8,128)(2,1)} %get-tuple-element.642) | copy-start | bytes 98308 | tf_op jit(solution)/shard_map/while
  64.1 49.3 %all-reduce.5.cloned.1.call-start = ((), (), s32[]{:S(2)}) async-start(), calls=%async_computation.7 | async-start | bytes 1179648 | tf_op jit(solution)/shard_map/while/body/eval_jaxpr/psum | solution.py:12
  117.7 9.5 %copy-start.4 = (bf16[2,64,128]{2,1,0:T(8,128)(2,1)S(1)}, bf16[2,64,128]{2,1,0:T(8,128)(2,1)}, u32[]{:S(2)}) copy-start(bf16[2,64,128]{2,1,0:T(8,128)(2,1)} %get-tuple-element.642) | copy-start | bytes 98308 | tf_op jit(solution)/shard_map/while
  117.7 49.3 %all-reduce.5.cloned.1.call-start = ((), (), s32[]{:S(2)}) async-start(), calls=%async_computation.7 | async-start | bytes 1179648 | tf_op jit(solution)/shard_map/while/body/eval_jaxpr/psum | solution.py:12
  171.4 9.5 %copy-start.4 = (bf16[2,64,128]{2,1,0:T(8,128)(2,1)S(1)}, bf16[2,64,128]{2,1,0:T(8,128)(2,1)}, u32[]{:S(2)}) copy-start(bf16[2,64,128]{2,1,0:T(8,128)(2,1)} %get-tuple-element.642) | copy-start | bytes 98308 | tf_op jit(solution)/shard_map/while
  171.4 49.3 %all-reduce.5.cloned.1.call-start = ((), (), s32[]{:S(2)}) async-start(), calls=%async_computation.7 | async-start | bytes 1179648 | tf_op jit(solution)/shard_map/while/body/eval_jaxpr/psum | solution.py:12
  225.1 30.7 %all-gather.8.cloned.1.call-start = ((), (), s32[]{:S(2)}) async-start(), calls=%async_computation.1 | async-start | bytes 1638400 | tf_op jit(solution)/shard_map/all_gather | solution.py:178
  225.7 53.0 %all-gather.12.cloned.1.call-start = ((), (), s32[]{:S(2)}) async-start(), calls=%async_computation.3 | async-start | bytes 1638400 | tf_op jit(solution)/shard_map/all_gather | solution.py:181
  226.2 0.7 copy-start.11
  226.3 3.4 copy-start.12
  226.3 3.4 copy-start.2
  226.3 236.7 %all-gather.10.cloned.1.call-start = ((), (), s32[]{:S(2)}) async-start(), calls=%async_computation.2 | async-start | bytes 13107200 | tf_op jit(solution)/shard_map/all_gather | solution.py:180
  226.9 14.0 %copy-start.5 = (bf16[1280,16]{0,1:T(8,128)(2,1)S(1)}, bf16[1280,16]{0,1:T(8,128)(2,1)}, u32[]{:S(2)}) copy-start(bf16[1280,16]{0,1:T(8,128)(2,1)} %param.29) | copy-start | bytes 122884
  226.9 27.6 %copy-start.7 = (f32[4,1024]{1,0:T(4,128)S(1)}, f32[4,1024]{1,0:T(4,128)}, u32[]{:S(2)}) copy-start(f32[4,1024]{1,0:T(4,128)} %param.30) | copy-start | bytes 49156
  226.9 27.6 %copy-start.8 = (f32[4,128]{1,0:T(4,128)S(1)}, f32[4,128]{1,0:T(4,128)}, u32[]{:S(2)}) copy-start(f32[4,128]{1,0:T(4,128)} %param.31) | copy-start | bytes 6148
  226.9 298.9 %all-gather.16.cloned.1.call-start = ((), (), s32[]{:S(2)}) async-start(), calls=%async_computation.6 | async-start | bytes 2621440 | tf_op jit(solution)/shard_map/all_gather | solution.py:24
  229.7 26.1 %copy-start.9 = (f32[16]{0:T(128)S(1)}, f32[16]{0:T(128)}, u32[]{:S(2)}) copy-start(f32[16]{0:T(128)} %param.32) | copy-start | bytes 196
  255.8 22.8 %copy-start.1 = (bf16[128,5120]{1,0:T(8,128)(2,1)S(1)}, bf16[128,5120]{1,0:T(8,128)(2,1)}, u32[]{:S(2)}) copy-start(bf16[128,5120]{1,0:T(8,128)(2,1)} %all-gather.8.cloned.1.call-done) | copy-start | bytes 3932164
  468.6 2.7 collective-permute-start
  479.0 231.0 %all-gather.14.cloned.1.call-start = ((), (), s32[]{:S(2)}) async-start(), calls=%async_computation.4 | async-start | bytes 13107200 | tf_op jit(solution)/shard_map/all_gather | solution.py:236
  479.8 260.5 %reduce-scatter.2.cloned.1.call-start = ((), (), s32[]{:S(2)}) async-start(), calls=%async_computation.5 | async-start | bytes 1638400 | tf_op jit(solution)/shard_map/reduce_scatter | solution.py:239
  525.8 5.4 copy-start.10
  531.2 0.7 copy-start.6
  716.6 1.0 copy-start.3
Sparse Core Ops, SparseCore 0:
  18.4 41.2 all-reduce.4
  73.7 39.6 all-reduce.4
  127.4 39.6 all-reduce.4
  181.1 39.6 all-reduce.4
Sparse Core Ops, SparseCore 1:
  227.1 16.5 all-gather.7
  245.1 33.5 all-gather.11
  280.1 182.8 all-gather.9
  479.1 46.6 all-gather.15
  527.4 182.5 all-gather.13
  716.7 23.5 reduce-scatter.1
where the time goes:
time: 754 us; the launch traced here: 749 us
  waiting for transfers between devices  519 us (69%)
  blocking collectives  122 us (16%)
  other arithmetic  34.3 us (5%)
  matrix products  23.5 us (3%)
  local copies, waits for them, and re-layouts  22.5 us (3%)
  between operations  16.1 us (2%)
  loops' own time  10.7 us (1%)
    all_gather x1, waiting for transfers between devices, body(): lax.all_gather(xchan_input_weight, 'ctx', axis=0, tiled=True)  182 us
    all_gather x1, waiting for transfers between devices, body(): lax.all_gather(output_weight, 'ctx', axis=1, tiled=True)  178 us
    psum x4, waiting for transfers between devices, from_root(): return lax.psum(block, axis)  89.7 us
    psum x4, blocking collectives, from_root(): return lax.psum(block, axis)  70.9 us
    all_gather x1, waiting for transfers between devices, prefix(): lax.all_gather(part.astype(kind), axis)  32.3 us
    all_gather x1, waiting for transfers between devices, body(): lax.all_gather(bc_input_weight, 'ctx', axis=0, tiled=True)  20.5 us
    dynamic_update_slice x20, local copies, waits for them, and re-layouts, fetch(): lax.dynamic_update_index_in_dim(stack, panel, request_item, along)  17.5 us
  transfers between devices with their start and end apart: 11, of which 10 were waited for; matrix products, arithmetic and copies ran while one was open for 2% of the time, Pallas kernels for 0%

commit v1 on v0

--- a/solution.py
+++ b/solution.py
@@ -85,7 +85,7 @@
     return (values[:, None, :] * onehot_b[:, :, None]).reshape(values.shape[0], -1)
 
 
-def body(
+def general_body(
     tokens,
     lengths,
     request_adapter_ids,
@@ -250,7 +250,165 @@
     return (base + adapter_term).astype(jnp.bfloat16)
 
 
+def transposed(block):
+    side = lax.axis_size("ctx")
+    pairs = [(row * side + col, col * side + row) for row in range(side) for col in range(side)]
+    return lax.ppermute(block, ("ctx", "tp", "dp"), pairs)
+
+
+def owned_rows(values, owned):
+    return jnp.concatenate(
+        [values * owned[:, i : i + 1].astype(values.dtype) for i in range(owned.shape[1])], axis=1
+    )
+
+
+def square_body(
+    tokens,
+    lengths,
+    request_adapter_ids,
+    adapter_store_slot,
+    xchan_input_weight,
+    bc_input_weight,
+    step_input_weight,
+    convolution_x_taps,
+    convolution_bc_taps,
+    step_bias,
+    decay_log_rate,
+    head_skip_gain,
+    output_norm_gain,
+    output_weight,
+    adapter_down_input,
+    adapter_up_xchan,
+    adapter_up_bc,
+    adapter_down_output,
+    adapter_up_output,
+):
+    length = tokens.shape[0]
+    side = lax.axis_size("ctx")
+    stream = side * length
+    taps = convolution_x_taps.shape[0]
+    bank_entries = adapter_down_input.shape[0]
+    rank_value = adapter_down_input.shape[2]
+    head_count = step_bias.shape[0]
+    channels = xchan_input_weight.shape[1]
+    bc_width = bc_input_weight.shape[1]
+    here = lax.axis_index("ctx")
+    lane = lax.axis_index(("tp", "dp"))
+    start_pos = here * length
+    request_ends = jnp.cumsum(lengths, dtype=jnp.int32)
+    every_position = jnp.arange(stream, dtype=jnp.int32)
+    every_segment = segment_of(every_position, request_ends)
+    slot_indices = adapter_store_slot[request_adapter_ids]
+    request_count = lengths.shape[0]
+    stream_onehot = every_segment[:, None] == jnp.arange(request_count, dtype=jnp.int32)[None, :]
+    slot_of_position = jnp.sum(
+        jnp.where(stream_onehot, slot_indices[None, :], 0), axis=1, dtype=jnp.int32
+    )
+    entry_ids = jnp.arange(bank_entries, dtype=jnp.int32)[None, :]
+    owned_here = slot_of_position[:, None] == here * bank_entries + entry_ids
+    owned_lane = slot_of_position[:, None] == lane * bank_entries + entry_ids
+    positions = start_pos + jnp.arange(length, dtype=jnp.int32)
+    segment = segment_of(positions, request_ends)
+    previous = segment_of(jnp.reshape(start_pos - 1, (1,)), request_ends)[0]
+
+    stream_rows = lax.all_gather(transposed(tokens), ("tp", "dp"), axis=0, tiled=True)
+    down_in_t = transposed(adapter_down_input)
+    up_out_t = transposed(adapter_up_output)
+    down_part = jnp.einsum(
+        "pf,efr->per", stream_rows, down_in_t, preferred_element_type=jnp.float32
+    )
+    down_pick = jnp.sum(
+        down_part * owned_lane[:, :, None].astype(jnp.float32), axis=1
+    )
+    rank_hidden = lax.psum(down_pick, ("ctx", "tp", "dp"))
+    hidden_wide = owned_rows(rank_hidden, owned_here).astype(jnp.bfloat16)
+    xchan_part = jnp.dot(
+        stream_rows, xchan_input_weight, preferred_element_type=jnp.float32
+    ) + jnp.dot(
+        hidden_wide,
+        adapter_up_xchan.reshape(bank_entries * rank_value, -1),
+        preferred_element_type=jnp.float32,
+    )
+    bc_part = jnp.dot(stream_rows, bc_input_weight, preferred_element_type=jnp.float32) + jnp.dot(
+        hidden_wide,
+        adapter_up_bc.reshape(bank_entries * rank_value, -1),
+        preferred_element_type=jnp.float32,
+    )
+    step_part = jnp.dot(stream_rows, step_input_weight, preferred_element_type=jnp.float32)
+    summed = lax.psum_scatter(
+        jnp.concatenate([xchan_part, bc_part, step_part], axis=1),
+        "ctx",
+        scatter_dimension=0,
+        tiled=True,
+    )
+    values = summed[:, : channels + bc_width]
+    step_raw = summed[:, channels + bc_width :]
+
+    kernel = jnp.concatenate([convolution_x_taps, convolution_bc_taps], axis=1)
+    tail_rows = passed_along(values[length - (taps - 1) :], "ctx", 1)
+    extended = jnp.concatenate([tail_rows, values], axis=0)
+    extended_segment = segment_of(
+        start_pos - (taps - 1) + jnp.arange(length + taps - 1, dtype=jnp.int32), request_ends
+    )
+    convolved = jnp.zeros_like(values)
+    for tap in range(taps):
+        keep = (extended_segment[tap : tap + length] == segment).astype(jnp.float32)
+        convolved = convolved + kernel[tap][None, :] * extended[tap : tap + length] * keep[:, None]
+    act = jax.nn.silu(convolved)
+    x_heads = act[:, :channels].reshape(length, head_count, -1)
+    bc_local = act[:, channels:].astype(jnp.bfloat16)
+    bc_all = lax.all_gather(bc_local, ("tp", "dp"), axis=1, tiled=True)
+    state_width = bc_all.shape[1] // 2
+    b_proj = bc_all[:, :state_width]
+    c_proj = bc_all[:, state_width:]
+    step_size = jax.nn.softplus(step_raw + step_bias[None, :])
+    log_decay = -step_size * jnp.exp(decay_log_rate)[None, :]
+    inner_out, local_state, enter_weight, carry_decay = span_parts(
+        x_heads, b_proj, c_proj, step_size, log_decay, segment, previous
+    )
+
+    def compose(earlier, later):
+        return (earlier[0] * later[0], later[0][:, None, None] * earlier[1] + later[1])
+
+    carried = prefix(
+        (carry_decay, local_state),
+        "ctx",
+        compose,
+        (jnp.ones_like(carry_decay), jnp.zeros_like(local_state)),
+    )
+    entering = carried[1]
+    entered = (
+        jnp.einsum("tn,hdn->thd", c_proj.astype(jnp.float32), entering, precision=FULL_PRECISION)
+        * enter_weight[:, :, None]
+    )
+    mixer_out = (inner_out + entered + head_skip_gain[None, :, None] * x_heads).reshape(
+        length, channels
+    )
+    scale = lax.rsqrt(jnp.mean(mixer_out * mixer_out, axis=1, keepdims=True) + NORM_EPSILON)
+    normalized_rows = (mixer_out * scale * output_norm_gain[None, :]).astype(jnp.bfloat16)
+
+    normed_stream = lax.all_gather(normalized_rows, "ctx", axis=0, tiled=True)
+    out_down_part = jnp.einsum(
+        "pc,ecr->per", normed_stream, adapter_down_output, preferred_element_type=jnp.float32
+    )
+    out_down_pick = jnp.sum(out_down_part * owned_here[:, :, None].astype(jnp.float32), axis=1)
+    rank_hidden_output = lax.psum(out_down_pick, ("ctx", "tp", "dp"))
+    base_part = jnp.dot(
+        normed_stream, output_weight, preferred_element_type=jnp.float32
+    ).astype(jnp.bfloat16).astype(jnp.float32)
+    adapter_part = jnp.dot(
+        owned_rows(rank_hidden_output, owned_lane).astype(jnp.bfloat16),
+        up_out_t.reshape(bank_entries * rank_value, -1),
+        preferred_element_type=jnp.float32,
+    )
+    mixed_t = lax.psum_scatter(
+        base_part + adapter_part, ("tp", "dp"), scatter_dimension=0, tiled=True
+    ).astype(jnp.bfloat16)
+    return transposed(mixed_t)
+
+
 def solution(mesh):
+    body = square_body if mesh.shape["ctx"] == mesh.shape["tp"] * mesh.shape["dp"] else general_body
     placed = (
         P(("groups", "ctx"), ("tp", "dp")),
         P("groups"),

time: 754 us -> 478 us (0.63)
  waiting for transfers between devices: 519 us -> 365 us
  blocking collectives: 122 us -> 16.6 us
  starting transfers between devices: 1.54 us -> 17.6 us
  local copies, waits for them, and re-layouts: 22.5 us -> 9.99 us
  loops' own time: 10.7 us -> 0.01 us
  other arithmetic: 34.3 us -> 26.5 us
    all_gather x4 -> x2, waiting for transfers between devices: 381 us -> 33.7 us  [the longest x1 30.3 us: square_body(): normed_stream = lax.all_gather(normalized_rows, 'ctx', axis=0, tiled=True)]
    psum x6 -> x0, blocking collectives: 92 us -> none  [the longest x4 70.9 us: from_root(): return lax.psum(block, axis)]
    psum x4 -> x2, waiting for transfers between devices: 89.7 us -> 172 us  [the longest x1 86.6 us: square_body(): rank_hidden = lax.psum(down_pick, ('ctx', 'tp', 'dp'))]
    reduce_scatter x1 -> x2, waiting for transfers between devices: 12 us -> 82.6 us  [the longest x1 46.7 us: square_body(): lax.psum_scatter(jnp.concatenate([xchan_part, bc_part, step_part], axis=1...]
    ppermute x0 -> x4, waiting for transfers between devices: none -> 43 us  [transposed(): return lax.ppermute(block, ('ctx', 'tp', 'dp'), pairs)]
    dynamic_update_slice x20 -> x0, local copies, waits for them, and re-layouts: 17.5 us -> none  [fetch(): lax.dynamic_update_index_in_dim(stack, panel, request_item, along)]
    ppermute x0 -> x4, starting transfers between devices: none -> 15.1 us  [transposed(): return lax.ppermute(block, ('ctx', 'tp', 'dp'), pairs)]
    all_gather x2 -> x1, blocking collectives: 19.1 us -> 5.43 us  [square_body(): bc_all = lax.all_gather(bc_local, ('tp', 'dp'), axis=1, tiled=True)]
  transfers between devices with their start and end apart: 11 -> 12, of which waited for: 10 -> 11; matrix products, arithmetic and copies ran while one was open for 2% -> 4% of each run, Pallas kernels for 0% -> 0%
where the time goes in v1:
time: 478 us; the launch traced here: 477 us
  waiting for transfers between devices  365 us (76%)
  other arithmetic  26.5 us (6%)
  matrix products  25.9 us (5%)
  starting transfers between devices  17.6 us (4%)
  blocking collectives  16.6 us (3%)
  between operations  15.1 us (3%)
  local copies, waits for them, and re-layouts  9.99 us (2%)
    psum x1, waiting for transfers between devices, square_body(): rank_hidden = lax.psum(down_pick, ('ctx', 'tp', 'dp'))  86.6 us
    psum x1, waiting for transfers between devices, square_body(): rank_hidden_output = lax.psum(out_down_pick, ('ctx', 'tp', 'dp'))  85.4 us
    reduce_scatter x1, waiting for transfers between devices, square_body(): lax.psum_scatter(jnp.concatenate([xchan_part, bc_part, step_part], axis=1...  46.7 us
    ppermute x4, waiting for transfers between devices, transposed(): return lax.ppermute(block, ('ctx', 'tp', 'dp'), pairs)  43 us
    reduce_scatter x1, waiting for transfers between devices, square_body(): lax.psum_scatter(base_part + adapter_part, ('tp', 'dp'), scatter_dimensio...  35.9 us
    all_gather x1, waiting for transfers between devices, prefix(): lax.all_gather(part.astype(kind), axis)  32.7 us
    all_gather x1, waiting for transfers between devices, square_body(): normed_stream = lax.all_gather(normalized_rows, 'ctx', axis=0, tiled=True)  30.3 us
    ppermute x4, starting transfers between devices, transposed(): return lax.ppermute(block, ('ctx', 'tp', 'dp'), pairs)  15.1 us
  transfers between devices with their start and end apart: 12, of which 11 were waited for; matrix products, arithmetic and copies ran while one was open for 4% of the time, Pallas kernels for 0%

profile of v1, /device:TPU:2, one launch (start us, length us, event | category | flops | bytes accessed | tf_op | source)
XLA Modules:
  0.0 476.7 jit_solution(3911669677601614109)
XLA Ops:
  6.5 4.7 collective-permute-start
  11.3 16.6 %collective-permute-done = bf16[128,1280]{1,0:T(8,128)(2,1)S(1)} collective-permute-done((bf16[128,1280]{1,0:T(8,128)(2,1)}, bf16[128,1280]{1,0:T(8,128)(2,1)S(1)}, u32[]{:S(2)}, u32[]{:S(2)}) %collective-permute-start) | collective-permute-done | bytes 327712 | tf_op jit(solution)/shard_map/ppermute | solution.py:256
  28.7 1.9 collective-permute-start.1
  33.7 10.9 %collective-permute-done.1 = bf16[2,1280,64]{1,2,0:T(8,128)(2,1)S(1)} collective-permute-done((bf16[2,1280,64]{1,2,0:T(8,128)(2,1)}, bf16[2,1280,64]{1,2,0:T(8,128)(2,1)S(1)}, u32[]{:S(2)}, u32[]{:S(2)}) %collective-permute-start.1) | collective-permute-done | bytes 327712 | tf_op jit(solution)/shard_map/ppermute | solution.py:256
  44.6 3.4 all-gather.6.cloned.1.call-done
  48.0 1.9 fusion.51
  50.6 1.8 fusion.52
  52.4 86.6 %all-reduce.3.cloned.1.call-done = f32[512,64]{0,1:T(8,128)} async-done(((f32[512,64]{0,1:T(8,128)}), f32[512,64]{0,1:T(8,128)}) %all-reduce.3.cloned.1.call-update) | async-done | bytes 131088 | tf_op jit(solution)/shard_map/psum | solution.py:323
  140.8 3.4 convolution_add_fusion.1
  150.6 46.7 %reduce-scatter.3.cloned.1.call-done = f32[128,1168]{0,1:T(8,128)} async-done(((f32[512,1168]{0,1:T(8,128)}), f32[128,1168]{0,1:T(8,128)}) %reduce-scatter.3.cloned.1.call-update) | async-done | bytes 598032 | tf_op jit(solution)/shard_map/reduce_scatter | solution.py:338
  198.5 2.1 slice.104
  201.9 2.3 collective-permute-start.2
  206.8 3.0 divide_multiply_fusion
  209.9 5.4 %all_gather.20 = bf16[128,512]{0,1:T(8,128)(2,1)S(1)} all-gather(bf16[128,128]{0,1:T(8,128)(2,1)S(1)} %slice.193), channel_id=1, replica_groups=mesh['groups'=2,'ctx'=4,'tp'=2,'dp'=2] {'tp','dp'}, dimensions={1}, use_global_device_ids=true | all-gather | bytes 163840 | tf_op jit(solution)/shard_map/all_gather | solution.py:360
  216.9 11.2 %all-gather.1 = bf16[4,1,16]{2,1,0:T(2,128)(2,1)S(1)} all-gather(bf16[1,1,16]{2,1,0:T(2,128)(2,1)S(1)} %get-tuple-element.145), channel_id=1, replica_groups=mesh['groups'=2,'ctx'=4,'tp'=2,'dp'=2] {'ctx'}, dimensions={0}, use_global_device_ids=true | all-gather | bytes 160 | tf_op jit(solution)/shard_map/all_gather | solution.py:24
  228.5 3.0 convolution_bitcast_fusion
  231.5 32.7 %all-gather.10.cloned.1.call-done = bf16[64,64,256]{2,1,0:T(8,128)(2,1)} async-done(((bf16[16,64,256]{2,1,0:T(8,128)(2,1)}), bf16[64,64,256]{2,1,0:T(8,128)(2,1)}) %all-gather.10.cloned.1.call-update) | async-done | bytes 2097168 | tf_op jit(solution)/shard_map/all_gather | solution.py:24
  264.2 9.9 %while.14 = (s32[]{:T(128)}, f32[16,64,256]{2,1,0:T(8,128)}, s32[]{:T(128)}, bf16[4,16]{1,0:T(4,128)(2,1)S(1)}, bf16[4,16,64,256]{3,2,1,0:T(8,128)(2,1)}, /*index=5*/s32[]{:T(128)}, s32[]{:T(128)}) while((s32[]{:T(128)}, f32[16,64,256]{2,1,0:T(8,128)}, s32[]{:T(128)}, bf16[4,16]{1,0:T(4,128)(2,1)S(1)}, ...), condition=%wide.region_11.12_spmd.clone, body=%wide.region_10.11_spmd.clone.sunk | while | flops 1310740 | bytes 2621705 | solution.py:41
  264.2 2.2 fusion.72
  266.5 2.6 fusion.72
  269.0 2.6 fusion.72
  271.6 2.6 fusion.72
  274.2 3.3 multiply_reduce_fusion
  281.0 3.0 collective-permute-start.3
  284.0 30.3 %all-gather.8.cloned.1.call-done = bf16[512,1024]{1,0:T(8,128)(2,1)} async-done(((bf16[128,1024]{1,0:T(8,128)(2,1)}), bf16[512,1024]{1,0:T(8,128)(2,1)}) %all-gather.8.cloned.1.call-update) | async-done | bytes 1048592 | tf_op jit(solution)/shard_map/all_gather | solution.py:390
  314.3 1.7 fusion.53
  316.8 4.3 fusion.1
  321.0 85.4 %all-reduce.5.cloned.1.call-done = f32[512,64]{0,1:T(8,128)} async-done(((f32[512,64]{0,1:T(8,128)}), f32[512,64]{0,1:T(8,128)}) %all-reduce.5.cloned.1.call-update) | async-done | bytes 131088 | tf_op jit(solution)/shard_map/psum | solution.py:395
  407.3 3.8 convolution_add_fusion
  411.1 35.9 %reduce-scatter.5.cloned.1.call-done = f32[128,1280]{1,0:T(8,128)} async-done(((f32[512,1280]{1,0:T(8,128)}), f32[128,1280]{1,0:T(8,128)}) %reduce-scatter.5.cloned.1.call-update) | async-done | bytes 655376 | tf_op jit(solution)/shard_map/reduce_scatter | solution.py:404
  448.1 5.5 %collective-permute-start.4 = (bf16[128,1280]{1,0:T(8,128)(2,1)S(1)}, bf16[128,1280]{1,0:T(8,128)(2,1)S(1)}, u32[]{:S(2)}, u32[]{:S(2)}) collective-permute-start(bf16[128,1280]{1,0:T(8,128)(2,1)S(1)} %convert_element_type.144), channel_id=1, source_target_pairs={{0,0},{1,4},{2,8},{3,12},{4,1},{5,5},{6,9},{7,13},{8,2},{9,6},{10,... | collective-permute-start | bytes 983048 | tf_op jit(solution)/shard_map/ppermute | solution.py:256
  453.6 15.5 %collective-permute-done.4 = bf16[128,1280]{1,0:T(8,128)(2,1)S(1)} collective-permute-done((bf16[128,1280]{1,0:T(8,128)(2,1)S(1)}, bf16[128,1280]{1,0:T(8,128)(2,1)S(1)}, u32[]{:S(2)}, u32[]{:S(2)}) %collective-permute-start.4) | collective-permute-done | bytes 327712 | tf_op jit(solution)/shard_map/ppermute | solution.py:256
  (100 shorter events, 25.3 us)
Async XLA Ops:
  6.5 310.2 %copy-start = (bf16[1024,1280]{1,0:T(8,128)(2,1)S(1)}, bf16[1024,1280]{1,0:T(8,128)(2,1)}, u32[]{:S(2)}) copy-start(bf16[1024,1280]{1,0:T(8,128)(2,1)} %param.34) | copy-start | bytes 7864324
  6.5 44.1 %copy-start.6 = (bf16[1280,16]{0,1:T(8,128)(2,1)S(1)}, bf16[1280,16]{0,1:T(8,128)(2,1)}, u32[]{:S(2)}) copy-start(bf16[1280,16]{0,1:T(8,128)(2,1)} %param.27) | copy-start | bytes 122884
  6.5 41.5 %all-gather.6.cloned.1.call-start = ((), (), s32[]{:S(2)}) async-start(), calls=%async_computation.2 | async-start | bytes 1638400 | tf_op jit(solution)/shard_map/all_gather | solution.py:314
  6.5 21.3 %collective-permute-start = (bf16[128,1280]{1,0:T(8,128)(2,1)}, bf16[128,1280]{1,0:T(8,128)(2,1)S(1)}, u32[]{:S(2)}, u32[]{:S(2)}) collective-permute-start(bf16[128,1280]{1,0:T(8,128)(2,1)} %param.21), channel_id=1, source_target_pairs={{0,0},{1,4},{2,8},{3,12},{4,1},{5,5},{6,9},{7,13},{8,2},{9,6},{10,... | collective-permute-start | bytes 983048 | tf_op jit(solution)/shard_map/ppermute | solution.py:256
  27.9 0.7 copy-start.2
  28.6 110.4 %all-reduce.3.cloned.1.call-start = ((), (), s32[]{:S(2)}) async-start(), calls=%async_computation.3 | async-start | bytes 262144 | tf_op jit(solution)/shard_map/psum | solution.py:323
  28.7 15.9 %collective-permute-start.1 = (bf16[2,1280,64]{1,2,0:T(8,128)(2,1)}, bf16[2,1280,64]{1,2,0:T(8,128)(2,1)S(1)}, u32[]{:S(2)}, u32[]{:S(2)}) collective-permute-start(bf16[2,1280,64]{1,2,0:T(8,128)(2,1)} %param.35), channel_id=1, source_target_pairs={{0,0},{1,4},{2,8},{3,12},{4,1},{5,5},{6,9},{7,13},{8,2},{9,6},{10,... | collective-permute-start | bytes 983048 | tf_op jit(solution)/shard_map/ppermute | solution.py:256
  33.4 106.6 %copy-start.4 = (bf16[2,64,1024]{2,1,0:T(8,128)(2,1)S(1)}, bf16[2,64,1024]{2,1,0:T(8,128)(2,1)}, u32[]{:S(2)}) copy-start(bf16[2,64,1024]{2,1,0:T(8,128)(2,1)} %param.36) | copy-start | bytes 786436
  50.6 90.0 %copy-start.7 = (bf16[2,64,128]{2,1,0:T(8,128)(2,1)S(1)}, bf16[2,64,128]{2,1,0:T(8,128)(2,1)}, u32[]{:S(2)}) copy-start(bf16[2,64,128]{2,1,0:T(8,128)(2,1)} %param.37) | copy-start | bytes 98308
  50.6 146.8 %reduce-scatter.3.cloned.1.call-start = ((), (), s32[]{:S(2)}) async-start(), calls=%async_computation.4 | async-start | bytes 2990080 | tf_op jit(solution)/shard_map/reduce_scatter | solution.py:338
  139.0 1.8 copy-start.1
  140.8 3.4 copy-start.3
  146.4 0.7 copy-start.11
  146.4 3.3 copy-start.8
  146.4 3.3 copy-start.10
  146.4 51.0 %copy-start.9 = (f32[16]{0:T(128)S(1)}, f32[16]{0:T(128)}, u32[]{:S(2)}) copy-start(f32[16]{0:T(128)} %param.30) | copy-start | bytes 196
  146.4 117.8 %all-gather.10.cloned.1.call-start = ((), (), s32[]{:S(2)}) async-start(), calls=%async_computation.8 | async-start | bytes 2621440 | tf_op jit(solution)/shard_map/all_gather | solution.py:24
  197.4 9.4 %slice-start = ((f32[128,1168]{0,1:T(8,128)}), f32[128,1152]{0,1:T(8,128)S(1)}, s32[]{:S(2)}) async-start(f32[128,1168]{0,1:T(8,128)} %reduce-scatter.3.cloned.1.call-done), calls=%async_computation.9 | async-start | bytes 1179648 | tf_op jit(solution)/shard_map/slice | solution.py:344
  201.9 3.8 collective-permute-start.2
  216.7 97.6 %all-gather.8.cloned.1.call-start = ((), (), s32[]{:S(2)}) async-start(), calls=%async_computation.5 | async-start | bytes 1310720 | tf_op jit(solution)/shard_map/all_gather | solution.py:390
  274.2 40.1 %copy-start.5 = (bf16[2,1024,64]{1,2,0:T(8,128)(2,1)S(1)}, bf16[2,1024,64]{1,2,0:T(8,128)(2,1)}, u32[]{:S(2)}) copy-start(bf16[2,1024,64]{1,2,0:T(8,128)(2,1)} %param.38) | copy-start | bytes 786436
  280.9 125.5 %all-reduce.5.cloned.1.call-start = ((), (), s32[]{:S(2)}) async-start(), calls=%async_computation.6 | async-start | bytes 262144 | tf_op jit(solution)/shard_map/psum | solution.py:395
  281.0 126.3 %collective-permute-start.3 = (bf16[2,64,1280]{2,1,0:T(8,128)(2,1)}, bf16[2,64,1280]{2,1,0:T(8,128)(2,1)S(1)}, u32[]{:S(2)}, u32[]{:S(2)}) collective-permute-start(bf16[2,64,1280]{2,1,0:T(8,128)(2,1)} %param.39), channel_id=1, source_target_pairs={{0,0},{1,4},{2,8},{3,12},{4,1},{5,5},{6,9},{7,13},{8,2},{9,6},{10,... | collective-permute-start | bytes 983048 | tf_op jit(solution)/shard_map/ppermute | solution.py:256
  316.7 130.3 %reduce-scatter.5.cloned.1.call-start = ((), (), s32[]{:S(2)}) async-start(), calls=%async_computation.7 | async-start | bytes 3276800 | tf_op jit(solution)/shard_map/reduce_scatter | solution.py:404
  448.1 21.0 %collective-permute-start.4 = (bf16[128,1280]{1,0:T(8,128)(2,1)S(1)}, bf16[128,1280]{1,0:T(8,128)(2,1)S(1)}, u32[]{:S(2)}, u32[]{:S(2)}) collective-permute-start(bf16[128,1280]{1,0:T(8,128)(2,1)S(1)} %convert_element_type.144), channel_id=1, source_target_pairs={{0,0},{1,4},{2,8},{3,12},{4,1},{5,5},{6,9},{7,13},{8,2},{9,6},{10,... | collective-permute-start | bytes 983048 | tf_op jit(solution)/shard_map/ppermute | solution.py:256
Sparse Core Ops, SparseCore 0:
  28.8 19.1 all-gather.5
  51.4 87.5 all-reduce.2
  146.5 50.7 reduce-scatter.2
  216.8 47.3 all-gather.9
  281.0 33.1 all-gather.7
  317.6 88.7 all-reduce.4
  411.2 35.7 reduce-scatter.4

commit v2 on v1

--- a/solution.py
+++ b/solution.py
@@ -250,10 +250,30 @@
     return (base + adapter_term).astype(jnp.bfloat16)
 
 
+def moved(block, shift, kind):
+    side = lax.axis_size("ctx")
+    if kind == "ctx":
+        pairs = [(a, (a + shift) % side) for a in range(side)]
+        return lax.ppermute(block, "ctx", pairs)
+    if kind == "rows":
+        pairs = [(a * side + b, b * side + (a + shift) % side) for a in range(side) for b in range(side)]
+    else:
+        pairs = [(a * side + b, ((b + shift) % side) * side + a) for a in range(side) for b in range(side)]
+    return lax.ppermute(block, ("ctx", "tp", "dp"), pairs)
+
+
 def transposed(block):
-    side = lax.axis_size("ctx")
-    pairs = [(row * side + col, col * side + row) for row in range(side) for col in range(side)]
-    return lax.ppermute(block, ("ctx", "tp", "dp"), pairs)
+    return moved(block, 0, "rows")
+
+
+def in_order(pieces, place):
+    stacked = jnp.stack(pieces[::-1], axis=0)
+    ordered = jnp.roll(stacked, place + 1, axis=0)
+    return ordered.reshape((-1,) + pieces[0].shape[1:])
+
+
+def block_rows(values, index, length):
+    return lax.dynamic_slice_in_dim(values, index * length, length, 0)
 
 
 def owned_rows(values, owned):
@@ -311,7 +331,7 @@
     segment = segment_of(positions, request_ends)
     previous = segment_of(jnp.reshape(start_pos - 1, (1,)), request_ends)[0]
 
-    stream_rows = lax.all_gather(transposed(tokens), ("tp", "dp"), axis=0, tiled=True)
+    stream_rows = in_order([moved(tokens, s, "rows") for s in range(side)], lane)
     down_in_t = transposed(adapter_down_input)
     up_out_t = transposed(adapter_up_output)
     down_part = jnp.einsum(
@@ -320,7 +340,7 @@
     down_pick = jnp.sum(
         down_part * owned_lane[:, :, None].astype(jnp.float32), axis=1
     )
-    rank_hidden = lax.psum(down_pick, ("ctx", "tp", "dp"))
+    rank_hidden = sum(moved(down_pick, s, "rows") for s in range(side))
     hidden_wide = owned_rows(rank_hidden, owned_here).astype(jnp.bfloat16)
     xchan_part = jnp.dot(
         stream_rows, xchan_input_weight, preferred_element_type=jnp.float32
@@ -335,12 +355,10 @@
         preferred_element_type=jnp.float32,
     )
     step_part = jnp.dot(stream_rows, step_input_weight, preferred_element_type=jnp.float32)
-    summed = lax.psum_scatter(
-        jnp.concatenate([xchan_part, bc_part, step_part], axis=1),
-        "ctx",
-        scatter_dimension=0,
-        tiled=True,
-    )
+    projected = jnp.concatenate([xchan_part, bc_part, step_part], axis=1)
+    summed = block_rows(projected, here, length)
+    for s in range(1, side):
+        summed = summed + moved(block_rows(projected, (here + s) % side, length), s, "ctx")
     values = summed[:, : channels + bc_width]
     step_raw = summed[:, channels + bc_width :]
 
@@ -367,16 +385,14 @@
         x_heads, b_proj, c_proj, step_size, log_decay, segment, previous
     )
 
-    def compose(earlier, later):
-        return (earlier[0] * later[0], later[0][:, None, None] * earlier[1] + later[1])
-
-    carried = prefix(
-        (carry_decay, local_state),
-        "ctx",
-        compose,
-        (jnp.ones_like(carry_decay), jnp.zeros_like(local_state)),
-    )
-    entering = carried[1]
+    entering = jnp.zeros_like(local_state)
+    for s in range(side - 1, 0, -1):
+        pairs = [(a, a + s) for a in range(side - s)]
+        decay_in = lax.ppermute(carry_decay.astype(jnp.bfloat16), "ctx", pairs)
+        state_in = lax.ppermute(local_state.astype(jnp.bfloat16), "ctx", pairs)
+        entering = decay_in.astype(jnp.float32)[:, None, None] * entering + state_in.astype(
+            jnp.float32
+        )
     entered = (
         jnp.einsum("tn,hdn->thd", c_proj.astype(jnp.float32), entering, precision=FULL_PRECISION)
         * enter_weight[:, :, None]
@@ -387,12 +403,14 @@
     scale = lax.rsqrt(jnp.mean(mixer_out * mixer_out, axis=1, keepdims=True) + NORM_EPSILON)
     normalized_rows = (mixer_out * scale * output_norm_gain[None, :]).astype(jnp.bfloat16)
 
-    normed_stream = lax.all_gather(normalized_rows, "ctx", axis=0, tiled=True)
+    normed_stream = in_order(
+        [normalized_rows] + [moved(normalized_rows, s, "ctx") for s in range(1, side)], here
+    )
     out_down_part = jnp.einsum(
         "pc,ecr->per", normed_stream, adapter_down_output, preferred_element_type=jnp.float32
     )
     out_down_pick = jnp.sum(out_down_part * owned_here[:, :, None].astype(jnp.float32), axis=1)
-    rank_hidden_output = lax.psum(out_down_pick, ("ctx", "tp", "dp"))
+    rank_hidden_output = sum(moved(out_down_pick, s, "cols") for s in range(side))
     base_part = jnp.dot(
         normed_stream, output_weight, preferred_element_type=jnp.float32
     ).astype(jnp.bfloat16).astype(jnp.float32)
@@ -401,10 +419,11 @@
         up_out_t.reshape(bank_entries * rank_value, -1),
         preferred_element_type=jnp.float32,
     )
-    mixed_t = lax.psum_scatter(
-        base_part + adapter_part, ("tp", "dp"), scatter_dimension=0, tiled=True
-    ).astype(jnp.bfloat16)
-    return transposed(mixed_t)
+    out_part = base_part + adapter_part
+    mixed = sum(
+        moved(block_rows(out_part, (lane + s) % side, length), s, "cols") for s in range(side)
+    )
+    return mixed.astype(jnp.bfloat16)
 
 
 def solution(mesh):

time: 478 us -> 361 us (0.76)
  waiting for transfers between devices: 365 us -> 214 us
  starting transfers between devices: 17.6 us -> 90.1 us
  other arithmetic: 26.5 us -> 13.2 us
  between operations: 15.1 us -> 2 us
  matrix products: 25.9 us -> 14.7 us
  blocking collectives: 16.6 us -> 5.43 us
  local copies, waits for them, and re-layouts: 9.99 us -> 19.8 us
    psum x2 -> x0, waiting for transfers between devices: 172 us -> none  [the longest x1 86.6 us: square_body(): rank_hidden = lax.psum(down_pick, ('ctx', 'tp', 'dp'))]
    ppermute x4 -> x30, waiting for transfers between devices: 43 us -> 214 us  [the longest x18 116 us: moved(): return lax.ppermute(block, ('ctx', 'tp', 'dp'), pairs)]
    reduce_scatter x2 -> x0, waiting for transfers between devices: 82.6 us -> none  [the longest x1 46.7 us: square_body(): lax.psum_scatter(jnp.concatenate([xchan_part, bc_part, step_part], axis=1...]
    ppermute x4 -> x30, starting transfers between devices: 15.1 us -> 88.8 us  [the longest x18 56 us: moved(): return lax.ppermute(block, ('ctx', 'tp', 'dp'), pairs)]
    all_gather x3 -> x0, waiting for transfers between devices: 66.4 us -> none  [the longest x1 32.7 us: prefix(): lax.all_gather(part.astype(kind), axis)]
    all_gather x1 -> x0, blocking collectives: 11.2 us -> none  [prefix(): lax.all_gather(part.astype(kind), axis)]
    select_n x4 -> x0, other arithmetic: 9.92 us -> none  [lap(): return jax.tree.map(lambda a, b: jnp.where(reached, a, b), new, before)]
    unnamed x27 -> x42, local copies, waits for them, and re-layouts: 2.07 us -> 8.04 us
  transfers between devices with their start and end apart: 12 -> 31, of which waited for: 11 -> 17; matrix products, arithmetic and copies ran while one was open for 4% -> 9% of each run, Pallas kernels for 0% -> 0%
where the time goes in v2:
time: 361 us; the launch traced here: 360 us
  waiting for transfers between devices  214 us (59%)
  starting transfers between devices  90.1 us (25%)
  local copies, waits for them, and re-layouts  19.8 us (5%)
  matrix products  14.7 us (4%)
  other arithmetic  13.2 us (4%)
  blocking collectives  5.43 us (2%)
    ppermute x18, waiting for transfers between devices, moved(): return lax.ppermute(block, ('ctx', 'tp', 'dp'), pairs)  116 us
    ppermute x6, waiting for transfers between devices, moved(): return lax.ppermute(block, 'ctx', pairs)  71.2 us
    ppermute x18, starting transfers between devices, moved(): return lax.ppermute(block, ('ctx', 'tp', 'dp'), pairs)  56 us
    ppermute x3, waiting for transfers between devices, square_body(): state_in = lax.ppermute(local_state.astype(jnp.bfloat16), 'ctx', pairs)  27.1 us
    ppermute x6, starting transfers between devices, moved(): return lax.ppermute(block, 'ctx', pairs)  20.5 us
    unnamed x42, local copies, waits for them, and re-layouts  8.04 us
  transfers between devices with their start and end apart: 31, of which 17 were waited for; matrix products, arithmetic and copies ran while one was open for 9% of the time, Pallas kernels for 0%

profile of v2, /device:TPU:2, one launch (start us, length us, event | category | flops | bytes accessed | tf_op | source)
XLA Modules:
  0.0 359.6 jit_solution(9221994332203433111)
XLA Ops:
  0.0 2.0 collective-permute-start
  2.8 6.7 %collective-permute-start.3 = (bf16[128,1280]{1,0:T(8,128)(2,1)}, bf16[128,1280]{1,0:T(8,128)(2,1)}, u32[]{:S(2)}, u32[]{:S(2)}) collective-permute-start(bf16[128,1280]{1,0:T(8,128)(2,1)} %param.19), channel_id=1, source_target_pairs={{0,0},{1,4},{2,8},{3,12},{4,1},{5,5},{6,9},{7,13},{8,2},{9,6},{10,... | collective-permute-start | bytes 983048 | tf_op jit(solution)/shard_map/ppermute | solution.py:262
  18.6 5.6 %collective-permute-done.2 = bf16[128,1280]{1,0:T(8,128)(2,1)} collective-permute-done((bf16[128,1280]{1,0:T(8,128)(2,1)}, bf16[128,1280]{1,0:T(8,128)(2,1)}, u32[]{:S(2)}, u32[]{:S(2)}) %collective-permute-start.2) | collective-permute-done | bytes 327712 | tf_op jit(solution)/shard_map/ppermute | solution.py:262
  25.2 42.4 %collective-permute-done.3 = bf16[128,1280]{1,0:T(8,128)(2,1)} collective-permute-done((bf16[128,1280]{1,0:T(8,128)(2,1)}, bf16[128,1280]{1,0:T(8,128)(2,1)}, u32[]{:S(2)}, u32[]{:S(2)}) %collective-permute-start.3) | collective-permute-done | bytes 327712 | tf_op jit(solution)/shard_map/ppermute | solution.py:262
  70.8 3.3 collective-permute-done.4
  75.7 6.0 %collective-permute-start.7 = (f32[512,64]{0,1:T(8,128)S(1)}, f32[512,64]{0,1:T(8,128)S(1)}, u32[]{:S(2)}, u32[]{:S(2)}) collective-permute-start(f32[512,64]{0,1:T(8,128)S(1)} %multiply_reduce_fusion.2), channel_id=1, source_target_pairs={{0,2},{1,6},{2,10},{3,14},{4,3},{5,7},{6,11},{7,15},{8,0},{9,4},{1... | collective-permute-start | bytes 393224 | tf_op jit(solution)/shard_map/ppermute | solution.py:262
  83.6 3.7 %collective-permute-start.6 = (f32[512,64]{0,1:T(8,128)S(1)}, f32[512,64]{0,1:T(8,128)S(1)}, u32[]{:S(2)}, u32[]{:S(2)}) collective-permute-start(f32[512,64]{0,1:T(8,128)S(1)} %multiply_reduce_fusion.2), channel_id=1, source_target_pairs={{0,1},{1,5},{2,9},{3,13},{4,2},{5,6},{6,10},{7,14},{8,3},{9,7},{10... | collective-permute-start | bytes 393224 | tf_op jit(solution)/shard_map/ppermute | solution.py:262
  87.7 9.1 %collective-permute-done.5 = f32[512,64]{0,1:T(8,128)S(1)} collective-permute-done((f32[512,64]{0,1:T(8,128)S(1)}, f32[512,64]{0,1:T(8,128)S(1)}, u32[]{:S(2)}, u32[]{:S(2)}) %collective-permute-start.5) | collective-permute-done | bytes 131104 | tf_op jit(solution)/shard_map/ppermute | solution.py:262
  103.4 3.0 collective-permute-start.11
  106.4 2.4 collective-permute-start.10
  111.0 10.5 %collective-permute-done.11 = f32[128,1168]{0,1:T(8,128)S(1)} collective-permute-done((f32[128,1168]{0,1:T(8,128)}, f32[128,1168]{0,1:T(8,128)S(1)}, u32[]{:S(2)}, u32[]{:S(2)}) %collective-permute-start.11) | collective-permute-done | bytes 598048 | tf_op jit(solution)/shard_map/ppermute | solution.py:257
  121.5 40.2 %collective-permute-done.10 = f32[128,1168]{0,1:T(8,128)} collective-permute-done((f32[128,1168]{0,1:T(8,128)}, f32[128,1168]{0,1:T(8,128)}, u32[]{:S(2)}, u32[]{:S(2)}) %collective-permute-start.10) | collective-permute-done | bytes 598048 | tf_op jit(solution)/shard_map/ppermute | solution.py:257
  174.7 3.3 divide_multiply_fusion
  178.0 5.4 %all_gather.3 = bf16[128,512]{0,1:T(8,128)(2,1)S(1)} all-gather(bf16[128,128]{0,1:T(8,128)(2,1)S(1)} %slice.194), channel_id=1, replica_groups=mesh['groups'=2,'ctx'=4,'tp'=2,'dp'=2] {'tp','dp'}, dimensions={1}, use_global_device_ids=true | all-gather | bytes 163840 | tf_op jit(solution)/shard_map/all_gather | solution.py:378
  184.1 4.2 %collective-permute-start.18 = (bf16[16,64,256]{2,1,0:T(8,128)(2,1)S(1)}, bf16[16,64,256]{2,1,0:T(8,128)(2,1)S(1)}, u32[]{:S(2)}, u32[]{:S(2)}) collective-permute-start(bf16[16,64,256]{2,1,0:T(8,128)(2,1)S(1)} %convolution_convert_fusion.1), channel_id=1, source_target_pairs={{0,4},{4,8},{8,12},{1,5},{5,9},{9,13},{2,6},{6,10},{10,14},{3,7},{... | collective-permute-start | bytes 1572872 | tf_op jit(solution)/shard_map/ppermute | solution.py:392
  193.1 2.2 convolution_bitcast_fusion
  195.3 5.2 %collective-permute-done.18 = bf16[16,64,256]{2,1,0:T(8,128)(2,1)S(1)} collective-permute-done((bf16[16,64,256]{2,1,0:T(8,128)(2,1)S(1)}, bf16[16,64,256]{2,1,0:T(8,128)(2,1)S(1)}, u32[]{:S(2)}, u32[]{:S(2)}) %collective-permute-start.18) | collective-permute-done | bytes 524320 | tf_op jit(solution)/shard_map/ppermute | solution.py:392
  200.5 11.3 %collective-permute-done.17 = bf16[16,64,256]{2,1,0:T(8,128)(2,1)S(1)} collective-permute-done((bf16[16,64,256]{2,1,0:T(8,128)(2,1)S(1)}, bf16[16,64,256]{2,1,0:T(8,128)(2,1)S(1)}, u32[]{:S(2)}, u32[]{:S(2)}) %collective-permute-start.17) | collective-permute-done | bytes 524320 | tf_op jit(solution)/shard_map/ppermute | solution.py:392
  211.8 10.7 %collective-permute-done.16 = bf16[16,64,256]{2,1,0:T(8,128)(2,1)S(1)} collective-permute-done((bf16[16,64,256]{2,1,0:T(8,128)(2,1)S(1)}, bf16[16,64,256]{2,1,0:T(8,128)(2,1)S(1)}, u32[]{:S(2)}, u32[]{:S(2)}) %collective-permute-start.16) | collective-permute-done | bytes 524320 | tf_op jit(solution)/shard_map/ppermute | solution.py:392
  224.3 14.3 %collective-permute-start.19 = (bf16[128,1024]{0,1:T(8,128)(2,1)}, bf16[128,1024]{0,1:T(8,128)(2,1)S(1)}, u32[]{:S(2)}, u32[]{:S(2)}) collective-permute-start(bf16[128,1024]{0,1:T(8,128)(2,1)} %fusion.31), channel_id=1, source_target_pairs={{0,12},{4,0},{8,4},{12,8},{1,13},{5,1},{9,5},{13,9},{2,14},{6,2},{... | collective-permute-start | bytes 786440 | tf_op jit(solution)/shard_map/ppermute | solution.py:257
  241.2 4.4 %collective-permute-done.19 = bf16[128,1024]{0,1:T(8,128)(2,1)S(1)} collective-permute-done((bf16[128,1024]{0,1:T(8,128)(2,1)}, bf16[128,1024]{0,1:T(8,128)(2,1)S(1)}, u32[]{:S(2)}, u32[]{:S(2)}) %collective-permute-start.19) | collective-permute-done | bytes 262176 | tf_op jit(solution)/shard_map/ppermute | solution.py:257
  245.7 15.2 %collective-permute-done.20 = bf16[128,1024]{0,1:T(8,128)(2,1)} collective-permute-done((bf16[128,1024]{0,1:T(8,128)(2,1)}, bf16[128,1024]{0,1:T(8,128)(2,1)}, u32[]{:S(2)}, u32[]{:S(2)}) %collective-permute-start.20) | collective-permute-done | bytes 262176 | tf_op jit(solution)/shard_map/ppermute | solution.py:257
  265.3 2.3 copy.95
  269.4 14.3 %collective-permute-start.24 = (f32[512,64]{0,1:T(8,128)S(1)}, f32[512,64]{0,1:T(8,128)S(1)}, u32[]{:S(2)}, u32[]{:S(2)}) collective-permute-start(f32[512,64]{0,1:T(8,128)S(1)} %multiply_reduce_fusion.1), channel_id=1, source_target_pairs={{0,8},{1,12},{2,0},{3,4},{4,9},{5,13},{6,1},{7,5},{8,10},{9,14},{1... | collective-permute-start | bytes 393224 | tf_op jit(solution)/shard_map/ppermute | solution.py:262
  283.7 4.0 %collective-permute-start.22 = (f32[512,64]{0,1:T(8,128)S(1)}, f32[512,64]{0,1:T(8,128)S(1)}, u32[]{:S(2)}, u32[]{:S(2)}) collective-permute-start(f32[512,64]{0,1:T(8,128)S(1)} %multiply_reduce_fusion.1), channel_id=1, source_target_pairs={{0,0},{1,4},{2,8},{3,12},{4,1},{5,5},{6,9},{7,13},{8,2},{9,6},{10,... | collective-permute-start | bytes 393224 | tf_op jit(solution)/shard_map/ppermute | solution.py:262
  289.1 2.7 fusion
  291.8 5.1 %collective-permute-done.24 = f32[512,64]{0,1:T(8,128)S(1)} collective-permute-done((f32[512,64]{0,1:T(8,128)S(1)}, f32[512,64]{0,1:T(8,128)S(1)}, u32[]{:S(2)}, u32[]{:S(2)}) %collective-permute-start.24) | collective-permute-done | bytes 131104 | tf_op jit(solution)/shard_map/ppermute | solution.py:262
  298.8 1.9 collective-permute-start.29
  300.8 4.7 %collective-permute-start.27 = (f32[128,1280]{1,0:T(8,128)S(1)}, f32[128,1280]{1,0:T(8,128)S(1)}, u32[]{:S(2)}, u32[]{:S(2)}) collective-permute-start(f32[128,1280]{1,0:T(8,128)S(1)} %get-tuple-element.22), channel_id=1, source_target_pairs={{0,0},{1,4},{2,8},{3,12},{4,1},{5,5},{6,9},{7,13},{8,2},{9,6},{10,... | collective-permute-start | bytes 1966088 | tf_op jit(solution)/shard_map/ppermute | solution.py:262
  305.5 4.5 %collective-permute-start.28 = (f32[128,1280]{1,0:T(8,128)S(1)}, f32[128,1280]{1,0:T(8,128)S(1)}, u32[]{:S(2)}, u32[]{:S(2)}) collective-permute-start(f32[128,1280]{1,0:T(8,128)S(1)} %get-tuple-element.19), channel_id=1, source_target_pairs={{0,4},{1,8},{2,12},{3,0},{4,5},{5,9},{6,13},{7,1},{8,6},{9,10},{10... | collective-permute-start | bytes 1966088 | tf_op jit(solution)/shard_map/ppermute | solution.py:262
  310.0 33.2 %collective-permute-done.30 = f32[128,1280]{1,0:T(8,128)S(1)} collective-permute-done((f32[128,1280]{1,0:T(8,128)S(1)}, f32[128,1280]{1,0:T(8,128)S(1)}, u32[]{:S(2)}, u32[]{:S(2)}) %collective-permute-start.30) | collective-permute-done | bytes 655392 | tf_op jit(solution)/shard_map/ppermute | solution.py:262
  343.2 15.5 %collective-permute-done.29 = f32[128,1280]{1,0:T(8,128)S(1)} collective-permute-done((f32[128,1280]{1,0:T(8,128)S(1)}, f32[128,1280]{1,0:T(8,128)S(1)}, u32[]{:S(2)}, u32[]{:S(2)}) %collective-permute-start.29) | collective-permute-done | bytes 655392 | tf_op jit(solution)/shard_map/ppermute | solution.py:262
  (148 shorter events, 58.1 us)
Async XLA Ops:
  0.0 289.1 %copy-start = (bf16[1024,1280]{1,0:T(8,128)(2,1)S(1)}, bf16[1024,1280]{1,0:T(8,128)(2,1)}, u32[]{:S(2)}) copy-start(bf16[1024,1280]{1,0:T(8,128)(2,1)} %param.32) | copy-start | bytes 7864324
  0.0 16.8 %collective-permute-start = (bf16[128,1280]{1,0:T(8,128)(2,1)}, bf16[128,1280]{1,0:T(8,128)(2,1)S(1)}, u32[]{:S(2)}, u32[]{:S(2)}) collective-permute-start(bf16[128,1280]{1,0:T(8,128)(2,1)} %param.19), channel_id=1, source_target_pairs={{0,3},{1,7},{2,11},{3,15},{4,0},{5,4},{6,8},{7,12},{8,1},{9,5},{10... | collective-permute-start | bytes 983048 | tf_op jit(solution)/shard_map/ppermute | solution.py:262
  2.0 16.5 %collective-permute-start.1 = (bf16[128,1280]{1,0:T(8,128)(2,1)}, bf16[128,1280]{1,0:T(8,128)(2,1)S(1)}, u32[]{:S(2)}, u32[]{:S(2)}) collective-permute-start(bf16[128,1280]{1,0:T(8,128)(2,1)} %param.19), channel_id=1, source_target_pairs={{0,2},{1,6},{2,10},{3,14},{4,3},{5,7},{6,11},{7,15},{8,0},{9,4},{1... | collective-permute-start | bytes 983048 | tf_op jit(solution)/shard_map/ppermute | solution.py:262
  2.7 21.5 %collective-permute-start.2 = (bf16[128,1280]{1,0:T(8,128)(2,1)}, bf16[128,1280]{1,0:T(8,128)(2,1)}, u32[]{:S(2)}, u32[]{:S(2)}) collective-permute-start(bf16[128,1280]{1,0:T(8,128)(2,1)} %param.19), channel_id=1, source_target_pairs={{0,1},{1,5},{2,9},{3,13},{4,2},{5,6},{6,10},{7,14},{8,3},{9,7},{10... | collective-permute-start | bytes 983048 | tf_op jit(solution)/shard_map/ppermute | solution.py:262
  2.8 64.8 %collective-permute-start.3 = (bf16[128,1280]{1,0:T(8,128)(2,1)}, bf16[128,1280]{1,0:T(8,128)(2,1)}, u32[]{:S(2)}, u32[]{:S(2)}) collective-permute-start(bf16[128,1280]{1,0:T(8,128)(2,1)} %param.19), channel_id=1, source_target_pairs={{0,0},{1,4},{2,8},{3,12},{4,1},{5,5},{6,9},{7,13},{8,2},{9,6},{10,... | collective-permute-start | bytes 983048 | tf_op jit(solution)/shard_map/ppermute | solution.py:262
  9.5 64.5 %collective-permute-start.4 = (bf16[2,1280,64]{1,2,0:T(8,128)(2,1)}, bf16[2,1280,64]{1,2,0:T(8,128)(2,1)}, u32[]{:S(2)}, u32[]{:S(2)}) collective-permute-start(bf16[2,1280,64]{1,2,0:T(8,128)(2,1)} %param.33), channel_id=1, source_target_pairs={{0,0},{1,4},{2,8},{3,12},{4,1},{5,5},{6,9},{7,13},{8,2},{9,6},{10,... | collective-permute-start | bytes 983048 | tf_op jit(solution)/shard_map/ppermute | solution.py:262
  75.6 12.1 %collective-permute-start.8 = (f32[512,64]{0,1:T(8,128)S(1)}, f32[512,64]{0,1:T(8,128)S(1)}, u32[]{:S(2)}, u32[]{:S(2)}) collective-permute-start(f32[512,64]{0,1:T(8,128)S(1)} %multiply_reduce_fusion.2), channel_id=1, source_target_pairs={{0,3},{1,7},{2,11},{3,15},{4,0},{5,4},{6,8},{7,12},{8,1},{9,5},{10... | collective-permute-start | bytes 393224 | tf_op jit(solution)/shard_map/ppermute | solution.py:262
  75.7 12.0 %collective-permute-start.7 = (f32[512,64]{0,1:T(8,128)S(1)}, f32[512,64]{0,1:T(8,128)S(1)}, u32[]{:S(2)}, u32[]{:S(2)}) collective-permute-start(f32[512,64]{0,1:T(8,128)S(1)} %multiply_reduce_fusion.2), channel_id=1, source_target_pairs={{0,2},{1,6},{2,10},{3,14},{4,3},{5,7},{6,11},{7,15},{8,0},{9,4},{1... | collective-permute-start | bytes 393224 | tf_op jit(solution)/shard_map/ppermute | solution.py:262
  81.7 15.1 %collective-permute-start.5 = (f32[512,64]{0,1:T(8,128)S(1)}, f32[512,64]{0,1:T(8,128)S(1)}, u32[]{:S(2)}, u32[]{:S(2)}) collective-permute-start(f32[512,64]{0,1:T(8,128)S(1)} %multiply_reduce_fusion.2), channel_id=1, source_target_pairs={{0,0},{1,4},{2,8},{3,12},{4,1},{5,5},{6,9},{7,13},{8,2},{9,6},{10,... | collective-permute-start | bytes 393224 | tf_op jit(solution)/shard_map/ppermute | solution.py:262
  83.6 13.2 %collective-permute-start.6 = (f32[512,64]{0,1:T(8,128)S(1)}, f32[512,64]{0,1:T(8,128)S(1)}, u32[]{:S(2)}, u32[]{:S(2)}) collective-permute-start(f32[512,64]{0,1:T(8,128)S(1)} %multiply_reduce_fusion.2), channel_id=1, source_target_pairs={{0,1},{1,5},{2,9},{3,13},{4,2},{5,6},{6,10},{7,14},{8,3},{9,7},{10... | collective-permute-start | bytes 393224 | tf_op jit(solution)/shard_map/ppermute | solution.py:262
  103.4 18.1 %collective-permute-start.11 = (f32[128,1168]{0,1:T(8,128)}, f32[128,1168]{0,1:T(8,128)S(1)}, u32[]{:S(2)}, u32[]{:S(2)}) collective-permute-start(f32[128,1168]{0,1:T(8,128)} %get-tuple-element.24), channel_id=1, source_target_pairs={{0,12},{4,0},{8,4},{12,8},{1,13},{5,1},{9,5},{13,9},{2,14},{6,2},{... | collective-permute-start | bytes 1794056 | tf_op jit(solution)/shard_map/ppermute | solution.py:257
  106.4 55.3 %collective-permute-start.10 = (f32[128,1168]{0,1:T(8,128)}, f32[128,1168]{0,1:T(8,128)}, u32[]{:S(2)}, u32[]{:S(2)}) collective-permute-start(f32[128,1168]{0,1:T(8,128)} %get-tuple-element.25), channel_id=1, source_target_pairs={{0,8},{4,12},{8,0},{12,4},{1,9},{5,13},{9,1},{13,5},{2,10},{6,14},... | collective-permute-start | bytes 1794056 | tf_op jit(solution)/shard_map/ppermute | solution.py:257
  108.8 52.9 %collective-permute-start.9 = (f32[128,1168]{0,1:T(8,128)}, f32[128,1168]{0,1:T(8,128)}, u32[]{:S(2)}, u32[]{:S(2)}) collective-permute-start(f32[128,1168]{0,1:T(8,128)} %get-tuple-element.23), channel_id=1, source_target_pairs={{0,4},{4,8},{8,12},{12,0},{1,5},{5,9},{9,13},{13,1},{2,6},{6,10},{... | collective-permute-start | bytes 1794056 | tf_op jit(solution)/shard_map/ppermute | solution.py:257
  164.9 24.7 %collective-permute-start.15 = (bf16[16]{0:T(256)(128)(2,1)S(1)}, bf16[16]{0:T(256)(128)(2,1)}, u32[]{:S(2)}, u32[]{:S(2)}) collective-permute-start(bf16[16]{0:T(256)(128)(2,1)S(1)} %multiply_convert_fusion.4), channel_id=1, source_target_pairs={{0,12},{1,13},{2,14},{3,15},{16,28},{17,29},{18,30},{19,31}} | collective-permute-start | bytes 104 | tf_op jit(solution)/shard_map/ppermute | solution.py:391
  166.7 24.9 %collective-permute-start.14 = (bf16[16]{0:T(256)(128)(2,1)S(1)}, bf16[16]{0:T(256)(128)(2,1)}, u32[]{:S(2)}, u32[]{:S(2)}) collective-permute-start(bf16[16]{0:T(256)(128)(2,1)S(1)} %multiply_convert_fusion.4), channel_id=1, source_target_pairs={{0,8},{4,12},{1,9},{5,13},{2,10},{6,14},{3,11},{7,15},{16,24},{20,... | collective-permute-start | bytes 104 | tf_op jit(solution)/shard_map/ppermute | solution.py:391
  168.6 23.7 %collective-permute-start.13 = (bf16[16]{0:T(256)(128)(2,1)S(1)}, bf16[16]{0:T(256)(128)(2,1)}, u32[]{:S(2)}, u32[]{:S(2)}) collective-permute-start(bf16[16]{0:T(256)(128)(2,1)S(1)} %multiply_convert_fusion.4), channel_id=1, source_target_pairs={{0,4},{4,8},{8,12},{1,5},{5,9},{9,13},{2,6},{6,10},{10,14},{3,7},{... | collective-permute-start | bytes 104 | tf_op jit(solution)/shard_map/ppermute | solution.py:391
  171.6 2.8 collective-permute-start.12
  184.1 16.4 %collective-permute-start.18 = (bf16[16,64,256]{2,1,0:T(8,128)(2,1)S(1)}, bf16[16,64,256]{2,1,0:T(8,128)(2,1)S(1)}, u32[]{:S(2)}, u32[]{:S(2)}) collective-permute-start(bf16[16,64,256]{2,1,0:T(8,128)(2,1)S(1)} %convolution_convert_fusion.1), channel_id=1, source_target_pairs={{0,4},{4,8},{8,12},{1,5},{5,9},{9,13},{2,6},{6,10},{10,14},{3,7},{... | collective-permute-start | bytes 1572872 | tf_op jit(solution)/shard_map/ppermute | solution.py:392
  188.3 23.5 %collective-permute-start.17 = (bf16[16,64,256]{2,1,0:T(8,128)(2,1)S(1)}, bf16[16,64,256]{2,1,0:T(8,128)(2,1)S(1)}, u32[]{:S(2)}, u32[]{:S(2)}) collective-permute-start(bf16[16,64,256]{2,1,0:T(8,128)(2,1)S(1)} %convolution_convert_fusion.1), channel_id=1, source_target_pairs={{0,8},{4,12},{1,9},{5,13},{2,10},{6,14},{3,11},{7,15},{16,24},{20,... | collective-permute-start | bytes 1572872 | tf_op jit(solution)/shard_map/ppermute | solution.py:392
  189.6 32.8 %collective-permute-start.16 = (bf16[16,64,256]{2,1,0:T(8,128)(2,1)S(1)}, bf16[16,64,256]{2,1,0:T(8,128)(2,1)S(1)}, u32[]{:S(2)}, u32[]{:S(2)}) collective-permute-start(bf16[16,64,256]{2,1,0:T(8,128)(2,1)S(1)} %convolution_convert_fusion.1), channel_id=1, source_target_pairs={{0,12},{1,13},{2,14},{3,15},{16,28},{17,29},{18,30},{19,31}} | collective-permute-start | bytes 1572872 | tf_op jit(solution)/shard_map/ppermute | solution.py:392
  224.3 21.4 %collective-permute-start.19 = (bf16[128,1024]{0,1:T(8,128)(2,1)}, bf16[128,1024]{0,1:T(8,128)(2,1)S(1)}, u32[]{:S(2)}, u32[]{:S(2)}) collective-permute-start(bf16[128,1024]{0,1:T(8,128)(2,1)} %fusion.31), channel_id=1, source_target_pairs={{0,12},{4,0},{8,4},{12,8},{1,13},{5,1},{9,5},{13,9},{2,14},{6,2},{... | collective-permute-start | bytes 786440 | tf_op jit(solution)/shard_map/ppermute | solution.py:257
  238.6 58.4 %collective-permute-start.26 = (bf16[2,64,1280]{2,1,0:T(8,128)(2,1)}, bf16[2,64,1280]{2,1,0:T(8,128)(2,1)}, u32[]{:S(2)}, u32[]{:S(2)}) collective-permute-start(bf16[2,64,1280]{2,1,0:T(8,128)(2,1)} %param.37), channel_id=1, source_target_pairs={{0,0},{1,4},{2,8},{3,12},{4,1},{5,5},{6,9},{7,13},{8,2},{9,6},{10,... | collective-permute-start | bytes 983048 | tf_op jit(solution)/shard_map/ppermute | solution.py:262
  240.5 20.4 %collective-permute-start.20 = (bf16[128,1024]{0,1:T(8,128)(2,1)}, bf16[128,1024]{0,1:T(8,128)(2,1)}, u32[]{:S(2)}, u32[]{:S(2)}) collective-permute-start(bf16[128,1024]{0,1:T(8,128)(2,1)} %fusion.31), channel_id=1, source_target_pairs={{0,8},{4,12},{8,0},{12,4},{1,9},{5,13},{9,1},{13,5},{2,10},{6,14},... | collective-permute-start | bytes 786440 | tf_op jit(solution)/shard_map/ppermute | solution.py:257
  241.1 21.7 %collective-permute-start.21 = (bf16[128,1024]{0,1:T(8,128)(2,1)}, bf16[128,1024]{0,1:T(8,128)(2,1)S(1)}, u32[]{:S(2)}, u32[]{:S(2)}) collective-permute-start(bf16[128,1024]{0,1:T(8,128)(2,1)} %fusion.31), channel_id=1, source_target_pairs={{0,4},{4,8},{8,12},{12,0},{1,5},{5,9},{9,13},{13,1},{2,6},{6,10},{... | collective-permute-start | bytes 786440 | tf_op jit(solution)/shard_map/ppermute | solution.py:257
  269.3 22.5 %collective-permute-start.25 = (f32[512,64]{0,1:T(8,128)S(1)}, f32[512,64]{0,1:T(8,128)S(1)}, u32[]{:S(2)}, u32[]{:S(2)}) collective-permute-start(f32[512,64]{0,1:T(8,128)S(1)} %multiply_reduce_fusion.1), channel_id=1, source_target_pairs={{0,12},{1,0},{2,4},{3,8},{4,13},{5,1},{6,5},{7,9},{8,14},{9,2},{10... | collective-permute-start | bytes 393224 | tf_op jit(solution)/shard_map/ppermute | solution.py:262
  269.4 27.5 %collective-permute-start.24 = (f32[512,64]{0,1:T(8,128)S(1)}, f32[512,64]{0,1:T(8,128)S(1)}, u32[]{:S(2)}, u32[]{:S(2)}) collective-permute-start(f32[512,64]{0,1:T(8,128)S(1)} %multiply_reduce_fusion.1), channel_id=1, source_target_pairs={{0,8},{1,12},{2,0},{3,4},{4,9},{5,13},{6,1},{7,5},{8,10},{9,14},{1... | collective-permute-start | bytes 393224 | tf_op jit(solution)/shard_map/ppermute | solution.py:262
  283.7 13.2 %collective-permute-start.22 = (f32[512,64]{0,1:T(8,128)S(1)}, f32[512,64]{0,1:T(8,128)S(1)}, u32[]{:S(2)}, u32[]{:S(2)}) collective-permute-start(f32[512,64]{0,1:T(8,128)S(1)} %multiply_reduce_fusion.1), channel_id=1, source_target_pairs={{0,0},{1,4},{2,8},{3,12},{4,1},{5,5},{6,9},{7,13},{8,2},{9,6},{10,... | collective-permute-start | bytes 393224 | tf_op jit(solution)/shard_map/ppermute | solution.py:262
  287.8 9.2 %collective-permute-start.23 = (f32[512,64]{0,1:T(8,128)S(1)}, f32[512,64]{0,1:T(8,128)S(1)}, u32[]{:S(2)}, u32[]{:S(2)}) collective-permute-start(f32[512,64]{0,1:T(8,128)S(1)} %multiply_reduce_fusion.1), channel_id=1, source_target_pairs={{0,4},{1,8},{2,12},{3,0},{4,5},{5,9},{6,13},{7,1},{8,6},{9,10},{10... | collective-permute-start | bytes 393224 | tf_op jit(solution)/shard_map/ppermute | solution.py:262
  298.8 44.4 %collective-permute-start.30 = (f32[128,1280]{1,0:T(8,128)S(1)}, f32[128,1280]{1,0:T(8,128)S(1)}, u32[]{:S(2)}, u32[]{:S(2)}) collective-permute-start(f32[128,1280]{1,0:T(8,128)S(1)} %get-tuple-element.20), channel_id=1, source_target_pairs={{0,12},{1,0},{2,4},{3,8},{4,13},{5,1},{6,5},{7,9},{8,14},{9,2},{10... | collective-permute-start | bytes 1966088 | tf_op jit(solution)/shard_map/ppermute | solution.py:262
  298.8 59.9 %collective-permute-start.29 = (f32[128,1280]{1,0:T(8,128)S(1)}, f32[128,1280]{1,0:T(8,128)S(1)}, u32[]{:S(2)}, u32[]{:S(2)}) collective-permute-start(f32[128,1280]{1,0:T(8,128)S(1)} %get-tuple-element.21), channel_id=1, source_target_pairs={{0,8},{1,12},{2,0},{3,4},{4,9},{5,13},{6,1},{7,5},{8,10},{9,14},{1... | collective-permute-start | bytes 1966088 | tf_op jit(solution)/shard_map/ppermute | solution.py:262
  300.8 58.0 %collective-permute-start.27 = (f32[128,1280]{1,0:T(8,128)S(1)}, f32[128,1280]{1,0:T(8,128)S(1)}, u32[]{:S(2)}, u32[]{:S(2)}) collective-permute-start(f32[128,1280]{1,0:T(8,128)S(1)} %get-tuple-element.22), channel_id=1, source_target_pairs={{0,0},{1,4},{2,8},{3,12},{4,1},{5,5},{6,9},{7,13},{8,2},{9,6},{10,... | collective-permute-start | bytes 1966088 | tf_op jit(solution)/shard_map/ppermute | solution.py:262
  305.5 53.2 %collective-permute-start.28 = (f32[128,1280]{1,0:T(8,128)S(1)}, f32[128,1280]{1,0:T(8,128)S(1)}, u32[]{:S(2)}, u32[]{:S(2)}) collective-permute-start(f32[128,1280]{1,0:T(8,128)S(1)} %get-tuple-element.19), channel_id=1, source_target_pairs={{0,4},{1,8},{2,12},{3,0},{4,5},{5,9},{6,13},{7,1},{8,6},{9,10},{10... | collective-permute-start | bytes 1966088 | tf_op jit(solution)/shard_map/ppermute | solution.py:262
  (13 other events, 284.8 us)

commit v3 on v2

--- a/solution.py
+++ b/solution.py
@@ -255,6 +255,9 @@
     if kind == "ctx":
         pairs = [(a, (a + shift) % side) for a in range(side)]
         return lax.ppermute(block, "ctx", pairs)
+    if kind == "lane":
+        pairs = [(a, (a + shift) % side) for a in range(side)]
+        return lax.ppermute(block, ("tp", "dp"), pairs)
     if kind == "rows":
         pairs = [(a * side + b, b * side + (a + shift) % side) for a in range(side) for b in range(side)]
     else:
@@ -331,7 +334,10 @@
     segment = segment_of(positions, request_ends)
     previous = segment_of(jnp.reshape(start_pos - 1, (1,)), request_ends)[0]
 
-    stream_rows = in_order([moved(tokens, s, "rows") for s in range(side)], lane)
+    tokens_t = transposed(tokens)
+    stream_rows = in_order(
+        [tokens_t] + [moved(tokens_t, s, "lane") for s in range(1, side)], lane
+    )
     down_in_t = transposed(adapter_down_input)
     up_out_t = transposed(adapter_up_output)
     down_part = jnp.einsum(
@@ -410,7 +416,9 @@
         "pc,ecr->per", normed_stream, adapter_down_output, preferred_element_type=jnp.float32
     )
     out_down_pick = jnp.sum(out_down_part * owned_here[:, :, None].astype(jnp.float32), axis=1)
-    rank_hidden_output = sum(moved(out_down_pick, s, "cols") for s in range(side))
+    rank_hidden_output = transposed(
+        out_down_pick + sum(moved(out_down_pick, s, "lane") for s in range(1, side))
+    )
     base_part = jnp.dot(
         normed_stream, output_weight, preferred_element_type=jnp.float32
     ).astype(jnp.bfloat16).astype(jnp.float32)
@@ -420,10 +428,10 @@
         preferred_element_type=jnp.float32,
     )
     out_part = base_part + adapter_part
-    mixed = sum(
-        moved(block_rows(out_part, (lane + s) % side, length), s, "cols") for s in range(side)
-    )
-    return mixed.astype(jnp.bfloat16)
+    mixed_t = block_rows(out_part, lane, length)
+    for s in range(1, side):
+        mixed_t = mixed_t + moved(block_rows(out_part, (lane + s) % side, length), s, "lane")
+    return transposed(mixed_t.astype(jnp.bfloat16))
 
 
 def solution(mesh):

time: 361 us -> 329 us (0.911)
  waiting for transfers between devices: 214 us -> 193 us
  starting transfers between devices: 90.1 us -> 81.8 us
    ppermute x18 -> x9, waiting for transfers between devices: 116 us -> 49.6 us  [moved(): return lax.ppermute(block, ('ctx', 'tp', 'dp'), pairs)]
    ppermute x0 -> x9, waiting for transfers between devices: none -> 49.8 us  [moved(): return lax.ppermute(block, ('tp', 'dp'), pairs)]
    ppermute x18 -> x9, starting transfers between devices: 56 us -> 38.1 us  [moved(): return lax.ppermute(block, ('ctx', 'tp', 'dp'), pairs)]
    ppermute x0 -> x9, starting transfers between devices: none -> 8.6 us  [moved(): return lax.ppermute(block, ('tp', 'dp'), pairs)]
    ppermute x6, waiting for transfers between devices: 71.2 us -> 66.4 us  [moved(): return lax.ppermute(block, 'ctx', pairs)]
    unnamed x42 -> x47, local copies, waits for them, and re-layouts: 8.04 us -> 7.35 us
  transfers between devices with their start and end apart: 31 -> 31, of which waited for: 17 -> 21; matrix products, arithmetic and copies ran while one was open for 9% -> 8% of each run, Pallas kernels for 0% -> 0%
where the time goes in v3:
time: 329 us; the launch traced here: 328 us
  waiting for transfers between devices  193 us (59%)
  starting transfers between devices  81.8 us (25%)
  local copies, waits for them, and re-layouts  19.1 us (6%)
  other arithmetic  14.2 us (4%)
  matrix products  12.5 us (4%)
  blocking collectives  5.43 us (2%)
    ppermute x6, waiting for transfers between devices, moved(): return lax.ppermute(block, 'ctx', pairs)  66.4 us
    ppermute x9, waiting for transfers between devices, moved(): return lax.ppermute(block, ('tp', 'dp'), pairs)  49.8 us
    ppermute x9, waiting for transfers between devices, moved(): return lax.ppermute(block, ('ctx', 'tp', 'dp'), pairs)  49.6 us
    ppermute x9, starting transfers between devices, moved(): return lax.ppermute(block, ('ctx', 'tp', 'dp'), pairs)  38.1 us
    ppermute x3, waiting for transfers between devices, square_body(): state_in = lax.ppermute(local_state.astype(jnp.bfloat16), 'ctx', pairs)  27 us
    ppermute x6, starting transfers between devices, moved(): return lax.ppermute(block, 'ctx', pairs)  20.1 us
    ppermute x9, starting transfers between devices, moved(): return lax.ppermute(block, ('tp', 'dp'), pairs)  8.6 us
    unnamed x47, local copies, waits for them, and re-layouts  7.35 us
  transfers between devices with their start and end apart: 31, of which 21 were waited for; matrix products, arithmetic and copies ran while one was open for 8% of the time, Pallas kernels for 0%

profile of v3, /device:TPU:2, one launch (start us, length us, event | category | flops | bytes accessed | tf_op | source)
XLA Modules:
  0.0 328.2 jit_solution(13904573668089616956)
XLA Ops:
  0.0 4.7 %collective-permute-start = (bf16[128,1280]{1,0:T(8,128)(2,1)}, bf16[128,1280]{1,0:T(8,128)(2,1)S(1)}, u32[]{:S(2)}, u32[]{:S(2)}) collective-permute-start(bf16[128,1280]{1,0:T(8,128)(2,1)} %param.19), channel_id=1, source_target_pairs={{0,0},{1,4},{2,8},{3,12},{4,1},{5,5},{6,9},{7,13},{8,2},{9,6},{10,... | collective-permute-start | bytes 983048 | tf_op jit(solution)/shard_map/ppermute | solution.py:265
  4.7 3.2 collective-permute-start.4
  12.5 16.2 %collective-permute-done = bf16[128,1280]{1,0:T(8,128)(2,1)S(1)} collective-permute-done((bf16[128,1280]{1,0:T(8,128)(2,1)}, bf16[128,1280]{1,0:T(8,128)(2,1)S(1)}, u32[]{:S(2)}, u32[]{:S(2)}) %collective-permute-start) | collective-permute-done | bytes 327712 | tf_op jit(solution)/shard_map/ppermute | solution.py:265
  30.1 6.2 %collective-permute-done.1 = bf16[128,1280]{1,0:T(8,128)(2,1)S(1)} collective-permute-done((bf16[128,1280]{1,0:T(8,128)(2,1)S(1)}, bf16[128,1280]{1,0:T(8,128)(2,1)S(1)}, u32[]{:S(2)}, u32[]{:S(2)}) %collective-permute-start.1) | collective-permute-done | bytes 327712 | tf_op jit(solution)/shard_map/ppermute | solution.py:260
  36.2 7.0 %collective-permute-done.2 = bf16[128,1280]{1,0:T(8,128)(2,1)S(1)} collective-permute-done((bf16[128,1280]{1,0:T(8,128)(2,1)S(1)}, bf16[128,1280]{1,0:T(8,128)(2,1)S(1)}, u32[]{:S(2)}, u32[]{:S(2)}) %collective-permute-start.2) | collective-permute-done | bytes 327712 | tf_op jit(solution)/shard_map/ppermute | solution.py:260
  47.7 4.0 %collective-permute-start.5 = (f32[512,64]{0,1:T(8,128)S(1)}, f32[512,64]{0,1:T(8,128)S(1)}, u32[]{:S(2)}, u32[]{:S(2)}) collective-permute-start(f32[512,64]{0,1:T(8,128)S(1)} %multiply_reduce_fusion.2), channel_id=1, source_target_pairs={{0,0},{1,4},{2,8},{3,12},{4,1},{5,5},{6,9},{7,13},{8,2},{9,6},{10,... | collective-permute-start | bytes 393224 | tf_op jit(solution)/shard_map/ppermute | solution.py:265
  51.6 2.6 collective-permute-start.6
  55.6 15.1 %collective-permute-done.5 = f32[512,64]{0,1:T(8,128)S(1)} collective-permute-done((f32[512,64]{0,1:T(8,128)S(1)}, f32[512,64]{0,1:T(8,128)S(1)}, u32[]{:S(2)}, u32[]{:S(2)}) %collective-permute-start.5) | collective-permute-done | bytes 131104 | tf_op jit(solution)/shard_map/ppermute | solution.py:265
  77.3 4.5 %collective-permute-start.11 = (f32[128,1168]{0,1:T(8,128)}, f32[128,1168]{0,1:T(8,128)S(1)}, u32[]{:S(2)}, u32[]{:S(2)}) collective-permute-start(f32[128,1168]{0,1:T(8,128)} %get-tuple-element.21), channel_id=1, source_target_pairs={{0,12},{4,0},{8,4},{12,8},{1,13},{5,1},{9,5},{13,9},{2,14},{6,2},{... | collective-permute-start | bytes 1794056 | tf_op jit(solution)/shard_map/ppermute | solution.py:257
  85.0 11.2 %collective-permute-done.11 = f32[128,1168]{0,1:T(8,128)S(1)} collective-permute-done((f32[128,1168]{0,1:T(8,128)}, f32[128,1168]{0,1:T(8,128)S(1)}, u32[]{:S(2)}, u32[]{:S(2)}) %collective-permute-start.11) | collective-permute-done | bytes 598048 | tf_op jit(solution)/shard_map/ppermute | solution.py:257
  96.2 36.7 %collective-permute-done.10 = f32[128,1168]{0,1:T(8,128)} collective-permute-done((f32[128,1168]{0,1:T(8,128)}, f32[128,1168]{0,1:T(8,128)}, u32[]{:S(2)}, u32[]{:S(2)}) %collective-permute-start.10) | collective-permute-done | bytes 598048 | tf_op jit(solution)/shard_map/ppermute | solution.py:257
  137.9 3.0 collective-permute-start.14
  147.1 3.3 %divide_multiply_fusion = f32[128,1152]{0,1:T(8,128)S(1)} fusion(f32[128,1152]{0,1:T(8,128)} %slice.105, f32[3,1152]{0,1:T(8,128)S(1)} %copy.87, f32[128]{0:T(128)S(1)} %get-tuple-element.34, f32[1152]{0:T(1024)S(1)} %get-tuple-element.6, f32[128]{0:T(128)S(1)} %get-tuple-element.35, f32[1152]{0:T(1024)S(1)} %get-tuple-element.7, ...), kind=kLoop, calls=%fused_computation.44 | loop fusion | flops 2654208 | bytes 1213952 | tf_op jit(solution)/shard_map/jit(silu)/mul | solution.py:381
  150.5 5.4 %all_gather.3 = bf16[128,512]{0,1:T(8,128)(2,1)S(1)} all-gather(bf16[128,128]{0,1:T(8,128)(2,1)S(1)} %slice.194), channel_id=1, replica_groups=mesh['groups'=2,'ctx'=4,'tp'=2,'dp'=2] {'tp','dp'}, dimensions={1}, use_global_device_ids=true | all-gather | bytes 163840 | tf_op jit(solution)/shard_map/all_gather | solution.py:384
  156.5 4.2 %collective-permute-start.18 = (bf16[16,64,256]{2,1,0:T(8,128)(2,1)S(1)}, bf16[16,64,256]{2,1,0:T(8,128)(2,1)S(1)}, u32[]{:S(2)}, u32[]{:S(2)}) collective-permute-start(bf16[16,64,256]{2,1,0:T(8,128)(2,1)S(1)} %convolution_convert_fusion.1), channel_id=1, source_target_pairs={{0,4},{4,8},{8,12},{1,5},{5,9},{9,13},{2,6},{6,10},{10,14},{3,7},{... | collective-permute-start | bytes 1572872 | tf_op jit(solution)/shard_map/ppermute | solution.py:398
  167.9 5.1 %collective-permute-done.18 = bf16[16,64,256]{2,1,0:T(8,128)(2,1)S(1)} collective-permute-done((bf16[16,64,256]{2,1,0:T(8,128)(2,1)S(1)}, bf16[16,64,256]{2,1,0:T(8,128)(2,1)S(1)}, u32[]{:S(2)}, u32[]{:S(2)}) %collective-permute-start.18) | collective-permute-done | bytes 524320 | tf_op jit(solution)/shard_map/ppermute | solution.py:398
  173.0 11.3 %collective-permute-done.17 = bf16[16,64,256]{2,1,0:T(8,128)(2,1)S(1)} collective-permute-done((bf16[16,64,256]{2,1,0:T(8,128)(2,1)S(1)}, bf16[16,64,256]{2,1,0:T(8,128)(2,1)S(1)}, u32[]{:S(2)}, u32[]{:S(2)}) %collective-permute-start.17) | collective-permute-done | bytes 524320 | tf_op jit(solution)/shard_map/ppermute | solution.py:398
  184.2 10.7 %collective-permute-done.16 = bf16[16,64,256]{2,1,0:T(8,128)(2,1)S(1)} collective-permute-done((bf16[16,64,256]{2,1,0:T(8,128)(2,1)S(1)}, bf16[16,64,256]{2,1,0:T(8,128)(2,1)S(1)}, u32[]{:S(2)}, u32[]{:S(2)}) %collective-permute-start.16) | collective-permute-done | bytes 524320 | tf_op jit(solution)/shard_map/ppermute | solution.py:398
  196.8 14.3 %collective-permute-start.19 = (bf16[128,1024]{0,1:T(8,128)(2,1)}, bf16[128,1024]{0,1:T(8,128)(2,1)S(1)}, u32[]{:S(2)}, u32[]{:S(2)}) collective-permute-start(bf16[128,1024]{0,1:T(8,128)(2,1)} %fusion.31), channel_id=1, source_target_pairs={{0,12},{4,0},{8,4},{12,8},{1,13},{5,1},{9,5},{13,9},{2,14},{6,2},{... | collective-permute-start | bytes 786440 | tf_op jit(solution)/shard_map/ppermute | solution.py:257
  211.1 4.4 %collective-permute-start.26 = (bf16[2,64,1280]{2,1,0:T(8,128)(2,1)}, bf16[2,64,1280]{2,1,0:T(8,128)(2,1)}, u32[]{:S(2)}, u32[]{:S(2)}) collective-permute-start(bf16[2,64,1280]{2,1,0:T(8,128)(2,1)} %param.37), channel_id=1, source_target_pairs={{0,0},{1,4},{2,8},{3,12},{4,1},{5,5},{6,9},{7,13},{8,2},{9,6},{10,... | collective-permute-start | bytes 983048 | tf_op jit(solution)/shard_map/ppermute | solution.py:265
  215.8 2.4 collective-permute-done.19
  218.2 14.8 %collective-permute-done.20 = bf16[128,1024]{0,1:T(8,128)(2,1)} collective-permute-done((bf16[128,1024]{0,1:T(8,128)(2,1)}, bf16[128,1024]{0,1:T(8,128)(2,1)}, u32[]{:S(2)}, u32[]{:S(2)}) %collective-permute-start.20) | collective-permute-done | bytes 262176 | tf_op jit(solution)/shard_map/ppermute | solution.py:257
  241.9 4.4 %collective-permute-start.24 = (f32[512,64]{0,1:T(8,128)S(1)}, f32[512,64]{0,1:T(8,128)S(1)}, u32[]{:S(2)}, u32[]{:S(2)}) collective-permute-start(f32[512,64]{0,1:T(8,128)S(1)} %multiply_reduce_fusion.1), channel_id=1, source_target_pairs={{0,3},{1,0},{2,1},{3,2},{4,7},{5,4},{6,5},{7,6},{8,11},{9,8},{10,9... | collective-permute-start | bytes 393224 | tf_op jit(solution)/shard_map/ppermute | solution.py:260
  246.4 3.0 collective-permute-start.23
  249.4 3.5 %collective-permute-done.22 = f32[512,64]{0,1:T(8,128)S(1)} collective-permute-done((f32[512,64]{0,1:T(8,128)S(1)}, f32[512,64]{0,1:T(8,128)S(1)}, u32[]{:S(2)}, u32[]{:S(2)}) %collective-permute-start.22) | collective-permute-done | bytes 131104 | tf_op jit(solution)/shard_map/ppermute | solution.py:260
  252.9 3.0 collective-permute-done.23
  255.9 11.5 %collective-permute-start.25 = (f32[512,64]{0,1:T(8,128)S(1)}, f32[512,64]{0,1:T(8,128)S(1)}, u32[]{:S(2)}, u32[]{:S(2)}) collective-permute-start(f32[512,64]{0,1:T(8,128)S(1)} %add_add_fusion.1), channel_id=1, source_target_pairs={{0,0},{1,4},{2,8},{3,12},{4,1},{5,5},{6,9},{7,13},{8,2},{9,6},{10,... | collective-permute-start | bytes 393224 | tf_op jit(solution)/shard_map/ppermute | solution.py:265
  268.9 3.6 %collective-permute-done.25 = f32[512,64]{0,1:T(8,128)S(1)} collective-permute-done((f32[512,64]{0,1:T(8,128)S(1)}, f32[512,64]{0,1:T(8,128)S(1)}, u32[]{:S(2)}, u32[]{:S(2)}) %collective-permute-start.25) | collective-permute-done | bytes 131104 | tf_op jit(solution)/shard_map/ppermute | solution.py:265
  277.3 14.9 %collective-permute-done.29 = f32[128,1280]{1,0:T(8,128)} collective-permute-done((f32[128,1280]{1,0:T(8,128)}, f32[128,1280]{1,0:T(8,128)}, u32[]{:S(2)}, u32[]{:S(2)}) %collective-permute-start.29) | collective-permute-done | bytes 655392 | tf_op jit(solution)/shard_map/ppermute | solution.py:260
  292.3 13.9 %collective-permute-done.28 = f32[128,1280]{1,0:T(8,128)} collective-permute-done((f32[128,1280]{1,0:T(8,128)}, f32[128,1280]{1,0:T(8,128)}, u32[]{:S(2)}, u32[]{:S(2)}) %collective-permute-start.28) | collective-permute-done | bytes 655392 | tf_op jit(solution)/shard_map/ppermute | solution.py:260
  307.9 5.8 %collective-permute-start.30 = (bf16[128,1280]{1,0:T(8,128)(2,1)S(1)}, bf16[128,1280]{1,0:T(8,128)(2,1)S(1)}, u32[]{:S(2)}, u32[]{:S(2)}) collective-permute-start(bf16[128,1280]{1,0:T(8,128)(2,1)S(1)} %add_convert_fusion), channel_id=1, source_target_pairs={{0,0},{1,4},{2,8},{3,12},{4,1},{5,5},{6,9},{7,13},{8,2},{9,6},{10,... | collective-permute-start | bytes 983048 | tf_op jit(solution)/shard_map/ppermute | solution.py:265
  313.7 13.7 %collective-permute-done.30 = bf16[128,1280]{1,0:T(8,128)(2,1)S(1)} collective-permute-done((bf16[128,1280]{1,0:T(8,128)(2,1)S(1)}, bf16[128,1280]{1,0:T(8,128)(2,1)S(1)}, u32[]{:S(2)}, u32[]{:S(2)}) %collective-permute-start.30) | collective-permute-done | bytes 327712 | tf_op jit(solution)/shard_map/ppermute | solution.py:265
  (153 shorter events, 58.8 us)
Async XLA Ops:
  0.0 267.4 %copy-start = (bf16[1024,1280]{1,0:T(8,128)(2,1)S(1)}, bf16[1024,1280]{1,0:T(8,128)(2,1)}, u32[]{:S(2)}) copy-start(bf16[1024,1280]{1,0:T(8,128)(2,1)} %param.32) | copy-start | bytes 7864324
  0.0 28.7 %collective-permute-start = (bf16[128,1280]{1,0:T(8,128)(2,1)}, bf16[128,1280]{1,0:T(8,128)(2,1)S(1)}, u32[]{:S(2)}, u32[]{:S(2)}) collective-permute-start(bf16[128,1280]{1,0:T(8,128)(2,1)} %param.19), channel_id=1, source_target_pairs={{0,0},{1,4},{2,8},{3,12},{4,1},{5,5},{6,9},{7,13},{8,2},{9,6},{10,... | collective-permute-start | bytes 983048 | tf_op jit(solution)/shard_map/ppermute | solution.py:265
  4.7 40.3 %collective-permute-start.4 = (bf16[2,1280,64]{1,2,0:T(8,128)(2,1)}, bf16[2,1280,64]{1,2,0:T(8,128)(2,1)S(1)}, u32[]{:S(2)}, u32[]{:S(2)}) collective-permute-start(bf16[2,1280,64]{1,2,0:T(8,128)(2,1)} %param.33), channel_id=1, source_target_pairs={{0,0},{1,4},{2,8},{3,12},{4,1},{5,5},{6,9},{7,13},{8,2},{9,6},{10,... | collective-permute-start | bytes 983048 | tf_op jit(solution)/shard_map/ppermute | solution.py:265
  28.7 7.5 %collective-permute-start.1 = (bf16[128,1280]{1,0:T(8,128)(2,1)S(1)}, bf16[128,1280]{1,0:T(8,128)(2,1)S(1)}, u32[]{:S(2)}, u32[]{:S(2)}) collective-permute-start(bf16[128,1280]{1,0:T(8,128)(2,1)S(1)} %collective-permute-done), channel_id=1, source_target_pairs={{0,3},{1,0},{2,1},{3,2},{4,7},{5,4},{6,5},{7,6},{8,11},{9,8},{10,9... | collective-permute-start | bytes 983048 | tf_op jit(solution)/shard_map/ppermute | solution.py:260
  29.4 13.8 %collective-permute-start.2 = (bf16[128,1280]{1,0:T(8,128)(2,1)S(1)}, bf16[128,1280]{1,0:T(8,128)(2,1)S(1)}, u32[]{:S(2)}, u32[]{:S(2)}) collective-permute-start(bf16[128,1280]{1,0:T(8,128)(2,1)S(1)} %collective-permute-done), channel_id=1, source_target_pairs={{0,2},{1,3},{2,0},{3,1},{4,6},{5,7},{6,4},{7,5},{8,10},{9,11},{10,... | collective-permute-start | bytes 983048 | tf_op jit(solution)/shard_map/ppermute | solution.py:260
  29.5 15.2 %collective-permute-start.3 = (bf16[128,1280]{1,0:T(8,128)(2,1)S(1)}, bf16[128,1280]{1,0:T(8,128)(2,1)S(1)}, u32[]{:S(2)}, u32[]{:S(2)}) collective-permute-start(bf16[128,1280]{1,0:T(8,128)(2,1)S(1)} %collective-permute-done), channel_id=1, source_target_pairs={{0,1},{1,2},{2,3},{3,0},{4,5},{5,6},{6,7},{7,4},{8,9},{9,10},{10,1... | collective-permute-start | bytes 983048 | tf_op jit(solution)/shard_map/ppermute | solution.py:260
  45.6 10.0 %collective-permute-start.8 = (f32[512,64]{0,1:T(8,128)S(1)}, f32[512,64]{0,1:T(8,128)S(1)}, u32[]{:S(2)}, u32[]{:S(2)}) collective-permute-start(f32[512,64]{0,1:T(8,128)S(1)} %multiply_reduce_fusion.2), channel_id=1, source_target_pairs={{0,3},{1,7},{2,11},{3,15},{4,0},{5,4},{6,8},{7,12},{8,1},{9,5},{10... | collective-permute-start | bytes 393224 | tf_op jit(solution)/shard_map/ppermute | solution.py:265
  47.4 8.2 %collective-permute-start.7 = (f32[512,64]{0,1:T(8,128)S(1)}, f32[512,64]{0,1:T(8,128)S(1)}, u32[]{:S(2)}, u32[]{:S(2)}) collective-permute-start(f32[512,64]{0,1:T(8,128)S(1)} %multiply_reduce_fusion.2), channel_id=1, source_target_pairs={{0,2},{1,6},{2,10},{3,14},{4,3},{5,7},{6,11},{7,15},{8,0},{9,4},{1... | collective-permute-start | bytes 393224 | tf_op jit(solution)/shard_map/ppermute | solution.py:265
  47.7 23.1 %collective-permute-start.5 = (f32[512,64]{0,1:T(8,128)S(1)}, f32[512,64]{0,1:T(8,128)S(1)}, u32[]{:S(2)}, u32[]{:S(2)}) collective-permute-start(f32[512,64]{0,1:T(8,128)S(1)} %multiply_reduce_fusion.2), channel_id=1, source_target_pairs={{0,0},{1,4},{2,8},{3,12},{4,1},{5,5},{6,9},{7,13},{8,2},{9,6},{10,... | collective-permute-start | bytes 393224 | tf_op jit(solution)/shard_map/ppermute | solution.py:265
  51.6 19.1 %collective-permute-start.6 = (f32[512,64]{0,1:T(8,128)S(1)}, f32[512,64]{0,1:T(8,128)S(1)}, u32[]{:S(2)}, u32[]{:S(2)}) collective-permute-start(f32[512,64]{0,1:T(8,128)S(1)} %multiply_reduce_fusion.2), channel_id=1, source_target_pairs={{0,1},{1,5},{2,9},{3,13},{4,2},{5,6},{6,10},{7,14},{8,3},{9,7},{10... | collective-permute-start | bytes 393224 | tf_op jit(solution)/shard_map/ppermute | solution.py:265
  77.3 18.9 %collective-permute-start.11 = (f32[128,1168]{0,1:T(8,128)}, f32[128,1168]{0,1:T(8,128)S(1)}, u32[]{:S(2)}, u32[]{:S(2)}) collective-permute-start(f32[128,1168]{0,1:T(8,128)} %get-tuple-element.21), channel_id=1, source_target_pairs={{0,12},{4,0},{8,4},{12,8},{1,13},{5,1},{9,5},{13,9},{2,14},{6,2},{... | collective-permute-start | bytes 1794056 | tf_op jit(solution)/shard_map/ppermute | solution.py:257
  81.9 51.0 %collective-permute-start.10 = (f32[128,1168]{0,1:T(8,128)}, f32[128,1168]{0,1:T(8,128)}, u32[]{:S(2)}, u32[]{:S(2)}) collective-permute-start(f32[128,1168]{0,1:T(8,128)} %get-tuple-element.22), channel_id=1, source_target_pairs={{0,8},{4,12},{8,0},{12,4},{1,9},{5,13},{9,1},{13,5},{2,10},{6,14},... | collective-permute-start | bytes 1794056 | tf_op jit(solution)/shard_map/ppermute | solution.py:257
  81.9 51.0 %collective-permute-start.9 = (f32[128,1168]{0,1:T(8,128)}, f32[128,1168]{0,1:T(8,128)}, u32[]{:S(2)}, u32[]{:S(2)}) collective-permute-start(f32[128,1168]{0,1:T(8,128)} %get-tuple-element.20), channel_id=1, source_target_pairs={{0,4},{4,8},{8,12},{12,0},{1,5},{5,9},{9,13},{13,1},{2,6},{6,10},{... | collective-permute-start | bytes 1794056 | tf_op jit(solution)/shard_map/ppermute | solution.py:257
  136.1 26.0 %collective-permute-start.15 = (bf16[16]{0:T(256)(128)(2,1)S(1)}, bf16[16]{0:T(256)(128)(2,1)}, u32[]{:S(2)}, u32[]{:S(2)}) collective-permute-start(bf16[16]{0:T(256)(128)(2,1)S(1)} %multiply_convert_fusion.4), channel_id=1, source_target_pairs={{0,12},{1,13},{2,14},{3,15},{16,28},{17,29},{18,30},{19,31}} | collective-permute-start | bytes 104 | tf_op jit(solution)/shard_map/ppermute | solution.py:397
  137.9 26.2 %collective-permute-start.14 = (bf16[16]{0:T(256)(128)(2,1)S(1)}, bf16[16]{0:T(256)(128)(2,1)}, u32[]{:S(2)}, u32[]{:S(2)}) collective-permute-start(bf16[16]{0:T(256)(128)(2,1)S(1)} %multiply_convert_fusion.4), channel_id=1, source_target_pairs={{0,8},{4,12},{1,9},{5,13},{2,10},{6,14},{3,11},{7,15},{16,24},{20,... | collective-permute-start | bytes 104 | tf_op jit(solution)/shard_map/ppermute | solution.py:397
  140.9 23.9 %collective-permute-start.13 = (bf16[16]{0:T(256)(128)(2,1)S(1)}, bf16[16]{0:T(256)(128)(2,1)}, u32[]{:S(2)}, u32[]{:S(2)}) collective-permute-start(bf16[16]{0:T(256)(128)(2,1)S(1)} %multiply_convert_fusion.4), channel_id=1, source_target_pairs={{0,4},{4,8},{8,12},{1,5},{5,9},{9,13},{2,6},{6,10},{10,14},{3,7},{... | collective-permute-start | bytes 104 | tf_op jit(solution)/shard_map/ppermute | solution.py:397
  144.0 2.8 collective-permute-start.12
  156.5 16.4 %collective-permute-start.18 = (bf16[16,64,256]{2,1,0:T(8,128)(2,1)S(1)}, bf16[16,64,256]{2,1,0:T(8,128)(2,1)S(1)}, u32[]{:S(2)}, u32[]{:S(2)}) collective-permute-start(bf16[16,64,256]{2,1,0:T(8,128)(2,1)S(1)} %convolution_convert_fusion.1), channel_id=1, source_target_pairs={{0,4},{4,8},{8,12},{1,5},{5,9},{9,13},{2,6},{6,10},{10,14},{3,7},{... | collective-permute-start | bytes 1572872 | tf_op jit(solution)/shard_map/ppermute | solution.py:398
  160.8 23.5 %collective-permute-start.17 = (bf16[16,64,256]{2,1,0:T(8,128)(2,1)S(1)}, bf16[16,64,256]{2,1,0:T(8,128)(2,1)S(1)}, u32[]{:S(2)}, u32[]{:S(2)}) collective-permute-start(bf16[16,64,256]{2,1,0:T(8,128)(2,1)S(1)} %convolution_convert_fusion.1), channel_id=1, source_target_pairs={{0,8},{4,12},{1,9},{5,13},{2,10},{6,14},{3,11},{7,15},{16,24},{20,... | collective-permute-start | bytes 1572872 | tf_op jit(solution)/shard_map/ppermute | solution.py:398
  162.1 32.8 %collective-permute-start.16 = (bf16[16,64,256]{2,1,0:T(8,128)(2,1)S(1)}, bf16[16,64,256]{2,1,0:T(8,128)(2,1)S(1)}, u32[]{:S(2)}, u32[]{:S(2)}) collective-permute-start(bf16[16,64,256]{2,1,0:T(8,128)(2,1)S(1)} %convolution_convert_fusion.1), channel_id=1, source_target_pairs={{0,12},{1,13},{2,14},{3,15},{16,28},{17,29},{18,30},{19,31}} | collective-permute-start | bytes 1572872 | tf_op jit(solution)/shard_map/ppermute | solution.py:398
  196.8 21.4 %collective-permute-start.19 = (bf16[128,1024]{0,1:T(8,128)(2,1)}, bf16[128,1024]{0,1:T(8,128)(2,1)S(1)}, u32[]{:S(2)}, u32[]{:S(2)}) collective-permute-start(bf16[128,1024]{0,1:T(8,128)(2,1)} %fusion.31), channel_id=1, source_target_pairs={{0,12},{4,0},{8,4},{12,8},{1,13},{5,1},{9,5},{13,9},{2,14},{6,2},{... | collective-permute-start | bytes 786440 | tf_op jit(solution)/shard_map/ppermute | solution.py:257
  211.1 21.9 %collective-permute-start.20 = (bf16[128,1024]{0,1:T(8,128)(2,1)}, bf16[128,1024]{0,1:T(8,128)(2,1)}, u32[]{:S(2)}, u32[]{:S(2)}) collective-permute-start(bf16[128,1024]{0,1:T(8,128)(2,1)} %fusion.31), channel_id=1, source_target_pairs={{0,8},{4,12},{8,0},{12,4},{1,9},{5,13},{9,1},{13,5},{2,10},{6,14},... | collective-permute-start | bytes 786440 | tf_op jit(solution)/shard_map/ppermute | solution.py:257
  211.1 61.5 %collective-permute-start.26 = (bf16[2,64,1280]{2,1,0:T(8,128)(2,1)}, bf16[2,64,1280]{2,1,0:T(8,128)(2,1)}, u32[]{:S(2)}, u32[]{:S(2)}) collective-permute-start(bf16[2,64,1280]{2,1,0:T(8,128)(2,1)} %param.37), channel_id=1, source_target_pairs={{0,0},{1,4},{2,8},{3,12},{4,1},{5,5},{6,9},{7,13},{8,2},{9,6},{10,... | collective-permute-start | bytes 983048 | tf_op jit(solution)/shard_map/ppermute | solution.py:265
  215.5 19.8 %collective-permute-start.21 = (bf16[128,1024]{0,1:T(8,128)(2,1)}, bf16[128,1024]{0,1:T(8,128)(2,1)S(1)}, u32[]{:S(2)}, u32[]{:S(2)}) collective-permute-start(bf16[128,1024]{0,1:T(8,128)(2,1)} %fusion.31), channel_id=1, source_target_pairs={{0,4},{4,8},{8,12},{12,0},{1,5},{5,9},{9,13},{13,1},{2,6},{6,10},{... | collective-permute-start | bytes 786440 | tf_op jit(solution)/shard_map/ppermute | solution.py:257
  241.9 7.5 %collective-permute-start.24 = (f32[512,64]{0,1:T(8,128)S(1)}, f32[512,64]{0,1:T(8,128)S(1)}, u32[]{:S(2)}, u32[]{:S(2)}) collective-permute-start(f32[512,64]{0,1:T(8,128)S(1)} %multiply_reduce_fusion.1), channel_id=1, source_target_pairs={{0,3},{1,0},{2,1},{3,2},{4,7},{5,4},{6,5},{7,6},{8,11},{9,8},{10,9... | collective-permute-start | bytes 393224 | tf_op jit(solution)/shard_map/ppermute | solution.py:260
  246.4 6.5 %collective-permute-start.22 = (f32[512,64]{0,1:T(8,128)S(1)}, f32[512,64]{0,1:T(8,128)S(1)}, u32[]{:S(2)}, u32[]{:S(2)}) collective-permute-start(f32[512,64]{0,1:T(8,128)S(1)} %multiply_reduce_fusion.1), channel_id=1, source_target_pairs={{0,1},{1,2},{2,3},{3,0},{4,5},{5,6},{6,7},{7,4},{8,9},{9,10},{10,1... | collective-permute-start | bytes 393224 | tf_op jit(solution)/shard_map/ppermute | solution.py:260
  246.4 9.5 %collective-permute-start.23 = (f32[512,64]{0,1:T(8,128)S(1)}, f32[512,64]{0,1:T(8,128)S(1)}, u32[]{:S(2)}, u32[]{:S(2)}) collective-permute-start(f32[512,64]{0,1:T(8,128)S(1)} %multiply_reduce_fusion.1), channel_id=1, source_target_pairs={{0,2},{1,3},{2,0},{3,1},{4,6},{5,7},{6,4},{7,5},{8,10},{9,11},{10,... | collective-permute-start | bytes 393224 | tf_op jit(solution)/shard_map/ppermute | solution.py:260
  255.9 16.7 %collective-permute-start.25 = (f32[512,64]{0,1:T(8,128)S(1)}, f32[512,64]{0,1:T(8,128)S(1)}, u32[]{:S(2)}, u32[]{:S(2)}) collective-permute-start(f32[512,64]{0,1:T(8,128)S(1)} %add_add_fusion.1), channel_id=1, source_target_pairs={{0,0},{1,4},{2,8},{3,12},{4,1},{5,5},{6,9},{7,13},{8,2},{9,6},{10,... | collective-permute-start | bytes 393224 | tf_op jit(solution)/shard_map/ppermute | solution.py:265
  276.8 15.4 %collective-permute-start.29 = (f32[128,1280]{1,0:T(8,128)}, f32[128,1280]{1,0:T(8,128)}, u32[]{:S(2)}, u32[]{:S(2)}) collective-permute-start(f32[128,1280]{1,0:T(8,128)} %get-tuple-element.18), channel_id=1, source_target_pairs={{0,3},{1,0},{2,1},{3,2},{4,7},{5,4},{6,5},{7,6},{8,11},{9,8},{10,9... | collective-permute-start | bytes 1966088 | tf_op jit(solution)/shard_map/ppermute | solution.py:260
  276.8 29.3 %collective-permute-start.28 = (f32[128,1280]{1,0:T(8,128)}, f32[128,1280]{1,0:T(8,128)}, u32[]{:S(2)}, u32[]{:S(2)}) collective-permute-start(f32[128,1280]{1,0:T(8,128)} %get-tuple-element.19), channel_id=1, source_target_pairs={{0,2},{1,3},{2,0},{3,1},{4,6},{5,7},{6,4},{7,5},{8,10},{9,11},{10,... | collective-permute-start | bytes 1966088 | tf_op jit(solution)/shard_map/ppermute | solution.py:260
  276.8 29.3 %collective-permute-start.27 = (f32[128,1280]{1,0:T(8,128)S(1)}, f32[128,1280]{1,0:T(8,128)}, u32[]{:S(2)}, u32[]{:S(2)}) collective-permute-start(f32[128,1280]{1,0:T(8,128)S(1)} %get-tuple-element.17), channel_id=1, source_target_pairs={{0,1},{1,2},{2,3},{3,0},{4,5},{5,6},{6,7},{7,4},{8,9},{9,10},{10,1... | collective-permute-start | bytes 1966088 | tf_op jit(solution)/shard_map/ppermute | solution.py:260
  307.9 19.5 %collective-permute-start.30 = (bf16[128,1280]{1,0:T(8,128)(2,1)S(1)}, bf16[128,1280]{1,0:T(8,128)(2,1)S(1)}, u32[]{:S(2)}, u32[]{:S(2)}) collective-permute-start(bf16[128,1280]{1,0:T(8,128)(2,1)S(1)} %add_convert_fusion), channel_id=1, source_target_pairs={{0,0},{1,4},{2,8},{3,12},{4,1},{5,5},{6,9},{7,13},{8,2},{9,6},{10,... | collective-permute-start | bytes 983048 | tf_op jit(solution)/shard_map/ppermute | solution.py:265
  (15 other events, 306.6 us)

commit v4 on v3

--- a/solution.py
+++ b/solution.py
@@ -364,7 +364,8 @@
     projected = jnp.concatenate([xchan_part, bc_part, step_part], axis=1)
     summed = block_rows(projected, here, length)
     for s in range(1, side):
-        summed = summed + moved(block_rows(projected, (here + s) % side, length), s, "ctx")
+        sent = block_rows(projected, (here + s) % side, length).astype(jnp.bfloat16)
+        summed = summed + moved(sent, s, "ctx").astype(jnp.float32)
     values = summed[:, : channels + bc_width]
     step_raw = summed[:, channels + bc_width :]
 
@@ -430,7 +431,8 @@
     out_part = base_part + adapter_part
     mixed_t = block_rows(out_part, lane, length)
     for s in range(1, side):
-        mixed_t = mixed_t + moved(block_rows(out_part, (lane + s) % side, length), s, "lane")
+        sent = block_rows(out_part, (lane + s) % side, length).astype(jnp.bfloat16)
+        mixed_t = mixed_t + moved(sent, s, "lane").astype(jnp.float32)
     return transposed(mixed_t.astype(jnp.bfloat16))
 
 

time: 329 us -> 284 us (0.86)
  waiting for transfers between devices: 193 us -> 152 us
    ppermute x6, waiting for transfers between devices: 66.4 us -> 42.4 us  [moved(): return lax.ppermute(block, 'ctx', pairs)]
    ppermute x9, waiting for transfers between devices: 49.8 us -> 35.8 us  [moved(): return lax.ppermute(block, ('tp', 'dp'), pairs)]
    unnamed x47 -> x39, local copies, waits for them, and re-layouts: 7.35 us -> 5.91 us
  transfers between devices with their start and end apart: 31 -> 31, of which waited for: 21 -> 21; matrix products, arithmetic and copies ran while one was open for 8% -> 10% of each run, Pallas kernels for 0% -> 0%
where the time goes in v4:
time: 284 us
  waiting for transfers between devices  152 us (54%)
  starting transfers between devices  81.8 us (29%)
  local copies, waits for them, and re-layouts  17.6 us (6%)
  matrix products  12.5 us (4%)
  other arithmetic  12.2 us (4%)
  blocking collectives  5.43 us (2%)
    ppermute x9, waiting for transfers between devices, moved(): return lax.ppermute(block, ('ctx', 'tp', 'dp'), pairs)  46.3 us
    ppermute x6, waiting for transfers between devices, moved(): return lax.ppermute(block, 'ctx', pairs)  42.4 us
    ppermute x9, starting transfers between devices, moved(): return lax.ppermute(block, ('ctx', 'tp', 'dp'), pairs)  38 us
    ppermute x9, waiting for transfers between devices, moved(): return lax.ppermute(block, ('tp', 'dp'), pairs)  35.8 us
    ppermute x3, waiting for transfers between devices, square_body(): state_in = lax.ppermute(local_state.astype(jnp.bfloat16), 'ctx', pairs)  27.1 us
    ppermute x6, starting transfers between devices, moved(): return lax.ppermute(block, 'ctx', pairs)  20.2 us
    ppermute x9, starting transfers between devices, moved(): return lax.ppermute(block, ('tp', 'dp'), pairs)  8.6 us
    ppermute x3, starting transfers between devices, square_body(): state_in = lax.ppermute(local_state.astype(jnp.bfloat16), 'ctx', pairs)  6.92 us
  transfers between devices with their start and end apart: 31, of which 21 were waited for; matrix products, arithmetic and copies ran while one was open for 10% of the time, Pallas kernels for 0%

profile of v4, /device:TPU:2, one launch (start us, length us, event | category | flops | bytes accessed | tf_op | source)
XLA Modules:
  0.0 283.5 jit_solution(6043097599061177917)
XLA Ops:
  0.0 4.7 %collective-permute-start = (bf16[128,1280]{1,0:T(8,128)(2,1)}, bf16[128,1280]{1,0:T(8,128)(2,1)S(1)}, u32[]{:S(2)}, u32[]{:S(2)}) collective-permute-start(bf16[128,1280]{1,0:T(8,128)(2,1)} %param.19), channel_id=1, source_target_pairs={{0,0},{1,4},{2,8},{3,12},{4,1},{5,5},{6,9},{7,13},{8,2},{9,6},{10,... | collective-permute-start | bytes 983048 | tf_op jit(solution)/shard_map/ppermute | solution.py:265
  4.7 3.2 %collective-permute-start.4 = (bf16[2,1280,64]{1,2,0:T(8,128)(2,1)}, bf16[2,1280,64]{1,2,0:T(8,128)(2,1)S(1)}, u32[]{:S(2)}, u32[]{:S(2)}) collective-permute-start(bf16[2,1280,64]{1,2,0:T(8,128)(2,1)} %param.33), channel_id=1, source_target_pairs={{0,0},{1,4},{2,8},{3,12},{4,1},{5,5},{6,9},{7,13},{8,2},{9,6},{10,... | collective-permute-start | bytes 983048 | tf_op jit(solution)/shard_map/ppermute | solution.py:265
  15.9 12.8 %collective-permute-done = bf16[128,1280]{1,0:T(8,128)(2,1)S(1)} collective-permute-done((bf16[128,1280]{1,0:T(8,128)(2,1)}, bf16[128,1280]{1,0:T(8,128)(2,1)S(1)}, u32[]{:S(2)}, u32[]{:S(2)}) %collective-permute-start) | collective-permute-done | bytes 327712 | tf_op jit(solution)/shard_map/ppermute | solution.py:265
  30.0 6.2 %collective-permute-done.1 = bf16[128,1280]{1,0:T(8,128)(2,1)S(1)} collective-permute-done((bf16[128,1280]{1,0:T(8,128)(2,1)S(1)}, bf16[128,1280]{1,0:T(8,128)(2,1)S(1)}, u32[]{:S(2)}, u32[]{:S(2)}) %collective-permute-start.1) | collective-permute-done | bytes 327712 | tf_op jit(solution)/shard_map/ppermute | solution.py:260
  36.3 7.0 %collective-permute-done.2 = bf16[128,1280]{1,0:T(8,128)(2,1)S(1)} collective-permute-done((bf16[128,1280]{1,0:T(8,128)(2,1)S(1)}, bf16[128,1280]{1,0:T(8,128)(2,1)S(1)}, u32[]{:S(2)}, u32[]{:S(2)}) %collective-permute-start.2) | collective-permute-done | bytes 327712 | tf_op jit(solution)/shard_map/ppermute | solution.py:260
  47.7 3.9 %collective-permute-start.5 = (f32[512,64]{0,1:T(8,128)S(1)}, f32[512,64]{0,1:T(8,128)S(1)}, u32[]{:S(2)}, u32[]{:S(2)}) collective-permute-start(f32[512,64]{0,1:T(8,128)S(1)} %multiply_reduce_fusion.2), channel_id=1, source_target_pairs={{0,0},{1,4},{2,8},{3,12},{4,1},{5,5},{6,9},{7,13},{8,2},{9,6},{10,... | collective-permute-start | bytes 393224 | tf_op jit(solution)/shard_map/ppermute | solution.py:265
  51.6 2.6 collective-permute-start.6
  55.6 15.1 %collective-permute-done.5 = f32[512,64]{0,1:T(8,128)S(1)} collective-permute-done((f32[512,64]{0,1:T(8,128)S(1)}, f32[512,64]{0,1:T(8,128)S(1)}, u32[]{:S(2)}, u32[]{:S(2)}) %collective-permute-start.5) | collective-permute-done | bytes 131104 | tf_op jit(solution)/shard_map/ppermute | solution.py:265
  74.8 4.6 %collective-permute-start.11 = (bf16[128,1168]{0,1:T(8,128)(2,1)S(1)}, bf16[128,1168]{0,1:T(8,128)(2,1)S(1)}, u32[]{:S(2)}, u32[]{:S(2)}) collective-permute-start(bf16[128,1168]{0,1:T(8,128)(2,1)S(1)} %get-tuple-element.21), channel_id=1, source_target_pairs={{0,12},{4,0},{8,4},{12,8},{1,13},{5,1},{9,5},{13,9},{2,14},{6,2},{... | collective-permute-start | bytes 897032 | tf_op jit(solution)/shard_map/ppermute | solution.py:257
  80.6 6.4 %collective-permute-done.11 = bf16[128,1168]{0,1:T(8,128)(2,1)S(1)} collective-permute-done((bf16[128,1168]{0,1:T(8,128)(2,1)S(1)}, bf16[128,1168]{0,1:T(8,128)(2,1)S(1)}, u32[]{:S(2)}, u32[]{:S(2)}) %collective-permute-start.11) | collective-permute-done | bytes 299040 | tf_op jit(solution)/shard_map/ppermute | solution.py:257
  87.0 17.5 %collective-permute-done.10 = bf16[128,1168]{0,1:T(8,128)(2,1)S(1)} collective-permute-done((bf16[128,1168]{0,1:T(8,128)(2,1)S(1)}, bf16[128,1168]{0,1:T(8,128)(2,1)S(1)}, u32[]{:S(2)}, u32[]{:S(2)}) %collective-permute-start.10) | collective-permute-done | bytes 299040 | tf_op jit(solution)/shard_map/ppermute | solution.py:257
  108.0 3.0 %collective-permute-start.14 = (bf16[16]{0:T(256)(128)(2,1)S(1)}, bf16[16]{0:T(256)(128)(2,1)}, u32[]{:S(2)}, u32[]{:S(2)}) collective-permute-start(bf16[16]{0:T(256)(128)(2,1)S(1)} %multiply_convert_fusion.4), channel_id=1, source_target_pairs={{0,8},{4,12},{1,9},{5,13},{2,10},{6,14},{3,11},{7,15},{16,24},{20,... | collective-permute-start | bytes 104 | tf_op jit(solution)/shard_map/ppermute | solution.py:398
  117.2 3.3 %divide_multiply_fusion = f32[128,1152]{0,1:T(8,128)S(1)} fusion(f32[128,1152]{0,1:T(8,128)} %slice.105, f32[3,1152]{0,1:T(8,128)S(1)} %copy.75, f32[128]{0:T(128)S(1)} %get-tuple-element.34, f32[1152]{0:T(1024)S(1)} %get-tuple-element.6, f32[128]{0:T(128)S(1)} %get-tuple-element.35, f32[1152]{0:T(1024)S(1)} %get-tuple-element.7, ...), kind=kLoop, calls=%fused_computation.50 | loop fusion | flops 2654208 | bytes 1213952 | tf_op jit(solution)/shard_map/jit(silu)/mul | solution.py:382
  120.6 5.4 %all_gather.3 = bf16[128,512]{0,1:T(8,128)(2,1)S(1)} all-gather(bf16[128,128]{0,1:T(8,128)(2,1)S(1)} %slice.194), channel_id=1, replica_groups=mesh['groups'=2,'ctx'=4,'tp'=2,'dp'=2] {'tp','dp'}, dimensions={1}, use_global_device_ids=true | all-gather | bytes 163840 | tf_op jit(solution)/shard_map/all_gather | solution.py:385
  126.6 4.2 %collective-permute-start.18 = (bf16[16,64,256]{2,1,0:T(8,128)(2,1)S(1)}, bf16[16,64,256]{2,1,0:T(8,128)(2,1)S(1)}, u32[]{:S(2)}, u32[]{:S(2)}) collective-permute-start(bf16[16,64,256]{2,1,0:T(8,128)(2,1)S(1)} %convolution_convert_fusion.1), channel_id=1, source_target_pairs={{0,4},{4,8},{8,12},{1,5},{5,9},{9,13},{2,6},{6,10},{10,14},{3,7},{... | collective-permute-start | bytes 1572872 | tf_op jit(solution)/shard_map/ppermute | solution.py:399
  137.9 5.2 %collective-permute-done.18 = bf16[16,64,256]{2,1,0:T(8,128)(2,1)S(1)} collective-permute-done((bf16[16,64,256]{2,1,0:T(8,128)(2,1)S(1)}, bf16[16,64,256]{2,1,0:T(8,128)(2,1)S(1)}, u32[]{:S(2)}, u32[]{:S(2)}) %collective-permute-start.18) | collective-permute-done | bytes 524320 | tf_op jit(solution)/shard_map/ppermute | solution.py:399
  143.0 11.3 %collective-permute-done.17 = bf16[16,64,256]{2,1,0:T(8,128)(2,1)S(1)} collective-permute-done((bf16[16,64,256]{2,1,0:T(8,128)(2,1)S(1)}, bf16[16,64,256]{2,1,0:T(8,128)(2,1)S(1)}, u32[]{:S(2)}, u32[]{:S(2)}) %collective-permute-start.17) | collective-permute-done | bytes 524320 | tf_op jit(solution)/shard_map/ppermute | solution.py:399
  154.3 10.7 %collective-permute-done.16 = bf16[16,64,256]{2,1,0:T(8,128)(2,1)S(1)} collective-permute-done((bf16[16,64,256]{2,1,0:T(8,128)(2,1)S(1)}, bf16[16,64,256]{2,1,0:T(8,128)(2,1)S(1)}, u32[]{:S(2)}, u32[]{:S(2)}) %collective-permute-start.16) | collective-permute-done | bytes 524320 | tf_op jit(solution)/shard_map/ppermute | solution.py:399
  166.8 14.3 %collective-permute-start.19 = (bf16[128,1024]{0,1:T(8,128)(2,1)}, bf16[128,1024]{0,1:T(8,128)(2,1)S(1)}, u32[]{:S(2)}, u32[]{:S(2)}) collective-permute-start(bf16[128,1024]{0,1:T(8,128)(2,1)} %fusion.31), channel_id=1, source_target_pairs={{0,12},{4,0},{8,4},{12,8},{1,13},{5,1},{9,5},{13,9},{2,14},{6,2},{... | collective-permute-start | bytes 786440 | tf_op jit(solution)/shard_map/ppermute | solution.py:257
  181.1 4.4 %collective-permute-start.26 = (bf16[2,64,1280]{2,1,0:T(8,128)(2,1)}, bf16[2,64,1280]{2,1,0:T(8,128)(2,1)}, u32[]{:S(2)}, u32[]{:S(2)}) collective-permute-start(bf16[2,64,1280]{2,1,0:T(8,128)(2,1)} %param.37), channel_id=1, source_target_pairs={{0,0},{1,4},{2,8},{3,12},{4,1},{5,5},{6,9},{7,13},{8,2},{9,6},{10,... | collective-permute-start | bytes 983048 | tf_op jit(solution)/shard_map/ppermute | solution.py:265
  185.8 2.4 collective-permute-done.19
  188.2 14.8 %collective-permute-done.20 = bf16[128,1024]{0,1:T(8,128)(2,1)} collective-permute-done((bf16[128,1024]{0,1:T(8,128)(2,1)}, bf16[128,1024]{0,1:T(8,128)(2,1)}, u32[]{:S(2)}, u32[]{:S(2)}) %collective-permute-start.20) | collective-permute-done | bytes 262176 | tf_op jit(solution)/shard_map/ppermute | solution.py:257
  212.0 4.4 %collective-permute-start.24 = (f32[512,64]{0,1:T(8,128)S(1)}, f32[512,64]{0,1:T(8,128)S(1)}, u32[]{:S(2)}, u32[]{:S(2)}) collective-permute-start(f32[512,64]{0,1:T(8,128)S(1)} %multiply_reduce_fusion.1), channel_id=1, source_target_pairs={{0,3},{1,0},{2,1},{3,2},{4,7},{5,4},{6,5},{7,6},{8,11},{9,8},{10,9... | collective-permute-start | bytes 393224 | tf_op jit(solution)/shard_map/ppermute | solution.py:260
  216.4 3.0 %collective-permute-start.23 = (f32[512,64]{0,1:T(8,128)S(1)}, f32[512,64]{0,1:T(8,128)S(1)}, u32[]{:S(2)}, u32[]{:S(2)}) collective-permute-start(f32[512,64]{0,1:T(8,128)S(1)} %multiply_reduce_fusion.1), channel_id=1, source_target_pairs={{0,2},{1,3},{2,0},{3,1},{4,6},{5,7},{6,4},{7,5},{8,10},{9,11},{10,... | collective-permute-start | bytes 393224 | tf_op jit(solution)/shard_map/ppermute | solution.py:260
  219.5 3.5 %collective-permute-done.22 = f32[512,64]{0,1:T(8,128)S(1)} collective-permute-done((f32[512,64]{0,1:T(8,128)S(1)}, f32[512,64]{0,1:T(8,128)S(1)}, u32[]{:S(2)}, u32[]{:S(2)}) %collective-permute-start.22) | collective-permute-done | bytes 131104 | tf_op jit(solution)/shard_map/ppermute | solution.py:260
  222.9 3.0 %collective-permute-done.23 = f32[512,64]{0,1:T(8,128)S(1)} collective-permute-done((f32[512,64]{0,1:T(8,128)S(1)}, f32[512,64]{0,1:T(8,128)S(1)}, u32[]{:S(2)}, u32[]{:S(2)}) %collective-permute-start.23) | collective-permute-done | bytes 131104 | tf_op jit(solution)/shard_map/ppermute | solution.py:260
  226.0 11.5 %collective-permute-start.25 = (f32[512,64]{0,1:T(8,128)S(1)}, f32[512,64]{0,1:T(8,128)S(1)}, u32[]{:S(2)}, u32[]{:S(2)}) collective-permute-start(f32[512,64]{0,1:T(8,128)S(1)} %add_add_fusion), channel_id=1, source_target_pairs={{0,0},{1,4},{2,8},{3,12},{4,1},{5,5},{6,9},{7,13},{8,2},{9,6},{10,... | collective-permute-start | bytes 393224 | tf_op jit(solution)/shard_map/ppermute | solution.py:265
  239.0 3.7 %collective-permute-done.25 = f32[512,64]{0,1:T(8,128)S(1)} collective-permute-done((f32[512,64]{0,1:T(8,128)S(1)}, f32[512,64]{0,1:T(8,128)S(1)}, u32[]{:S(2)}, u32[]{:S(2)}) %collective-permute-start.25) | collective-permute-done | bytes 131104 | tf_op jit(solution)/shard_map/ppermute | solution.py:265
  247.2 7.9 %collective-permute-done.29 = bf16[128,1280]{1,0:T(8,128)(2,1)S(1)} collective-permute-done((bf16[128,1280]{1,0:T(8,128)(2,1)}, bf16[128,1280]{1,0:T(8,128)(2,1)S(1)}, u32[]{:S(2)}, u32[]{:S(2)}) %collective-permute-start.29) | collective-permute-done | bytes 327712 | tf_op jit(solution)/shard_map/ppermute | solution.py:260
  255.1 6.8 %collective-permute-done.28 = bf16[128,1280]{1,0:T(8,128)(2,1)} collective-permute-done((bf16[128,1280]{1,0:T(8,128)(2,1)}, bf16[128,1280]{1,0:T(8,128)(2,1)}, u32[]{:S(2)}, u32[]{:S(2)}) %collective-permute-start.28) | collective-permute-done | bytes 327712 | tf_op jit(solution)/shard_map/ppermute | solution.py:260
  263.4 5.7 %collective-permute-start.30 = (bf16[128,1280]{1,0:T(8,128)(2,1)S(1)}, bf16[128,1280]{1,0:T(8,128)(2,1)S(1)}, u32[]{:S(2)}, u32[]{:S(2)}) collective-permute-start(bf16[128,1280]{1,0:T(8,128)(2,1)S(1)} %add_convert_fusion), channel_id=1, source_target_pairs={{0,0},{1,4},{2,8},{3,12},{4,1},{5,5},{6,9},{7,13},{8,2},{9,6},{10,... | collective-permute-start | bytes 983048 | tf_op jit(solution)/shard_map/ppermute | solution.py:265
  269.1 13.7 %collective-permute-done.30 = bf16[128,1280]{1,0:T(8,128)(2,1)S(1)} collective-permute-done((bf16[128,1280]{1,0:T(8,128)(2,1)S(1)}, bf16[128,1280]{1,0:T(8,128)(2,1)S(1)}, u32[]{:S(2)}, u32[]{:S(2)}) %collective-permute-start.30) | collective-permute-done | bytes 327712 | tf_op jit(solution)/shard_map/ppermute | solution.py:265
  (145 shorter events, 55.3 us)
Async XLA Ops:
  0.0 237.4 %copy-start = (bf16[1024,1280]{1,0:T(8,128)(2,1)S(1)}, bf16[1024,1280]{1,0:T(8,128)(2,1)}, u32[]{:S(2)}) copy-start(bf16[1024,1280]{1,0:T(8,128)(2,1)} %param.32) | copy-start | bytes 7864324
  0.0 28.7 %collective-permute-start = (bf16[128,1280]{1,0:T(8,128)(2,1)}, bf16[128,1280]{1,0:T(8,128)(2,1)S(1)}, u32[]{:S(2)}, u32[]{:S(2)}) collective-permute-start(bf16[128,1280]{1,0:T(8,128)(2,1)} %param.19), channel_id=1, source_target_pairs={{0,0},{1,4},{2,8},{3,12},{4,1},{5,5},{6,9},{7,13},{8,2},{9,6},{10,... | collective-permute-start | bytes 983048 | tf_op jit(solution)/shard_map/ppermute | solution.py:265
  4.7 40.2 %collective-permute-start.4 = (bf16[2,1280,64]{1,2,0:T(8,128)(2,1)}, bf16[2,1280,64]{1,2,0:T(8,128)(2,1)S(1)}, u32[]{:S(2)}, u32[]{:S(2)}) collective-permute-start(bf16[2,1280,64]{1,2,0:T(8,128)(2,1)} %param.33), channel_id=1, source_target_pairs={{0,0},{1,4},{2,8},{3,12},{4,1},{5,5},{6,9},{7,13},{8,2},{9,6},{10,... | collective-permute-start | bytes 983048 | tf_op jit(solution)/shard_map/ppermute | solution.py:265
  28.7 7.6 %collective-permute-start.1 = (bf16[128,1280]{1,0:T(8,128)(2,1)S(1)}, bf16[128,1280]{1,0:T(8,128)(2,1)S(1)}, u32[]{:S(2)}, u32[]{:S(2)}) collective-permute-start(bf16[128,1280]{1,0:T(8,128)(2,1)S(1)} %collective-permute-done), channel_id=1, source_target_pairs={{0,3},{1,0},{2,1},{3,2},{4,7},{5,4},{6,5},{7,6},{8,11},{9,8},{10,9... | collective-permute-start | bytes 983048 | tf_op jit(solution)/shard_map/ppermute | solution.py:260
  29.4 13.9 %collective-permute-start.2 = (bf16[128,1280]{1,0:T(8,128)(2,1)S(1)}, bf16[128,1280]{1,0:T(8,128)(2,1)S(1)}, u32[]{:S(2)}, u32[]{:S(2)}) collective-permute-start(bf16[128,1280]{1,0:T(8,128)(2,1)S(1)} %collective-permute-done), channel_id=1, source_target_pairs={{0,2},{1,3},{2,0},{3,1},{4,6},{5,7},{6,4},{7,5},{8,10},{9,11},{10,... | collective-permute-start | bytes 983048 | tf_op jit(solution)/shard_map/ppermute | solution.py:260
  29.5 15.2 %collective-permute-start.3 = (bf16[128,1280]{1,0:T(8,128)(2,1)S(1)}, bf16[128,1280]{1,0:T(8,128)(2,1)S(1)}, u32[]{:S(2)}, u32[]{:S(2)}) collective-permute-start(bf16[128,1280]{1,0:T(8,128)(2,1)S(1)} %collective-permute-done), channel_id=1, source_target_pairs={{0,1},{1,2},{2,3},{3,0},{4,5},{5,6},{6,7},{7,4},{8,9},{9,10},{10,1... | collective-permute-start | bytes 983048 | tf_op jit(solution)/shard_map/ppermute | solution.py:260
  45.6 10.0 %collective-permute-start.8 = (f32[512,64]{0,1:T(8,128)S(1)}, f32[512,64]{0,1:T(8,128)S(1)}, u32[]{:S(2)}, u32[]{:S(2)}) collective-permute-start(f32[512,64]{0,1:T(8,128)S(1)} %multiply_reduce_fusion.2), channel_id=1, source_target_pairs={{0,3},{1,7},{2,11},{3,15},{4,0},{5,4},{6,8},{7,12},{8,1},{9,5},{10... | collective-permute-start | bytes 393224 | tf_op jit(solution)/shard_map/ppermute | solution.py:265
  47.5 8.2 %collective-permute-start.7 = (f32[512,64]{0,1:T(8,128)S(1)}, f32[512,64]{0,1:T(8,128)S(1)}, u32[]{:S(2)}, u32[]{:S(2)}) collective-permute-start(f32[512,64]{0,1:T(8,128)S(1)} %multiply_reduce_fusion.2), channel_id=1, source_target_pairs={{0,2},{1,6},{2,10},{3,14},{4,3},{5,7},{6,11},{7,15},{8,0},{9,4},{1... | collective-permute-start | bytes 393224 | tf_op jit(solution)/shard_map/ppermute | solution.py:265
  47.7 23.1 %collective-permute-start.5 = (f32[512,64]{0,1:T(8,128)S(1)}, f32[512,64]{0,1:T(8,128)S(1)}, u32[]{:S(2)}, u32[]{:S(2)}) collective-permute-start(f32[512,64]{0,1:T(8,128)S(1)} %multiply_reduce_fusion.2), channel_id=1, source_target_pairs={{0,0},{1,4},{2,8},{3,12},{4,1},{5,5},{6,9},{7,13},{8,2},{9,6},{10,... | collective-permute-start | bytes 393224 | tf_op jit(solution)/shard_map/ppermute | solution.py:265
  51.6 19.1 %collective-permute-start.6 = (f32[512,64]{0,1:T(8,128)S(1)}, f32[512,64]{0,1:T(8,128)S(1)}, u32[]{:S(2)}, u32[]{:S(2)}) collective-permute-start(f32[512,64]{0,1:T(8,128)S(1)} %multiply_reduce_fusion.2), channel_id=1, source_target_pairs={{0,1},{1,5},{2,9},{3,13},{4,2},{5,6},{6,10},{7,14},{8,3},{9,7},{10... | collective-permute-start | bytes 393224 | tf_op jit(solution)/shard_map/ppermute | solution.py:265
  74.8 12.2 %collective-permute-start.11 = (bf16[128,1168]{0,1:T(8,128)(2,1)S(1)}, bf16[128,1168]{0,1:T(8,128)(2,1)S(1)}, u32[]{:S(2)}, u32[]{:S(2)}) collective-permute-start(bf16[128,1168]{0,1:T(8,128)(2,1)S(1)} %get-tuple-element.21), channel_id=1, source_target_pairs={{0,12},{4,0},{8,4},{12,8},{1,13},{5,1},{9,5},{13,9},{2,14},{6,2},{... | collective-permute-start | bytes 897032 | tf_op jit(solution)/shard_map/ppermute | solution.py:257
  79.5 25.1 %collective-permute-start.10 = (bf16[128,1168]{0,1:T(8,128)(2,1)S(1)}, bf16[128,1168]{0,1:T(8,128)(2,1)S(1)}, u32[]{:S(2)}, u32[]{:S(2)}) collective-permute-start(bf16[128,1168]{0,1:T(8,128)(2,1)S(1)} %get-tuple-element.22), channel_id=1, source_target_pairs={{0,8},{4,12},{8,0},{12,4},{1,9},{5,13},{9,1},{13,5},{2,10},{6,14},... | collective-permute-start | bytes 897032 | tf_op jit(solution)/shard_map/ppermute | solution.py:257
  79.5 25.1 %collective-permute-start.9 = (bf16[128,1168]{0,1:T(8,128)(2,1)S(1)}, bf16[128,1168]{0,1:T(8,128)(2,1)S(1)}, u32[]{:S(2)}, u32[]{:S(2)}) collective-permute-start(bf16[128,1168]{0,1:T(8,128)(2,1)S(1)} %get-tuple-element.20), channel_id=1, source_target_pairs={{0,4},{4,8},{8,12},{12,0},{1,5},{5,9},{9,13},{13,1},{2,6},{6,10},{... | collective-permute-start | bytes 897032 | tf_op jit(solution)/shard_map/ppermute | solution.py:257
  106.1 26.1 %collective-permute-start.15 = (bf16[16]{0:T(256)(128)(2,1)S(1)}, bf16[16]{0:T(256)(128)(2,1)}, u32[]{:S(2)}, u32[]{:S(2)}) collective-permute-start(bf16[16]{0:T(256)(128)(2,1)S(1)} %multiply_convert_fusion.4), channel_id=1, source_target_pairs={{0,12},{1,13},{2,14},{3,15},{16,28},{17,29},{18,30},{19,31}} | collective-permute-start | bytes 104 | tf_op jit(solution)/shard_map/ppermute | solution.py:398
  108.0 26.2 %collective-permute-start.14 = (bf16[16]{0:T(256)(128)(2,1)S(1)}, bf16[16]{0:T(256)(128)(2,1)}, u32[]{:S(2)}, u32[]{:S(2)}) collective-permute-start(bf16[16]{0:T(256)(128)(2,1)S(1)} %multiply_convert_fusion.4), channel_id=1, source_target_pairs={{0,8},{4,12},{1,9},{5,13},{2,10},{6,14},{3,11},{7,15},{16,24},{20,... | collective-permute-start | bytes 104 | tf_op jit(solution)/shard_map/ppermute | solution.py:398
  111.0 23.9 %collective-permute-start.13 = (bf16[16]{0:T(256)(128)(2,1)S(1)}, bf16[16]{0:T(256)(128)(2,1)}, u32[]{:S(2)}, u32[]{:S(2)}) collective-permute-start(bf16[16]{0:T(256)(128)(2,1)S(1)} %multiply_convert_fusion.4), channel_id=1, source_target_pairs={{0,4},{4,8},{8,12},{1,5},{5,9},{9,13},{2,6},{6,10},{10,14},{3,7},{... | collective-permute-start | bytes 104 | tf_op jit(solution)/shard_map/ppermute | solution.py:398
  114.0 2.9 %collective-permute-start.12 = (f32[3,1152]{1,0:T(4,128)S(1)}, f32[3,1152]{1,0:T(4,128)S(1)}, u32[]{:S(2)}, u32[]{:S(2)}) collective-permute-start(f32[3,1152]{1,0:T(4,128)S(1)} %copy.74), channel_id=1, source_target_pairs={{0,4},{4,8},{8,12},{1,5},{5,9},{9,13},{2,6},{6,10},{10,14},{3,7},{... | collective-permute-start | bytes 41480 | tf_op jit(solution)/shard_map/ppermute | solution.py:18
  126.6 16.4 %collective-permute-start.18 = (bf16[16,64,256]{2,1,0:T(8,128)(2,1)S(1)}, bf16[16,64,256]{2,1,0:T(8,128)(2,1)S(1)}, u32[]{:S(2)}, u32[]{:S(2)}) collective-permute-start(bf16[16,64,256]{2,1,0:T(8,128)(2,1)S(1)} %convolution_convert_fusion.1), channel_id=1, source_target_pairs={{0,4},{4,8},{8,12},{1,5},{5,9},{9,13},{2,6},{6,10},{10,14},{3,7},{... | collective-permute-start | bytes 1572872 | tf_op jit(solution)/shard_map/ppermute | solution.py:399
  130.8 23.5 %collective-permute-start.17 = (bf16[16,64,256]{2,1,0:T(8,128)(2,1)S(1)}, bf16[16,64,256]{2,1,0:T(8,128)(2,1)S(1)}, u32[]{:S(2)}, u32[]{:S(2)}) collective-permute-start(bf16[16,64,256]{2,1,0:T(8,128)(2,1)S(1)} %convolution_convert_fusion.1), channel_id=1, source_target_pairs={{0,8},{4,12},{1,9},{5,13},{2,10},{6,14},{3,11},{7,15},{16,24},{20,... | collective-permute-start | bytes 1572872 | tf_op jit(solution)/shard_map/ppermute | solution.py:399
  132.2 32.8 %collective-permute-start.16 = (bf16[16,64,256]{2,1,0:T(8,128)(2,1)S(1)}, bf16[16,64,256]{2,1,0:T(8,128)(2,1)S(1)}, u32[]{:S(2)}, u32[]{:S(2)}) collective-permute-start(bf16[16,64,256]{2,1,0:T(8,128)(2,1)S(1)} %convolution_convert_fusion.1), channel_id=1, source_target_pairs={{0,12},{1,13},{2,14},{3,15},{16,28},{17,29},{18,30},{19,31}} | collective-permute-start | bytes 1572872 | tf_op jit(solution)/shard_map/ppermute | solution.py:399
  166.8 21.4 %collective-permute-start.19 = (bf16[128,1024]{0,1:T(8,128)(2,1)}, bf16[128,1024]{0,1:T(8,128)(2,1)S(1)}, u32[]{:S(2)}, u32[]{:S(2)}) collective-permute-start(bf16[128,1024]{0,1:T(8,128)(2,1)} %fusion.31), channel_id=1, source_target_pairs={{0,12},{4,0},{8,4},{12,8},{1,13},{5,1},{9,5},{13,9},{2,14},{6,2},{... | collective-permute-start | bytes 786440 | tf_op jit(solution)/shard_map/ppermute | solution.py:257
  181.1 21.9 %collective-permute-start.20 = (bf16[128,1024]{0,1:T(8,128)(2,1)}, bf16[128,1024]{0,1:T(8,128)(2,1)}, u32[]{:S(2)}, u32[]{:S(2)}) collective-permute-start(bf16[128,1024]{0,1:T(8,128)(2,1)} %fusion.31), channel_id=1, source_target_pairs={{0,8},{4,12},{8,0},{12,4},{1,9},{5,13},{9,1},{13,5},{2,10},{6,14},... | collective-permute-start | bytes 786440 | tf_op jit(solution)/shard_map/ppermute | solution.py:257
  181.1 61.6 %collective-permute-start.26 = (bf16[2,64,1280]{2,1,0:T(8,128)(2,1)}, bf16[2,64,1280]{2,1,0:T(8,128)(2,1)}, u32[]{:S(2)}, u32[]{:S(2)}) collective-permute-start(bf16[2,64,1280]{2,1,0:T(8,128)(2,1)} %param.37), channel_id=1, source_target_pairs={{0,0},{1,4},{2,8},{3,12},{4,1},{5,5},{6,9},{7,13},{8,2},{9,6},{10,... | collective-permute-start | bytes 983048 | tf_op jit(solution)/shard_map/ppermute | solution.py:265
  185.6 19.8 %collective-permute-start.21 = (bf16[128,1024]{0,1:T(8,128)(2,1)}, bf16[128,1024]{0,1:T(8,128)(2,1)S(1)}, u32[]{:S(2)}, u32[]{:S(2)}) collective-permute-start(bf16[128,1024]{0,1:T(8,128)(2,1)} %fusion.31), channel_id=1, source_target_pairs={{0,4},{4,8},{8,12},{12,0},{1,5},{5,9},{9,13},{13,1},{2,6},{6,10},{... | collective-permute-start | bytes 786440 | tf_op jit(solution)/shard_map/ppermute | solution.py:257
  212.0 7.5 %collective-permute-start.24 = (f32[512,64]{0,1:T(8,128)S(1)}, f32[512,64]{0,1:T(8,128)S(1)}, u32[]{:S(2)}, u32[]{:S(2)}) collective-permute-start(f32[512,64]{0,1:T(8,128)S(1)} %multiply_reduce_fusion.1), channel_id=1, source_target_pairs={{0,3},{1,0},{2,1},{3,2},{4,7},{5,4},{6,5},{7,6},{8,11},{9,8},{10,9... | collective-permute-start | bytes 393224 | tf_op jit(solution)/shard_map/ppermute | solution.py:260
  216.4 6.5 %collective-permute-start.22 = (f32[512,64]{0,1:T(8,128)S(1)}, f32[512,64]{0,1:T(8,128)S(1)}, u32[]{:S(2)}, u32[]{:S(2)}) collective-permute-start(f32[512,64]{0,1:T(8,128)S(1)} %multiply_reduce_fusion.1), channel_id=1, source_target_pairs={{0,1},{1,2},{2,3},{3,0},{4,5},{5,6},{6,7},{7,4},{8,9},{9,10},{10,1... | collective-permute-start | bytes 393224 | tf_op jit(solution)/shard_map/ppermute | solution.py:260
  216.4 9.5 %collective-permute-start.23 = (f32[512,64]{0,1:T(8,128)S(1)}, f32[512,64]{0,1:T(8,128)S(1)}, u32[]{:S(2)}, u32[]{:S(2)}) collective-permute-start(f32[512,64]{0,1:T(8,128)S(1)} %multiply_reduce_fusion.1), channel_id=1, source_target_pairs={{0,2},{1,3},{2,0},{3,1},{4,6},{5,7},{6,4},{7,5},{8,10},{9,11},{10,... | collective-permute-start | bytes 393224 | tf_op jit(solution)/shard_map/ppermute | solution.py:260
  226.0 16.8 %collective-permute-start.25 = (f32[512,64]{0,1:T(8,128)S(1)}, f32[512,64]{0,1:T(8,128)S(1)}, u32[]{:S(2)}, u32[]{:S(2)}) collective-permute-start(f32[512,64]{0,1:T(8,128)S(1)} %add_add_fusion), channel_id=1, source_target_pairs={{0,0},{1,4},{2,8},{3,12},{4,1},{5,5},{6,9},{7,13},{8,2},{9,6},{10,... | collective-permute-start | bytes 393224 | tf_op jit(solution)/shard_map/ppermute | solution.py:265
  246.7 8.4 %collective-permute-start.29 = (bf16[128,1280]{1,0:T(8,128)(2,1)}, bf16[128,1280]{1,0:T(8,128)(2,1)S(1)}, u32[]{:S(2)}, u32[]{:S(2)}) collective-permute-start(bf16[128,1280]{1,0:T(8,128)(2,1)} %get-tuple-element.18), channel_id=1, source_target_pairs={{0,3},{1,0},{2,1},{3,2},{4,7},{5,4},{6,5},{7,6},{8,11},{9,8},{10,9... | collective-permute-start | bytes 983048 | tf_op jit(solution)/shard_map/ppermute | solution.py:260
  246.7 15.3 %collective-permute-start.28 = (bf16[128,1280]{1,0:T(8,128)(2,1)}, bf16[128,1280]{1,0:T(8,128)(2,1)}, u32[]{:S(2)}, u32[]{:S(2)}) collective-permute-start(bf16[128,1280]{1,0:T(8,128)(2,1)} %get-tuple-element.19), channel_id=1, source_target_pairs={{0,2},{1,3},{2,0},{3,1},{4,6},{5,7},{6,4},{7,5},{8,10},{9,11},{10,... | collective-permute-start | bytes 983048 | tf_op jit(solution)/shard_map/ppermute | solution.py:260
  246.7 15.3 %collective-permute-start.27 = (bf16[128,1280]{1,0:T(8,128)(2,1)S(1)}, bf16[128,1280]{1,0:T(8,128)(2,1)}, u32[]{:S(2)}, u32[]{:S(2)}) collective-permute-start(bf16[128,1280]{1,0:T(8,128)(2,1)S(1)} %get-tuple-element.17), channel_id=1, source_target_pairs={{0,1},{1,2},{2,3},{3,0},{4,5},{5,6},{6,7},{7,4},{8,9},{9,10},{10,1... | collective-permute-start | bytes 983048 | tf_op jit(solution)/shard_map/ppermute | solution.py:260
  263.4 19.4 %collective-permute-start.30 = (bf16[128,1280]{1,0:T(8,128)(2,1)S(1)}, bf16[128,1280]{1,0:T(8,128)(2,1)S(1)}, u32[]{:S(2)}, u32[]{:S(2)}) collective-permute-start(bf16[128,1280]{1,0:T(8,128)(2,1)S(1)} %add_convert_fusion), channel_id=1, source_target_pairs={{0,0},{1,4},{2,8},{3,12},{4,1},{5,5},{6,9},{7,13},{8,2},{9,6},{10,... | collective-permute-start | bytes 983048 | tf_op jit(solution)/shard_map/ppermute | solution.py:265
  (11 other events, 227.1 us)

commit v5 on v4

--- a/solution.py
+++ b/solution.py
@@ -308,7 +308,6 @@
 ):
     length = tokens.shape[0]
     side = lax.axis_size("ctx")
-    stream = side * length
     taps = convolution_x_taps.shape[0]
     bank_entries = adapter_down_input.shape[0]
     rank_value = adapter_down_input.shape[2]
@@ -319,54 +318,78 @@
     lane = lax.axis_index(("tp", "dp"))
     start_pos = here * length
     request_ends = jnp.cumsum(lengths, dtype=jnp.int32)
-    every_position = jnp.arange(stream, dtype=jnp.int32)
-    every_segment = segment_of(every_position, request_ends)
-    slot_indices = adapter_store_slot[request_adapter_ids]
-    request_count = lengths.shape[0]
-    stream_onehot = every_segment[:, None] == jnp.arange(request_count, dtype=jnp.int32)[None, :]
-    slot_of_position = jnp.sum(
-        jnp.where(stream_onehot, slot_indices[None, :], 0), axis=1, dtype=jnp.int32
-    )
-    entry_ids = jnp.arange(bank_entries, dtype=jnp.int32)[None, :]
-    owned_here = slot_of_position[:, None] == here * bank_entries + entry_ids
-    owned_lane = slot_of_position[:, None] == lane * bank_entries + entry_ids
     positions = start_pos + jnp.arange(length, dtype=jnp.int32)
     segment = segment_of(positions, request_ends)
     previous = segment_of(jnp.reshape(start_pos - 1, (1,)), request_ends)[0]
+    slot_indices = adapter_store_slot[request_adapter_ids]
+    request_count = lengths.shape[0]
+    local_onehot = segment[:, None] == jnp.arange(request_count, dtype=jnp.int32)[None, :]
+    slot_of_position = jnp.sum(
+        jnp.where(local_onehot, slot_indices[None, :], 0), axis=1, dtype=jnp.int32
+    )
+    slot_owned = slot_of_position[:, None] == jnp.arange(side * bank_entries, dtype=jnp.int32)[None, :]
+
+    panels = (
+        adapter_down_input,
+        adapter_up_xchan,
+        adapter_up_bc,
+        adapter_down_output,
+        adapter_up_output,
+    )
+    packed = jnp.concatenate([panel.reshape(bank_entries, -1) for panel in panels], axis=1)
+    store = in_order([packed] + [moved(packed, s, "ctx") for s in range(1, side)], here)
+    offsets = [0]
+    for panel in panels:
+        offsets.append(offsets[-1] + panel[0].size)
+    down_in_all, up_x_all, up_bc_all, down_out_all, up_out_all = [
+        store[:, offsets[i] : offsets[i + 1]].reshape((side * bank_entries,) + panel.shape[1:])
+        for i, panel in enumerate(panels)
+    ]
+
+    def lane_total(part):
+        return part + sum(moved(part, s, "lane") for s in range(1, side))
+
+    def picked(rows, bank):
+        every = jnp.einsum("pf,afr->par", rows, bank, preferred_element_type=jnp.float32)
+        return jnp.sum(every * slot_owned[:, :, None].astype(jnp.float32), axis=1)
+
+    def spread(hidden):
+        return owned_rows(hidden, slot_owned).astype(jnp.bfloat16)
+
+    hidden_wide = spread(lane_total(picked(tokens, down_in_all)))
 
     tokens_t = transposed(tokens)
     stream_rows = in_order(
         [tokens_t] + [moved(tokens_t, s, "lane") for s in range(1, side)], lane
     )
-    down_in_t = transposed(adapter_down_input)
-    up_out_t = transposed(adapter_up_output)
-    down_part = jnp.einsum(
-        "pf,efr->per", stream_rows, down_in_t, preferred_element_type=jnp.float32
-    )
-    down_pick = jnp.sum(
-        down_part * owned_lane[:, :, None].astype(jnp.float32), axis=1
-    )
-    rank_hidden = sum(moved(down_pick, s, "rows") for s in range(side))
-    hidden_wide = owned_rows(rank_hidden, owned_here).astype(jnp.bfloat16)
-    xchan_part = jnp.dot(
-        stream_rows, xchan_input_weight, preferred_element_type=jnp.float32
-    ) + jnp.dot(
-        hidden_wide,
-        adapter_up_xchan.reshape(bank_entries * rank_value, -1),
-        preferred_element_type=jnp.float32,
-    )
-    bc_part = jnp.dot(stream_rows, bc_input_weight, preferred_element_type=jnp.float32) + jnp.dot(
-        hidden_wide,
-        adapter_up_bc.reshape(bank_entries * rank_value, -1),
-        preferred_element_type=jnp.float32,
-    )
-    step_part = jnp.dot(stream_rows, step_input_weight, preferred_element_type=jnp.float32)
-    projected = jnp.concatenate([xchan_part, bc_part, step_part], axis=1)
+    projected = jnp.concatenate(
+        [
+            jnp.dot(stream_rows, xchan_input_weight, preferred_element_type=jnp.float32),
+            jnp.dot(stream_rows, bc_input_weight, preferred_element_type=jnp.float32),
+            jnp.dot(stream_rows, step_input_weight, preferred_element_type=jnp.float32),
+        ],
+        axis=1,
+    )
     summed = block_rows(projected, here, length)
     for s in range(1, side):
         sent = block_rows(projected, (here + s) % side, length).astype(jnp.bfloat16)
         summed = summed + moved(sent, s, "ctx").astype(jnp.float32)
-    values = summed[:, : channels + bc_width]
+    adapter_values = jnp.concatenate(
+        [
+            jnp.dot(
+                hidden_wide,
+                up_x_all.reshape(side * bank_entries * rank_value, -1),
+                preferred_element_type=jnp.float32,
+            ),
+            jnp.dot(
+                hidden_wide,
+                up_bc_all.reshape(side * bank_entries * rank_value, -1),
+                preferred_element_type=jnp.float32,
+            ),
+        ],
+        axis=1,
+    )
+    values = summed[:, : channels + bc_width] + adapter_values
     step_raw = summed[:, channels + bc_width :]
 
     kernel = jnp.concatenate([convolution_x_taps, convolution_bc_taps], axis=1)
@@ -391,7 +414,6 @@
     inner_out, local_state, enter_weight, carry_decay = span_parts(
         x_heads, b_proj, c_proj, step_size, log_decay, segment, previous
     )
-
     entering = jnp.zeros_like(local_state)
     for s in range(side - 1, 0, -1):
         pairs = [(a, a + s) for a in range(side - s)]
@@ -410,30 +432,25 @@
     scale = lax.rsqrt(jnp.mean(mixer_out * mixer_out, axis=1, keepdims=True) + NORM_EPSILON)
     normalized_rows = (mixer_out * scale * output_norm_gain[None, :]).astype(jnp.bfloat16)
 
+    output_wide = spread(lane_total(picked(normalized_rows, down_out_all)))
+    adapter_output = jnp.dot(
+        output_wide,
+        up_out_all.reshape(side * bank_entries * rank_value, -1),
+        preferred_element_type=jnp.float32,
+    )
     normed_stream = in_order(
         [normalized_rows] + [moved(normalized_rows, s, "ctx") for s in range(1, side)], here
     )
-    out_down_part = jnp.einsum(
-        "pc,ecr->per", normed_stream, adapter_down_output, preferred_element_type=jnp.float32
-    )
-    out_down_pick = jnp.sum(out_down_part * owned_here[:, :, None].astype(jnp.float32), axis=1)
-    rank_hidden_output = transposed(
-        out_down_pick + sum(moved(out_down_pick, s, "lane") for s in range(1, side))
-    )
-    base_part = jnp.dot(
-        normed_stream, output_weight, preferred_element_type=jnp.float32
-    ).astype(jnp.bfloat16).astype(jnp.float32)
-    adapter_part = jnp.dot(
-        owned_rows(rank_hidden_output, owned_lane).astype(jnp.bfloat16),
-        up_out_t.reshape(bank_entries * rank_value, -1),
-        preferred_element_type=jnp.float32,
-    )
-    out_part = base_part + adapter_part
-    mixed_t = block_rows(out_part, lane, length)
+    base_part = jnp.dot(normed_stream, output_weight, preferred_element_type=jnp.float32).astype(
+        jnp.bfloat16
+    )
+    mixed_t = block_rows(base_part, lane, length).astype(jnp.float32)
     for s in range(1, side):
-        sent = block_rows(out_part, (lane + s) % side, length).astype(jnp.bfloat16)
-        mixed_t = mixed_t + moved(sent, s, "lane").astype(jnp.float32)
-    return transposed(mixed_t.astype(jnp.bfloat16))
+        mixed_t = mixed_t + moved(
+            block_rows(base_part, (lane + s) % side, length), s, "lane"
+        ).astype(jnp.float32)
+    mixed = transposed(mixed_t.astype(jnp.bfloat16)).astype(jnp.float32) + adapter_output
+    return mixed.astype(jnp.bfloat16)
 
 
 def solution(mesh):

time: 284 us -> 394 us (1.39)
  local copies, waits for them, and re-layouts: 17.6 us -> 87.7 us
  starting transfers between devices: 81.8 us -> 101 us
  waiting for transfers between devices: 152 us -> 163 us
  matrix products: 12.5 us -> 16.5 us
    ppermute x9 -> x2, waiting for transfers between devices: 46.3 us -> 98 us  [moved(): return lax.ppermute(block, ('ctx', 'tp', 'dp'), pairs)]
    unnamed x39 -> x84, local copies, waits for them, and re-layouts: 5.91 us -> 39.4 us
    ppermute x9 -> x2, starting transfers between devices: 38 us -> 6.71 us  [moved(): return lax.ppermute(block, ('ctx', 'tp', 'dp'), pairs)]
    ppermute x3, starting transfers between devices: 6.59 us -> 37.9 us  [square_body(): decay_in = lax.ppermute(carry_decay.astype(jnp.bfloat16), 'ctx', pairs)]
    reshape x0 -> x8, local copies, waits for them, and re-layouts: none -> 21.6 us  [the longest x3 11.5 us: square_body(): store[:, offsets[i]:offsets[i + 1]]]
    ppermute x6 -> x9, waiting for transfers between devices: 42.4 us -> 23.6 us  [moved(): return lax.ppermute(block, 'ctx', pairs)]
    ppermute x6 -> x9, starting transfers between devices: 20.2 us -> 38.4 us  [moved(): return lax.ppermute(block, 'ctx', pairs)]
    ppermute x3, waiting for transfers between devices: 27.1 us -> 13.1 us  [square_body(): state_in = lax.ppermute(local_state.astype(jnp.bfloat16), 'ctx', pairs)]
  transfers between devices with their start and end apart: 31 -> 30, of which waited for: 21 -> 13; matrix products, arithmetic and copies ran while one was open for 10% -> 25% of each run, Pallas kernels for 0% -> 0%
where the time goes in v5:
time: 394 us; the launch traced here: 391 us
  waiting for transfers between devices  163 us (41%)
  starting transfers between devices  101 us (26%)
  local copies, waits for them, and re-layouts  87.7 us (22%)
  matrix products  16.5 us (4%)
  other arithmetic  15.5 us (4%)
  blocking collectives  5.43 us (1%)
    ppermute x2, waiting for transfers between devices, moved(): return lax.ppermute(block, ('ctx', 'tp', 'dp'), pairs)  98 us
    unnamed x84, local copies, waits for them, and re-layouts  39.4 us
    ppermute x9, starting transfers between devices, moved(): return lax.ppermute(block, 'ctx', pairs)  38.4 us
    ppermute x3, starting transfers between devices, square_body(): decay_in = lax.ppermute(carry_decay.astype(jnp.bfloat16), 'ctx', pairs)  37.9 us
    ppermute x12, waiting for transfers between devices, moved(): return lax.ppermute(block, ('tp', 'dp'), pairs)  27.4 us
    ppermute x9, waiting for transfers between devices, moved(): return lax.ppermute(block, 'ctx', pairs)  23.6 us
    ppermute x3, waiting for transfers between devices, square_body(): state_in = lax.ppermute(local_state.astype(jnp.bfloat16), 'ctx', pairs)  13.1 us
    reshape x3, local copies, waits for them, and re-layouts, square_body(): store[:, offsets[i]:offsets[i + 1]]  11.5 us
  transfers between devices with their start and end apart: 30, of which 13 were waited for; matrix products, arithmetic and copies ran while one was open for 25% of the time, Pallas kernels for 0%

profile of v5, /device:TPU:2, one launch (start us, length us, event | category | flops | bytes accessed | tf_op | source)
XLA Modules:
  0.0 391.4 jit_solution(671372769681969373)
XLA Ops:
  13.7 3.6 collective-permute-start.7
  17.3 4.8 %collective-permute-start = (bf16[128,1280]{1,0:T(8,128)(2,1)}, bf16[128,1280]{1,0:T(8,128)(2,1)S(1)}, u32[]{:S(2)}, u32[]{:S(2)}) collective-permute-start(bf16[128,1280]{1,0:T(8,128)(2,1)} %param.19), channel_id=1, source_target_pairs={{0,0},{1,4},{2,8},{3,12},{4,1},{5,5},{6,9},{7,13},{8,2},{9,6},{10,... | collective-permute-start | bytes 983048 | tf_op jit(solution)/shard_map/ppermute | solution.py:265
  26.7 82.6 %collective-permute-done = bf16[128,1280]{1,0:T(8,128)(2,1)S(1)} collective-permute-done((bf16[128,1280]{1,0:T(8,128)(2,1)}, bf16[128,1280]{1,0:T(8,128)(2,1)S(1)}, u32[]{:S(2)}, u32[]{:S(2)}) %collective-permute-start) | collective-permute-done | bytes 327712 | tf_op jit(solution)/shard_map/ppermute | solution.py:265
  110.0 7.4 %collective-permute-done.1 = bf16[128,1280]{1,0:T(8,128)(2,1)S(1)} collective-permute-done((bf16[128,1280]{1,0:T(8,128)(2,1)S(1)}, bf16[128,1280]{1,0:T(8,128)(2,1)S(1)}, u32[]{:S(2)}, u32[]{:S(2)}) %collective-permute-start.1) | collective-permute-done | bytes 327712 | tf_op jit(solution)/shard_map/ppermute | solution.py:260
  117.5 7.0 %collective-permute-done.2 = bf16[128,1280]{1,0:T(8,128)(2,1)S(1)} collective-permute-done((bf16[128,1280]{1,0:T(8,128)(2,1)S(1)}, bf16[128,1280]{1,0:T(8,128)(2,1)S(1)}, u32[]{:S(2)}, u32[]{:S(2)}) %collective-permute-start.2) | collective-permute-done | bytes 327712 | tf_op jit(solution)/shard_map/ppermute | solution.py:260
  135.9 5.5 %collective-permute-done.4 = bf16[128,1168]{0,1:T(8,128)(2,1)S(1)} collective-permute-done((bf16[128,1168]{0,1:T(8,128)(2,1)S(1)}, bf16[128,1168]{0,1:T(8,128)(2,1)S(1)}, u32[]{:S(2)}, u32[]{:S(2)}) %collective-permute-start.4) | collective-permute-done | bytes 299040 | tf_op jit(solution)/shard_map/ppermute | solution.py:257
  141.4 11.9 %collective-permute-start.9 = (bf16[2,303104]{1,0:T(2,128)(2,1)}, bf16[2,303104]{1,0:T(2,128)(2,1)}, u32[]{:S(2)}, u32[]{:S(2)}) collective-permute-start(bf16[2,303104]{1,0:T(2,128)(2,1)} %constant_dynamic-update-slice_fusion.2), channel_id=1, source_target_pairs={{0,4},{4,8},{8,12},{12,0},{1,5},{5,9},{9,13},{13,1},{2,6},{6,10},{... | collective-permute-start | bytes 3637256 | tf_op jit(solution)/shard_map/ppermute | solution.py:257
  156.3 34.2 %collective-permute-start.14 = (bf16[16]{0:T(256)(128)(2,1)}, bf16[16]{0:T(256)(128)(2,1)}, u32[]{:S(2)}, u32[]{:S(2)}) collective-permute-start(bf16[16]{0:T(256)(128)(2,1)} %multiply_convert_fusion.19), channel_id=1, source_target_pairs={{0,4},{4,8},{8,12},{1,5},{5,9},{9,13},{2,6},{6,10},{10,14},{3,7},{... | collective-permute-start | bytes 104 | tf_op jit(solution)/shard_map/ppermute | solution.py:420
  195.5 3.0 bitcast_dynamic-update-slice_fusion.4
  198.6 3.0 bitcast_dynamic-update-slice_fusion.2
  201.6 3.0 bitcast_dynamic-update-slice_fusion
  204.6 3.0 bitcast_dynamic-update-slice_fusion.7
  207.7 3.0 bitcast_dynamic-update-slice_fusion.5
  210.7 3.0 bitcast_dynamic-update-slice_fusion.3
  213.7 3.0 bitcast_dynamic-update-slice_fusion.1
  216.8 4.4 %constant_dynamic-slice_fusion.4 = bf16[4,2,303104]{2,1,0:T(2,128)(2,1)} fusion(bf16[8,2,303104]{2,1,0:T(2,128)(2,1)S(1)} %bitcast_dynamic-update-slice_fusion.1, s32[]{:T(128)S(6)} %select_n.122), kind=kLoop, calls=%fused_computation.159 | loop fusion | bytes 9699332 | tf_op jit(solution)/shard_map/jit(_roll_dynamic)/dynamic_slice | solution.py:274
  221.2 6.4 %reshape.284 = bf16[8,303104]{1,0:T(8,128)(2,1)} reshape(bf16[4,2,303104]{2,1,0:T(2,128)(2,1)} %constant_dynamic-slice_fusion.4) | data formatting | bytes 9699328 | tf_op jit(solution)/shard_map/reshape | solution.py:275
  227.6 3.4 fusion.62
  234.0 4.3 %reshape.285 = bf16[8,1280,64]{2,1,0:T(8,128)(2,1)} reshape(bf16[655360]{0:T(1024)(128)(2,1)} %reshape.318) | data formatting | bytes 2621440 | tf_op jit(solution)/shard_map/reshape | solution.py:345
  242.8 3.1 fusion.63
  260.0 3.1 divide_multiply_fusion
  263.2 5.4 %all_gather.3 = bf16[128,512]{0,1:T(8,128)(2,1)S(1)} all-gather(bf16[128,128]{0,1:T(8,128)(2,1)S(1)} %slice.259), channel_id=1, replica_groups=mesh['groups'=2,'ctx'=4,'tp'=2,'dp'=2] {'tp','dp'}, dimensions={1}, use_global_device_ids=true | all-gather | bytes 163840 | tf_op jit(solution)/shard_map/all_gather | solution.py:408
  275.4 3.2 collective-permute-start.19
  280.5 4.5 %reshape.291 = bf16[8,1024,64]{2,1,0:T(8,128)(2,1)} reshape(bf16[8,65536]{1,0:T(8,128)(2,1)} %get-tuple-element.18) | data formatting | bytes 2097152 | tf_op jit(solution)/shard_map/reshape | solution.py:345
  287.7 3.0 reshape_reshape.11
  295.6 10.7 %collective-permute-done.19 = bf16[16,64,256]{2,1,0:T(8,128)(2,1)} collective-permute-done((bf16[16,64,256]{2,1,0:T(8,128)(2,1)}, bf16[16,64,256]{2,1,0:T(8,128)(2,1)}, u32[]{:S(2)}, u32[]{:S(2)}) %collective-permute-start.19) | collective-permute-done | bytes 524320 | tf_op jit(solution)/shard_map/ppermute | solution.py:421
  315.5 4.3 %collective-permute-start.20 = (bf16[128,1024]{1,0:T(8,128)(2,1)}, bf16[128,1024]{1,0:T(8,128)(2,1)S(1)}, u32[]{:S(2)}, u32[]{:S(2)}) collective-permute-start(bf16[128,1024]{1,0:T(8,128)(2,1)} %multiply_convert_fusion.2), channel_id=1, source_target_pairs={{0,12},{4,0},{8,4},{12,8},{1,13},{5,1},{9,5},{13,9},{2,14},{6,2},{... | collective-permute-start | bytes 786440 | tf_op jit(solution)/shard_map/ppermute | solution.py:257
  319.8 10.3 %collective-permute-start.21 = (bf16[128,1024]{1,0:T(8,128)(2,1)}, bf16[128,1024]{1,0:T(8,128)(2,1)}, u32[]{:S(2)}, u32[]{:S(2)}) collective-permute-start(bf16[128,1024]{1,0:T(8,128)(2,1)} %multiply_convert_fusion.2), channel_id=1, source_target_pairs={{0,8},{4,12},{8,0},{12,4},{1,9},{5,13},{9,1},{13,5},{2,10},{6,14},... | collective-permute-start | bytes 786440 | tf_op jit(solution)/shard_map/ppermute | solution.py:257
  335.8 17.1 %collective-permute-done.21 = bf16[128,1024]{1,0:T(8,128)(2,1)} collective-permute-done((bf16[128,1024]{1,0:T(8,128)(2,1)}, bf16[128,1024]{1,0:T(8,128)(2,1)}, u32[]{:S(2)}, u32[]{:S(2)}) %collective-permute-start.21) | collective-permute-done | bytes 262176 | tf_op jit(solution)/shard_map/ppermute | solution.py:257
  359.7 6.6 %collective-permute-done.23 = bf16[128,1280]{1,0:T(8,128)(2,1)S(1)} collective-permute-done((bf16[128,1280]{1,0:T(8,128)(2,1)S(1)}, bf16[128,1280]{1,0:T(8,128)(2,1)S(1)}, u32[]{:S(2)}, u32[]{:S(2)}) %collective-permute-start.23) | collective-permute-done | bytes 327712 | tf_op jit(solution)/shard_map/ppermute | solution.py:260
  367.6 5.2 %collective-permute-done.25 = bf16[128,1280]{1,0:T(8,128)(2,1)S(1)} collective-permute-done((bf16[128,1280]{1,0:T(8,128)(2,1)S(1)}, bf16[128,1280]{1,0:T(8,128)(2,1)S(1)}, u32[]{:S(2)}, u32[]{:S(2)}) %collective-permute-start.25) | collective-permute-done | bytes 327712 | tf_op jit(solution)/shard_map/ppermute | solution.py:260
  374.9 15.4 %collective-permute-done.26 = bf16[128,1280]{1,0:T(8,128)(2,1)S(1)} collective-permute-done((bf16[128,1280]{1,0:T(8,128)(2,1)S(1)}, bf16[128,1280]{1,0:T(8,128)(2,1)S(1)}, u32[]{:S(2)}, u32[]{:S(2)}) %collective-permute-start.26) | collective-permute-done | bytes 327712 | tf_op jit(solution)/shard_map/ppermute | solution.py:265
  (215 shorter events, 100.5 us)
Async XLA Ops:
  0.0 355.2 %copy-start = (bf16[1024,1280]{1,0:T(8,128)(2,1)S(1)}, bf16[1024,1280]{1,0:T(8,128)(2,1)}, u32[]{:S(2)}) copy-start(bf16[1024,1280]{1,0:T(8,128)(2,1)} %param.32) | copy-start | bytes 7864324
  13.7 179.2 %collective-permute-start.7 = (bf16[2,303104]{1,0:T(2,128)(2,1)}, bf16[2,303104]{1,0:T(2,128)(2,1)}, u32[]{:S(2)}, u32[]{:S(2)}) collective-permute-start(bf16[2,303104]{1,0:T(2,128)(2,1)} %constant_dynamic-update-slice_fusion.2), channel_id=1, source_target_pairs={{0,12},{4,0},{8,4},{12,8},{1,13},{5,1},{9,5},{13,9},{2,14},{6,2},{... | collective-permute-start | bytes 3637256 | tf_op jit(solution)/shard_map/ppermute | solution.py:257
  17.3 178.2 %collective-permute-start.8 = (bf16[2,303104]{1,0:T(2,128)(2,1)}, bf16[2,303104]{1,0:T(2,128)(2,1)}, u32[]{:S(2)}, u32[]{:S(2)}) collective-permute-start(bf16[2,303104]{1,0:T(2,128)(2,1)} %constant_dynamic-update-slice_fusion.2), channel_id=1, source_target_pairs={{0,8},{4,12},{8,0},{12,4},{1,9},{5,13},{9,1},{13,5},{2,10},{6,14},... | collective-permute-start | bytes 3637256 | tf_op jit(solution)/shard_map/ppermute | solution.py:257
  17.3 92.0 %collective-permute-start = (bf16[128,1280]{1,0:T(8,128)(2,1)}, bf16[128,1280]{1,0:T(8,128)(2,1)S(1)}, u32[]{:S(2)}, u32[]{:S(2)}) collective-permute-start(bf16[128,1280]{1,0:T(8,128)(2,1)} %param.19), channel_id=1, source_target_pairs={{0,0},{1,4},{2,8},{3,12},{4,1},{5,5},{6,9},{7,13},{8,2},{9,6},{10,... | collective-permute-start | bytes 983048 | tf_op jit(solution)/shard_map/ppermute | solution.py:265
  109.3 8.1 %collective-permute-start.1 = (bf16[128,1280]{1,0:T(8,128)(2,1)S(1)}, bf16[128,1280]{1,0:T(8,128)(2,1)S(1)}, u32[]{:S(2)}, u32[]{:S(2)}) collective-permute-start(bf16[128,1280]{1,0:T(8,128)(2,1)S(1)} %collective-permute-done), channel_id=1, source_target_pairs={{0,3},{1,0},{2,1},{3,2},{4,7},{5,4},{6,5},{7,6},{8,11},{9,8},{10,9... | collective-permute-start | bytes 983048 | tf_op jit(solution)/shard_map/ppermute | solution.py:260
  109.4 141.3 %copy-start.12 = (f32[128]{0:T(128)}, f32[128]{0:T(128)S(1)}, u32[]{:S(2)}) copy-start(f32[128]{0:T(128)S(1)} %get-tuple-element.33) | copy-start | bytes 1540
  109.4 15.0 %collective-permute-start.2 = (bf16[128,1280]{1,0:T(8,128)(2,1)S(1)}, bf16[128,1280]{1,0:T(8,128)(2,1)S(1)}, u32[]{:S(2)}, u32[]{:S(2)}) collective-permute-start(bf16[128,1280]{1,0:T(8,128)(2,1)S(1)} %collective-permute-done), channel_id=1, source_target_pairs={{0,2},{1,3},{2,0},{3,1},{4,6},{5,7},{6,4},{7,5},{8,10},{9,11},{10,... | collective-permute-start | bytes 983048 | tf_op jit(solution)/shard_map/ppermute | solution.py:260
  109.5 15.0 %collective-permute-start.3 = (bf16[128,1280]{1,0:T(8,128)(2,1)S(1)}, bf16[128,1280]{1,0:T(8,128)(2,1)S(1)}, u32[]{:S(2)}, u32[]{:S(2)}) collective-permute-start(bf16[128,1280]{1,0:T(8,128)(2,1)S(1)} %collective-permute-done), channel_id=1, source_target_pairs={{0,1},{1,2},{2,3},{3,0},{4,5},{5,6},{6,7},{7,4},{8,9},{9,10},{10,1... | collective-permute-start | bytes 983048 | tf_op jit(solution)/shard_map/ppermute | solution.py:260
  129.5 12.0 %collective-permute-start.4 = (bf16[128,1168]{0,1:T(8,128)(2,1)S(1)}, bf16[128,1168]{0,1:T(8,128)(2,1)S(1)}, u32[]{:S(2)}, u32[]{:S(2)}) collective-permute-start(bf16[128,1168]{0,1:T(8,128)(2,1)S(1)} %get-tuple-element.19), channel_id=1, source_target_pairs={{0,4},{4,8},{8,12},{12,0},{1,5},{5,9},{9,13},{13,1},{2,6},{6,10},{... | collective-permute-start | bytes 897032 | tf_op jit(solution)/shard_map/ppermute | solution.py:257
  131.8 22.4 %collective-permute-start.5 = (bf16[128,1168]{0,1:T(8,128)(2,1)S(1)}, bf16[128,1168]{0,1:T(8,128)(2,1)S(1)}, u32[]{:S(2)}, u32[]{:S(2)}) collective-permute-start(bf16[128,1168]{0,1:T(8,128)(2,1)S(1)} %get-tuple-element.21), channel_id=1, source_target_pairs={{0,8},{4,12},{8,0},{12,4},{1,9},{5,13},{9,1},{13,5},{2,10},{6,14},... | collective-permute-start | bytes 897032 | tf_op jit(solution)/shard_map/ppermute | solution.py:257
  133.4 20.9 %collective-permute-start.6 = (bf16[128,1168]{0,1:T(8,128)(2,1)S(1)}, bf16[128,1168]{0,1:T(8,128)(2,1)S(1)}, u32[]{:S(2)}, u32[]{:S(2)}) collective-permute-start(bf16[128,1168]{0,1:T(8,128)(2,1)S(1)} %get-tuple-element.20), channel_id=1, source_target_pairs={{0,12},{4,0},{8,4},{12,8},{1,13},{5,1},{9,5},{13,9},{2,14},{6,2},{... | collective-permute-start | bytes 897032 | tf_op jit(solution)/shard_map/ppermute | solution.py:257
  141.4 57.1 %collective-permute-start.9 = (bf16[2,303104]{1,0:T(2,128)(2,1)}, bf16[2,303104]{1,0:T(2,128)(2,1)}, u32[]{:S(2)}, u32[]{:S(2)}) collective-permute-start(bf16[2,303104]{1,0:T(2,128)(2,1)} %constant_dynamic-update-slice_fusion.2), channel_id=1, source_target_pairs={{0,4},{4,8},{8,12},{12,0},{1,5},{5,9},{9,13},{13,1},{2,6},{6,10},{... | collective-permute-start | bytes 3637256 | tf_op jit(solution)/shard_map/ppermute | solution.py:257
  156.3 122.9 %collective-permute-start.14 = (bf16[16]{0:T(256)(128)(2,1)}, bf16[16]{0:T(256)(128)(2,1)}, u32[]{:S(2)}, u32[]{:S(2)}) collective-permute-start(bf16[16]{0:T(256)(128)(2,1)} %multiply_convert_fusion.19), channel_id=1, source_target_pairs={{0,4},{4,8},{8,12},{1,5},{5,9},{9,13},{2,6},{6,10},{10,14},{3,7},{... | collective-permute-start | bytes 104 | tf_op jit(solution)/shard_map/ppermute | solution.py:420
  190.5 89.4 %collective-permute-start.15 = (bf16[16]{0:T(256)(128)(2,1)}, bf16[16]{0:T(256)(128)(2,1)}, u32[]{:S(2)}, u32[]{:S(2)}) collective-permute-start(bf16[16]{0:T(256)(128)(2,1)} %multiply_convert_fusion.19), channel_id=1, source_target_pairs={{0,8},{4,12},{1,9},{5,13},{2,10},{6,14},{3,11},{7,15},{16,24},{20,... | collective-permute-start | bytes 104 | tf_op jit(solution)/shard_map/ppermute | solution.py:420
  241.0 7.7 %collective-permute-start.10 = (f32[128,64]{0,1:T(8,128)S(1)}, f32[128,64]{0,1:T(8,128)S(1)}, u32[]{:S(2)}, u32[]{:S(2)}) collective-permute-start(f32[128,64]{0,1:T(8,128)S(1)} %fusion.3), channel_id=1, source_target_pairs={{0,1},{1,2},{2,3},{3,0},{4,5},{5,6},{6,7},{7,4},{8,9},{9,10},{10,1... | collective-permute-start | bytes 98312 | tf_op jit(solution)/shard_map/ppermute | solution.py:260
  241.0 9.5 %collective-permute-start.11 = (f32[128,64]{0,1:T(8,128)S(1)}, f32[128,64]{0,1:T(8,128)S(1)}, u32[]{:S(2)}, u32[]{:S(2)}) collective-permute-start(f32[128,64]{0,1:T(8,128)S(1)} %fusion.3), channel_id=1, source_target_pairs={{0,2},{1,3},{2,0},{3,1},{4,6},{5,7},{6,4},{7,5},{8,10},{9,11},{10,... | collective-permute-start | bytes 98312 | tf_op jit(solution)/shard_map/ppermute | solution.py:260
  241.1 9.4 %collective-permute-start.12 = (f32[128,64]{0,1:T(8,128)S(1)}, f32[128,64]{0,1:T(8,128)S(1)}, u32[]{:S(2)}, u32[]{:S(2)}) collective-permute-start(f32[128,64]{0,1:T(8,128)S(1)} %fusion.3), channel_id=1, source_target_pairs={{0,3},{1,0},{2,1},{3,2},{4,7},{5,4},{6,5},{7,6},{8,11},{9,8},{10,9... | collective-permute-start | bytes 98312 | tf_op jit(solution)/shard_map/ppermute | solution.py:260
  248.7 26.7 %collective-permute-start.16 = (bf16[16]{0:T(256)(128)(2,1)}, bf16[16]{0:T(256)(128)(2,1)}, u32[]{:S(2)}, u32[]{:S(2)}) collective-permute-start(bf16[16]{0:T(256)(128)(2,1)} %multiply_convert_fusion.19), channel_id=1, source_target_pairs={{0,12},{1,13},{2,14},{3,15},{16,28},{17,29},{18,30},{19,31}} | collective-permute-start | bytes 104 | tf_op jit(solution)/shard_map/ppermute | solution.py:420
  256.2 2.8 collective-permute-start.13
  270.0 23.1 %collective-permute-start.17 = (bf16[16,64,256]{2,1,0:T(8,128)(2,1)}, bf16[16,64,256]{2,1,0:T(8,128)(2,1)}, u32[]{:S(2)}, u32[]{:S(2)}) collective-permute-start(bf16[16,64,256]{2,1,0:T(8,128)(2,1)} %convolution_convert_fusion.1), channel_id=1, source_target_pairs={{0,12},{1,13},{2,14},{3,15},{16,28},{17,29},{18,30},{19,31}} | collective-permute-start | bytes 1572872 | tf_op jit(solution)/shard_map/ppermute | solution.py:421
  272.5 23.1 %collective-permute-start.18 = (bf16[16,64,256]{2,1,0:T(8,128)(2,1)}, bf16[16,64,256]{2,1,0:T(8,128)(2,1)}, u32[]{:S(2)}, u32[]{:S(2)}) collective-permute-start(bf16[16,64,256]{2,1,0:T(8,128)(2,1)} %convolution_convert_fusion.1), channel_id=1, source_target_pairs={{0,8},{4,12},{1,9},{5,13},{2,10},{6,14},{3,11},{7,15},{16,24},{20,... | collective-permute-start | bytes 1572872 | tf_op jit(solution)/shard_map/ppermute | solution.py:421
  275.4 30.9 %collective-permute-start.19 = (bf16[16,64,256]{2,1,0:T(8,128)(2,1)}, bf16[16,64,256]{2,1,0:T(8,128)(2,1)}, u32[]{:S(2)}, u32[]{:S(2)}) collective-permute-start(bf16[16,64,256]{2,1,0:T(8,128)(2,1)} %convolution_convert_fusion.1), channel_id=1, source_target_pairs={{0,4},{4,8},{8,12},{1,5},{5,9},{9,13},{2,6},{6,10},{10,14},{3,7},{... | collective-permute-start | bytes 1572872 | tf_op jit(solution)/shard_map/ppermute | solution.py:421
  309.4 21.7 %collective-permute-start.27 = (f32[128,64]{0,1:T(8,128)S(1)}, f32[128,64]{0,1:T(8,128)S(1)}, u32[]{:S(2)}, u32[]{:S(2)}) collective-permute-start(f32[128,64]{0,1:T(8,128)S(1)} %multiply_reduce_fusion.1), channel_id=1, source_target_pairs={{0,1},{1,2},{2,3},{3,0},{4,5},{5,6},{6,7},{7,4},{8,9},{9,10},{10,1... | collective-permute-start | bytes 98312 | tf_op jit(solution)/shard_map/ppermute | solution.py:260
  309.5 23.7 %collective-permute-start.28 = (f32[128,64]{0,1:T(8,128)S(1)}, f32[128,64]{0,1:T(8,128)S(1)}, u32[]{:S(2)}, u32[]{:S(2)}) collective-permute-start(f32[128,64]{0,1:T(8,128)S(1)} %multiply_reduce_fusion.1), channel_id=1, source_target_pairs={{0,2},{1,3},{2,0},{3,1},{4,6},{5,7},{6,4},{7,5},{8,10},{9,11},{10,... | collective-permute-start | bytes 98312 | tf_op jit(solution)/shard_map/ppermute | solution.py:260
  311.3 21.9 %collective-permute-start.29 = (f32[128,64]{0,1:T(8,128)S(1)}, f32[128,64]{0,1:T(8,128)S(1)}, u32[]{:S(2)}, u32[]{:S(2)}) collective-permute-start(f32[128,64]{0,1:T(8,128)S(1)} %multiply_reduce_fusion.1), channel_id=1, source_target_pairs={{0,3},{1,0},{2,1},{3,2},{4,7},{5,4},{6,5},{7,6},{8,11},{9,8},{10,9... | collective-permute-start | bytes 98312 | tf_op jit(solution)/shard_map/ppermute | solution.py:260
  315.5 20.2 %collective-permute-start.20 = (bf16[128,1024]{1,0:T(8,128)(2,1)}, bf16[128,1024]{1,0:T(8,128)(2,1)S(1)}, u32[]{:S(2)}, u32[]{:S(2)}) collective-permute-start(bf16[128,1024]{1,0:T(8,128)(2,1)} %multiply_convert_fusion.2), channel_id=1, source_target_pairs={{0,12},{4,0},{8,4},{12,8},{1,13},{5,1},{9,5},{13,9},{2,14},{6,2},{... | collective-permute-start | bytes 786440 | tf_op jit(solution)/shard_map/ppermute | solution.py:257
  319.8 33.1 %collective-permute-start.21 = (bf16[128,1024]{1,0:T(8,128)(2,1)}, bf16[128,1024]{1,0:T(8,128)(2,1)}, u32[]{:S(2)}, u32[]{:S(2)}) collective-permute-start(bf16[128,1024]{1,0:T(8,128)(2,1)} %multiply_convert_fusion.2), channel_id=1, source_target_pairs={{0,8},{4,12},{8,0},{12,4},{1,9},{5,13},{9,1},{13,5},{2,10},{6,14},... | collective-permute-start | bytes 786440 | tf_op jit(solution)/shard_map/ppermute | solution.py:257
  331.1 22.7 %collective-permute-start.22 = (bf16[128,1024]{1,0:T(8,128)(2,1)}, bf16[128,1024]{1,0:T(8,128)(2,1)S(1)}, u32[]{:S(2)}, u32[]{:S(2)}) collective-permute-start(bf16[128,1024]{1,0:T(8,128)(2,1)} %multiply_convert_fusion.2), channel_id=1, source_target_pairs={{0,4},{4,8},{8,12},{12,0},{1,5},{5,9},{9,13},{13,1},{2,6},{6,10},{... | collective-permute-start | bytes 786440 | tf_op jit(solution)/shard_map/ppermute | solution.py:257
  356.9 9.5 %collective-permute-start.23 = (bf16[128,1280]{1,0:T(8,128)(2,1)S(1)}, bf16[128,1280]{1,0:T(8,128)(2,1)S(1)}, u32[]{:S(2)}, u32[]{:S(2)}) collective-permute-start(bf16[128,1280]{1,0:T(8,128)(2,1)S(1)} %get-tuple-element.22), channel_id=1, source_target_pairs={{0,1},{1,2},{2,3},{3,0},{4,5},{5,6},{6,7},{7,4},{8,9},{9,10},{10,1... | collective-permute-start | bytes 983048 | tf_op jit(solution)/shard_map/ppermute | solution.py:260
  357.0 10.6 %collective-permute-start.24 = (bf16[128,1280]{1,0:T(8,128)(2,1)S(1)}, bf16[128,1280]{1,0:T(8,128)(2,1)S(1)}, u32[]{:S(2)}, u32[]{:S(2)}) collective-permute-start(bf16[128,1280]{1,0:T(8,128)(2,1)S(1)} %get-tuple-element.24), channel_id=1, source_target_pairs={{0,2},{1,3},{2,0},{3,1},{4,6},{5,7},{6,4},{7,5},{8,10},{9,11},{10,... | collective-permute-start | bytes 983048 | tf_op jit(solution)/shard_map/ppermute | solution.py:260
  358.3 14.5 %collective-permute-start.25 = (bf16[128,1280]{1,0:T(8,128)(2,1)S(1)}, bf16[128,1280]{1,0:T(8,128)(2,1)S(1)}, u32[]{:S(2)}, u32[]{:S(2)}) collective-permute-start(bf16[128,1280]{1,0:T(8,128)(2,1)S(1)} %get-tuple-element.23), channel_id=1, source_target_pairs={{0,3},{1,0},{2,1},{3,2},{4,7},{5,4},{6,5},{7,6},{8,11},{9,8},{10,9... | collective-permute-start | bytes 983048 | tf_op jit(solution)/shard_map/ppermute | solution.py:260
  373.0 17.3 %collective-permute-start.26 = (bf16[128,1280]{1,0:T(8,128)(2,1)S(1)}, bf16[128,1280]{1,0:T(8,128)(2,1)S(1)}, u32[]{:S(2)}, u32[]{:S(2)}) collective-permute-start(bf16[128,1280]{1,0:T(8,128)(2,1)S(1)} %add_convert_fusion.1), channel_id=1, source_target_pairs={{0,0},{1,4},{2,8},{3,12},{4,1},{5,5},{6,9},{7,13},{8,2},{9,6},{10,... | collective-permute-start | bytes 983048 | tf_op jit(solution)/shard_map/ppermute | solution.py:265
  (26 other events, 1086.7 us)

commit v6 on v4

--- a/solution.py
+++ b/solution.py
@@ -362,16 +362,22 @@
     )
     step_part = jnp.dot(stream_rows, step_input_weight, preferred_element_type=jnp.float32)
     projected = jnp.concatenate([xchan_part, bc_part, step_part], axis=1)
-    summed = block_rows(projected, here, length)
+    padded = jnp.concatenate(
+        [jnp.zeros((taps - 1, projected.shape[1]), projected.dtype), projected], axis=0
+    )
+
+    def with_tail(index):
+        return lax.dynamic_slice_in_dim(padded, index * length, length + taps - 1, 0)
+
+    summed = with_tail(here)
     for s in range(1, side):
-        sent = block_rows(projected, (here + s) % side, length).astype(jnp.bfloat16)
+        sent = with_tail((here + s) % side).astype(jnp.bfloat16)
         summed = summed + moved(sent, s, "ctx").astype(jnp.float32)
-    values = summed[:, : channels + bc_width]
-    step_raw = summed[:, channels + bc_width :]
+    extended = summed[:, : channels + bc_width]
+    values = extended[taps - 1 :]
+    step_raw = summed[taps - 1 :, channels + bc_width :]
 
     kernel = jnp.concatenate([convolution_x_taps, convolution_bc_taps], axis=1)
-    tail_rows = passed_along(values[length - (taps - 1) :], "ctx", 1)
-    extended = jnp.concatenate([tail_rows, values], axis=0)
     extended_segment = segment_of(
         start_pos - (taps - 1) + jnp.arange(length + taps - 1, dtype=jnp.int32), request_ends
     )
@@ -392,14 +398,13 @@
         x_heads, b_proj, c_proj, step_size, log_decay, segment, previous
     )
 
+    decay_row = jnp.broadcast_to(carry_decay[:, None, None], (head_count, 1, local_state.shape[2]))
+    state_and_decay = jnp.concatenate([decay_row, local_state], axis=1).astype(jnp.bfloat16)
     entering = jnp.zeros_like(local_state)
     for s in range(side - 1, 0, -1):
         pairs = [(a, a + s) for a in range(side - s)]
-        decay_in = lax.ppermute(carry_decay.astype(jnp.bfloat16), "ctx", pairs)
-        state_in = lax.ppermute(local_state.astype(jnp.bfloat16), "ctx", pairs)
-        entering = decay_in.astype(jnp.float32)[:, None, None] * entering + state_in.astype(
-            jnp.float32
-        )
+        both_in = lax.ppermute(state_and_decay, "ctx", pairs).astype(jnp.float32)
+        entering = both_in[:, :1, : local_state.shape[2]][:, :, :1] * entering + both_in[:, 1:]
     entered = (
         jnp.einsum("tn,hdn->thd", c_proj.astype(jnp.float32), entering, precision=FULL_PRECISION)
         * enter_weight[:, :, None]

time: 284 us -> 288 us (1.014)
  starting transfers between devices: 81.8 us -> 60.9 us
  local copies, waits for them, and re-layouts: 17.6 us -> 30.5 us
  other arithmetic: 12.2 us -> 18.9 us
  waiting for transfers between devices: 152 us -> 155 us
    ppermute x9, starting transfers between devices: 38 us -> 26.7 us  [moved(): return lax.ppermute(block, ('ctx', 'tp', 'dp'), pairs)]
    ppermute x7 -> x3, starting transfers between devices: 15 us -> 6.45 us  [square_body(): both_in = lax.ppermute(state_and_decay, 'ctx', pairs).astype(jnp.float32)]
    convert_element_type x1 -> x4, local copies, waits for them, and re-layouts: 0.24 us -> 6.71 us  [square_body(): sent = with_tail((here + s) % side).astype(jnp.bfloat16)]
    ppermute x9, waiting for transfers between devices: 46.3 us -> 51.5 us  [moved(): return lax.ppermute(block, ('ctx', 'tp', 'dp'), pairs)]
    ppermute x1 -> x3, local copies, waits for them, and re-layouts: 0.24 us -> 5.28 us  [moved(): return lax.ppermute(block, 'ctx', pairs)]
    unnamed x39 -> x47, local copies, waits for them, and re-layouts: 5.91 us -> 9.22 us
    ppermute x7 -> x3, waiting for transfers between devices: 27.4 us -> 24.2 us  [square_body(): both_in = lax.ppermute(state_and_decay, 'ctx', pairs).astype(jnp.float32)]
    slice x3 -> x2, local copies, waits for them, and re-layouts: 3.16 us -> 0.23 us  [square_body(): both_in[:, :1, :local_state.shape[2]][:, :, :1] * entering + both_in[:, 1:]]
  transfers between devices with their start and end apart: 31 -> 27, of which waited for: 21 -> 20; matrix products, arithmetic and copies ran while one was open for 10% -> 10% of each run, Pallas kernels for 0% -> 0%
where the time goes in v6:
time: 288 us; the launch traced here: 286 us
  waiting for transfers between devices  155 us (54%)
  starting transfers between devices  60.9 us (21%)
  local copies, waits for them, and re-layouts  30.5 us (11%)
  other arithmetic  18.9 us (7%)
  matrix products  13.5 us (5%)
  blocking collectives  5.43 us (2%)
    ppermute x9, waiting for transfers between devices, moved(): return lax.ppermute(block, ('ctx', 'tp', 'dp'), pairs)  51.5 us
    ppermute x6, waiting for transfers between devices, moved(): return lax.ppermute(block, 'ctx', pairs)  43.6 us
    ppermute x9, waiting for transfers between devices, moved(): return lax.ppermute(block, ('tp', 'dp'), pairs)  35.8 us
    ppermute x9, starting transfers between devices, moved(): return lax.ppermute(block, ('ctx', 'tp', 'dp'), pairs)  26.7 us
    ppermute x3, waiting for transfers between devices, square_body(): both_in = lax.ppermute(state_and_decay, 'ctx', pairs).astype(jnp.float32)  24.2 us
    ppermute x6, starting transfers between devices, moved(): return lax.ppermute(block, 'ctx', pairs)  18.1 us
    ppermute x9, starting transfers between devices, moved(): return lax.ppermute(block, ('tp', 'dp'), pairs)  9.67 us
    unnamed x47, local copies, waits for them, and re-layouts  9.22 us
  transfers between devices with their start and end apart: 27, of which 20 were waited for; matrix products, arithmetic and copies ran while one was open for 10% of the time, Pallas kernels for 0%

profile of v6, /device:TPU:2, one launch (start us, length us, event | category | flops | bytes accessed | tf_op | source)
XLA Modules:
  0.0 286.5 jit_solution(6351010523440355143)
XLA Ops:
  0.0 4.7 %collective-permute-start = (bf16[128,1280]{1,0:T(8,128)(2,1)}, bf16[128,1280]{1,0:T(8,128)(2,1)S(1)}, u32[]{:S(2)}, u32[]{:S(2)}) collective-permute-start(bf16[128,1280]{1,0:T(8,128)(2,1)} %param.19), channel_id=1, source_target_pairs={{0,0},{1,4},{2,8},{3,12},{4,1},{5,5},{6,9},{7,13},{8,2},{9,6},{10,... | collective-permute-start | bytes 983048 | tf_op jit(solution)/shard_map/ppermute | solution.py:265
  4.7 3.2 %collective-permute-start.4 = (bf16[2,1280,64]{1,2,0:T(8,128)(2,1)}, bf16[2,1280,64]{1,2,0:T(8,128)(2,1)S(1)}, u32[]{:S(2)}, u32[]{:S(2)}) collective-permute-start(bf16[2,1280,64]{1,2,0:T(8,128)(2,1)} %param.33), channel_id=1, source_target_pairs={{0,0},{1,4},{2,8},{3,12},{4,1},{5,5},{6,9},{7,13},{8,2},{9,6},{10,... | collective-permute-start | bytes 983048 | tf_op jit(solution)/shard_map/ppermute | solution.py:265
  15.9 12.8 %collective-permute-done = bf16[128,1280]{1,0:T(8,128)(2,1)S(1)} collective-permute-done((bf16[128,1280]{1,0:T(8,128)(2,1)}, bf16[128,1280]{1,0:T(8,128)(2,1)S(1)}, u32[]{:S(2)}, u32[]{:S(2)}) %collective-permute-start) | collective-permute-done | bytes 327712 | tf_op jit(solution)/shard_map/ppermute | solution.py:265
  30.0 6.2 %collective-permute-done.1 = bf16[128,1280]{1,0:T(8,128)(2,1)S(1)} collective-permute-done((bf16[128,1280]{1,0:T(8,128)(2,1)S(1)}, bf16[128,1280]{1,0:T(8,128)(2,1)S(1)}, u32[]{:S(2)}, u32[]{:S(2)}) %collective-permute-start.1) | collective-permute-done | bytes 327712 | tf_op jit(solution)/shard_map/ppermute | solution.py:260
  36.3 7.0 %collective-permute-done.2 = bf16[128,1280]{1,0:T(8,128)(2,1)S(1)} collective-permute-done((bf16[128,1280]{1,0:T(8,128)(2,1)S(1)}, bf16[128,1280]{1,0:T(8,128)(2,1)S(1)}, u32[]{:S(2)}, u32[]{:S(2)}) %collective-permute-start.2) | collective-permute-done | bytes 327712 | tf_op jit(solution)/shard_map/ppermute | solution.py:260
  47.7 3.9 %collective-permute-start.5 = (f32[512,64]{0,1:T(8,128)S(1)}, f32[512,64]{0,1:T(8,128)S(1)}, u32[]{:S(2)}, u32[]{:S(2)}) collective-permute-start(f32[512,64]{0,1:T(8,128)S(1)} %multiply_reduce_fusion.2), channel_id=1, source_target_pairs={{0,0},{1,4},{2,8},{3,12},{4,1},{5,5},{6,9},{7,13},{8,2},{9,6},{10,... | collective-permute-start | bytes 393224 | tf_op jit(solution)/shard_map/ppermute | solution.py:265
  51.6 2.6 collective-permute-start.6
  55.6 15.1 %collective-permute-done.5 = f32[512,64]{0,1:T(8,128)S(1)} collective-permute-done((f32[512,64]{0,1:T(8,128)S(1)}, f32[512,64]{0,1:T(8,128)S(1)}, u32[]{:S(2)}, u32[]{:S(2)}) %collective-permute-start.5) | collective-permute-done | bytes 131104 | tf_op jit(solution)/shard_map/ppermute | solution.py:265
  80.6 4.6 %collective-permute-start.11 = (bf16[131,1168]{1,0:T(8,128)(2,1)}, bf16[131,1168]{1,0:T(8,128)(2,1)}, u32[]{:S(2)}, u32[]{:S(2)}) collective-permute-start(bf16[131,1168]{1,0:T(8,128)(2,1)} %copy.90), channel_id=1, source_target_pairs={{0,12},{4,0},{8,4},{12,8},{1,13},{5,1},{9,5},{13,9},{2,14},{6,2},{... | collective-permute-start | bytes 918056 | tf_op jit(solution)/shard_map/ppermute | solution.py:257
  89.3 4.8 %collective-permute-done.11 = bf16[131,1168]{1,0:T(8,128)(2,1)} collective-permute-done((bf16[131,1168]{1,0:T(8,128)(2,1)}, bf16[131,1168]{1,0:T(8,128)(2,1)}, u32[]{:S(2)}, u32[]{:S(2)}) %collective-permute-start.11) | collective-permute-done | bytes 306048 | tf_op jit(solution)/shard_map/ppermute | solution.py:257
  95.3 19.4 %collective-permute-done.10 = bf16[131,1168]{1,0:T(8,128)(2,1)} collective-permute-done((bf16[131,1168]{1,0:T(8,128)(2,1)}, bf16[131,1168]{1,0:T(8,128)(2,1)}, u32[]{:S(2)}, u32[]{:S(2)}) %collective-permute-start.10) | collective-permute-done | bytes 306048 | tf_op jit(solution)/shard_map/ppermute | solution.py:257
  118.8 2.2 convert_add_fusion
  122.5 3.7 %divide_multiply_fusion = f32[128,1152]{0,1:T(8,128)S(1)} fusion(f32[131,1168]{0,1:T(8,128)} %copy-done.2, f32[128]{0:T(128)S(1)} %get-tuple-element.34, f32[1152]{0:T(1024)S(1)} %get-tuple-element.6, f32[128]{0:T(128)S(1)} %get-tuple-element.35, f32[1152]{0:T(1024)S(1)} %get-tuple-element.7, f32[128]{0:T(128)S(1)} %get-tuple-element.36, ...), kind=kLoop, calls=%fused_computation.46 | loop fusion | flops 2211840 | bytes 2969600 | tf_op jit(solution)/shard_map/jit(silu)/mul | solution.py:388
  126.3 5.4 %all_gather.3 = bf16[128,512]{0,1:T(8,128)(2,1)S(1)} all-gather(bf16[128,128]{0,1:T(8,128)(2,1)S(1)} %slice.240), channel_id=1, replica_groups=mesh['groups'=2,'ctx'=4,'tp'=2,'dp'=2] {'tp','dp'}, dimensions={1}, use_global_device_ids=true | all-gather | bytes 163840 | tf_op jit(solution)/shard_map/all_gather | solution.py:391
  141.8 2.9 %convolution_bitcast_fusion = f32[128,16,64]{0,2,1:T(8,128)S(1)} fusion(f32[128,16,64]{0,2,1:T(8,128)S(1)} %bitcast.92, f32[16,128]{1,0:T(8,128)} %get-tuple-element.24, f32[128,128]{1,0:T(8,128)S(1)} %fusion.39, f32[16,128]{1,0:T(8,128)S(1)} %copy.93, f32[128,128]{1,0:T(8,128)S(1)} %fusion.41), kind=kOutput, calls=%fused_computation.12 | convolution fusion | flops 202637312 | bytes 1196032 | tf_op jit(solution)/shard_map/hts,shd->thd/dot_general | solution.py:64
  144.7 4.4 %collective-permute-done.13 = bf16[16,65,256]{2,0,1:T(8,128)(2,1)} collective-permute-done((bf16[16,65,256]{2,0,1:T(8,128)(2,1)}, bf16[16,65,256]{2,0,1:T(8,128)(2,1)}, u32[]{:S(2)}, u32[]{:S(2)}) %collective-permute-start.13) | collective-permute-done | bytes 532512 | tf_op jit(solution)/shard_map/ppermute | solution.py:406
  150.3 10.3 %collective-permute-done.14 = bf16[16,65,256]{2,0,1:T(8,128)(2,1)} collective-permute-done((bf16[16,65,256]{2,0,1:T(8,128)(2,1)}, bf16[16,65,256]{2,0,1:T(8,128)(2,1)}, u32[]{:S(2)}, u32[]{:S(2)}) %collective-permute-start.14) | collective-permute-done | bytes 532512 | tf_op jit(solution)/shard_map/ppermute | solution.py:406
  162.0 9.6 %collective-permute-done.12 = bf16[16,65,256]{2,0,1:T(8,128)(2,1)} collective-permute-done((bf16[16,65,256]{2,0,1:T(8,128)(2,1)}, bf16[16,65,256]{2,0,1:T(8,128)(2,1)}, u32[]{:S(2)}, u32[]{:S(2)}) %collective-permute-start.12) | collective-permute-done | bytes 532512 | tf_op jit(solution)/shard_map/ppermute | solution.py:406
  176.0 2.8 collective-permute-start.15
  178.8 7.6 %collective-permute-start.16 = (bf16[128,1024]{0,1:T(8,128)(2,1)}, bf16[128,1024]{0,1:T(8,128)(2,1)}, u32[]{:S(2)}, u32[]{:S(2)}) collective-permute-start(bf16[128,1024]{0,1:T(8,128)(2,1)} %fusion.22), channel_id=1, source_target_pairs={{0,8},{4,12},{8,0},{12,4},{1,9},{5,13},{9,1},{13,5},{2,10},{6,14},... | collective-permute-start | bytes 786440 | tf_op jit(solution)/shard_map/ppermute | solution.py:257
  191.1 18.9 %collective-permute-done.16 = bf16[128,1024]{0,1:T(8,128)(2,1)} collective-permute-done((bf16[128,1024]{0,1:T(8,128)(2,1)}, bf16[128,1024]{0,1:T(8,128)(2,1)}, u32[]{:S(2)}, u32[]{:S(2)}) %collective-permute-start.16) | collective-permute-done | bytes 262176 | tf_op jit(solution)/shard_map/ppermute | solution.py:257
  213.4 2.3 copy.103
  217.5 6.1 %collective-permute-start.20 = (f32[512,64]{0,1:T(8,128)S(1)}, f32[512,64]{0,1:T(8,128)S(1)}, u32[]{:S(2)}, u32[]{:S(2)}) collective-permute-start(f32[512,64]{0,1:T(8,128)S(1)} %multiply_reduce_fusion.1), channel_id=1, source_target_pairs={{0,3},{1,0},{2,1},{3,2},{4,7},{5,4},{6,5},{7,6},{8,11},{9,8},{10,9... | collective-permute-start | bytes 393224 | tf_op jit(solution)/shard_map/ppermute | solution.py:260
  223.7 2.4 collective-permute-start.19
  226.2 3.4 %collective-permute-done.18 = f32[512,64]{0,1:T(8,128)S(1)} collective-permute-done((f32[512,64]{0,1:T(8,128)S(1)}, f32[512,64]{0,1:T(8,128)S(1)}, u32[]{:S(2)}, u32[]{:S(2)}) %collective-permute-start.18) | collective-permute-done | bytes 131104 | tf_op jit(solution)/shard_map/ppermute | solution.py:260
  229.5 3.0 %collective-permute-done.19 = f32[512,64]{0,1:T(8,128)S(1)} collective-permute-done((f32[512,64]{0,1:T(8,128)S(1)}, f32[512,64]{0,1:T(8,128)S(1)}, u32[]{:S(2)}, u32[]{:S(2)}) %collective-permute-start.19) | collective-permute-done | bytes 131104 | tf_op jit(solution)/shard_map/ppermute | solution.py:260
  232.6 4.6 %collective-permute-start.21 = (f32[512,64]{0,1:T(8,128)S(1)}, f32[512,64]{0,1:T(8,128)S(1)}, u32[]{:S(2)}, u32[]{:S(2)}) collective-permute-start(f32[512,64]{0,1:T(8,128)S(1)} %add_add_fusion), channel_id=1, source_target_pairs={{0,0},{1,4},{2,8},{3,12},{4,1},{5,5},{6,9},{7,13},{8,2},{9,6},{10,... | collective-permute-start | bytes 393224 | tf_op jit(solution)/shard_map/ppermute | solution.py:265
  238.8 6.6 %collective-permute-done.21 = f32[512,64]{0,1:T(8,128)S(1)} collective-permute-done((f32[512,64]{0,1:T(8,128)S(1)}, f32[512,64]{0,1:T(8,128)S(1)}, u32[]{:S(2)}, u32[]{:S(2)}) %collective-permute-start.21) | collective-permute-done | bytes 131104 | tf_op jit(solution)/shard_map/ppermute | solution.py:265
  249.9 7.9 %collective-permute-done.25 = bf16[128,1280]{1,0:T(8,128)(2,1)S(1)} collective-permute-done((bf16[128,1280]{1,0:T(8,128)(2,1)}, bf16[128,1280]{1,0:T(8,128)(2,1)S(1)}, u32[]{:S(2)}, u32[]{:S(2)}) %collective-permute-start.25) | collective-permute-done | bytes 327712 | tf_op jit(solution)/shard_map/ppermute | solution.py:260
  257.8 6.8 %collective-permute-done.24 = bf16[128,1280]{1,0:T(8,128)(2,1)} collective-permute-done((bf16[128,1280]{1,0:T(8,128)(2,1)}, bf16[128,1280]{1,0:T(8,128)(2,1)}, u32[]{:S(2)}, u32[]{:S(2)}) %collective-permute-start.24) | collective-permute-done | bytes 327712 | tf_op jit(solution)/shard_map/ppermute | solution.py:260
  266.0 3.7 %collective-permute-start.26 = (bf16[128,1280]{1,0:T(8,128)(2,1)S(1)}, bf16[128,1280]{1,0:T(8,128)(2,1)S(1)}, u32[]{:S(2)}, u32[]{:S(2)}) collective-permute-start(bf16[128,1280]{1,0:T(8,128)(2,1)S(1)} %add_convert_fusion), channel_id=1, source_target_pairs={{0,0},{1,4},{2,8},{3,12},{4,1},{5,5},{6,9},{7,13},{8,2},{9,6},{10,... | collective-permute-start | bytes 983048 | tf_op jit(solution)/shard_map/ppermute | solution.py:265
  269.7 16.0 %collective-permute-done.26 = bf16[128,1280]{1,0:T(8,128)(2,1)S(1)} collective-permute-done((bf16[128,1280]{1,0:T(8,128)(2,1)S(1)}, bf16[128,1280]{1,0:T(8,128)(2,1)S(1)}, u32[]{:S(2)}, u32[]{:S(2)}) %collective-permute-start.26) | collective-permute-done | bytes 327712 | tf_op jit(solution)/shard_map/ppermute | solution.py:265
  (154 shorter events, 69.5 us)
Async XLA Ops:
  0.0 237.2 %copy-start = (bf16[1024,1280]{1,0:T(8,128)(2,1)S(1)}, bf16[1024,1280]{1,0:T(8,128)(2,1)}, u32[]{:S(2)}) copy-start(bf16[1024,1280]{1,0:T(8,128)(2,1)} %param.32) | copy-start | bytes 7864324
  0.0 28.7 %collective-permute-start = (bf16[128,1280]{1,0:T(8,128)(2,1)}, bf16[128,1280]{1,0:T(8,128)(2,1)S(1)}, u32[]{:S(2)}, u32[]{:S(2)}) collective-permute-start(bf16[128,1280]{1,0:T(8,128)(2,1)} %param.19), channel_id=1, source_target_pairs={{0,0},{1,4},{2,8},{3,12},{4,1},{5,5},{6,9},{7,13},{8,2},{9,6},{10,... | collective-permute-start | bytes 983048 | tf_op jit(solution)/shard_map/ppermute | solution.py:265
  4.7 40.2 %collective-permute-start.4 = (bf16[2,1280,64]{1,2,0:T(8,128)(2,1)}, bf16[2,1280,64]{1,2,0:T(8,128)(2,1)S(1)}, u32[]{:S(2)}, u32[]{:S(2)}) collective-permute-start(bf16[2,1280,64]{1,2,0:T(8,128)(2,1)} %param.33), channel_id=1, source_target_pairs={{0,0},{1,4},{2,8},{3,12},{4,1},{5,5},{6,9},{7,13},{8,2},{9,6},{10,... | collective-permute-start | bytes 983048 | tf_op jit(solution)/shard_map/ppermute | solution.py:265
  28.7 7.6 %collective-permute-start.1 = (bf16[128,1280]{1,0:T(8,128)(2,1)S(1)}, bf16[128,1280]{1,0:T(8,128)(2,1)S(1)}, u32[]{:S(2)}, u32[]{:S(2)}) collective-permute-start(bf16[128,1280]{1,0:T(8,128)(2,1)S(1)} %collective-permute-done), channel_id=1, source_target_pairs={{0,3},{1,0},{2,1},{3,2},{4,7},{5,4},{6,5},{7,6},{8,11},{9,8},{10,9... | collective-permute-start | bytes 983048 | tf_op jit(solution)/shard_map/ppermute | solution.py:260
  29.4 13.9 %collective-permute-start.2 = (bf16[128,1280]{1,0:T(8,128)(2,1)S(1)}, bf16[128,1280]{1,0:T(8,128)(2,1)S(1)}, u32[]{:S(2)}, u32[]{:S(2)}) collective-permute-start(bf16[128,1280]{1,0:T(8,128)(2,1)S(1)} %collective-permute-done), channel_id=1, source_target_pairs={{0,2},{1,3},{2,0},{3,1},{4,6},{5,7},{6,4},{7,5},{8,10},{9,11},{10,... | collective-permute-start | bytes 983048 | tf_op jit(solution)/shard_map/ppermute | solution.py:260
  29.5 15.2 %collective-permute-start.3 = (bf16[128,1280]{1,0:T(8,128)(2,1)S(1)}, bf16[128,1280]{1,0:T(8,128)(2,1)S(1)}, u32[]{:S(2)}, u32[]{:S(2)}) collective-permute-start(bf16[128,1280]{1,0:T(8,128)(2,1)S(1)} %collective-permute-done), channel_id=1, source_target_pairs={{0,1},{1,2},{2,3},{3,0},{4,5},{5,6},{6,7},{7,4},{8,9},{9,10},{10,1... | collective-permute-start | bytes 983048 | tf_op jit(solution)/shard_map/ppermute | solution.py:260
  45.0 25.8 %copy-start.11 = (bf16[2,64,128]{2,1,0:T(8,128)(2,1)S(1)}, bf16[2,64,128]{2,1,0:T(8,128)(2,1)}, u32[]{:S(2)}) copy-start(bf16[2,64,128]{2,1,0:T(8,128)(2,1)} %param.35) | copy-start | bytes 98308
  45.0 26.0 %copy-start.8 = (bf16[2,64,1024]{2,1,0:T(8,128)(2,1)S(1)}, bf16[2,64,1024]{2,1,0:T(8,128)(2,1)}, u32[]{:S(2)}) copy-start(bf16[2,64,1024]{2,1,0:T(8,128)(2,1)} %param.34) | copy-start | bytes 786436
  45.6 10.0 %collective-permute-start.8 = (f32[512,64]{0,1:T(8,128)S(1)}, f32[512,64]{0,1:T(8,128)S(1)}, u32[]{:S(2)}, u32[]{:S(2)}) collective-permute-start(f32[512,64]{0,1:T(8,128)S(1)} %multiply_reduce_fusion.2), channel_id=1, source_target_pairs={{0,3},{1,7},{2,11},{3,15},{4,0},{5,4},{6,8},{7,12},{8,1},{9,5},{10... | collective-permute-start | bytes 393224 | tf_op jit(solution)/shard_map/ppermute | solution.py:265
  47.5 8.2 %collective-permute-start.7 = (f32[512,64]{0,1:T(8,128)S(1)}, f32[512,64]{0,1:T(8,128)S(1)}, u32[]{:S(2)}, u32[]{:S(2)}) collective-permute-start(f32[512,64]{0,1:T(8,128)S(1)} %multiply_reduce_fusion.2), channel_id=1, source_target_pairs={{0,2},{1,6},{2,10},{3,14},{4,3},{5,7},{6,11},{7,15},{8,0},{9,4},{1... | collective-permute-start | bytes 393224 | tf_op jit(solution)/shard_map/ppermute | solution.py:265
  47.7 23.1 %collective-permute-start.5 = (f32[512,64]{0,1:T(8,128)S(1)}, f32[512,64]{0,1:T(8,128)S(1)}, u32[]{:S(2)}, u32[]{:S(2)}) collective-permute-start(f32[512,64]{0,1:T(8,128)S(1)} %multiply_reduce_fusion.2), channel_id=1, source_target_pairs={{0,0},{1,4},{2,8},{3,12},{4,1},{5,5},{6,9},{7,13},{8,2},{9,6},{10,... | collective-permute-start | bytes 393224 | tf_op jit(solution)/shard_map/ppermute | solution.py:265
  51.6 19.1 %collective-permute-start.6 = (f32[512,64]{0,1:T(8,128)S(1)}, f32[512,64]{0,1:T(8,128)S(1)}, u32[]{:S(2)}, u32[]{:S(2)}) collective-permute-start(f32[512,64]{0,1:T(8,128)S(1)} %multiply_reduce_fusion.2), channel_id=1, source_target_pairs={{0,1},{1,5},{2,9},{3,13},{4,2},{5,6},{6,10},{7,14},{8,3},{9,7},{10... | collective-permute-start | bytes 393224 | tf_op jit(solution)/shard_map/ppermute | solution.py:265
  80.6 13.5 %collective-permute-start.11 = (bf16[131,1168]{1,0:T(8,128)(2,1)}, bf16[131,1168]{1,0:T(8,128)(2,1)}, u32[]{:S(2)}, u32[]{:S(2)}) collective-permute-start(bf16[131,1168]{1,0:T(8,128)(2,1)} %copy.90), channel_id=1, source_target_pairs={{0,12},{4,0},{8,4},{12,8},{1,13},{5,1},{9,5},{13,9},{2,14},{6,2},{... | collective-permute-start | bytes 918056 | tf_op jit(solution)/shard_map/ppermute | solution.py:257
  87.2 27.6 %collective-permute-start.10 = (bf16[131,1168]{1,0:T(8,128)(2,1)}, bf16[131,1168]{1,0:T(8,128)(2,1)}, u32[]{:S(2)}, u32[]{:S(2)}) collective-permute-start(bf16[131,1168]{1,0:T(8,128)(2,1)} %copy.88), channel_id=1, source_target_pairs={{0,8},{4,12},{8,0},{12,4},{1,9},{5,13},{9,1},{13,5},{2,10},{6,14},... | collective-permute-start | bytes 918056 | tf_op jit(solution)/shard_map/ppermute | solution.py:257
  88.1 28.6 %collective-permute-start.9 = (bf16[131,1168]{1,0:T(8,128)(2,1)}, bf16[131,1168]{1,0:T(8,128)(2,1)}, u32[]{:S(2)}, u32[]{:S(2)}) collective-permute-start(bf16[131,1168]{1,0:T(8,128)(2,1)} %copy.86), channel_id=1, source_target_pairs={{0,4},{4,8},{8,12},{12,0},{1,5},{5,9},{9,13},{13,1},{2,6},{6,10},{... | collective-permute-start | bytes 918056 | tf_op jit(solution)/shard_map/ppermute | solution.py:257
  126.2 18.5 %copy-start.4 = (f32[128,1024]{0,1:T(8,128)}, f32[128,1024]{0,1:T(8,128)S(1)}, u32[]{:S(2)}) copy-start(f32[128,1024]{0,1:T(8,128)S(1)} %slice.141) | copy-start | bytes 1572868
  134.9 14.2 %collective-permute-start.13 = (bf16[16,65,256]{2,0,1:T(8,128)(2,1)}, bf16[16,65,256]{2,0,1:T(8,128)(2,1)}, u32[]{:S(2)}, u32[]{:S(2)}) collective-permute-start(bf16[16,65,256]{2,0,1:T(8,128)(2,1)} %copy.97), channel_id=1, source_target_pairs={{0,8},{4,12},{1,9},{5,13},{2,10},{6,14},{3,11},{7,15},{16,24},{20,... | collective-permute-start | bytes 1597448 | tf_op jit(solution)/shard_map/ppermute | solution.py:406
  137.1 23.4 %collective-permute-start.14 = (bf16[16,65,256]{2,0,1:T(8,128)(2,1)}, bf16[16,65,256]{2,0,1:T(8,128)(2,1)}, u32[]{:S(2)}, u32[]{:S(2)}) collective-permute-start(bf16[16,65,256]{2,0,1:T(8,128)(2,1)} %copy.97), channel_id=1, source_target_pairs={{0,12},{1,13},{2,14},{3,15},{16,28},{17,29},{18,30},{19,31}} | collective-permute-start | bytes 1597448 | tf_op jit(solution)/shard_map/ppermute | solution.py:406
  139.4 32.1 %collective-permute-start.12 = (bf16[16,65,256]{2,0,1:T(8,128)(2,1)}, bf16[16,65,256]{2,0,1:T(8,128)(2,1)}, u32[]{:S(2)}, u32[]{:S(2)}) collective-permute-start(bf16[16,65,256]{2,0,1:T(8,128)(2,1)} %copy.97), channel_id=1, source_target_pairs={{0,4},{4,8},{8,12},{1,5},{5,9},{9,13},{2,6},{6,10},{10,14},{3,7},{... | collective-permute-start | bytes 1597448 | tf_op jit(solution)/shard_map/ppermute | solution.py:406
  176.0 15.0 %collective-permute-start.15 = (bf16[128,1024]{0,1:T(8,128)(2,1)}, bf16[128,1024]{0,1:T(8,128)(2,1)S(1)}, u32[]{:S(2)}, u32[]{:S(2)}) collective-permute-start(bf16[128,1024]{0,1:T(8,128)(2,1)} %fusion.22), channel_id=1, source_target_pairs={{0,12},{4,0},{8,4},{12,8},{1,13},{5,1},{9,5},{13,9},{2,14},{6,2},{... | collective-permute-start | bytes 786440 | tf_op jit(solution)/shard_map/ppermute | solution.py:257
  178.8 31.1 %collective-permute-start.16 = (bf16[128,1024]{0,1:T(8,128)(2,1)}, bf16[128,1024]{0,1:T(8,128)(2,1)}, u32[]{:S(2)}, u32[]{:S(2)}) collective-permute-start(bf16[128,1024]{0,1:T(8,128)(2,1)} %fusion.22), channel_id=1, source_target_pairs={{0,8},{4,12},{8,0},{12,4},{1,9},{5,13},{9,1},{13,5},{2,10},{6,14},... | collective-permute-start | bytes 786440 | tf_op jit(solution)/shard_map/ppermute | solution.py:257
  186.4 58.9 %collective-permute-start.22 = (bf16[2,64,1280]{2,1,0:T(8,128)(2,1)}, bf16[2,64,1280]{2,1,0:T(8,128)(2,1)}, u32[]{:S(2)}, u32[]{:S(2)}) collective-permute-start(bf16[2,64,1280]{2,1,0:T(8,128)(2,1)} %param.37), channel_id=1, source_target_pairs={{0,0},{1,4},{2,8},{3,12},{4,1},{5,5},{6,9},{7,13},{8,2},{9,6},{10,... | collective-permute-start | bytes 983048 | tf_op jit(solution)/shard_map/ppermute | solution.py:265
  188.4 22.5 %collective-permute-start.17 = (bf16[128,1024]{0,1:T(8,128)(2,1)}, bf16[128,1024]{0,1:T(8,128)(2,1)S(1)}, u32[]{:S(2)}, u32[]{:S(2)}) collective-permute-start(bf16[128,1024]{0,1:T(8,128)(2,1)} %fusion.22), channel_id=1, source_target_pairs={{0,4},{4,8},{8,12},{12,0},{1,5},{5,9},{9,13},{13,1},{2,6},{6,10},{... | collective-permute-start | bytes 786440 | tf_op jit(solution)/shard_map/ppermute | solution.py:257
  215.7 21.5 %copy-start.6 = (bf16[4,128,1024]{2,1,0:T(8,128)(2,1)S(1)}, bf16[4,128,1024]{2,1,0:T(8,128)(2,1)}, u32[]{:S(2)}) copy-start(bf16[4,128,1024]{2,1,0:T(8,128)(2,1)} %copy.103) | copy-start | bytes 3145732
  217.5 8.7 %collective-permute-start.20 = (f32[512,64]{0,1:T(8,128)S(1)}, f32[512,64]{0,1:T(8,128)S(1)}, u32[]{:S(2)}, u32[]{:S(2)}) collective-permute-start(f32[512,64]{0,1:T(8,128)S(1)} %multiply_reduce_fusion.1), channel_id=1, source_target_pairs={{0,3},{1,0},{2,1},{3,2},{4,7},{5,4},{6,5},{7,6},{8,11},{9,8},{10,9... | collective-permute-start | bytes 393224 | tf_op jit(solution)/shard_map/ppermute | solution.py:260
  223.7 5.9 %collective-permute-start.18 = (f32[512,64]{0,1:T(8,128)S(1)}, f32[512,64]{0,1:T(8,128)S(1)}, u32[]{:S(2)}, u32[]{:S(2)}) collective-permute-start(f32[512,64]{0,1:T(8,128)S(1)} %multiply_reduce_fusion.1), channel_id=1, source_target_pairs={{0,1},{1,2},{2,3},{3,0},{4,5},{5,6},{6,7},{7,4},{8,9},{9,10},{10,1... | collective-permute-start | bytes 393224 | tf_op jit(solution)/shard_map/ppermute | solution.py:260
  223.7 8.9 %collective-permute-start.19 = (f32[512,64]{0,1:T(8,128)S(1)}, f32[512,64]{0,1:T(8,128)S(1)}, u32[]{:S(2)}, u32[]{:S(2)}) collective-permute-start(f32[512,64]{0,1:T(8,128)S(1)} %multiply_reduce_fusion.1), channel_id=1, source_target_pairs={{0,2},{1,3},{2,0},{3,1},{4,6},{5,7},{6,4},{7,5},{8,10},{9,11},{10,... | collective-permute-start | bytes 393224 | tf_op jit(solution)/shard_map/ppermute | solution.py:260
  232.6 12.8 %collective-permute-start.21 = (f32[512,64]{0,1:T(8,128)S(1)}, f32[512,64]{0,1:T(8,128)S(1)}, u32[]{:S(2)}, u32[]{:S(2)}) collective-permute-start(f32[512,64]{0,1:T(8,128)S(1)} %add_add_fusion), channel_id=1, source_target_pairs={{0,0},{1,4},{2,8},{3,12},{4,1},{5,5},{6,9},{7,13},{8,2},{9,6},{10,... | collective-permute-start | bytes 393224 | tf_op jit(solution)/shard_map/ppermute | solution.py:265
  249.3 8.4 %collective-permute-start.25 = (bf16[128,1280]{1,0:T(8,128)(2,1)}, bf16[128,1280]{1,0:T(8,128)(2,1)S(1)}, u32[]{:S(2)}, u32[]{:S(2)}) collective-permute-start(bf16[128,1280]{1,0:T(8,128)(2,1)} %get-tuple-element.21), channel_id=1, source_target_pairs={{0,3},{1,0},{2,1},{3,2},{4,7},{5,4},{6,5},{7,6},{8,11},{9,8},{10,9... | collective-permute-start | bytes 983048 | tf_op jit(solution)/shard_map/ppermute | solution.py:260
  249.3 15.3 %collective-permute-start.24 = (bf16[128,1280]{1,0:T(8,128)(2,1)}, bf16[128,1280]{1,0:T(8,128)(2,1)}, u32[]{:S(2)}, u32[]{:S(2)}) collective-permute-start(bf16[128,1280]{1,0:T(8,128)(2,1)} %get-tuple-element.22), channel_id=1, source_target_pairs={{0,2},{1,3},{2,0},{3,1},{4,6},{5,7},{6,4},{7,5},{8,10},{9,11},{10,... | collective-permute-start | bytes 983048 | tf_op jit(solution)/shard_map/ppermute | solution.py:260
  249.3 15.3 %collective-permute-start.23 = (bf16[128,1280]{1,0:T(8,128)(2,1)S(1)}, bf16[128,1280]{1,0:T(8,128)(2,1)}, u32[]{:S(2)}, u32[]{:S(2)}) collective-permute-start(bf16[128,1280]{1,0:T(8,128)(2,1)S(1)} %get-tuple-element.20), channel_id=1, source_target_pairs={{0,1},{1,2},{2,3},{3,0},{4,5},{5,6},{6,7},{7,4},{8,9},{9,10},{10,1... | collective-permute-start | bytes 983048 | tf_op jit(solution)/shard_map/ppermute | solution.py:260
  266.0 19.7 %collective-permute-start.26 = (bf16[128,1280]{1,0:T(8,128)(2,1)S(1)}, bf16[128,1280]{1,0:T(8,128)(2,1)S(1)}, u32[]{:S(2)}, u32[]{:S(2)}) collective-permute-start(bf16[128,1280]{1,0:T(8,128)(2,1)S(1)} %add_convert_fusion), channel_id=1, source_target_pairs={{0,0},{1,4},{2,8},{3,12},{4,1},{5,5},{6,9},{7,13},{8,2},{9,6},{10,... | collective-permute-start | bytes 983048 | tf_op jit(solution)/shard_map/ppermute | solution.py:265
  (11 other events, 42.2 us)

commit v7 on v4

--- a/solution.py
+++ b/solution.py
@@ -382,7 +382,8 @@
     act = jax.nn.silu(convolved)
     x_heads = act[:, :channels].reshape(length, head_count, -1)
     bc_local = act[:, channels:].astype(jnp.bfloat16)
-    bc_all = lax.all_gather(bc_local, ("tp", "dp"), axis=1, tiled=True)
+    bc_pieces = [bc_local] + [moved(bc_local, s, "lane") for s in range(1, side)]
+    bc_all = jnp.transpose(in_order([piece.T for piece in bc_pieces], lane))
     state_width = bc_all.shape[1] // 2
     b_proj = bc_all[:, :state_width]
     c_proj = bc_all[:, state_width:]
@@ -392,14 +393,13 @@
         x_heads, b_proj, c_proj, step_size, log_decay, segment, previous
     )
 
+    decay_row = jnp.broadcast_to(carry_decay[:, None, None], (head_count, 1, local_state.shape[2]))
+    state_and_decay = jnp.concatenate([decay_row, local_state], axis=1).astype(jnp.bfloat16)
     entering = jnp.zeros_like(local_state)
     for s in range(side - 1, 0, -1):
         pairs = [(a, a + s) for a in range(side - s)]
-        decay_in = lax.ppermute(carry_decay.astype(jnp.bfloat16), "ctx", pairs)
-        state_in = lax.ppermute(local_state.astype(jnp.bfloat16), "ctx", pairs)
-        entering = decay_in.astype(jnp.float32)[:, None, None] * entering + state_in.astype(
-            jnp.float32
-        )
+        both_in = lax.ppermute(state_and_decay, "ctx", pairs).astype(jnp.float32)
+        entering = both_in[:, :1, :1] * entering + both_in[:, 1:]
     entered = (
         jnp.einsum("tn,hdn->thd", c_proj.astype(jnp.float32), entering, precision=FULL_PRECISION)
         * enter_weight[:, :, None]

time: 284 us -> 278 us (0.979)
  starting transfers between devices: 81.8 us -> 75.1 us
  blocking collectives: 5.43 us -> 0 us
  other arithmetic: 12.2 us -> 15.7 us
    ppermute x9, starting transfers between devices: 38 us -> 22.9 us  [moved(): return lax.ppermute(block, ('ctx', 'tp', 'dp'), pairs)]
    ppermute x6, starting transfers between devices: 20.2 us -> 26.5 us  [moved(): return lax.ppermute(block, 'ctx', pairs)]
    ppermute x9 -> x12, starting transfers between devices: 8.6 us -> 14.5 us  [moved(): return lax.ppermute(block, ('tp', 'dp'), pairs)]
    all_gather x1 -> x0, blocking collectives: 5.43 us -> none  [square_body(): bc_all = lax.all_gather(bc_local, ('tp', 'dp'), axis=1, tiled=True)]
    ppermute x9 -> x12, waiting for transfers between devices: 35.8 us -> 40.3 us  [moved(): return lax.ppermute(block, ('tp', 'dp'), pairs)]
    ppermute x6 -> x3, waiting for transfers between devices: 27.1 us -> 23.6 us  [square_body(): both_in = lax.ppermute(state_and_decay, 'ctx', pairs).astype(jnp.float32)]
    ppermute x6 -> x3, starting transfers between devices: 13.5 us -> 10 us  [square_body(): both_in = lax.ppermute(state_and_decay, 'ctx', pairs).astype(jnp.float32)]
    ppermute x6, waiting for transfers between devices: 42.4 us -> 39.1 us  [moved(): return lax.ppermute(block, 'ctx', pairs)]
  transfers between devices with their start and end apart: 31 -> 31, of which waited for: 21 -> 21; matrix products, arithmetic and copies ran while one was open for 10% -> 9% of each run, Pallas kernels for 0% -> 0%
where the time goes in v7:
time: 278 us; the launch traced here: 277 us
  waiting for transfers between devices  151 us (54%)
  starting transfers between devices  75.1 us (27%)
  local copies, waits for them, and re-layouts  20.3 us (7%)
  other arithmetic  15.7 us (6%)
  matrix products  12.7 us (5%)
    ppermute x9, waiting for transfers between devices, moved(): return lax.ppermute(block, ('ctx', 'tp', 'dp'), pairs)  48 us
    ppermute x12, waiting for transfers between devices, moved(): return lax.ppermute(block, ('tp', 'dp'), pairs)  40.3 us
    ppermute x6, waiting for transfers between devices, moved(): return lax.ppermute(block, 'ctx', pairs)  39.1 us
    ppermute x6, starting transfers between devices, moved(): return lax.ppermute(block, 'ctx', pairs)  26.5 us
    ppermute x3, waiting for transfers between devices, square_body(): both_in = lax.ppermute(state_and_decay, 'ctx', pairs).astype(jnp.float32)  23.6 us
    ppermute x9, starting transfers between devices, moved(): return lax.ppermute(block, ('ctx', 'tp', 'dp'), pairs)  22.9 us
    ppermute x12, starting transfers between devices, moved(): return lax.ppermute(block, ('tp', 'dp'), pairs)  14.5 us
    ppermute x3, starting transfers between devices, square_body(): both_in = lax.ppermute(state_and_decay, 'ctx', pairs).astype(jnp.float32)  10 us
  transfers between devices with their start and end apart: 31, of which 21 were waited for; matrix products, arithmetic and copies ran while one was open for 9% of the time, Pallas kernels for 0%

profile of v7, /device:TPU:2, one launch (start us, length us, event | category | flops | bytes accessed | tf_op | source)
XLA Modules:
  0.0 276.9 jit_solution(10416577622995553066)
XLA Ops:
  0.0 4.7 %collective-permute-start = (bf16[128,1280]{1,0:T(8,128)(2,1)}, bf16[128,1280]{1,0:T(8,128)(2,1)S(1)}, u32[]{:S(2)}, u32[]{:S(2)}) collective-permute-start(bf16[128,1280]{1,0:T(8,128)(2,1)} %param.19), channel_id=1, source_target_pairs={{0,0},{1,4},{2,8},{3,12},{4,1},{5,5},{6,9},{7,13},{8,2},{9,6},{10,... | collective-permute-start | bytes 983048 | tf_op jit(solution)/shard_map/ppermute | solution.py:265
  4.7 3.2 %collective-permute-start.4 = (bf16[2,1280,64]{1,2,0:T(8,128)(2,1)}, bf16[2,1280,64]{1,2,0:T(8,128)(2,1)S(1)}, u32[]{:S(2)}, u32[]{:S(2)}) collective-permute-start(bf16[2,1280,64]{1,2,0:T(8,128)(2,1)} %param.33), channel_id=1, source_target_pairs={{0,0},{1,4},{2,8},{3,12},{4,1},{5,5},{6,9},{7,13},{8,2},{9,6},{10,... | collective-permute-start | bytes 983048 | tf_op jit(solution)/shard_map/ppermute | solution.py:265
  16.3 12.3 %collective-permute-done = bf16[128,1280]{1,0:T(8,128)(2,1)S(1)} collective-permute-done((bf16[128,1280]{1,0:T(8,128)(2,1)}, bf16[128,1280]{1,0:T(8,128)(2,1)S(1)}, u32[]{:S(2)}, u32[]{:S(2)}) %collective-permute-start) | collective-permute-done | bytes 327712 | tf_op jit(solution)/shard_map/ppermute | solution.py:265
  30.0 6.2 %collective-permute-done.1 = bf16[128,1280]{1,0:T(8,128)(2,1)S(1)} collective-permute-done((bf16[128,1280]{1,0:T(8,128)(2,1)S(1)}, bf16[128,1280]{1,0:T(8,128)(2,1)S(1)}, u32[]{:S(2)}, u32[]{:S(2)}) %collective-permute-start.1) | collective-permute-done | bytes 327712 | tf_op jit(solution)/shard_map/ppermute | solution.py:260
  36.3 7.0 %collective-permute-done.2 = bf16[128,1280]{1,0:T(8,128)(2,1)S(1)} collective-permute-done((bf16[128,1280]{1,0:T(8,128)(2,1)S(1)}, bf16[128,1280]{1,0:T(8,128)(2,1)S(1)}, u32[]{:S(2)}, u32[]{:S(2)}) %collective-permute-start.2) | collective-permute-done | bytes 327712 | tf_op jit(solution)/shard_map/ppermute | solution.py:260
  47.7 3.9 %collective-permute-start.5 = (f32[512,64]{0,1:T(8,128)S(1)}, f32[512,64]{0,1:T(8,128)S(1)}, u32[]{:S(2)}, u32[]{:S(2)}) collective-permute-start(f32[512,64]{0,1:T(8,128)S(1)} %multiply_reduce_fusion.2), channel_id=1, source_target_pairs={{0,0},{1,4},{2,8},{3,12},{4,1},{5,5},{6,9},{7,13},{8,2},{9,6},{10,... | collective-permute-start | bytes 393224 | tf_op jit(solution)/shard_map/ppermute | solution.py:265
  51.6 2.6 collective-permute-start.6
  55.6 15.1 %collective-permute-done.5 = f32[512,64]{0,1:T(8,128)S(1)} collective-permute-done((f32[512,64]{0,1:T(8,128)S(1)}, f32[512,64]{0,1:T(8,128)S(1)}, u32[]{:S(2)}, u32[]{:S(2)}) %collective-permute-start.5) | collective-permute-done | bytes 131104 | tf_op jit(solution)/shard_map/ppermute | solution.py:265
  74.8 4.6 %collective-permute-start.11 = (bf16[128,1168]{0,1:T(8,128)(2,1)S(1)}, bf16[128,1168]{0,1:T(8,128)(2,1)S(1)}, u32[]{:S(2)}, u32[]{:S(2)}) collective-permute-start(bf16[128,1168]{0,1:T(8,128)(2,1)S(1)} %get-tuple-element.21), channel_id=1, source_target_pairs={{0,12},{4,0},{8,4},{12,8},{1,13},{5,1},{9,5},{13,9},{2,14},{6,2},{... | collective-permute-start | bytes 897032 | tf_op jit(solution)/shard_map/ppermute | solution.py:257
  80.6 6.4 %collective-permute-done.11 = bf16[128,1168]{0,1:T(8,128)(2,1)S(1)} collective-permute-done((bf16[128,1168]{0,1:T(8,128)(2,1)S(1)}, bf16[128,1168]{0,1:T(8,128)(2,1)S(1)}, u32[]{:S(2)}, u32[]{:S(2)}) %collective-permute-start.11) | collective-permute-done | bytes 299040 | tf_op jit(solution)/shard_map/ppermute | solution.py:257
  87.0 17.5 %collective-permute-done.10 = bf16[128,1168]{0,1:T(8,128)(2,1)S(1)} collective-permute-done((bf16[128,1168]{0,1:T(8,128)(2,1)S(1)}, bf16[128,1168]{0,1:T(8,128)(2,1)S(1)}, u32[]{:S(2)}, u32[]{:S(2)}) %collective-permute-start.10) | collective-permute-done | bytes 299040 | tf_op jit(solution)/shard_map/ppermute | solution.py:257
  110.5 3.3 %divide_multiply_fusion = f32[128,1152]{0,1:T(8,128)S(1)} fusion(f32[128,1152]{0,1:T(8,128)} %slice.129, f32[3,1152]{0,1:T(8,128)S(1)} %copy.92, f32[128]{0:T(128)S(1)} %get-tuple-element.34, f32[1152]{0:T(1024)S(1)} %get-tuple-element.6, f32[128]{0:T(128)S(1)} %get-tuple-element.35, f32[1152]{0:T(1024)S(1)} %get-tuple-element.7, ...), kind=kLoop, calls=%fused_computation.49 | loop fusion | flops 2654208 | bytes 1213952 | tf_op jit(solution)/shard_map/jit(silu)/mul | solution.py:382
  115.8 2.7 collective-permute-done.14
  121.8 6.3 %collective-permute-start.17 = (bf16[16,65,256]{2,0,1:T(8,128)(2,1)}, bf16[16,65,256]{2,0,1:T(8,128)(2,1)}, u32[]{:S(2)}, u32[]{:S(2)}) collective-permute-start(bf16[16,65,256]{2,0,1:T(8,128)(2,1)} %copy.98), channel_id=1, source_target_pairs={{0,8},{4,12},{1,9},{5,13},{2,10},{6,14},{3,11},{7,15},{16,24},{20,... | collective-permute-start | bytes 1597448 | tf_op jit(solution)/shard_map/ppermute | solution.py:401
  128.2 2.1 collective-permute-start.18
  132.8 2.2 convolution_bitcast_fusion
  135.0 5.2 %collective-permute-done.17 = bf16[16,65,256]{2,0,1:T(8,128)(2,1)} collective-permute-done((bf16[16,65,256]{2,0,1:T(8,128)(2,1)}, bf16[16,65,256]{2,0,1:T(8,128)(2,1)}, u32[]{:S(2)}, u32[]{:S(2)}) %collective-permute-start.17) | collective-permute-done | bytes 532512 | tf_op jit(solution)/shard_map/ppermute | solution.py:401
  141.4 10.3 %collective-permute-done.18 = bf16[16,65,256]{2,0,1:T(8,128)(2,1)} collective-permute-done((bf16[16,65,256]{2,0,1:T(8,128)(2,1)}, bf16[16,65,256]{2,0,1:T(8,128)(2,1)}, u32[]{:S(2)}, u32[]{:S(2)}) %collective-permute-start.18) | collective-permute-done | bytes 532512 | tf_op jit(solution)/shard_map/ppermute | solution.py:401
  153.1 8.1 %collective-permute-done.16 = bf16[16,65,256]{2,0,1:T(8,128)(2,1)S(1)} collective-permute-done((bf16[16,65,256]{2,0,1:T(8,128)(2,1)}, bf16[16,65,256]{2,0,1:T(8,128)(2,1)S(1)}, u32[]{:S(2)}, u32[]{:S(2)}) %collective-permute-start.16) | collective-permute-done | bytes 532512 | tf_op jit(solution)/shard_map/ppermute | solution.py:401
  164.6 7.0 %collective-permute-start.19 = (bf16[128,1024]{0,1:T(8,128)(2,1)}, bf16[128,1024]{0,1:T(8,128)(2,1)S(1)}, u32[]{:S(2)}, u32[]{:S(2)}) collective-permute-start(bf16[128,1024]{0,1:T(8,128)(2,1)} %fusion.26), channel_id=1, source_target_pairs={{0,12},{4,0},{8,4},{12,8},{1,13},{5,1},{9,5},{13,9},{2,14},{6,2},{... | collective-permute-start | bytes 786440 | tf_op jit(solution)/shard_map/ppermute | solution.py:257
  171.6 11.8 %collective-permute-start.20 = (bf16[128,1024]{0,1:T(8,128)(2,1)}, bf16[128,1024]{0,1:T(8,128)(2,1)}, u32[]{:S(2)}, u32[]{:S(2)}) collective-permute-start(bf16[128,1024]{0,1:T(8,128)(2,1)} %fusion.26), channel_id=1, source_target_pairs={{0,8},{4,12},{8,0},{12,4},{1,9},{5,13},{9,1},{13,5},{2,10},{6,14},... | collective-permute-start | bytes 786440 | tf_op jit(solution)/shard_map/ppermute | solution.py:257
  187.5 15.3 %collective-permute-done.20 = bf16[128,1024]{0,1:T(8,128)(2,1)} collective-permute-done((bf16[128,1024]{0,1:T(8,128)(2,1)}, bf16[128,1024]{0,1:T(8,128)(2,1)}, u32[]{:S(2)}, u32[]{:S(2)}) %collective-permute-start.20) | collective-permute-done | bytes 262176 | tf_op jit(solution)/shard_map/ppermute | solution.py:257
  206.2 2.3 copy.103
  210.3 3.2 %collective-permute-start.24 = (f32[512,64]{0,1:T(8,128)S(1)}, f32[512,64]{0,1:T(8,128)S(1)}, u32[]{:S(2)}, u32[]{:S(2)}) collective-permute-start(f32[512,64]{0,1:T(8,128)S(1)} %multiply_reduce_fusion.1), channel_id=1, source_target_pairs={{0,3},{1,0},{2,1},{3,2},{4,7},{5,4},{6,5},{7,6},{8,11},{9,8},{10,9... | collective-permute-start | bytes 393224 | tf_op jit(solution)/shard_map/ppermute | solution.py:260
  213.5 8.7 %collective-permute-start.23 = (f32[512,64]{0,1:T(8,128)S(1)}, f32[512,64]{0,1:T(8,128)S(1)}, u32[]{:S(2)}, u32[]{:S(2)}) collective-permute-start(f32[512,64]{0,1:T(8,128)S(1)} %multiply_reduce_fusion.1), channel_id=1, source_target_pairs={{0,2},{1,3},{2,0},{3,1},{4,6},{5,7},{6,4},{7,5},{8,10},{9,11},{10,... | collective-permute-start | bytes 393224 | tf_op jit(solution)/shard_map/ppermute | solution.py:260
  222.3 3.5 %collective-permute-done.22 = f32[512,64]{0,1:T(8,128)S(1)} collective-permute-done((f32[512,64]{0,1:T(8,128)S(1)}, f32[512,64]{0,1:T(8,128)S(1)}, u32[]{:S(2)}, u32[]{:S(2)}) %collective-permute-start.22) | collective-permute-done | bytes 131104 | tf_op jit(solution)/shard_map/ppermute | solution.py:260
  225.7 3.0 %collective-permute-done.23 = f32[512,64]{0,1:T(8,128)S(1)} collective-permute-done((f32[512,64]{0,1:T(8,128)S(1)}, f32[512,64]{0,1:T(8,128)S(1)}, u32[]{:S(2)}, u32[]{:S(2)}) %collective-permute-start.23) | collective-permute-done | bytes 131104 | tf_op jit(solution)/shard_map/ppermute | solution.py:260
  232.2 6.6 %collective-permute-done.25 = f32[512,64]{0,1:T(8,128)S(1)} collective-permute-done((f32[512,64]{0,1:T(8,128)S(1)}, f32[512,64]{0,1:T(8,128)S(1)}, u32[]{:S(2)}, u32[]{:S(2)}) %collective-permute-start.25) | collective-permute-done | bytes 131104 | tf_op jit(solution)/shard_map/ppermute | solution.py:265
  243.4 7.8 %collective-permute-done.29 = bf16[128,1280]{1,0:T(8,128)(2,1)S(1)} collective-permute-done((bf16[128,1280]{1,0:T(8,128)(2,1)}, bf16[128,1280]{1,0:T(8,128)(2,1)S(1)}, u32[]{:S(2)}, u32[]{:S(2)}) %collective-permute-start.29) | collective-permute-done | bytes 327712 | tf_op jit(solution)/shard_map/ppermute | solution.py:260
  251.2 7.1 %collective-permute-done.28 = bf16[128,1280]{1,0:T(8,128)(2,1)} collective-permute-done((bf16[128,1280]{1,0:T(8,128)(2,1)}, bf16[128,1280]{1,0:T(8,128)(2,1)}, u32[]{:S(2)}, u32[]{:S(2)}) %collective-permute-start.28) | collective-permute-done | bytes 327712 | tf_op jit(solution)/shard_map/ppermute | solution.py:260
  260.7 2.5 collective-permute-start.30
  263.2 13.0 %collective-permute-done.30 = bf16[128,1280]{1,0:T(8,128)(2,1)S(1)} collective-permute-done((bf16[128,1280]{1,0:T(8,128)(2,1)S(1)}, bf16[128,1280]{1,0:T(8,128)(2,1)S(1)}, u32[]{:S(2)}, u32[]{:S(2)}) %collective-permute-start.30) | collective-permute-done | bytes 327712 | tf_op jit(solution)/shard_map/ppermute | solution.py:265
  (167 shorter events, 59.3 us)
Async XLA Ops:
  0.0 230.7 %copy-start = (bf16[1024,1280]{1,0:T(8,128)(2,1)S(1)}, bf16[1024,1280]{1,0:T(8,128)(2,1)}, u32[]{:S(2)}) copy-start(bf16[1024,1280]{1,0:T(8,128)(2,1)} %param.32) | copy-start | bytes 7864324
  0.0 28.7 %collective-permute-start = (bf16[128,1280]{1,0:T(8,128)(2,1)}, bf16[128,1280]{1,0:T(8,128)(2,1)S(1)}, u32[]{:S(2)}, u32[]{:S(2)}) collective-permute-start(bf16[128,1280]{1,0:T(8,128)(2,1)} %param.19), channel_id=1, source_target_pairs={{0,0},{1,4},{2,8},{3,12},{4,1},{5,5},{6,9},{7,13},{8,2},{9,6},{10,... | collective-permute-start | bytes 983048 | tf_op jit(solution)/shard_map/ppermute | solution.py:265
  4.7 40.2 %collective-permute-start.4 = (bf16[2,1280,64]{1,2,0:T(8,128)(2,1)}, bf16[2,1280,64]{1,2,0:T(8,128)(2,1)S(1)}, u32[]{:S(2)}, u32[]{:S(2)}) collective-permute-start(bf16[2,1280,64]{1,2,0:T(8,128)(2,1)} %param.33), channel_id=1, source_target_pairs={{0,0},{1,4},{2,8},{3,12},{4,1},{5,5},{6,9},{7,13},{8,2},{9,6},{10,... | collective-permute-start | bytes 983048 | tf_op jit(solution)/shard_map/ppermute | solution.py:265
  28.7 7.6 %collective-permute-start.1 = (bf16[128,1280]{1,0:T(8,128)(2,1)S(1)}, bf16[128,1280]{1,0:T(8,128)(2,1)S(1)}, u32[]{:S(2)}, u32[]{:S(2)}) collective-permute-start(bf16[128,1280]{1,0:T(8,128)(2,1)S(1)} %collective-permute-done), channel_id=1, source_target_pairs={{0,3},{1,0},{2,1},{3,2},{4,7},{5,4},{6,5},{7,6},{8,11},{9,8},{10,9... | collective-permute-start | bytes 983048 | tf_op jit(solution)/shard_map/ppermute | solution.py:260
  29.4 13.9 %collective-permute-start.2 = (bf16[128,1280]{1,0:T(8,128)(2,1)S(1)}, bf16[128,1280]{1,0:T(8,128)(2,1)S(1)}, u32[]{:S(2)}, u32[]{:S(2)}) collective-permute-start(bf16[128,1280]{1,0:T(8,128)(2,1)S(1)} %collective-permute-done), channel_id=1, source_target_pairs={{0,2},{1,3},{2,0},{3,1},{4,6},{5,7},{6,4},{7,5},{8,10},{9,11},{10,... | collective-permute-start | bytes 983048 | tf_op jit(solution)/shard_map/ppermute | solution.py:260
  29.5 15.2 %collective-permute-start.3 = (bf16[128,1280]{1,0:T(8,128)(2,1)S(1)}, bf16[128,1280]{1,0:T(8,128)(2,1)S(1)}, u32[]{:S(2)}, u32[]{:S(2)}) collective-permute-start(bf16[128,1280]{1,0:T(8,128)(2,1)S(1)} %collective-permute-done), channel_id=1, source_target_pairs={{0,1},{1,2},{2,3},{3,0},{4,5},{5,6},{6,7},{7,4},{8,9},{9,10},{10,1... | collective-permute-start | bytes 983048 | tf_op jit(solution)/shard_map/ppermute | solution.py:260
  45.6 10.0 %collective-permute-start.8 = (f32[512,64]{0,1:T(8,128)S(1)}, f32[512,64]{0,1:T(8,128)S(1)}, u32[]{:S(2)}, u32[]{:S(2)}) collective-permute-start(f32[512,64]{0,1:T(8,128)S(1)} %multiply_reduce_fusion.2), channel_id=1, source_target_pairs={{0,3},{1,7},{2,11},{3,15},{4,0},{5,4},{6,8},{7,12},{8,1},{9,5},{10... | collective-permute-start | bytes 393224 | tf_op jit(solution)/shard_map/ppermute | solution.py:265
  47.5 8.2 %collective-permute-start.7 = (f32[512,64]{0,1:T(8,128)S(1)}, f32[512,64]{0,1:T(8,128)S(1)}, u32[]{:S(2)}, u32[]{:S(2)}) collective-permute-start(f32[512,64]{0,1:T(8,128)S(1)} %multiply_reduce_fusion.2), channel_id=1, source_target_pairs={{0,2},{1,6},{2,10},{3,14},{4,3},{5,7},{6,11},{7,15},{8,0},{9,4},{1... | collective-permute-start | bytes 393224 | tf_op jit(solution)/shard_map/ppermute | solution.py:265
  47.7 23.1 %collective-permute-start.5 = (f32[512,64]{0,1:T(8,128)S(1)}, f32[512,64]{0,1:T(8,128)S(1)}, u32[]{:S(2)}, u32[]{:S(2)}) collective-permute-start(f32[512,64]{0,1:T(8,128)S(1)} %multiply_reduce_fusion.2), channel_id=1, source_target_pairs={{0,0},{1,4},{2,8},{3,12},{4,1},{5,5},{6,9},{7,13},{8,2},{9,6},{10,... | collective-permute-start | bytes 393224 | tf_op jit(solution)/shard_map/ppermute | solution.py:265
  51.6 19.1 %collective-permute-start.6 = (f32[512,64]{0,1:T(8,128)S(1)}, f32[512,64]{0,1:T(8,128)S(1)}, u32[]{:S(2)}, u32[]{:S(2)}) collective-permute-start(f32[512,64]{0,1:T(8,128)S(1)} %multiply_reduce_fusion.2), channel_id=1, source_target_pairs={{0,1},{1,5},{2,9},{3,13},{4,2},{5,6},{6,10},{7,14},{8,3},{9,7},{10... | collective-permute-start | bytes 393224 | tf_op jit(solution)/shard_map/ppermute | solution.py:265
  74.8 12.2 %collective-permute-start.11 = (bf16[128,1168]{0,1:T(8,128)(2,1)S(1)}, bf16[128,1168]{0,1:T(8,128)(2,1)S(1)}, u32[]{:S(2)}, u32[]{:S(2)}) collective-permute-start(bf16[128,1168]{0,1:T(8,128)(2,1)S(1)} %get-tuple-element.21), channel_id=1, source_target_pairs={{0,12},{4,0},{8,4},{12,8},{1,13},{5,1},{9,5},{13,9},{2,14},{6,2},{... | collective-permute-start | bytes 897032 | tf_op jit(solution)/shard_map/ppermute | solution.py:257
  79.5 25.1 %collective-permute-start.10 = (bf16[128,1168]{0,1:T(8,128)(2,1)S(1)}, bf16[128,1168]{0,1:T(8,128)(2,1)S(1)}, u32[]{:S(2)}, u32[]{:S(2)}) collective-permute-start(bf16[128,1168]{0,1:T(8,128)(2,1)S(1)} %get-tuple-element.22), channel_id=1, source_target_pairs={{0,8},{4,12},{8,0},{12,4},{1,9},{5,13},{9,1},{13,5},{2,10},{6,14},... | collective-permute-start | bytes 897032 | tf_op jit(solution)/shard_map/ppermute | solution.py:257
  79.5 25.1 %collective-permute-start.9 = (bf16[128,1168]{0,1:T(8,128)(2,1)S(1)}, bf16[128,1168]{0,1:T(8,128)(2,1)S(1)}, u32[]{:S(2)}, u32[]{:S(2)}) collective-permute-start(bf16[128,1168]{0,1:T(8,128)(2,1)S(1)} %get-tuple-element.20), channel_id=1, source_target_pairs={{0,4},{4,8},{8,12},{12,0},{1,5},{5,9},{9,13},{13,1},{2,6},{6,10},{... | collective-permute-start | bytes 897032 | tf_op jit(solution)/shard_map/ppermute | solution.py:257
  107.4 2.9 %collective-permute-start.12 = (f32[3,1152]{1,0:T(4,128)S(1)}, f32[3,1152]{1,0:T(4,128)S(1)}, u32[]{:S(2)}, u32[]{:S(2)}) collective-permute-start(f32[3,1152]{1,0:T(4,128)S(1)} %copy.91), channel_id=1, source_target_pairs={{0,4},{4,8},{8,12},{1,5},{5,9},{9,13},{2,6},{6,10},{10,14},{3,7},{... | collective-permute-start | bytes 41480 | tf_op jit(solution)/shard_map/ppermute | solution.py:18
  113.9 2.0 collective-permute-start.13
  114.5 4.0 %collective-permute-start.14 = (bf16[128,128]{0,1:T(8,128)(2,1)S(1)}, bf16[128,128]{0,1:T(8,128)(2,1)S(1)}, u32[]{:S(2)}, u32[]{:S(2)}) collective-permute-start(bf16[128,128]{0,1:T(8,128)(2,1)S(1)} %slice.240), channel_id=1, source_target_pairs={{0,2},{1,3},{2,0},{3,1},{4,6},{5,7},{6,4},{7,5},{8,10},{9,11},{10,... | collective-permute-start | bytes 98312 | tf_op jit(solution)/shard_map/ppermute | solution.py:260
  115.8 3.3 %collective-permute-start.15 = (bf16[128,128]{0,1:T(8,128)(2,1)S(1)}, bf16[128,128]{0,1:T(8,128)(2,1)S(1)}, u32[]{:S(2)}, u32[]{:S(2)}) collective-permute-start(bf16[128,128]{0,1:T(8,128)(2,1)S(1)} %slice.240), channel_id=1, source_target_pairs={{0,1},{1,2},{2,3},{3,0},{4,5},{5,6},{6,7},{7,4},{8,9},{9,10},{10,1... | collective-permute-start | bytes 98312 | tf_op jit(solution)/shard_map/ppermute | solution.py:260
  121.8 18.4 %collective-permute-start.17 = (bf16[16,65,256]{2,0,1:T(8,128)(2,1)}, bf16[16,65,256]{2,0,1:T(8,128)(2,1)}, u32[]{:S(2)}, u32[]{:S(2)}) collective-permute-start(bf16[16,65,256]{2,0,1:T(8,128)(2,1)} %copy.98), channel_id=1, source_target_pairs={{0,8},{4,12},{1,9},{5,13},{2,10},{6,14},{3,11},{7,15},{16,24},{20,... | collective-permute-start | bytes 1597448 | tf_op jit(solution)/shard_map/ppermute | solution.py:401
  128.2 23.5 %collective-permute-start.18 = (bf16[16,65,256]{2,0,1:T(8,128)(2,1)}, bf16[16,65,256]{2,0,1:T(8,128)(2,1)}, u32[]{:S(2)}, u32[]{:S(2)}) collective-permute-start(bf16[16,65,256]{2,0,1:T(8,128)(2,1)} %copy.98), channel_id=1, source_target_pairs={{0,12},{1,13},{2,14},{3,15},{16,28},{17,29},{18,30},{19,31}} | collective-permute-start | bytes 1597448 | tf_op jit(solution)/shard_map/ppermute | solution.py:401
  131.0 30.1 %collective-permute-start.16 = (bf16[16,65,256]{2,0,1:T(8,128)(2,1)}, bf16[16,65,256]{2,0,1:T(8,128)(2,1)S(1)}, u32[]{:S(2)}, u32[]{:S(2)}) collective-permute-start(bf16[16,65,256]{2,0,1:T(8,128)(2,1)} %copy.98), channel_id=1, source_target_pairs={{0,4},{4,8},{8,12},{1,5},{5,9},{9,13},{2,6},{6,10},{10,14},{3,7},{... | collective-permute-start | bytes 1597448 | tf_op jit(solution)/shard_map/ppermute | solution.py:401
  164.6 22.9 %collective-permute-start.19 = (bf16[128,1024]{0,1:T(8,128)(2,1)}, bf16[128,1024]{0,1:T(8,128)(2,1)S(1)}, u32[]{:S(2)}, u32[]{:S(2)}) collective-permute-start(bf16[128,1024]{0,1:T(8,128)(2,1)} %fusion.26), channel_id=1, source_target_pairs={{0,12},{4,0},{8,4},{12,8},{1,13},{5,1},{9,5},{13,9},{2,14},{6,2},{... | collective-permute-start | bytes 786440 | tf_op jit(solution)/shard_map/ppermute | solution.py:257
  171.6 31.1 %collective-permute-start.20 = (bf16[128,1024]{0,1:T(8,128)(2,1)}, bf16[128,1024]{0,1:T(8,128)(2,1)}, u32[]{:S(2)}, u32[]{:S(2)}) collective-permute-start(bf16[128,1024]{0,1:T(8,128)(2,1)} %fusion.26), channel_id=1, source_target_pairs={{0,8},{4,12},{8,0},{12,4},{1,9},{5,13},{9,1},{13,5},{2,10},{6,14},... | collective-permute-start | bytes 786440 | tf_op jit(solution)/shard_map/ppermute | solution.py:257
  183.4 55.4 %collective-permute-start.26 = (bf16[2,64,1280]{2,1,0:T(8,128)(2,1)}, bf16[2,64,1280]{2,1,0:T(8,128)(2,1)}, u32[]{:S(2)}, u32[]{:S(2)}) collective-permute-start(bf16[2,64,1280]{2,1,0:T(8,128)(2,1)} %param.37), channel_id=1, source_target_pairs={{0,0},{1,4},{2,8},{3,12},{4,1},{5,5},{6,9},{7,13},{8,2},{9,6},{10,... | collective-permute-start | bytes 983048 | tf_op jit(solution)/shard_map/ppermute | solution.py:265
  185.5 18.3 %collective-permute-start.21 = (bf16[128,1024]{0,1:T(8,128)(2,1)}, bf16[128,1024]{0,1:T(8,128)(2,1)S(1)}, u32[]{:S(2)}, u32[]{:S(2)}) collective-permute-start(bf16[128,1024]{0,1:T(8,128)(2,1)} %fusion.26), channel_id=1, source_target_pairs={{0,4},{4,8},{8,12},{12,0},{1,5},{5,9},{9,13},{13,1},{2,6},{6,10},{... | collective-permute-start | bytes 786440 | tf_op jit(solution)/shard_map/ppermute | solution.py:257
  210.3 11.9 %collective-permute-start.24 = (f32[512,64]{0,1:T(8,128)S(1)}, f32[512,64]{0,1:T(8,128)S(1)}, u32[]{:S(2)}, u32[]{:S(2)}) collective-permute-start(f32[512,64]{0,1:T(8,128)S(1)} %multiply_reduce_fusion.1), channel_id=1, source_target_pairs={{0,3},{1,0},{2,1},{3,2},{4,7},{5,4},{6,5},{7,6},{8,11},{9,8},{10,9... | collective-permute-start | bytes 393224 | tf_op jit(solution)/shard_map/ppermute | solution.py:260
  213.5 12.2 %collective-permute-start.22 = (f32[512,64]{0,1:T(8,128)S(1)}, f32[512,64]{0,1:T(8,128)S(1)}, u32[]{:S(2)}, u32[]{:S(2)}) collective-permute-start(f32[512,64]{0,1:T(8,128)S(1)} %multiply_reduce_fusion.1), channel_id=1, source_target_pairs={{0,1},{1,2},{2,3},{3,0},{4,5},{5,6},{6,7},{7,4},{8,9},{9,10},{10,1... | collective-permute-start | bytes 393224 | tf_op jit(solution)/shard_map/ppermute | solution.py:260
  213.5 15.2 %collective-permute-start.23 = (f32[512,64]{0,1:T(8,128)S(1)}, f32[512,64]{0,1:T(8,128)S(1)}, u32[]{:S(2)}, u32[]{:S(2)}) collective-permute-start(f32[512,64]{0,1:T(8,128)S(1)} %multiply_reduce_fusion.1), channel_id=1, source_target_pairs={{0,2},{1,3},{2,0},{3,1},{4,6},{5,7},{6,4},{7,5},{8,10},{9,11},{10,... | collective-permute-start | bytes 393224 | tf_op jit(solution)/shard_map/ppermute | solution.py:260
  228.8 10.1 %collective-permute-start.25 = (f32[512,64]{0,1:T(8,128)S(1)}, f32[512,64]{0,1:T(8,128)S(1)}, u32[]{:S(2)}, u32[]{:S(2)}) collective-permute-start(f32[512,64]{0,1:T(8,128)S(1)} %add_add_fusion), channel_id=1, source_target_pairs={{0,0},{1,4},{2,8},{3,12},{4,1},{5,5},{6,9},{7,13},{8,2},{9,6},{10,... | collective-permute-start | bytes 393224 | tf_op jit(solution)/shard_map/ppermute | solution.py:265
  242.8 8.4 %collective-permute-start.29 = (bf16[128,1280]{1,0:T(8,128)(2,1)}, bf16[128,1280]{1,0:T(8,128)(2,1)S(1)}, u32[]{:S(2)}, u32[]{:S(2)}) collective-permute-start(bf16[128,1280]{1,0:T(8,128)(2,1)} %get-tuple-element.18), channel_id=1, source_target_pairs={{0,3},{1,0},{2,1},{3,2},{4,7},{5,4},{6,5},{7,6},{8,11},{9,8},{10,9... | collective-permute-start | bytes 983048 | tf_op jit(solution)/shard_map/ppermute | solution.py:260
  242.8 15.5 %collective-permute-start.28 = (bf16[128,1280]{1,0:T(8,128)(2,1)}, bf16[128,1280]{1,0:T(8,128)(2,1)}, u32[]{:S(2)}, u32[]{:S(2)}) collective-permute-start(bf16[128,1280]{1,0:T(8,128)(2,1)} %get-tuple-element.19), channel_id=1, source_target_pairs={{0,2},{1,3},{2,0},{3,1},{4,6},{5,7},{6,4},{7,5},{8,10},{9,11},{10,... | collective-permute-start | bytes 983048 | tf_op jit(solution)/shard_map/ppermute | solution.py:260
  243.4 15.9 %collective-permute-start.27 = (bf16[128,1280]{1,0:T(8,128)(2,1)S(1)}, bf16[128,1280]{1,0:T(8,128)(2,1)}, u32[]{:S(2)}, u32[]{:S(2)}) collective-permute-start(bf16[128,1280]{1,0:T(8,128)(2,1)S(1)} %get-tuple-element.17), channel_id=1, source_target_pairs={{0,1},{1,2},{2,3},{3,0},{4,5},{5,6},{6,7},{7,4},{8,9},{9,10},{10,1... | collective-permute-start | bytes 983048 | tf_op jit(solution)/shard_map/ppermute | solution.py:260
  260.7 15.5 %collective-permute-start.30 = (bf16[128,1280]{1,0:T(8,128)(2,1)S(1)}, bf16[128,1280]{1,0:T(8,128)(2,1)S(1)}, u32[]{:S(2)}, u32[]{:S(2)}) collective-permute-start(bf16[128,1280]{1,0:T(8,128)(2,1)S(1)} %add_convert_fusion), channel_id=1, source_target_pairs={{0,0},{1,4},{2,8},{3,12},{4,1},{5,5},{6,9},{7,13},{8,2},{9,6},{10,... | collective-permute-start | bytes 983048 | tf_op jit(solution)/shard_map/ppermute | solution.py:265
  (14 other events, 172.7 us)

commit v8 on v7

--- a/solution.py
+++ b/solution.py
@@ -338,8 +338,17 @@
     stream_rows = in_order(
         [tokens_t] + [moved(tokens_t, s, "lane") for s in range(1, side)], lane
     )
-    down_in_t = transposed(adapter_down_input)
-    up_out_t = transposed(adapter_up_output)
+    both_t = transposed(
+        jnp.concatenate(
+            [
+                adapter_down_input.reshape(bank_entries, -1),
+                adapter_up_output.reshape(bank_entries, -1),
+            ],
+            axis=1,
+        )
+    )
+    down_in_t = both_t[:, : adapter_down_input[0].size].reshape(adapter_down_input.shape)
+    up_out_t = both_t[:, adapter_down_input[0].size :].reshape(adapter_up_output.shape)
     down_part = jnp.einsum(
         "pf,efr->per", stream_rows, down_in_t, preferred_element_type=jnp.float32
     )

time: 278 us -> 285 us (1.025)
  local copies, waits for them, and re-layouts: 20.3 us -> 34 us
  starting transfers between devices: 75.1 us -> 64.4 us
  other arithmetic: 15.7 us -> 19 us
    ppermute x12, waiting for transfers between devices: 40.3 us -> 25.1 us  [moved(): return lax.ppermute(block, ('tp', 'dp'), pairs)]
    ppermute x9 -> x8, waiting for transfers between devices: 48 us -> 61.1 us  [moved(): return lax.ppermute(block, ('ctx', 'tp', 'dp'), pairs)]
    ppermute x12, starting transfers between devices: 14.5 us -> 4.17 us  [moved(): return lax.ppermute(block, ('tp', 'dp'), pairs)]
    unnamed x52 -> x68, local copies, waits for them, and re-layouts: 6.64 us -> 16.1 us
    concatenate x0 -> x1, other arithmetic: none -> 3.75 us  [square_body(): jnp.concatenate([adapter_down_input.reshape(bank_entries, -1), adapter_up...]
    reshape x0 -> x3, local copies, waits for them, and re-layouts: none -> 3.67 us  [the longest x2 2.4 us: square_body(): both_t[:, :adapter_down_input[0].size].reshape(adapter_down_input.shape)]
    ppermute x9 -> x8, starting transfers between devices: 22.9 us -> 22.3 us  [moved(): return lax.ppermute(block, ('ctx', 'tp', 'dp'), pairs)]
  transfers between devices with their start and end apart: 31 -> 30, of which waited for: 21 -> 21; matrix products, arithmetic and copies ran while one was open for 9% -> 11% of each run, Pallas kernels for 0% -> 0%
where the time goes in v8:
time: 285 us; the launch traced here: 283 us
  waiting for transfers between devices  151 us (53%)
  starting transfers between devices  64.4 us (23%)
  local copies, waits for them, and re-layouts  34 us (12%)
  other arithmetic  19 us (7%)
  matrix products  12.9 us (5%)
    ppermute x8, waiting for transfers between devices, moved(): return lax.ppermute(block, ('ctx', 'tp', 'dp'), pairs)  61.1 us
    ppermute x6, waiting for transfers between devices, moved(): return lax.ppermute(block, 'ctx', pairs)  41.2 us
    ppermute x6, starting transfers between devices, moved(): return lax.ppermute(block, 'ctx', pairs)  26.5 us
    ppermute x12, waiting for transfers between devices, moved(): return lax.ppermute(block, ('tp', 'dp'), pairs)  25.1 us
    ppermute x3, waiting for transfers between devices, square_body(): both_in = lax.ppermute(state_and_decay, 'ctx', pairs).astype(jnp.float32)  23.5 us
    ppermute x8, starting transfers between devices, moved(): return lax.ppermute(block, ('ctx', 'tp', 'dp'), pairs)  22.3 us
    unnamed x68, local copies, waits for them, and re-layouts  16.1 us
    ppermute x3, starting transfers between devices, square_body(): both_in = lax.ppermute(state_and_decay, 'ctx', pairs).astype(jnp.float32)  10 us
  transfers between devices with their start and end apart: 30, of which 21 were waited for; matrix products, arithmetic and copies ran while one was open for 11% of the time, Pallas kernels for 0%

profile of v8, /device:TPU:2, one launch (start us, length us, event | category | flops | bytes accessed | tf_op | source)
XLA Modules:
  0.0 283.3 jit_solution(15796418339159533810)
XLA Ops:
  0.0 4.7 %collective-permute-start = (bf16[128,1280]{1,0:T(8,128)(2,1)}, bf16[128,1280]{1,0:T(8,128)(2,1)}, u32[]{:S(2)}, u32[]{:S(2)}) collective-permute-start(bf16[128,1280]{1,0:T(8,128)(2,1)} %param.19), channel_id=1, source_target_pairs={{0,0},{1,4},{2,8},{3,12},{4,1},{5,5},{6,9},{7,13},{8,2},{9,6},{10,... | collective-permute-start | bytes 983048 | tf_op jit(solution)/shard_map/ppermute | solution.py:265
  4.8 2.0 copy.116
  9.4 3.7 %pad_maximum_fusion.1 = bf16[2,163840]{1,0:T(2,128)(2,1)} fusion(bf16[2,81920]{1,0:T(2,128)(2,1)} %bitcast.119, bf16[2,81920]{1,0:T(2,128)(2,1)} %reshape.316), kind=kLoop, calls=%fused_computation.28 | loop fusion | flops 1310720 | bytes 1310720 | tf_op jit(solution)/shard_map/concatenate | solution.py:342
  13.2 3.2 %collective-permute-start.4 = (bf16[2,163840]{1,0:T(2,128)(2,1)}, bf16[2,163840]{1,0:T(2,128)(2,1)S(1)}, u32[]{:S(2)}, u32[]{:S(2)}) collective-permute-start(bf16[2,163840]{1,0:T(2,128)(2,1)} %pad_maximum_fusion.1), channel_id=1, source_target_pairs={{0,0},{1,4},{2,8},{3,12},{4,1},{5,5},{6,9},{7,13},{8,2},{9,6},{10,... | collective-permute-start | bytes 1966088 | tf_op jit(solution)/shard_map/ppermute | solution.py:265
  21.6 14.3 %collective-permute-done = bf16[128,1280]{1,0:T(8,128)(2,1)} collective-permute-done((bf16[128,1280]{1,0:T(8,128)(2,1)}, bf16[128,1280]{1,0:T(8,128)(2,1)}, u32[]{:S(2)}, u32[]{:S(2)}) %collective-permute-start) | collective-permute-done | bytes 327712 | tf_op jit(solution)/shard_map/ppermute | solution.py:265
  36.4 13.1 %collective-permute-done.4 = bf16[2,163840]{1,0:T(2,128)(2,1)S(1)} collective-permute-done((bf16[2,163840]{1,0:T(2,128)(2,1)}, bf16[2,163840]{1,0:T(2,128)(2,1)S(1)}, u32[]{:S(2)}, u32[]{:S(2)}) %collective-permute-start.4) | collective-permute-done | bytes 655392 | tf_op jit(solution)/shard_map/ppermute | solution.py:265
  65.2 3.8 %collective-permute-start.5 = (f32[512,64]{0,1:T(8,128)S(1)}, f32[512,64]{0,1:T(8,128)S(1)}, u32[]{:S(2)}, u32[]{:S(2)}) collective-permute-start(f32[512,64]{0,1:T(8,128)S(1)} %multiply_reduce_fusion.2), channel_id=1, source_target_pairs={{0,0},{1,4},{2,8},{3,12},{4,1},{5,5},{6,9},{7,13},{8,2},{9,6},{10,... | collective-permute-start | bytes 393224 | tf_op jit(solution)/shard_map/ppermute | solution.py:265
  69.0 2.6 collective-permute-start.6
  73.0 14.1 %collective-permute-done.5 = f32[512,64]{0,1:T(8,128)S(1)} collective-permute-done((f32[512,64]{0,1:T(8,128)S(1)}, f32[512,64]{0,1:T(8,128)S(1)}, u32[]{:S(2)}, u32[]{:S(2)}) %collective-permute-start.5) | collective-permute-done | bytes 131104 | tf_op jit(solution)/shard_map/ppermute | solution.py:265
  91.2 4.7 %collective-permute-start.11 = (bf16[128,1168]{0,1:T(8,128)(2,1)S(1)}, bf16[128,1168]{0,1:T(8,128)(2,1)S(1)}, u32[]{:S(2)}, u32[]{:S(2)}) collective-permute-start(bf16[128,1168]{0,1:T(8,128)(2,1)S(1)} %get-tuple-element.21), channel_id=1, source_target_pairs={{0,12},{4,0},{8,4},{12,8},{1,13},{5,1},{9,5},{13,9},{2,14},{6,2},{... | collective-permute-start | bytes 897032 | tf_op jit(solution)/shard_map/ppermute | solution.py:257
  97.0 6.4 %collective-permute-done.11 = bf16[128,1168]{0,1:T(8,128)(2,1)S(1)} collective-permute-done((bf16[128,1168]{0,1:T(8,128)(2,1)S(1)}, bf16[128,1168]{0,1:T(8,128)(2,1)S(1)}, u32[]{:S(2)}, u32[]{:S(2)}) %collective-permute-start.11) | collective-permute-done | bytes 299040 | tf_op jit(solution)/shard_map/ppermute | solution.py:257
  103.4 17.5 %collective-permute-done.10 = bf16[128,1168]{0,1:T(8,128)(2,1)S(1)} collective-permute-done((bf16[128,1168]{0,1:T(8,128)(2,1)S(1)}, bf16[128,1168]{0,1:T(8,128)(2,1)S(1)}, u32[]{:S(2)}, u32[]{:S(2)}) %collective-permute-start.10) | collective-permute-done | bytes 299040 | tf_op jit(solution)/shard_map/ppermute | solution.py:257
  126.9 3.3 %divide_multiply_fusion = f32[128,1152]{0,1:T(8,128)S(1)} fusion(f32[128,1152]{0,1:T(8,128)} %slice.138, f32[3,1152]{0,1:T(8,128)S(1)} %copy.102, f32[128]{0:T(128)S(1)} %get-tuple-element.36, f32[1152]{0:T(1024)S(1)} %get-tuple-element.6, f32[128]{0:T(128)S(1)} %get-tuple-element.37, f32[1152]{0:T(1024)S(1)} %get-tuple-element.7, ...), kind=kLoop, calls=%fused_computation.50 | loop fusion | flops 2654208 | bytes 1213952 | tf_op jit(solution)/shard_map/jit(silu)/mul | solution.py:391
  132.0 2.9 %collective-permute-done.14 = bf16[128,128]{0,1:T(8,128)(2,1)S(1)} collective-permute-done((bf16[128,128]{0,1:T(8,128)(2,1)S(1)}, bf16[128,128]{0,1:T(8,128)(2,1)S(1)}, u32[]{:S(2)}, u32[]{:S(2)}) %collective-permute-start.14) | collective-permute-done | bytes 32800 | tf_op jit(solution)/shard_map/ppermute | solution.py:260
  138.0 6.3 %collective-permute-start.17 = (bf16[16,65,256]{2,0,1:T(8,128)(2,1)}, bf16[16,65,256]{2,0,1:T(8,128)(2,1)}, u32[]{:S(2)}, u32[]{:S(2)}) collective-permute-start(bf16[16,65,256]{2,0,1:T(8,128)(2,1)} %copy.108), channel_id=1, source_target_pairs={{0,8},{4,12},{1,9},{5,13},{2,10},{6,14},{3,11},{7,15},{16,24},{20,... | collective-permute-start | bytes 1597448 | tf_op jit(solution)/shard_map/ppermute | solution.py:410
  144.3 2.3 collective-permute-start.18
  149.0 2.2 convolution_bitcast_fusion
  151.2 5.1 %collective-permute-done.17 = bf16[16,65,256]{2,0,1:T(8,128)(2,1)} collective-permute-done((bf16[16,65,256]{2,0,1:T(8,128)(2,1)}, bf16[16,65,256]{2,0,1:T(8,128)(2,1)}, u32[]{:S(2)}, u32[]{:S(2)}) %collective-permute-start.17) | collective-permute-done | bytes 532512 | tf_op jit(solution)/shard_map/ppermute | solution.py:410
  157.5 10.3 %collective-permute-done.18 = bf16[16,65,256]{2,0,1:T(8,128)(2,1)} collective-permute-done((bf16[16,65,256]{2,0,1:T(8,128)(2,1)}, bf16[16,65,256]{2,0,1:T(8,128)(2,1)}, u32[]{:S(2)}, u32[]{:S(2)}) %collective-permute-start.18) | collective-permute-done | bytes 532512 | tf_op jit(solution)/shard_map/ppermute | solution.py:410
  169.2 8.1 %collective-permute-done.16 = bf16[16,65,256]{2,0,1:T(8,128)(2,1)S(1)} collective-permute-done((bf16[16,65,256]{2,0,1:T(8,128)(2,1)}, bf16[16,65,256]{2,0,1:T(8,128)(2,1)S(1)}, u32[]{:S(2)}, u32[]{:S(2)}) %collective-permute-start.16) | collective-permute-done | bytes 532512 | tf_op jit(solution)/shard_map/ppermute | solution.py:410
  180.7 7.0 %collective-permute-start.19 = (bf16[128,1024]{0,1:T(8,128)(2,1)}, bf16[128,1024]{0,1:T(8,128)(2,1)S(1)}, u32[]{:S(2)}, u32[]{:S(2)}) collective-permute-start(bf16[128,1024]{0,1:T(8,128)(2,1)} %fusion.26), channel_id=1, source_target_pairs={{0,12},{4,0},{8,4},{12,8},{1,13},{5,1},{9,5},{13,9},{2,14},{6,2},{... | collective-permute-start | bytes 786440 | tf_op jit(solution)/shard_map/ppermute | solution.py:257
  187.7 11.8 %collective-permute-start.20 = (bf16[128,1024]{0,1:T(8,128)(2,1)}, bf16[128,1024]{0,1:T(8,128)(2,1)}, u32[]{:S(2)}, u32[]{:S(2)}) collective-permute-start(bf16[128,1024]{0,1:T(8,128)(2,1)} %fusion.26), channel_id=1, source_target_pairs={{0,8},{4,12},{8,0},{12,4},{1,9},{5,13},{9,1},{13,5},{2,10},{6,14},... | collective-permute-start | bytes 786440 | tf_op jit(solution)/shard_map/ppermute | solution.py:257
  203.3 15.5 %collective-permute-done.20 = bf16[128,1024]{0,1:T(8,128)(2,1)} collective-permute-done((bf16[128,1024]{0,1:T(8,128)(2,1)}, bf16[128,1024]{0,1:T(8,128)(2,1)}, u32[]{:S(2)}, u32[]{:S(2)}) %collective-permute-start.20) | collective-permute-done | bytes 262176 | tf_op jit(solution)/shard_map/ppermute | solution.py:257
  222.4 2.3 copy.113
  230.1 2.3 collective-permute-done.22
  234.9 2.4 collective-permute-start.25
  237.4 2.7 fusion
  240.1 5.0 %collective-permute-done.25 = f32[512,64]{0,1:T(8,128)S(1)} collective-permute-done((f32[512,64]{0,1:T(8,128)S(1)}, f32[512,64]{0,1:T(8,128)S(1)}, u32[]{:S(2)}, u32[]{:S(2)}) %collective-permute-start.25) | collective-permute-done | bytes 131104 | tf_op jit(solution)/shard_map/ppermute | solution.py:265
  249.2 7.4 %collective-permute-done.28 = bf16[128,1280]{1,0:T(8,128)(2,1)S(1)} collective-permute-done((bf16[128,1280]{1,0:T(8,128)(2,1)}, bf16[128,1280]{1,0:T(8,128)(2,1)S(1)}, u32[]{:S(2)}, u32[]{:S(2)}) %collective-permute-start.28) | collective-permute-done | bytes 327712 | tf_op jit(solution)/shard_map/ppermute | solution.py:260
  256.6 8.1 %collective-permute-done.27 = bf16[128,1280]{1,0:T(8,128)(2,1)} collective-permute-done((bf16[128,1280]{1,0:T(8,128)(2,1)}, bf16[128,1280]{1,0:T(8,128)(2,1)}, u32[]{:S(2)}, u32[]{:S(2)}) %collective-permute-start.27) | collective-permute-done | bytes 327712 | tf_op jit(solution)/shard_map/ppermute | solution.py:260
  266.5 2.4 collective-permute-start.29
  268.9 13.7 %collective-permute-done.29 = bf16[128,1280]{1,0:T(8,128)(2,1)S(1)} collective-permute-done((bf16[128,1280]{1,0:T(8,128)(2,1)S(1)}, bf16[128,1280]{1,0:T(8,128)(2,1)S(1)}, u32[]{:S(2)}, u32[]{:S(2)}) %collective-permute-start.29) | collective-permute-done | bytes 327712 | tf_op jit(solution)/shard_map/ppermute | solution.py:265
  (187 shorter events, 69.8 us)
Async XLA Ops:
  0.0 237.4 %copy-start = (bf16[1024,1280]{1,0:T(8,128)(2,1)S(1)}, bf16[1024,1280]{1,0:T(8,128)(2,1)}, u32[]{:S(2)}) copy-start(bf16[1024,1280]{1,0:T(8,128)(2,1)} %param.32) | copy-start | bytes 7864324
  0.0 35.8 %collective-permute-start = (bf16[128,1280]{1,0:T(8,128)(2,1)}, bf16[128,1280]{1,0:T(8,128)(2,1)}, u32[]{:S(2)}, u32[]{:S(2)}) collective-permute-start(bf16[128,1280]{1,0:T(8,128)(2,1)} %param.19), channel_id=1, source_target_pairs={{0,0},{1,4},{2,8},{3,12},{4,1},{5,5},{6,9},{7,13},{8,2},{9,6},{10,... | collective-permute-start | bytes 983048 | tf_op jit(solution)/shard_map/ppermute | solution.py:265
  13.2 36.3 %collective-permute-start.4 = (bf16[2,163840]{1,0:T(2,128)(2,1)}, bf16[2,163840]{1,0:T(2,128)(2,1)S(1)}, u32[]{:S(2)}, u32[]{:S(2)}) collective-permute-start(bf16[2,163840]{1,0:T(2,128)(2,1)} %pad_maximum_fusion.1), channel_id=1, source_target_pairs={{0,0},{1,4},{2,8},{3,12},{4,1},{5,5},{6,9},{7,13},{8,2},{9,6},{10,... | collective-permute-start | bytes 1966088 | tf_op jit(solution)/shard_map/ppermute | solution.py:265
  35.9 17.3 %collective-permute-start.1 = (bf16[128,1280]{1,0:T(8,128)(2,1)}, bf16[128,1280]{1,0:T(8,128)(2,1)}, u32[]{:S(2)}, u32[]{:S(2)}) collective-permute-start(bf16[128,1280]{1,0:T(8,128)(2,1)} %collective-permute-done), channel_id=1, source_target_pairs={{0,3},{1,0},{2,1},{3,2},{4,7},{5,4},{6,5},{7,6},{8,11},{9,8},{10,9... | collective-permute-start | bytes 983048 | tf_op jit(solution)/shard_map/ppermute | solution.py:260
  35.9 18.3 %collective-permute-start.2 = (bf16[128,1280]{1,0:T(8,128)(2,1)}, bf16[128,1280]{1,0:T(8,128)(2,1)}, u32[]{:S(2)}, u32[]{:S(2)}) collective-permute-start(bf16[128,1280]{1,0:T(8,128)(2,1)} %collective-permute-done), channel_id=1, source_target_pairs={{0,2},{1,3},{2,0},{3,1},{4,6},{5,7},{6,4},{7,5},{8,10},{9,11},{10,... | collective-permute-start | bytes 983048 | tf_op jit(solution)/shard_map/ppermute | solution.py:260
  35.9 19.3 %collective-permute-start.3 = (bf16[128,1280]{1,0:T(8,128)(2,1)}, bf16[128,1280]{1,0:T(8,128)(2,1)}, u32[]{:S(2)}, u32[]{:S(2)}) collective-permute-start(bf16[128,1280]{1,0:T(8,128)(2,1)} %collective-permute-done), channel_id=1, source_target_pairs={{0,1},{1,2},{2,3},{3,0},{4,5},{5,6},{6,7},{7,4},{8,9},{9,10},{10,1... | collective-permute-start | bytes 983048 | tf_op jit(solution)/shard_map/ppermute | solution.py:260
  62.0 11.0 %collective-permute-start.8 = (f32[512,64]{0,1:T(8,128)S(1)}, f32[512,64]{0,1:T(8,128)S(1)}, u32[]{:S(2)}, u32[]{:S(2)}) collective-permute-start(f32[512,64]{0,1:T(8,128)S(1)} %multiply_reduce_fusion.2), channel_id=1, source_target_pairs={{0,3},{1,7},{2,11},{3,15},{4,0},{5,4},{6,8},{7,12},{8,1},{9,5},{10... | collective-permute-start | bytes 393224 | tf_op jit(solution)/shard_map/ppermute | solution.py:265
  63.5 9.5 %collective-permute-start.7 = (f32[512,64]{0,1:T(8,128)S(1)}, f32[512,64]{0,1:T(8,128)S(1)}, u32[]{:S(2)}, u32[]{:S(2)}) collective-permute-start(f32[512,64]{0,1:T(8,128)S(1)} %multiply_reduce_fusion.2), channel_id=1, source_target_pairs={{0,2},{1,6},{2,10},{3,14},{4,3},{5,7},{6,11},{7,15},{8,0},{9,4},{1... | collective-permute-start | bytes 393224 | tf_op jit(solution)/shard_map/ppermute | solution.py:265
  65.2 21.9 %collective-permute-start.5 = (f32[512,64]{0,1:T(8,128)S(1)}, f32[512,64]{0,1:T(8,128)S(1)}, u32[]{:S(2)}, u32[]{:S(2)}) collective-permute-start(f32[512,64]{0,1:T(8,128)S(1)} %multiply_reduce_fusion.2), channel_id=1, source_target_pairs={{0,0},{1,4},{2,8},{3,12},{4,1},{5,5},{6,9},{7,13},{8,2},{9,6},{10,... | collective-permute-start | bytes 393224 | tf_op jit(solution)/shard_map/ppermute | solution.py:265
  69.0 18.0 %collective-permute-start.6 = (f32[512,64]{0,1:T(8,128)S(1)}, f32[512,64]{0,1:T(8,128)S(1)}, u32[]{:S(2)}, u32[]{:S(2)}) collective-permute-start(f32[512,64]{0,1:T(8,128)S(1)} %multiply_reduce_fusion.2), channel_id=1, source_target_pairs={{0,1},{1,5},{2,9},{3,13},{4,2},{5,6},{6,10},{7,14},{8,3},{9,7},{10... | collective-permute-start | bytes 393224 | tf_op jit(solution)/shard_map/ppermute | solution.py:265
  91.2 30.9 %copy-start.15 = (f32[16]{0:T(128)S(1)}, f32[16]{0:T(128)}, u32[]{:S(2)}) copy-start(f32[16]{0:T(128)} %param.28) | copy-start | bytes 196
  91.2 12.2 %collective-permute-start.11 = (bf16[128,1168]{0,1:T(8,128)(2,1)S(1)}, bf16[128,1168]{0,1:T(8,128)(2,1)S(1)}, u32[]{:S(2)}, u32[]{:S(2)}) collective-permute-start(bf16[128,1168]{0,1:T(8,128)(2,1)S(1)} %get-tuple-element.21), channel_id=1, source_target_pairs={{0,12},{4,0},{8,4},{12,8},{1,13},{5,1},{9,5},{13,9},{2,14},{6,2},{... | collective-permute-start | bytes 897032 | tf_op jit(solution)/shard_map/ppermute | solution.py:257
  95.9 25.1 %collective-permute-start.10 = (bf16[128,1168]{0,1:T(8,128)(2,1)S(1)}, bf16[128,1168]{0,1:T(8,128)(2,1)S(1)}, u32[]{:S(2)}, u32[]{:S(2)}) collective-permute-start(bf16[128,1168]{0,1:T(8,128)(2,1)S(1)} %get-tuple-element.22), channel_id=1, source_target_pairs={{0,8},{4,12},{8,0},{12,4},{1,9},{5,13},{9,1},{13,5},{2,10},{6,14},... | collective-permute-start | bytes 897032 | tf_op jit(solution)/shard_map/ppermute | solution.py:257
  95.9 25.1 %collective-permute-start.9 = (bf16[128,1168]{0,1:T(8,128)(2,1)S(1)}, bf16[128,1168]{0,1:T(8,128)(2,1)S(1)}, u32[]{:S(2)}, u32[]{:S(2)}) collective-permute-start(bf16[128,1168]{0,1:T(8,128)(2,1)S(1)} %get-tuple-element.20), channel_id=1, source_target_pairs={{0,4},{4,8},{8,12},{12,0},{1,5},{5,9},{9,13},{13,1},{2,6},{6,10},{... | collective-permute-start | bytes 897032 | tf_op jit(solution)/shard_map/ppermute | solution.py:257
  123.8 2.9 %collective-permute-start.12 = (f32[3,1152]{1,0:T(4,128)S(1)}, f32[3,1152]{1,0:T(4,128)S(1)}, u32[]{:S(2)}, u32[]{:S(2)}) collective-permute-start(f32[3,1152]{1,0:T(4,128)S(1)} %copy.101), channel_id=1, source_target_pairs={{0,4},{4,8},{8,12},{1,5},{5,9},{9,13},{2,6},{6,10},{10,14},{3,7},{... | collective-permute-start | bytes 41480 | tf_op jit(solution)/shard_map/ppermute | solution.py:18
  130.2 1.8 collective-permute-start.13
  130.9 4.0 %collective-permute-start.14 = (bf16[128,128]{0,1:T(8,128)(2,1)S(1)}, bf16[128,128]{0,1:T(8,128)(2,1)S(1)}, u32[]{:S(2)}, u32[]{:S(2)}) collective-permute-start(bf16[128,128]{0,1:T(8,128)(2,1)S(1)} %slice.250), channel_id=1, source_target_pairs={{0,2},{1,3},{2,0},{3,1},{4,6},{5,7},{6,4},{7,5},{8,10},{9,11},{10,... | collective-permute-start | bytes 98312 | tf_op jit(solution)/shard_map/ppermute | solution.py:260
  132.0 3.3 %collective-permute-start.15 = (bf16[128,128]{0,1:T(8,128)(2,1)S(1)}, bf16[128,128]{0,1:T(8,128)(2,1)S(1)}, u32[]{:S(2)}, u32[]{:S(2)}) collective-permute-start(bf16[128,128]{0,1:T(8,128)(2,1)S(1)} %slice.250), channel_id=1, source_target_pairs={{0,1},{1,2},{2,3},{3,0},{4,5},{5,6},{6,7},{7,4},{8,9},{9,10},{10,1... | collective-permute-start | bytes 98312 | tf_op jit(solution)/shard_map/ppermute | solution.py:260
  138.0 18.4 %collective-permute-start.17 = (bf16[16,65,256]{2,0,1:T(8,128)(2,1)}, bf16[16,65,256]{2,0,1:T(8,128)(2,1)}, u32[]{:S(2)}, u32[]{:S(2)}) collective-permute-start(bf16[16,65,256]{2,0,1:T(8,128)(2,1)} %copy.108), channel_id=1, source_target_pairs={{0,8},{4,12},{1,9},{5,13},{2,10},{6,14},{3,11},{7,15},{16,24},{20,... | collective-permute-start | bytes 1597448 | tf_op jit(solution)/shard_map/ppermute | solution.py:410
  144.3 23.5 %collective-permute-start.18 = (bf16[16,65,256]{2,0,1:T(8,128)(2,1)}, bf16[16,65,256]{2,0,1:T(8,128)(2,1)}, u32[]{:S(2)}, u32[]{:S(2)}) collective-permute-start(bf16[16,65,256]{2,0,1:T(8,128)(2,1)} %copy.108), channel_id=1, source_target_pairs={{0,12},{1,13},{2,14},{3,15},{16,28},{17,29},{18,30},{19,31}} | collective-permute-start | bytes 1597448 | tf_op jit(solution)/shard_map/ppermute | solution.py:410
  147.4 29.9 %collective-permute-start.16 = (bf16[16,65,256]{2,0,1:T(8,128)(2,1)}, bf16[16,65,256]{2,0,1:T(8,128)(2,1)S(1)}, u32[]{:S(2)}, u32[]{:S(2)}) collective-permute-start(bf16[16,65,256]{2,0,1:T(8,128)(2,1)} %copy.108), channel_id=1, source_target_pairs={{0,4},{4,8},{8,12},{1,5},{5,9},{9,13},{2,6},{6,10},{10,14},{3,7},{... | collective-permute-start | bytes 1597448 | tf_op jit(solution)/shard_map/ppermute | solution.py:410
  180.7 22.6 %collective-permute-start.19 = (bf16[128,1024]{0,1:T(8,128)(2,1)}, bf16[128,1024]{0,1:T(8,128)(2,1)S(1)}, u32[]{:S(2)}, u32[]{:S(2)}) collective-permute-start(bf16[128,1024]{0,1:T(8,128)(2,1)} %fusion.26), channel_id=1, source_target_pairs={{0,12},{4,0},{8,4},{12,8},{1,13},{5,1},{9,5},{13,9},{2,14},{6,2},{... | collective-permute-start | bytes 786440 | tf_op jit(solution)/shard_map/ppermute | solution.py:257
  187.7 31.1 %collective-permute-start.20 = (bf16[128,1024]{0,1:T(8,128)(2,1)}, bf16[128,1024]{0,1:T(8,128)(2,1)}, u32[]{:S(2)}, u32[]{:S(2)}) collective-permute-start(bf16[128,1024]{0,1:T(8,128)(2,1)} %fusion.26), channel_id=1, source_target_pairs={{0,8},{4,12},{8,0},{12,4},{1,9},{5,13},{9,1},{13,5},{2,10},{6,14},... | collective-permute-start | bytes 786440 | tf_op jit(solution)/shard_map/ppermute | solution.py:257
  199.5 20.3 %collective-permute-start.21 = (bf16[128,1024]{0,1:T(8,128)(2,1)}, bf16[128,1024]{0,1:T(8,128)(2,1)S(1)}, u32[]{:S(2)}, u32[]{:S(2)}) collective-permute-start(bf16[128,1024]{0,1:T(8,128)(2,1)} %fusion.26), channel_id=1, source_target_pairs={{0,4},{4,8},{8,12},{12,0},{1,5},{5,9},{9,13},{13,1},{2,6},{6,10},{... | collective-permute-start | bytes 786440 | tf_op jit(solution)/shard_map/ppermute | solution.py:257
  226.4 3.6 %collective-permute-start.24 = (f32[512,64]{0,1:T(8,128)S(1)}, f32[512,64]{0,1:T(8,128)S(1)}, u32[]{:S(2)}, u32[]{:S(2)}) collective-permute-start(f32[512,64]{0,1:T(8,128)S(1)} %multiply_reduce_fusion.1), channel_id=1, source_target_pairs={{0,3},{1,0},{2,1},{3,2},{4,7},{5,4},{6,5},{7,6},{8,11},{9,8},{10,9... | collective-permute-start | bytes 393224 | tf_op jit(solution)/shard_map/ppermute | solution.py:260
  226.5 5.9 %collective-permute-start.22 = (f32[512,64]{0,1:T(8,128)S(1)}, f32[512,64]{0,1:T(8,128)}, u32[]{:S(2)}, u32[]{:S(2)}) collective-permute-start(f32[512,64]{0,1:T(8,128)S(1)} %multiply_reduce_fusion.1), channel_id=1, source_target_pairs={{0,1},{1,2},{2,3},{3,0},{4,5},{5,6},{6,7},{7,4},{8,9},{9,10},{10,1... | collective-permute-start | bytes 393224 | tf_op jit(solution)/shard_map/ppermute | solution.py:260
  227.0 6.9 %collective-permute-start.23 = (f32[512,64]{0,1:T(8,128)S(1)}, f32[512,64]{0,1:T(8,128)}, u32[]{:S(2)}, u32[]{:S(2)}) collective-permute-start(f32[512,64]{0,1:T(8,128)S(1)} %multiply_reduce_fusion.1), channel_id=1, source_target_pairs={{0,2},{1,3},{2,0},{3,1},{4,6},{5,7},{6,4},{7,5},{8,10},{9,11},{10,... | collective-permute-start | bytes 393224 | tf_op jit(solution)/shard_map/ppermute | solution.py:260
  234.9 10.2 %collective-permute-start.25 = (f32[512,64]{0,1:T(8,128)S(1)}, f32[512,64]{0,1:T(8,128)S(1)}, u32[]{:S(2)}, u32[]{:S(2)}) collective-permute-start(f32[512,64]{0,1:T(8,128)S(1)} %add_add_fusion), channel_id=1, source_target_pairs={{0,0},{1,4},{2,8},{3,12},{4,1},{5,5},{6,9},{7,13},{8,2},{9,6},{10,... | collective-permute-start | bytes 393224 | tf_op jit(solution)/shard_map/ppermute | solution.py:265
  248.1 8.5 %collective-permute-start.28 = (bf16[128,1280]{1,0:T(8,128)(2,1)}, bf16[128,1280]{1,0:T(8,128)(2,1)S(1)}, u32[]{:S(2)}, u32[]{:S(2)}) collective-permute-start(bf16[128,1280]{1,0:T(8,128)(2,1)} %get-tuple-element.18), channel_id=1, source_target_pairs={{0,3},{1,0},{2,1},{3,2},{4,7},{5,4},{6,5},{7,6},{8,11},{9,8},{10,9... | collective-permute-start | bytes 983048 | tf_op jit(solution)/shard_map/ppermute | solution.py:260
  248.3 16.4 %collective-permute-start.27 = (bf16[128,1280]{1,0:T(8,128)(2,1)}, bf16[128,1280]{1,0:T(8,128)(2,1)}, u32[]{:S(2)}, u32[]{:S(2)}) collective-permute-start(bf16[128,1280]{1,0:T(8,128)(2,1)} %get-tuple-element.19), channel_id=1, source_target_pairs={{0,2},{1,3},{2,0},{3,1},{4,6},{5,7},{6,4},{7,5},{8,10},{9,11},{10,... | collective-permute-start | bytes 983048 | tf_op jit(solution)/shard_map/ppermute | solution.py:260
  249.2 15.9 %collective-permute-start.26 = (bf16[128,1280]{1,0:T(8,128)(2,1)S(1)}, bf16[128,1280]{1,0:T(8,128)(2,1)}, u32[]{:S(2)}, u32[]{:S(2)}) collective-permute-start(bf16[128,1280]{1,0:T(8,128)(2,1)S(1)} %get-tuple-element.17), channel_id=1, source_target_pairs={{0,1},{1,2},{2,3},{3,0},{4,5},{5,6},{6,7},{7,4},{8,9},{9,10},{10,1... | collective-permute-start | bytes 983048 | tf_op jit(solution)/shard_map/ppermute | solution.py:260
  266.5 16.0 %collective-permute-start.29 = (bf16[128,1280]{1,0:T(8,128)(2,1)S(1)}, bf16[128,1280]{1,0:T(8,128)(2,1)S(1)}, u32[]{:S(2)}, u32[]{:S(2)}) collective-permute-start(bf16[128,1280]{1,0:T(8,128)(2,1)S(1)} %add_convert_fusion), channel_id=1, source_target_pairs={{0,0},{1,4},{2,8},{3,12},{4,1},{5,5},{6,9},{7,13},{8,2},{9,6},{10,... | collective-permute-start | bytes 983048 | tf_op jit(solution)/shard_map/ppermute | solution.py:265
  (20 other events, 236.6 us)

commit v9 on v7

--- a/solution.py
+++ b/solution.py
@@ -338,16 +338,22 @@
     stream_rows = in_order(
         [tokens_t] + [moved(tokens_t, s, "lane") for s in range(1, side)], lane
     )
-    down_in_t = transposed(adapter_down_input)
+    local_owned = lax.dynamic_slice_in_dim(slot_of_position, start_pos, length, 0)
+    down_pick = jnp.zeros((length, rank_value), jnp.float32)
+    for s in range(side):
+        piece = adapter_down_input if s == 0 else moved(adapter_down_input, s, "ctx")
+        first = ((here - s) % side) * bank_entries
+        every = jnp.einsum("pf,efr->per", tokens, piece, preferred_element_type=jnp.float32)
+        chosen = local_owned[:, None] == first + jnp.arange(bank_entries, dtype=jnp.int32)[None, :]
+        down_pick = down_pick + jnp.sum(every * chosen[:, :, None].astype(jnp.float32), axis=1)
+    rank_local = (
+        down_pick + sum(moved(down_pick, s, "lane") for s in range(1, side))
+    ).astype(jnp.bfloat16)
+    rank_hidden = in_order(
+        [rank_local] + [moved(rank_local, s, "ctx") for s in range(1, side)], here
+    )
     up_out_t = transposed(adapter_up_output)
-    down_part = jnp.einsum(
-        "pf,efr->per", stream_rows, down_in_t, preferred_element_type=jnp.float32
-    )
-    down_pick = jnp.sum(
-        down_part * owned_lane[:, :, None].astype(jnp.float32), axis=1
-    )
-    rank_hidden = sum(moved(down_pick, s, "rows") for s in range(side))
-    hidden_wide = owned_rows(rank_hidden, owned_here).astype(jnp.bfloat16)
+    hidden_wide = owned_rows(rank_hidden, owned_here)
     xchan_part = jnp.dot(
         stream_rows, xchan_input_weight, preferred_element_type=jnp.float32
     ) + jnp.dot(

time: 278 us -> 275 us (0.989)
  waiting for transfers between devices: 151 us -> 128 us
  starting transfers between devices: 75.1 us -> 81.5 us
  matrix products: 12.7 us -> 18.7 us
  other arithmetic: 15.7 us -> 21.7 us
    ppermute x9 -> x4, waiting for transfers between devices: 48 us -> 19.3 us  [moved(): return lax.ppermute(block, ('ctx', 'tp', 'dp'), pairs)]
    ppermute x9 -> x4, starting transfers between devices: 22.9 us -> 10.7 us  [moved(): return lax.ppermute(block, ('ctx', 'tp', 'dp'), pairs)]
    ppermute x6 -> x12, waiting for transfers between devices: 39.1 us -> 49.8 us  [moved(): return lax.ppermute(block, 'ctx', pairs)]
    ppermute x12 -> x15, starting transfers between devices: 14.5 us -> 23.9 us  [moved(): return lax.ppermute(block, ('tp', 'dp'), pairs)]
    ppermute x6 -> x12, starting transfers between devices: 26.5 us -> 33.3 us  [moved(): return lax.ppermute(block, 'ctx', pairs)]
    ppermute x12 -> x15, waiting for transfers between devices: 40.3 us -> 35 us  [moved(): return lax.ppermute(block, ('tp', 'dp'), pairs)]
    unnamed x2 -> x5, matrix products: 2.34 us -> 7.48 us
    unnamed x52 -> x81, local copies, waits for them, and re-layouts: 6.64 us -> 7.28 us
  transfers between devices with their start and end apart: 31 -> 35, of which waited for: 21 -> 21; matrix products, arithmetic and copies ran while one was open for 9% -> 14% of each run, Pallas kernels for 0% -> 0%
where the time goes in v9:
time: 275 us; the launch traced here: 273 us
  waiting for transfers between devices  128 us (47%)
  starting transfers between devices  81.5 us (30%)
  other arithmetic  21.7 us (8%)
  local copies, waits for them, and re-layouts  21.6 us (8%)
  matrix products  18.7 us (7%)
    ppermute x12, waiting for transfers between devices, moved(): return lax.ppermute(block, 'ctx', pairs)  49.8 us
    ppermute x15, waiting for transfers between devices, moved(): return lax.ppermute(block, ('tp', 'dp'), pairs)  35 us
    ppermute x12, starting transfers between devices, moved(): return lax.ppermute(block, 'ctx', pairs)  33.3 us
    ppermute x15, starting transfers between devices, moved(): return lax.ppermute(block, ('tp', 'dp'), pairs)  23.9 us
    ppermute x3, waiting for transfers between devices, square_body(): both_in = lax.ppermute(state_and_decay, 'ctx', pairs).astype(jnp.float32)  23.6 us
    ppermute x4, waiting for transfers between devices, moved(): return lax.ppermute(block, ('ctx', 'tp', 'dp'), pairs)  19.3 us
    ppermute x4, starting transfers between devices, moved(): return lax.ppermute(block, ('ctx', 'tp', 'dp'), pairs)  10.7 us
    ppermute x3, starting transfers between devices, square_body(): both_in = lax.ppermute(state_and_decay, 'ctx', pairs).astype(jnp.float32)  10.4 us
  transfers between devices with their start and end apart: 35, of which 21 were waited for; matrix products, arithmetic and copies ran while one was open for 14% of the time, Pallas kernels for 0%

profile of v9, /device:TPU:2, one launch (start us, length us, event | category | flops | bytes accessed | tf_op | source)
XLA Modules:
  0.0 273.3 jit_solution(7422105307675079401)
XLA Ops:
  0.0 3.6 %collective-permute-start.6 = (bf16[2,1280,64]{1,2,0:T(8,128)(2,1)}, bf16[2,1280,64]{1,2,0:T(8,128)(2,1)}, u32[]{:S(2)}, u32[]{:S(2)}) collective-permute-start(bf16[2,1280,64]{1,2,0:T(8,128)(2,1)} %param.33), channel_id=1, source_target_pairs={{0,12},{4,0},{8,4},{12,8},{1,13},{5,1},{9,5},{13,9},{2,14},{6,2},{... | collective-permute-start | bytes 983048 | tf_op jit(solution)/shard_map/ppermute | solution.py:257
  4.6 3.8 %collective-permute-start = (bf16[128,1280]{1,0:T(8,128)(2,1)}, bf16[128,1280]{1,0:T(8,128)(2,1)S(1)}, u32[]{:S(2)}, u32[]{:S(2)}) collective-permute-start(bf16[128,1280]{1,0:T(8,128)(2,1)} %param.19), channel_id=1, source_target_pairs={{0,0},{1,4},{2,8},{3,12},{4,1},{5,5},{6,9},{7,13},{8,2},{9,6},{10,... | collective-permute-start | bytes 983048 | tf_op jit(solution)/shard_map/ppermute | solution.py:265
  24.6 7.2 %collective-permute-done.5 = bf16[2,1280,64]{1,2,0:T(8,128)(2,1)} collective-permute-done((bf16[2,1280,64]{1,2,0:T(8,128)(2,1)}, bf16[2,1280,64]{1,2,0:T(8,128)(2,1)}, u32[]{:S(2)}, u32[]{:S(2)}) %collective-permute-start.5) | collective-permute-done | bytes 327712 | tf_op jit(solution)/shard_map/ppermute | solution.py:257
  34.4 6.2 %collective-permute-start.9 = (f32[128,64]{0,1:T(8,128)S(1)}, f32[128,64]{0,1:T(8,128)S(1)}, u32[]{:S(2)}, u32[]{:S(2)}) collective-permute-start(f32[128,64]{0,1:T(8,128)S(1)} %add_add_fusion.1), channel_id=1, source_target_pairs={{0,3},{1,0},{2,1},{3,2},{4,7},{5,4},{6,5},{7,6},{8,11},{9,8},{10,9... | collective-permute-start | bytes 98312 | tf_op jit(solution)/shard_map/ppermute | solution.py:260
  40.6 3.1 %collective-permute-start.8 = (f32[128,64]{0,1:T(8,128)S(1)}, f32[128,64]{0,1:T(8,128)S(1)}, u32[]{:S(2)}, u32[]{:S(2)}) collective-permute-start(f32[128,64]{0,1:T(8,128)S(1)} %add_add_fusion.1), channel_id=1, source_target_pairs={{0,2},{1,3},{2,0},{3,1},{4,6},{5,7},{6,4},{7,5},{8,10},{9,11},{10,... | collective-permute-start | bytes 98312 | tf_op jit(solution)/shard_map/ppermute | solution.py:260
  56.1 2.8 %collective-permute-done.12 = bf16[128,64]{0,1:T(8,128)(2,1)S(1)} collective-permute-done((bf16[128,64]{0,1:T(8,128)(2,1)S(1)}, bf16[128,64]{0,1:T(8,128)(2,1)S(1)}, u32[]{:S(2)}, u32[]{:S(2)}) %collective-permute-start.12) | collective-permute-done | bytes 16416 | tf_op jit(solution)/shard_map/ppermute | solution.py:257
  60.5 6.3 %collective-permute-done.2 = bf16[128,1280]{1,0:T(8,128)(2,1)S(1)} collective-permute-done((bf16[128,1280]{1,0:T(8,128)(2,1)S(1)}, bf16[128,1280]{1,0:T(8,128)(2,1)S(1)}, u32[]{:S(2)}, u32[]{:S(2)}) %collective-permute-start.2) | collective-permute-done | bytes 327712 | tf_op jit(solution)/shard_map/ppermute | solution.py:260
  71.1 3.2 %collective-permute-start.15 = (bf16[128,1168]{0,1:T(8,128)(2,1)S(1)}, bf16[128,1168]{0,1:T(8,128)(2,1)S(1)}, u32[]{:S(2)}, u32[]{:S(2)}) collective-permute-start(bf16[128,1168]{0,1:T(8,128)(2,1)S(1)} %get-tuple-element.19), channel_id=1, source_target_pairs={{0,12},{4,0},{8,4},{12,8},{1,13},{5,1},{9,5},{13,9},{2,14},{6,2},{... | collective-permute-start | bytes 897032 | tf_op jit(solution)/shard_map/ppermute | solution.py:257
  75.0 6.8 %collective-permute-done.15 = bf16[128,1168]{0,1:T(8,128)(2,1)S(1)} collective-permute-done((bf16[128,1168]{0,1:T(8,128)(2,1)S(1)}, bf16[128,1168]{0,1:T(8,128)(2,1)S(1)}, u32[]{:S(2)}, u32[]{:S(2)}) %collective-permute-start.15) | collective-permute-done | bytes 299040 | tf_op jit(solution)/shard_map/ppermute | solution.py:257
  81.8 17.0 %collective-permute-done.14 = bf16[128,1168]{0,1:T(8,128)(2,1)S(1)} collective-permute-done((bf16[128,1168]{0,1:T(8,128)(2,1)S(1)}, bf16[128,1168]{0,1:T(8,128)(2,1)S(1)}, u32[]{:S(2)}, u32[]{:S(2)}) %collective-permute-start.14) | collective-permute-done | bytes 299040 | tf_op jit(solution)/shard_map/ppermute | solution.py:257
  101.7 3.1 %collective-permute-start.16 = (f32[3,1152]{1,0:T(4,128)S(1)}, f32[3,1152]{1,0:T(4,128)S(1)}, u32[]{:S(2)}, u32[]{:S(2)}) collective-permute-start(f32[3,1152]{1,0:T(4,128)S(1)} %copy.111), channel_id=1, source_target_pairs={{0,4},{4,8},{8,12},{1,5},{5,9},{9,13},{2,6},{6,10},{10,14},{3,7},{... | collective-permute-start | bytes 41480 | tf_op jit(solution)/shard_map/ppermute | solution.py:18
  106.7 3.3 %divide_multiply_fusion = f32[128,1152]{0,1:T(8,128)S(1)} fusion(f32[128,1152]{0,1:T(8,128)} %slice.129, f32[3,1152]{0,1:T(8,128)S(1)} %copy.112, f32[128]{0:T(128)S(1)} %copy-done.19, f32[1152]{0:T(1024)S(1)} %get-tuple-element.6, f32[128]{0:T(128)S(1)} %copy-done.20, f32[1152]{0:T(1024)S(1)} %get-tuple-element.7, f32[128]{0:T(128)S(1)} %copy-done.21, ...), kind=kLoop, calls=%fused_computation.49 | loop fusion | flops 2654208 | bytes 1213952 | tf_op jit(solution)/shard_map/jit(silu)/mul | solution.py:388
  111.7 3.2 %collective-permute-done.18 = bf16[128,128]{0,1:T(8,128)(2,1)S(1)} collective-permute-done((bf16[128,128]{0,1:T(8,128)(2,1)S(1)}, bf16[128,128]{0,1:T(8,128)(2,1)S(1)}, u32[]{:S(2)}, u32[]{:S(2)}) %collective-permute-start.18) | collective-permute-done | bytes 32800 | tf_op jit(solution)/shard_map/ppermute | solution.py:260
  117.6 6.8 %collective-permute-start.21 = (bf16[16,65,256]{2,0,1:T(8,128)(2,1)}, bf16[16,65,256]{2,0,1:T(8,128)(2,1)}, u32[]{:S(2)}, u32[]{:S(2)}) collective-permute-start(bf16[16,65,256]{2,0,1:T(8,128)(2,1)} %copy.118), channel_id=1, source_target_pairs={{0,8},{4,12},{1,9},{5,13},{2,10},{6,14},{3,11},{7,15},{16,24},{20,... | collective-permute-start | bytes 1597448 | tf_op jit(solution)/shard_map/ppermute | solution.py:407
  129.0 2.2 convolution_bitcast_fusion
  131.3 5.2 %collective-permute-done.21 = bf16[16,65,256]{2,0,1:T(8,128)(2,1)} collective-permute-done((bf16[16,65,256]{2,0,1:T(8,128)(2,1)}, bf16[16,65,256]{2,0,1:T(8,128)(2,1)}, u32[]{:S(2)}, u32[]{:S(2)}) %collective-permute-start.21) | collective-permute-done | bytes 532512 | tf_op jit(solution)/shard_map/ppermute | solution.py:407
  137.6 10.3 %collective-permute-done.22 = bf16[16,65,256]{2,0,1:T(8,128)(2,1)} collective-permute-done((bf16[16,65,256]{2,0,1:T(8,128)(2,1)}, bf16[16,65,256]{2,0,1:T(8,128)(2,1)}, u32[]{:S(2)}, u32[]{:S(2)}) %collective-permute-start.22) | collective-permute-done | bytes 532512 | tf_op jit(solution)/shard_map/ppermute | solution.py:407
  149.3 8.1 %collective-permute-done.20 = bf16[16,65,256]{2,0,1:T(8,128)(2,1)S(1)} collective-permute-done((bf16[16,65,256]{2,0,1:T(8,128)(2,1)}, bf16[16,65,256]{2,0,1:T(8,128)(2,1)S(1)}, u32[]{:S(2)}, u32[]{:S(2)}) %collective-permute-start.20) | collective-permute-done | bytes 532512 | tf_op jit(solution)/shard_map/ppermute | solution.py:407
  160.9 7.0 %collective-permute-start.23 = (bf16[128,1024]{0,1:T(8,128)(2,1)}, bf16[128,1024]{0,1:T(8,128)(2,1)S(1)}, u32[]{:S(2)}, u32[]{:S(2)}) collective-permute-start(bf16[128,1024]{0,1:T(8,128)(2,1)} %fusion.26), channel_id=1, source_target_pairs={{0,12},{4,0},{8,4},{12,8},{1,13},{5,1},{9,5},{13,9},{2,14},{6,2},{... | collective-permute-start | bytes 786440 | tf_op jit(solution)/shard_map/ppermute | solution.py:257
  167.9 11.8 %collective-permute-start.24 = (bf16[128,1024]{0,1:T(8,128)(2,1)}, bf16[128,1024]{0,1:T(8,128)(2,1)}, u32[]{:S(2)}, u32[]{:S(2)}) collective-permute-start(bf16[128,1024]{0,1:T(8,128)(2,1)} %fusion.26), channel_id=1, source_target_pairs={{0,8},{4,12},{8,0},{12,4},{1,9},{5,13},{9,1},{13,5},{2,10},{6,14},... | collective-permute-start | bytes 786440 | tf_op jit(solution)/shard_map/ppermute | solution.py:257
  183.8 15.3 %collective-permute-done.24 = bf16[128,1024]{0,1:T(8,128)(2,1)} collective-permute-done((bf16[128,1024]{0,1:T(8,128)(2,1)}, bf16[128,1024]{0,1:T(8,128)(2,1)}, u32[]{:S(2)}, u32[]{:S(2)}) %collective-permute-start.24) | collective-permute-done | bytes 262176 | tf_op jit(solution)/shard_map/ppermute | solution.py:257
  202.5 2.3 copy.123
  206.6 3.0 %collective-permute-start.28 = (f32[512,64]{0,1:T(8,128)S(1)}, f32[512,64]{0,1:T(8,128)S(1)}, u32[]{:S(2)}, u32[]{:S(2)}) collective-permute-start(f32[512,64]{0,1:T(8,128)S(1)} %multiply_reduce_fusion.1), channel_id=1, source_target_pairs={{0,3},{1,0},{2,1},{3,2},{4,7},{5,4},{6,5},{7,6},{8,11},{9,8},{10,9... | collective-permute-start | bytes 393224 | tf_op jit(solution)/shard_map/ppermute | solution.py:260
  209.6 8.7 %collective-permute-start.27 = (f32[512,64]{0,1:T(8,128)S(1)}, f32[512,64]{0,1:T(8,128)S(1)}, u32[]{:S(2)}, u32[]{:S(2)}) collective-permute-start(f32[512,64]{0,1:T(8,128)S(1)} %multiply_reduce_fusion.1), channel_id=1, source_target_pairs={{0,2},{1,3},{2,0},{3,1},{4,6},{5,7},{6,4},{7,5},{8,10},{9,11},{10,... | collective-permute-start | bytes 393224 | tf_op jit(solution)/shard_map/ppermute | solution.py:260
  218.4 3.5 %collective-permute-done.26 = f32[512,64]{0,1:T(8,128)S(1)} collective-permute-done((f32[512,64]{0,1:T(8,128)S(1)}, f32[512,64]{0,1:T(8,128)S(1)}, u32[]{:S(2)}, u32[]{:S(2)}) %collective-permute-start.26) | collective-permute-done | bytes 131104 | tf_op jit(solution)/shard_map/ppermute | solution.py:260
  221.8 3.0 %collective-permute-done.27 = f32[512,64]{0,1:T(8,128)S(1)} collective-permute-done((f32[512,64]{0,1:T(8,128)S(1)}, f32[512,64]{0,1:T(8,128)S(1)}, u32[]{:S(2)}, u32[]{:S(2)}) %collective-permute-start.27) | collective-permute-done | bytes 131104 | tf_op jit(solution)/shard_map/ppermute | solution.py:260
  224.9 2.2 collective-permute-start.29
  228.6 6.3 %collective-permute-done.29 = f32[512,64]{0,1:T(8,128)S(1)} collective-permute-done((f32[512,64]{0,1:T(8,128)S(1)}, f32[512,64]{0,1:T(8,128)S(1)}, u32[]{:S(2)}, u32[]{:S(2)}) %collective-permute-start.29) | collective-permute-done | bytes 131104 | tf_op jit(solution)/shard_map/ppermute | solution.py:265
  239.5 7.8 %collective-permute-done.33 = bf16[128,1280]{1,0:T(8,128)(2,1)S(1)} collective-permute-done((bf16[128,1280]{1,0:T(8,128)(2,1)}, bf16[128,1280]{1,0:T(8,128)(2,1)S(1)}, u32[]{:S(2)}, u32[]{:S(2)}) %collective-permute-start.33) | collective-permute-done | bytes 327712 | tf_op jit(solution)/shard_map/ppermute | solution.py:260
  247.3 7.1 %collective-permute-done.32 = bf16[128,1280]{1,0:T(8,128)(2,1)} collective-permute-done((bf16[128,1280]{1,0:T(8,128)(2,1)}, bf16[128,1280]{1,0:T(8,128)(2,1)}, u32[]{:S(2)}, u32[]{:S(2)}) %collective-permute-start.32) | collective-permute-done | bytes 327712 | tf_op jit(solution)/shard_map/ppermute | solution.py:260
  256.8 2.8 %collective-permute-start.34 = (bf16[128,1280]{1,0:T(8,128)(2,1)S(1)}, bf16[128,1280]{1,0:T(8,128)(2,1)S(1)}, u32[]{:S(2)}, u32[]{:S(2)}) collective-permute-start(bf16[128,1280]{1,0:T(8,128)(2,1)S(1)} %add_convert_fusion), channel_id=1, source_target_pairs={{0,0},{1,4},{2,8},{3,12},{4,1},{5,5},{6,9},{7,13},{8,2},{9,6},{10,... | collective-permute-start | bytes 983048 | tf_op jit(solution)/shard_map/ppermute | solution.py:265
  259.6 13.0 %collective-permute-done.34 = bf16[128,1280]{1,0:T(8,128)(2,1)S(1)} collective-permute-done((bf16[128,1280]{1,0:T(8,128)(2,1)S(1)}, bf16[128,1280]{1,0:T(8,128)(2,1)S(1)}, u32[]{:S(2)}, u32[]{:S(2)}) %collective-permute-start.34) | collective-permute-done | bytes 327712 | tf_op jit(solution)/shard_map/ppermute | solution.py:265
  (216 shorter events, 75.2 us)
Async XLA Ops:
  0.0 23.3 %collective-permute-start.6 = (bf16[2,1280,64]{1,2,0:T(8,128)(2,1)}, bf16[2,1280,64]{1,2,0:T(8,128)(2,1)}, u32[]{:S(2)}, u32[]{:S(2)}) collective-permute-start(bf16[2,1280,64]{1,2,0:T(8,128)(2,1)} %param.33), channel_id=1, source_target_pairs={{0,12},{4,0},{8,4},{12,8},{1,13},{5,1},{9,5},{13,9},{2,14},{6,2},{... | collective-permute-start | bytes 983048 | tf_op jit(solution)/shard_map/ppermute | solution.py:257
  3.6 28.2 %collective-permute-start.5 = (bf16[2,1280,64]{1,2,0:T(8,128)(2,1)}, bf16[2,1280,64]{1,2,0:T(8,128)(2,1)}, u32[]{:S(2)}, u32[]{:S(2)}) collective-permute-start(bf16[2,1280,64]{1,2,0:T(8,128)(2,1)} %param.33), channel_id=1, source_target_pairs={{0,8},{4,12},{8,0},{12,4},{1,9},{5,13},{9,1},{13,5},{2,10},{6,14},... | collective-permute-start | bytes 983048 | tf_op jit(solution)/shard_map/ppermute | solution.py:257
  3.6 29.5 %collective-permute-start.4 = (bf16[2,1280,64]{1,2,0:T(8,128)(2,1)}, bf16[2,1280,64]{1,2,0:T(8,128)(2,1)}, u32[]{:S(2)}, u32[]{:S(2)}) collective-permute-start(bf16[2,1280,64]{1,2,0:T(8,128)(2,1)} %param.33), channel_id=1, source_target_pairs={{0,4},{4,8},{8,12},{12,0},{1,5},{5,9},{9,13},{13,1},{2,6},{6,10},{... | collective-permute-start | bytes 983048 | tf_op jit(solution)/shard_map/ppermute | solution.py:257
  4.6 45.1 %collective-permute-start = (bf16[128,1280]{1,0:T(8,128)(2,1)}, bf16[128,1280]{1,0:T(8,128)(2,1)S(1)}, u32[]{:S(2)}, u32[]{:S(2)}) collective-permute-start(bf16[128,1280]{1,0:T(8,128)(2,1)} %param.19), channel_id=1, source_target_pairs={{0,0},{1,4},{2,8},{3,12},{4,1},{5,5},{6,9},{7,13},{8,2},{9,6},{10,... | collective-permute-start | bytes 983048 | tf_op jit(solution)/shard_map/ppermute | solution.py:265
  34.4 10.0 %collective-permute-start.9 = (f32[128,64]{0,1:T(8,128)S(1)}, f32[128,64]{0,1:T(8,128)S(1)}, u32[]{:S(2)}, u32[]{:S(2)}) collective-permute-start(f32[128,64]{0,1:T(8,128)S(1)} %add_add_fusion.1), channel_id=1, source_target_pairs={{0,3},{1,0},{2,1},{3,2},{4,7},{5,4},{6,5},{7,6},{8,11},{9,8},{10,9... | collective-permute-start | bytes 98312 | tf_op jit(solution)/shard_map/ppermute | solution.py:260
  40.6 5.7 %collective-permute-start.7 = (f32[128,64]{0,1:T(8,128)S(1)}, f32[128,64]{0,1:T(8,128)S(1)}, u32[]{:S(2)}, u32[]{:S(2)}) collective-permute-start(f32[128,64]{0,1:T(8,128)S(1)} %add_add_fusion.1), channel_id=1, source_target_pairs={{0,1},{1,2},{2,3},{3,0},{4,5},{5,6},{6,7},{7,4},{8,9},{9,10},{10,1... | collective-permute-start | bytes 98312 | tf_op jit(solution)/shard_map/ppermute | solution.py:260
  40.6 6.5 %collective-permute-start.8 = (f32[128,64]{0,1:T(8,128)S(1)}, f32[128,64]{0,1:T(8,128)S(1)}, u32[]{:S(2)}, u32[]{:S(2)}) collective-permute-start(f32[128,64]{0,1:T(8,128)S(1)} %add_add_fusion.1), channel_id=1, source_target_pairs={{0,2},{1,3},{2,0},{3,1},{4,6},{5,7},{6,4},{7,5},{8,10},{9,11},{10,... | collective-permute-start | bytes 98312 | tf_op jit(solution)/shard_map/ppermute | solution.py:260
  47.1 6.2 %collective-permute-start.10 = (bf16[128,64]{0,1:T(8,128)(2,1)S(1)}, bf16[128,64]{0,1:T(8,128)(2,1)S(1)}, u32[]{:S(2)}, u32[]{:S(2)}) collective-permute-start(bf16[128,64]{0,1:T(8,128)(2,1)S(1)} %add_convert_fusion.1), channel_id=1, source_target_pairs={{0,12},{4,0},{8,4},{12,8},{1,13},{5,1},{9,5},{13,9},{2,14},{6,2},{... | collective-permute-start | bytes 49160 | tf_op jit(solution)/shard_map/ppermute | solution.py:257
  49.7 10.8 %collective-permute-start.1 = (bf16[128,1280]{1,0:T(8,128)(2,1)S(1)}, bf16[128,1280]{1,0:T(8,128)(2,1)S(1)}, u32[]{:S(2)}, u32[]{:S(2)}) collective-permute-start(bf16[128,1280]{1,0:T(8,128)(2,1)S(1)} %collective-permute-done), channel_id=1, source_target_pairs={{0,3},{1,0},{2,1},{3,2},{4,7},{5,4},{6,5},{7,6},{8,11},{9,8},{10,9... | collective-permute-start | bytes 983048 | tf_op jit(solution)/shard_map/ppermute | solution.py:260
  49.7 17.1 %collective-permute-start.2 = (bf16[128,1280]{1,0:T(8,128)(2,1)S(1)}, bf16[128,1280]{1,0:T(8,128)(2,1)S(1)}, u32[]{:S(2)}, u32[]{:S(2)}) collective-permute-start(bf16[128,1280]{1,0:T(8,128)(2,1)S(1)} %collective-permute-done), channel_id=1, source_target_pairs={{0,2},{1,3},{2,0},{3,1},{4,6},{5,7},{6,4},{7,5},{8,10},{9,11},{10,... | collective-permute-start | bytes 983048 | tf_op jit(solution)/shard_map/ppermute | solution.py:260
  51.3 15.5 %collective-permute-start.3 = (bf16[128,1280]{1,0:T(8,128)(2,1)S(1)}, bf16[128,1280]{1,0:T(8,128)(2,1)S(1)}, u32[]{:S(2)}, u32[]{:S(2)}) collective-permute-start(bf16[128,1280]{1,0:T(8,128)(2,1)S(1)} %collective-permute-done), channel_id=1, source_target_pairs={{0,1},{1,2},{2,3},{3,0},{4,5},{5,6},{6,7},{7,4},{8,9},{9,10},{10,1... | collective-permute-start | bytes 983048 | tf_op jit(solution)/shard_map/ppermute | solution.py:260
  51.3 4.8 %collective-permute-start.11 = (bf16[128,64]{0,1:T(8,128)(2,1)S(1)}, bf16[128,64]{0,1:T(8,128)(2,1)S(1)}, u32[]{:S(2)}, u32[]{:S(2)}) collective-permute-start(bf16[128,64]{0,1:T(8,128)(2,1)S(1)} %add_convert_fusion.1), channel_id=1, source_target_pairs={{0,8},{4,12},{8,0},{12,4},{1,9},{5,13},{9,1},{13,5},{2,10},{6,14},... | collective-permute-start | bytes 49160 | tf_op jit(solution)/shard_map/ppermute | solution.py:257
  53.4 5.5 %collective-permute-start.12 = (bf16[128,64]{0,1:T(8,128)(2,1)S(1)}, bf16[128,64]{0,1:T(8,128)(2,1)S(1)}, u32[]{:S(2)}, u32[]{:S(2)}) collective-permute-start(bf16[128,64]{0,1:T(8,128)(2,1)S(1)} %add_convert_fusion.1), channel_id=1, source_target_pairs={{0,4},{4,8},{8,12},{12,0},{1,5},{5,9},{9,13},{13,1},{2,6},{6,10},{... | collective-permute-start | bytes 49160 | tf_op jit(solution)/shard_map/ppermute | solution.py:257
  71.1 10.8 %collective-permute-start.15 = (bf16[128,1168]{0,1:T(8,128)(2,1)S(1)}, bf16[128,1168]{0,1:T(8,128)(2,1)S(1)}, u32[]{:S(2)}, u32[]{:S(2)}) collective-permute-start(bf16[128,1168]{0,1:T(8,128)(2,1)S(1)} %get-tuple-element.19), channel_id=1, source_target_pairs={{0,12},{4,0},{8,4},{12,8},{1,13},{5,1},{9,5},{13,9},{2,14},{6,2},{... | collective-permute-start | bytes 897032 | tf_op jit(solution)/shard_map/ppermute | solution.py:257
  74.2 24.6 %collective-permute-start.14 = (bf16[128,1168]{0,1:T(8,128)(2,1)S(1)}, bf16[128,1168]{0,1:T(8,128)(2,1)S(1)}, u32[]{:S(2)}, u32[]{:S(2)}) collective-permute-start(bf16[128,1168]{0,1:T(8,128)(2,1)S(1)} %get-tuple-element.20), channel_id=1, source_target_pairs={{0,8},{4,12},{8,0},{12,4},{1,9},{5,13},{9,1},{13,5},{2,10},{6,14},... | collective-permute-start | bytes 897032 | tf_op jit(solution)/shard_map/ppermute | solution.py:257
  74.3 24.5 %collective-permute-start.13 = (bf16[128,1168]{0,1:T(8,128)(2,1)S(1)}, bf16[128,1168]{0,1:T(8,128)(2,1)S(1)}, u32[]{:S(2)}, u32[]{:S(2)}) collective-permute-start(bf16[128,1168]{0,1:T(8,128)(2,1)S(1)} %get-tuple-element.18), channel_id=1, source_target_pairs={{0,4},{4,8},{8,12},{12,0},{1,5},{5,9},{9,13},{13,1},{2,6},{6,10},{... | collective-permute-start | bytes 897032 | tf_op jit(solution)/shard_map/ppermute | solution.py:257
  101.7 4.7 %collective-permute-start.16 = (f32[3,1152]{1,0:T(4,128)S(1)}, f32[3,1152]{1,0:T(4,128)S(1)}, u32[]{:S(2)}, u32[]{:S(2)}) collective-permute-start(f32[3,1152]{1,0:T(4,128)S(1)} %copy.111), channel_id=1, source_target_pairs={{0,4},{4,8},{8,12},{1,5},{5,9},{9,13},{2,6},{6,10},{10,14},{3,7},{... | collective-permute-start | bytes 41480 | tf_op jit(solution)/shard_map/ppermute | solution.py:18
  117.6 18.8 %collective-permute-start.21 = (bf16[16,65,256]{2,0,1:T(8,128)(2,1)}, bf16[16,65,256]{2,0,1:T(8,128)(2,1)}, u32[]{:S(2)}, u32[]{:S(2)}) collective-permute-start(bf16[16,65,256]{2,0,1:T(8,128)(2,1)} %copy.118), channel_id=1, source_target_pairs={{0,8},{4,12},{1,9},{5,13},{2,10},{6,14},{3,11},{7,15},{16,24},{20,... | collective-permute-start | bytes 1597448 | tf_op jit(solution)/shard_map/ppermute | solution.py:407
  124.4 23.5 %collective-permute-start.22 = (bf16[16,65,256]{2,0,1:T(8,128)(2,1)}, bf16[16,65,256]{2,0,1:T(8,128)(2,1)}, u32[]{:S(2)}, u32[]{:S(2)}) collective-permute-start(bf16[16,65,256]{2,0,1:T(8,128)(2,1)} %copy.118), channel_id=1, source_target_pairs={{0,12},{1,13},{2,14},{3,15},{16,28},{17,29},{18,30},{19,31}} | collective-permute-start | bytes 1597448 | tf_op jit(solution)/shard_map/ppermute | solution.py:407
  127.3 30.1 %collective-permute-start.20 = (bf16[16,65,256]{2,0,1:T(8,128)(2,1)}, bf16[16,65,256]{2,0,1:T(8,128)(2,1)S(1)}, u32[]{:S(2)}, u32[]{:S(2)}) collective-permute-start(bf16[16,65,256]{2,0,1:T(8,128)(2,1)} %copy.118), channel_id=1, source_target_pairs={{0,4},{4,8},{8,12},{1,5},{5,9},{9,13},{2,6},{6,10},{10,14},{3,7},{... | collective-permute-start | bytes 1597448 | tf_op jit(solution)/shard_map/ppermute | solution.py:407
  160.9 22.8 %collective-permute-start.23 = (bf16[128,1024]{0,1:T(8,128)(2,1)}, bf16[128,1024]{0,1:T(8,128)(2,1)S(1)}, u32[]{:S(2)}, u32[]{:S(2)}) collective-permute-start(bf16[128,1024]{0,1:T(8,128)(2,1)} %fusion.26), channel_id=1, source_target_pairs={{0,12},{4,0},{8,4},{12,8},{1,13},{5,1},{9,5},{13,9},{2,14},{6,2},{... | collective-permute-start | bytes 786440 | tf_op jit(solution)/shard_map/ppermute | solution.py:257
  167.9 31.1 %collective-permute-start.24 = (bf16[128,1024]{0,1:T(8,128)(2,1)}, bf16[128,1024]{0,1:T(8,128)(2,1)}, u32[]{:S(2)}, u32[]{:S(2)}) collective-permute-start(bf16[128,1024]{0,1:T(8,128)(2,1)} %fusion.26), channel_id=1, source_target_pairs={{0,8},{4,12},{8,0},{12,4},{1,9},{5,13},{9,1},{13,5},{2,10},{6,14},... | collective-permute-start | bytes 786440 | tf_op jit(solution)/shard_map/ppermute | solution.py:257
  179.7 55.3 %collective-permute-start.30 = (bf16[2,64,1280]{2,1,0:T(8,128)(2,1)}, bf16[2,64,1280]{2,1,0:T(8,128)(2,1)}, u32[]{:S(2)}, u32[]{:S(2)}) collective-permute-start(bf16[2,64,1280]{2,1,0:T(8,128)(2,1)} %param.37), channel_id=1, source_target_pairs={{0,0},{1,4},{2,8},{3,12},{4,1},{5,5},{6,9},{7,13},{8,2},{9,6},{10,... | collective-permute-start | bytes 983048 | tf_op jit(solution)/shard_map/ppermute | solution.py:265
  181.7 18.3 %collective-permute-start.25 = (bf16[128,1024]{0,1:T(8,128)(2,1)}, bf16[128,1024]{0,1:T(8,128)(2,1)S(1)}, u32[]{:S(2)}, u32[]{:S(2)}) collective-permute-start(bf16[128,1024]{0,1:T(8,128)(2,1)} %fusion.26), channel_id=1, source_target_pairs={{0,4},{4,8},{8,12},{12,0},{1,5},{5,9},{9,13},{13,1},{2,6},{6,10},{... | collective-permute-start | bytes 786440 | tf_op jit(solution)/shard_map/ppermute | solution.py:257
  206.6 11.7 %collective-permute-start.28 = (f32[512,64]{0,1:T(8,128)S(1)}, f32[512,64]{0,1:T(8,128)S(1)}, u32[]{:S(2)}, u32[]{:S(2)}) collective-permute-start(f32[512,64]{0,1:T(8,128)S(1)} %multiply_reduce_fusion.1), channel_id=1, source_target_pairs={{0,3},{1,0},{2,1},{3,2},{4,7},{5,4},{6,5},{7,6},{8,11},{9,8},{10,9... | collective-permute-start | bytes 393224 | tf_op jit(solution)/shard_map/ppermute | solution.py:260
  209.6 12.2 %collective-permute-start.26 = (f32[512,64]{0,1:T(8,128)S(1)}, f32[512,64]{0,1:T(8,128)S(1)}, u32[]{:S(2)}, u32[]{:S(2)}) collective-permute-start(f32[512,64]{0,1:T(8,128)S(1)} %multiply_reduce_fusion.1), channel_id=1, source_target_pairs={{0,1},{1,2},{2,3},{3,0},{4,5},{5,6},{6,7},{7,4},{8,9},{9,10},{10,1... | collective-permute-start | bytes 393224 | tf_op jit(solution)/shard_map/ppermute | solution.py:260
  209.6 15.2 %collective-permute-start.27 = (f32[512,64]{0,1:T(8,128)S(1)}, f32[512,64]{0,1:T(8,128)S(1)}, u32[]{:S(2)}, u32[]{:S(2)}) collective-permute-start(f32[512,64]{0,1:T(8,128)S(1)} %multiply_reduce_fusion.1), channel_id=1, source_target_pairs={{0,2},{1,3},{2,0},{3,1},{4,6},{5,7},{6,4},{7,5},{8,10},{9,11},{10,... | collective-permute-start | bytes 393224 | tf_op jit(solution)/shard_map/ppermute | solution.py:260
  224.9 10.1 %collective-permute-start.29 = (f32[512,64]{0,1:T(8,128)S(1)}, f32[512,64]{0,1:T(8,128)S(1)}, u32[]{:S(2)}, u32[]{:S(2)}) collective-permute-start(f32[512,64]{0,1:T(8,128)S(1)} %add_add_fusion), channel_id=1, source_target_pairs={{0,0},{1,4},{2,8},{3,12},{4,1},{5,5},{6,9},{7,13},{8,2},{9,6},{10,... | collective-permute-start | bytes 393224 | tf_op jit(solution)/shard_map/ppermute | solution.py:265
  238.9 8.4 %collective-permute-start.33 = (bf16[128,1280]{1,0:T(8,128)(2,1)}, bf16[128,1280]{1,0:T(8,128)(2,1)S(1)}, u32[]{:S(2)}, u32[]{:S(2)}) collective-permute-start(bf16[128,1280]{1,0:T(8,128)(2,1)} %get-tuple-element.16), channel_id=1, source_target_pairs={{0,3},{1,0},{2,1},{3,2},{4,7},{5,4},{6,5},{7,6},{8,11},{9,8},{10,9... | collective-permute-start | bytes 983048 | tf_op jit(solution)/shard_map/ppermute | solution.py:260
  238.9 15.5 %collective-permute-start.32 = (bf16[128,1280]{1,0:T(8,128)(2,1)}, bf16[128,1280]{1,0:T(8,128)(2,1)}, u32[]{:S(2)}, u32[]{:S(2)}) collective-permute-start(bf16[128,1280]{1,0:T(8,128)(2,1)} %get-tuple-element.17), channel_id=1, source_target_pairs={{0,2},{1,3},{2,0},{3,1},{4,6},{5,7},{6,4},{7,5},{8,10},{9,11},{10,... | collective-permute-start | bytes 983048 | tf_op jit(solution)/shard_map/ppermute | solution.py:260
  239.5 15.9 %collective-permute-start.31 = (bf16[128,1280]{1,0:T(8,128)(2,1)S(1)}, bf16[128,1280]{1,0:T(8,128)(2,1)}, u32[]{:S(2)}, u32[]{:S(2)}) collective-permute-start(bf16[128,1280]{1,0:T(8,128)(2,1)S(1)} %get-tuple-element.15), channel_id=1, source_target_pairs={{0,1},{1,2},{2,3},{3,0},{4,5},{5,6},{6,7},{7,4},{8,9},{9,10},{10,1... | collective-permute-start | bytes 983048 | tf_op jit(solution)/shard_map/ppermute | solution.py:260
  256.8 15.7 %collective-permute-start.34 = (bf16[128,1280]{1,0:T(8,128)(2,1)S(1)}, bf16[128,1280]{1,0:T(8,128)(2,1)S(1)}, u32[]{:S(2)}, u32[]{:S(2)}) collective-permute-start(bf16[128,1280]{1,0:T(8,128)(2,1)S(1)} %add_convert_fusion), channel_id=1, source_target_pairs={{0,0},{1,4},{2,8},{3,12},{4,1},{5,5},{6,9},{7,13},{8,2},{9,6},{10,... | collective-permute-start | bytes 983048 | tf_op jit(solution)/shard_map/ppermute | solution.py:265
  (29 other events, 552.2 us)

commit v10 on v9

--- a/solution.py
+++ b/solution.py
@@ -416,21 +416,29 @@
     scale = lax.rsqrt(jnp.mean(mixer_out * mixer_out, axis=1, keepdims=True) + NORM_EPSILON)
     normalized_rows = (mixer_out * scale * output_norm_gain[None, :]).astype(jnp.bfloat16)
 
+    out_pick = jnp.zeros((length, rank_value), jnp.float32)
+    for s in range(side):
+        piece = adapter_down_output if s == 0 else moved(adapter_down_output, s, "ctx")
+        first = ((here - s) % side) * bank_entries
+        every = jnp.einsum(
+            "pf,efr->per", normalized_rows, piece, preferred_element_type=jnp.float32
+        )
+        chosen = local_owned[:, None] == first + jnp.arange(bank_entries, dtype=jnp.int32)[None, :]
+        out_pick = out_pick + jnp.sum(every * chosen[:, :, None].astype(jnp.float32), axis=1)
+    out_local = (
+        out_pick + sum(moved(out_pick, s, "lane") for s in range(1, side))
+    ).astype(jnp.bfloat16)
+    rank_hidden_output = in_order(
+        [out_local] + [moved(out_local, s, "ctx") for s in range(1, side)], here
+    )
     normed_stream = in_order(
         [normalized_rows] + [moved(normalized_rows, s, "ctx") for s in range(1, side)], here
-    )
-    out_down_part = jnp.einsum(
-        "pc,ecr->per", normed_stream, adapter_down_output, preferred_element_type=jnp.float32
-    )
-    out_down_pick = jnp.sum(out_down_part * owned_here[:, :, None].astype(jnp.float32), axis=1)
-    rank_hidden_output = transposed(
-        out_down_pick + sum(moved(out_down_pick, s, "lane") for s in range(1, side))
     )
     base_part = jnp.dot(
         normed_stream, output_weight, preferred_element_type=jnp.float32
     ).astype(jnp.bfloat16).astype(jnp.float32)
     adapter_part = jnp.dot(
-        owned_rows(rank_hidden_output, owned_lane).astype(jnp.bfloat16),
+        owned_rows(rank_hidden_output, owned_lane),
         up_out_t.reshape(bank_entries * rank_value, -1),
         preferred_element_type=jnp.float32,
     )

time: 275 us -> 276 us (level)
  waiting for transfers between devices: 128 us -> 94.3 us
  starting transfers between devices: 81.5 us -> 112 us
  matrix products: 18.7 us -> 21.6 us
    ppermute x12 -> x18, starting transfers between devices: 33.3 us -> 57.3 us  [moved(): return lax.ppermute(block, 'ctx', pairs)]
    ppermute x3, waiting for transfers between devices: 23.6 us -> 6 us  [square_body(): both_in = lax.ppermute(state_and_decay, 'ctx', pairs).astype(jnp.float32)]
    ppermute x4 -> x3, starting transfers between devices: 10.7 us -> 22.4 us  [moved(): return lax.ppermute(block, ('ctx', 'tp', 'dp'), pairs)]
    ppermute x12 -> x18, waiting for transfers between devices: 49.8 us -> 39.2 us  [moved(): return lax.ppermute(block, 'ctx', pairs)]
    ppermute x4 -> x3, waiting for transfers between devices: 19.3 us -> 14 us  [moved(): return lax.ppermute(block, ('ctx', 'tp', 'dp'), pairs)]
    ppermute x15, starting transfers between devices: 23.9 us -> 20.6 us  [moved(): return lax.ppermute(block, ('tp', 'dp'), pairs)]
    unnamed x5 -> x8, matrix products: 7.48 us -> 10.4 us
    unnamed x81 -> x86, local copies, waits for them, and re-layouts: 7.28 us -> 7.19 us
  transfers between devices with their start and end apart: 35 -> 40, of which waited for: 21 -> 19; matrix products, arithmetic and copies ran while one was open for 14% -> 20% of each run, Pallas kernels for 0% -> 0%
where the time goes in v10:
time: 276 us; the launch traced here: 275 us
  starting transfers between devices  112 us (41%)
  waiting for transfers between devices  94.3 us (34%)
  other arithmetic  23.5 us (9%)
  matrix products  21.6 us (8%)
  local copies, waits for them, and re-layouts  21.2 us (8%)
    ppermute x18, starting transfers between devices, moved(): return lax.ppermute(block, 'ctx', pairs)  57.3 us
    ppermute x18, waiting for transfers between devices, moved(): return lax.ppermute(block, 'ctx', pairs)  39.2 us
    ppermute x15, waiting for transfers between devices, moved(): return lax.ppermute(block, ('tp', 'dp'), pairs)  34.6 us
    ppermute x3, starting transfers between devices, moved(): return lax.ppermute(block, ('ctx', 'tp', 'dp'), pairs)  22.4 us
    ppermute x15, starting transfers between devices, moved(): return lax.ppermute(block, ('tp', 'dp'), pairs)  20.6 us
    ppermute x3, waiting for transfers between devices, moved(): return lax.ppermute(block, ('ctx', 'tp', 'dp'), pairs)  14 us
    unnamed x8, matrix products  10.4 us
    ppermute x3, starting transfers between devices, square_body(): both_in = lax.ppermute(state_and_decay, 'ctx', pairs).astype(jnp.float32)  10.4 us
  transfers between devices with their start and end apart: 40, of which 19 were waited for; matrix products, arithmetic and copies ran while one was open for 20% of the time, Pallas kernels for 0%

profile of v10, /device:TPU:2, one launch (start us, length us, event | category | flops | bytes accessed | tf_op | source)
XLA Modules:
  0.0 274.8 jit_solution(11220583763410915383)
XLA Ops:
  0.0 3.6 %collective-permute-start.6 = (bf16[2,1280,64]{1,2,0:T(8,128)(2,1)}, bf16[2,1280,64]{1,2,0:T(8,128)(2,1)}, u32[]{:S(2)}, u32[]{:S(2)}) collective-permute-start(bf16[2,1280,64]{1,2,0:T(8,128)(2,1)} %param.35), channel_id=1, source_target_pairs={{0,12},{4,0},{8,4},{12,8},{1,13},{5,1},{9,5},{13,9},{2,14},{6,2},{... | collective-permute-start | bytes 983048 | tf_op jit(solution)/shard_map/ppermute | solution.py:257
  4.6 3.8 %collective-permute-start = (bf16[128,1280]{1,0:T(8,128)(2,1)}, bf16[128,1280]{1,0:T(8,128)(2,1)S(1)}, u32[]{:S(2)}, u32[]{:S(2)}) collective-permute-start(bf16[128,1280]{1,0:T(8,128)(2,1)} %param.21), channel_id=1, source_target_pairs={{0,0},{1,4},{2,8},{3,12},{4,1},{5,5},{6,9},{7,13},{8,2},{9,6},{10,... | collective-permute-start | bytes 983048 | tf_op jit(solution)/shard_map/ppermute | solution.py:265
  14.8 2.0 fusion.72
  23.6 2.1 compare_convert_fusion.6
  27.6 5.4 %collective-permute-done.5 = bf16[2,1280,64]{1,2,0:T(8,128)(2,1)} collective-permute-done((bf16[2,1280,64]{1,2,0:T(8,128)(2,1)}, bf16[2,1280,64]{1,2,0:T(8,128)(2,1)}, u32[]{:S(2)}, u32[]{:S(2)}) %collective-permute-start.5) | collective-permute-done | bytes 327712 | tf_op jit(solution)/shard_map/ppermute | solution.py:257
  35.5 5.1 %collective-permute-start.9 = (f32[128,64]{0,1:T(8,128)S(1)}, f32[128,64]{0,1:T(8,128)S(1)}, u32[]{:S(2)}, u32[]{:S(2)}) collective-permute-start(f32[128,64]{0,1:T(8,128)S(1)} %add_add_fusion.1), channel_id=1, source_target_pairs={{0,3},{1,0},{2,1},{3,2},{4,7},{5,4},{6,5},{7,6},{8,11},{9,8},{10,9... | collective-permute-start | bytes 98312 | tf_op jit(solution)/shard_map/ppermute | solution.py:260
  40.6 3.1 %collective-permute-start.8 = (f32[128,64]{0,1:T(8,128)S(1)}, f32[128,64]{0,1:T(8,128)S(1)}, u32[]{:S(2)}, u32[]{:S(2)}) collective-permute-start(f32[128,64]{0,1:T(8,128)S(1)} %add_add_fusion.1), channel_id=1, source_target_pairs={{0,2},{1,3},{2,0},{3,1},{4,6},{5,7},{6,4},{7,5},{8,10},{9,11},{10,... | collective-permute-start | bytes 98312 | tf_op jit(solution)/shard_map/ppermute | solution.py:260
  47.1 2.0 collective-permute-start.10
  49.2 5.0 %collective-permute-start.11 = (bf16[128,64]{0,1:T(8,128)(2,1)S(1)}, bf16[128,64]{0,1:T(8,128)(2,1)S(1)}, u32[]{:S(2)}, u32[]{:S(2)}) collective-permute-start(bf16[128,64]{0,1:T(8,128)(2,1)S(1)} %add_convert_fusion.2), channel_id=1, source_target_pairs={{0,8},{4,12},{8,0},{12,4},{1,9},{5,13},{9,1},{13,5},{2,10},{6,14},... | collective-permute-start | bytes 49160 | tf_op jit(solution)/shard_map/ppermute | solution.py:257
  62.6 4.8 %collective-permute-done.1 = bf16[128,1280]{1,0:T(8,128)(2,1)S(1)} collective-permute-done((bf16[128,1280]{1,0:T(8,128)(2,1)S(1)}, bf16[128,1280]{1,0:T(8,128)(2,1)S(1)}, u32[]{:S(2)}, u32[]{:S(2)}) %collective-permute-start.1) | collective-permute-done | bytes 327712 | tf_op jit(solution)/shard_map/ppermute | solution.py:260
  67.4 8.0 %collective-permute-done.2 = bf16[128,1280]{1,0:T(8,128)(2,1)S(1)} collective-permute-done((bf16[128,1280]{1,0:T(8,128)(2,1)S(1)}, bf16[128,1280]{1,0:T(8,128)(2,1)S(1)}, u32[]{:S(2)}, u32[]{:S(2)}) %collective-permute-start.2) | collective-permute-done | bytes 327712 | tf_op jit(solution)/shard_map/ppermute | solution.py:260
  79.8 2.4 collective-permute-start.15
  85.5 4.3 %collective-permute-done.15 = bf16[128,1168]{0,1:T(8,128)(2,1)S(1)} collective-permute-done((bf16[128,1168]{0,1:T(8,128)(2,1)S(1)}, bf16[128,1168]{0,1:T(8,128)(2,1)S(1)}, u32[]{:S(2)}, u32[]{:S(2)}) %collective-permute-start.15) | collective-permute-done | bytes 299040 | tf_op jit(solution)/shard_map/ppermute | solution.py:257
  89.8 19.2 %collective-permute-done.14 = bf16[128,1168]{0,1:T(8,128)(2,1)S(1)} collective-permute-done((bf16[128,1168]{0,1:T(8,128)(2,1)S(1)}, bf16[128,1168]{0,1:T(8,128)(2,1)S(1)}, u32[]{:S(2)}, u32[]{:S(2)}) %collective-permute-start.14) | collective-permute-done | bytes 299040 | tf_op jit(solution)/shard_map/ppermute | solution.py:257
  115.1 3.3 %divide_multiply_fusion = f32[128,1152]{0,1:T(8,128)S(1)} fusion(f32[128,1152]{0,1:T(8,128)} %slice.129, f32[3,1152]{0,1:T(8,128)S(1)} %copy.121, f32[128]{0:T(128)S(1)} %copy-done.25, f32[1152]{0:T(1024)S(1)} %get-tuple-element.7, f32[128]{0:T(128)S(1)} %copy-done.26, f32[1152]{0:T(1024)S(1)} %get-tuple-element.8, f32[128]{0:T(128)S(1)} %copy-done.27, ...), kind=kLoop, calls=%fused_computation.49 | loop fusion | flops 2654208 | bytes 1213952 | tf_op jit(solution)/shard_map/jit(silu)/mul | solution.py:388
  120.0 2.5 collective-permute-done.18
  126.4 6.9 %collective-permute-start.21 = (bf16[16,65,256]{2,0,1:T(8,128)(2,1)}, bf16[16,65,256]{2,0,1:T(8,128)(2,1)}, u32[]{:S(2)}, u32[]{:S(2)}) collective-permute-start(bf16[16,65,256]{2,0,1:T(8,128)(2,1)} %copy.127), channel_id=1, source_target_pairs={{0,8},{4,12},{1,9},{5,13},{2,10},{6,14},{3,11},{7,15},{16,24},{20,... | collective-permute-start | bytes 1597448 | tf_op jit(solution)/shard_map/ppermute | solution.py:407
  133.4 2.1 collective-permute-start.22
  137.2 2.2 convolution_bitcast_fusion
  139.4 6.0 %collective-permute-done.21 = bf16[16,65,256]{2,0,1:T(8,128)(2,1)} collective-permute-done((bf16[16,65,256]{2,0,1:T(8,128)(2,1)}, bf16[16,65,256]{2,0,1:T(8,128)(2,1)}, u32[]{:S(2)}, u32[]{:S(2)}) %collective-permute-start.21) | collective-permute-done | bytes 532512 | tf_op jit(solution)/shard_map/ppermute | solution.py:407
  145.4 22.5 %collective-permute-start.26 = (bf16[2,1024,64]{1,2,0:T(8,128)(2,1)}, bf16[2,1024,64]{1,2,0:T(8,128)(2,1)}, u32[]{:S(2)}, u32[]{:S(2)}) collective-permute-start(bf16[2,1024,64]{1,2,0:T(8,128)(2,1)} %param.38), channel_id=1, source_target_pairs={{0,4},{4,8},{8,12},{12,0},{1,5},{5,9},{9,13},{13,1},{2,6},{6,10},{... | collective-permute-start | bytes 786440 | tf_op jit(solution)/shard_map/ppermute | solution.py:257
  181.3 13.3 %collective-permute-start.35 = (bf16[2,64,1280]{2,1,0:T(8,128)(2,1)}, bf16[2,64,1280]{2,1,0:T(8,128)(2,1)}, u32[]{:S(2)}, u32[]{:S(2)}) collective-permute-start(bf16[2,64,1280]{2,1,0:T(8,128)(2,1)} %param.39), channel_id=1, source_target_pairs={{0,0},{1,4},{2,8},{3,12},{4,1},{5,5},{6,9},{7,13},{8,2},{9,6},{10,... | collective-permute-start | bytes 983048 | tf_op jit(solution)/shard_map/ppermute | solution.py:265
  199.5 3.8 %collective-permute-done.32 = bf16[128,64]{0,1:T(8,128)(2,1)S(1)} collective-permute-done((bf16[128,64]{0,1:T(8,128)(2,1)S(1)}, bf16[128,64]{0,1:T(8,128)(2,1)S(1)}, u32[]{:S(2)}, u32[]{:S(2)}) %collective-permute-start.32) | collective-permute-done | bytes 16416 | tf_op jit(solution)/shard_map/ppermute | solution.py:257
  203.3 6.6 %collective-permute-start.24 = (bf16[128,1024]{1,0:T(8,128)(2,1)S(1)}, bf16[128,1024]{1,0:T(8,128)(2,1)S(1)}, u32[]{:S(2)}, u32[]{:S(2)}) collective-permute-start(bf16[128,1024]{1,0:T(8,128)(2,1)S(1)} %multiply_convert_fusion.1), channel_id=1, source_target_pairs={{0,8},{4,12},{8,0},{12,4},{1,9},{5,13},{9,1},{13,5},{2,10},{6,14},... | collective-permute-start | bytes 786440 | tf_op jit(solution)/shard_map/ppermute | solution.py:257
  209.9 5.0 %collective-permute-start.25 = (bf16[128,1024]{1,0:T(8,128)(2,1)S(1)}, bf16[128,1024]{1,0:T(8,128)(2,1)S(1)}, u32[]{:S(2)}, u32[]{:S(2)}) collective-permute-start(bf16[128,1024]{1,0:T(8,128)(2,1)S(1)} %multiply_convert_fusion.1), channel_id=1, source_target_pairs={{0,4},{4,8},{8,12},{12,0},{1,5},{5,9},{9,13},{13,1},{2,6},{6,10},{... | collective-permute-start | bytes 786440 | tf_op jit(solution)/shard_map/ppermute | solution.py:257
  215.9 2.9 %collective-permute-done.24 = bf16[128,1024]{1,0:T(8,128)(2,1)S(1)} collective-permute-done((bf16[128,1024]{1,0:T(8,128)(2,1)S(1)}, bf16[128,1024]{1,0:T(8,128)(2,1)S(1)}, u32[]{:S(2)}, u32[]{:S(2)}) %collective-permute-start.24) | collective-permute-done | bytes 262176 | tf_op jit(solution)/shard_map/ppermute | solution.py:257
  218.8 3.7 %collective-permute-done.25 = bf16[128,1024]{1,0:T(8,128)(2,1)S(1)} collective-permute-done((bf16[128,1024]{1,0:T(8,128)(2,1)S(1)}, bf16[128,1024]{1,0:T(8,128)(2,1)S(1)}, u32[]{:S(2)}, u32[]{:S(2)}) %collective-permute-start.25) | collective-permute-done | bytes 262176 | tf_op jit(solution)/shard_map/ppermute | solution.py:257
  229.4 6.8 %collective-permute-start.38 = (bf16[128,1280]{1,0:T(8,128)(2,1)}, bf16[128,1280]{1,0:T(8,128)(2,1)S(1)}, u32[]{:S(2)}, u32[]{:S(2)}) collective-permute-start(bf16[128,1280]{1,0:T(8,128)(2,1)} %get-tuple-element.17), channel_id=1, source_target_pairs={{0,3},{1,0},{2,1},{3,2},{4,7},{5,4},{6,5},{7,6},{8,11},{9,8},{10,9... | collective-permute-start | bytes 983048 | tf_op jit(solution)/shard_map/ppermute | solution.py:260
  237.9 5.8 %collective-permute-done.38 = bf16[128,1280]{1,0:T(8,128)(2,1)S(1)} collective-permute-done((bf16[128,1280]{1,0:T(8,128)(2,1)}, bf16[128,1280]{1,0:T(8,128)(2,1)S(1)}, u32[]{:S(2)}, u32[]{:S(2)}) %collective-permute-start.38) | collective-permute-done | bytes 327712 | tf_op jit(solution)/shard_map/ppermute | solution.py:260
  243.7 9.7 %collective-permute-done.37 = bf16[128,1280]{1,0:T(8,128)(2,1)} collective-permute-done((bf16[128,1280]{1,0:T(8,128)(2,1)}, bf16[128,1280]{1,0:T(8,128)(2,1)}, u32[]{:S(2)}, u32[]{:S(2)}) %collective-permute-start.37) | collective-permute-done | bytes 327712 | tf_op jit(solution)/shard_map/ppermute | solution.py:260
  254.8 5.3 %collective-permute-start.39 = (bf16[128,1280]{1,0:T(8,128)(2,1)S(1)}, bf16[128,1280]{1,0:T(8,128)(2,1)S(1)}, u32[]{:S(2)}, u32[]{:S(2)}) collective-permute-start(bf16[128,1280]{1,0:T(8,128)(2,1)S(1)} %add_convert_fusion), channel_id=1, source_target_pairs={{0,0},{1,4},{2,8},{3,12},{4,1},{5,5},{6,9},{7,13},{8,2},{9,6},{10,... | collective-permute-start | bytes 983048 | tf_op jit(solution)/shard_map/ppermute | solution.py:265
  260.1 14.0 %collective-permute-done.39 = bf16[128,1280]{1,0:T(8,128)(2,1)S(1)} collective-permute-done((bf16[128,1280]{1,0:T(8,128)(2,1)S(1)}, bf16[128,1280]{1,0:T(8,128)(2,1)S(1)}, u32[]{:S(2)}, u32[]{:S(2)}) %collective-permute-start.39) | collective-permute-done | bytes 327712 | tf_op jit(solution)/shard_map/ppermute | solution.py:265
  (239 shorter events, 79.8 us)
Async XLA Ops:
  0.0 26.3 %collective-permute-start.6 = (bf16[2,1280,64]{1,2,0:T(8,128)(2,1)}, bf16[2,1280,64]{1,2,0:T(8,128)(2,1)}, u32[]{:S(2)}, u32[]{:S(2)}) collective-permute-start(bf16[2,1280,64]{1,2,0:T(8,128)(2,1)} %param.35), channel_id=1, source_target_pairs={{0,12},{4,0},{8,4},{12,8},{1,13},{5,1},{9,5},{13,9},{2,14},{6,2},{... | collective-permute-start | bytes 983048 | tf_op jit(solution)/shard_map/ppermute | solution.py:257
  3.6 29.4 %collective-permute-start.5 = (bf16[2,1280,64]{1,2,0:T(8,128)(2,1)}, bf16[2,1280,64]{1,2,0:T(8,128)(2,1)}, u32[]{:S(2)}, u32[]{:S(2)}) collective-permute-start(bf16[2,1280,64]{1,2,0:T(8,128)(2,1)} %param.35), channel_id=1, source_target_pairs={{0,8},{4,12},{8,0},{12,4},{1,9},{5,13},{9,1},{13,5},{2,10},{6,14},... | collective-permute-start | bytes 983048 | tf_op jit(solution)/shard_map/ppermute | solution.py:257
  3.6 30.6 %collective-permute-start.4 = (bf16[2,1280,64]{1,2,0:T(8,128)(2,1)}, bf16[2,1280,64]{1,2,0:T(8,128)(2,1)}, u32[]{:S(2)}, u32[]{:S(2)}) collective-permute-start(bf16[2,1280,64]{1,2,0:T(8,128)(2,1)} %param.35), channel_id=1, source_target_pairs={{0,4},{4,8},{8,12},{12,0},{1,5},{5,9},{9,13},{13,1},{2,6},{6,10},{... | collective-permute-start | bytes 983048 | tf_op jit(solution)/shard_map/ppermute | solution.py:257
  4.6 54.0 %collective-permute-start = (bf16[128,1280]{1,0:T(8,128)(2,1)}, bf16[128,1280]{1,0:T(8,128)(2,1)S(1)}, u32[]{:S(2)}, u32[]{:S(2)}) collective-permute-start(bf16[128,1280]{1,0:T(8,128)(2,1)} %param.21), channel_id=1, source_target_pairs={{0,0},{1,4},{2,8},{3,12},{4,1},{5,5},{6,9},{7,13},{8,2},{9,6},{10,... | collective-permute-start | bytes 983048 | tf_op jit(solution)/shard_map/ppermute | solution.py:265
  8.4 166.8 %collective-permute-start.28 = (bf16[2,1024,64]{1,2,0:T(8,128)(2,1)}, bf16[2,1024,64]{1,2,0:T(8,128)(2,1)}, u32[]{:S(2)}, u32[]{:S(2)}) collective-permute-start(bf16[2,1024,64]{1,2,0:T(8,128)(2,1)} %param.38), channel_id=1, source_target_pairs={{0,12},{4,0},{8,4},{12,8},{1,13},{5,1},{9,5},{13,9},{2,14},{6,2},{... | collective-permute-start | bytes 786440 | tf_op jit(solution)/shard_map/ppermute | solution.py:257
  35.5 8.9 %collective-permute-start.9 = (f32[128,64]{0,1:T(8,128)S(1)}, f32[128,64]{0,1:T(8,128)S(1)}, u32[]{:S(2)}, u32[]{:S(2)}) collective-permute-start(f32[128,64]{0,1:T(8,128)S(1)} %add_add_fusion.1), channel_id=1, source_target_pairs={{0,3},{1,0},{2,1},{3,2},{4,7},{5,4},{6,5},{7,6},{8,11},{9,8},{10,9... | collective-permute-start | bytes 98312 | tf_op jit(solution)/shard_map/ppermute | solution.py:260
  47.1 11.5 %collective-permute-start.10 = (bf16[128,64]{0,1:T(8,128)(2,1)S(1)}, bf16[128,64]{0,1:T(8,128)(2,1)S(1)}, u32[]{:S(2)}, u32[]{:S(2)}) collective-permute-start(bf16[128,64]{0,1:T(8,128)(2,1)S(1)} %add_convert_fusion.2), channel_id=1, source_target_pairs={{0,12},{4,0},{8,4},{12,8},{1,13},{5,1},{9,5},{13,9},{2,14},{6,2},{... | collective-permute-start | bytes 49160 | tf_op jit(solution)/shard_map/ppermute | solution.py:257
  49.2 10.3 %collective-permute-start.11 = (bf16[128,64]{0,1:T(8,128)(2,1)S(1)}, bf16[128,64]{0,1:T(8,128)(2,1)S(1)}, u32[]{:S(2)}, u32[]{:S(2)}) collective-permute-start(bf16[128,64]{0,1:T(8,128)(2,1)S(1)} %add_convert_fusion.2), channel_id=1, source_target_pairs={{0,8},{4,12},{8,0},{12,4},{1,9},{5,13},{9,1},{13,5},{2,10},{6,14},... | collective-permute-start | bytes 49160 | tf_op jit(solution)/shard_map/ppermute | solution.py:257
  58.6 117.8 %collective-permute-start.27 = (bf16[2,1024,64]{1,2,0:T(8,128)(2,1)}, bf16[2,1024,64]{1,2,0:T(8,128)(2,1)}, u32[]{:S(2)}, u32[]{:S(2)}) collective-permute-start(bf16[2,1024,64]{1,2,0:T(8,128)(2,1)} %param.38), channel_id=1, source_target_pairs={{0,8},{4,12},{8,0},{12,4},{1,9},{5,13},{9,1},{13,5},{2,10},{6,14},... | collective-permute-start | bytes 786440 | tf_op jit(solution)/shard_map/ppermute | solution.py:257
  58.6 8.8 %collective-permute-start.1 = (bf16[128,1280]{1,0:T(8,128)(2,1)S(1)}, bf16[128,1280]{1,0:T(8,128)(2,1)S(1)}, u32[]{:S(2)}, u32[]{:S(2)}) collective-permute-start(bf16[128,1280]{1,0:T(8,128)(2,1)S(1)} %collective-permute-done), channel_id=1, source_target_pairs={{0,3},{1,0},{2,1},{3,2},{4,7},{5,4},{6,5},{7,6},{8,11},{9,8},{10,9... | collective-permute-start | bytes 983048 | tf_op jit(solution)/shard_map/ppermute | solution.py:260
  59.4 16.0 %collective-permute-start.2 = (bf16[128,1280]{1,0:T(8,128)(2,1)S(1)}, bf16[128,1280]{1,0:T(8,128)(2,1)S(1)}, u32[]{:S(2)}, u32[]{:S(2)}) collective-permute-start(bf16[128,1280]{1,0:T(8,128)(2,1)S(1)} %collective-permute-done), channel_id=1, source_target_pairs={{0,2},{1,3},{2,0},{3,1},{4,6},{5,7},{6,4},{7,5},{8,10},{9,11},{10,... | collective-permute-start | bytes 983048 | tf_op jit(solution)/shard_map/ppermute | solution.py:260
  60.1 15.5 %collective-permute-start.3 = (bf16[128,1280]{1,0:T(8,128)(2,1)S(1)}, bf16[128,1280]{1,0:T(8,128)(2,1)S(1)}, u32[]{:S(2)}, u32[]{:S(2)}) collective-permute-start(bf16[128,1280]{1,0:T(8,128)(2,1)S(1)} %collective-permute-done), channel_id=1, source_target_pairs={{0,1},{1,2},{2,3},{3,0},{4,5},{5,6},{6,7},{7,4},{8,9},{9,10},{10,1... | collective-permute-start | bytes 983048 | tf_op jit(solution)/shard_map/ppermute | solution.py:260
  79.8 10.0 %collective-permute-start.15 = (bf16[128,1168]{0,1:T(8,128)(2,1)S(1)}, bf16[128,1168]{0,1:T(8,128)(2,1)S(1)}, u32[]{:S(2)}, u32[]{:S(2)}) collective-permute-start(bf16[128,1168]{0,1:T(8,128)(2,1)S(1)} %get-tuple-element.20), channel_id=1, source_target_pairs={{0,12},{4,0},{8,4},{12,8},{1,13},{5,1},{9,5},{13,9},{2,14},{6,2},{... | collective-permute-start | bytes 897032 | tf_op jit(solution)/shard_map/ppermute | solution.py:257
  82.1 26.8 %collective-permute-start.14 = (bf16[128,1168]{0,1:T(8,128)(2,1)S(1)}, bf16[128,1168]{0,1:T(8,128)(2,1)S(1)}, u32[]{:S(2)}, u32[]{:S(2)}) collective-permute-start(bf16[128,1168]{0,1:T(8,128)(2,1)S(1)} %get-tuple-element.21), channel_id=1, source_target_pairs={{0,8},{4,12},{8,0},{12,4},{1,9},{5,13},{9,1},{13,5},{2,10},{6,14},... | collective-permute-start | bytes 897032 | tf_op jit(solution)/shard_map/ppermute | solution.py:257
  83.7 25.3 %collective-permute-start.13 = (bf16[128,1168]{0,1:T(8,128)(2,1)S(1)}, bf16[128,1168]{0,1:T(8,128)(2,1)S(1)}, u32[]{:S(2)}, u32[]{:S(2)}) collective-permute-start(bf16[128,1168]{0,1:T(8,128)(2,1)S(1)} %get-tuple-element.19), channel_id=1, source_target_pairs={{0,4},{4,8},{8,12},{12,0},{1,5},{5,9},{9,13},{13,1},{2,6},{6,10},{... | collective-permute-start | bytes 897032 | tf_op jit(solution)/shard_map/ppermute | solution.py:257
  126.4 19.0 %collective-permute-start.21 = (bf16[16,65,256]{2,0,1:T(8,128)(2,1)}, bf16[16,65,256]{2,0,1:T(8,128)(2,1)}, u32[]{:S(2)}, u32[]{:S(2)}) collective-permute-start(bf16[16,65,256]{2,0,1:T(8,128)(2,1)} %copy.127), channel_id=1, source_target_pairs={{0,8},{4,12},{1,9},{5,13},{2,10},{6,14},{3,11},{7,15},{16,24},{20,... | collective-permute-start | bytes 1597448 | tf_op jit(solution)/shard_map/ppermute | solution.py:407
  133.4 35.7 %collective-permute-start.22 = (bf16[16,65,256]{2,0,1:T(8,128)(2,1)}, bf16[16,65,256]{2,0,1:T(8,128)(2,1)}, u32[]{:S(2)}, u32[]{:S(2)}) collective-permute-start(bf16[16,65,256]{2,0,1:T(8,128)(2,1)} %copy.127), channel_id=1, source_target_pairs={{0,12},{1,13},{2,14},{3,15},{16,28},{17,29},{18,30},{19,31}} | collective-permute-start | bytes 1597448 | tf_op jit(solution)/shard_map/ppermute | solution.py:407
  135.7 34.8 %collective-permute-start.20 = (bf16[16,65,256]{2,0,1:T(8,128)(2,1)}, bf16[16,65,256]{2,0,1:T(8,128)(2,1)S(1)}, u32[]{:S(2)}, u32[]{:S(2)}) collective-permute-start(bf16[16,65,256]{2,0,1:T(8,128)(2,1)} %copy.127), channel_id=1, source_target_pairs={{0,4},{4,8},{8,12},{1,5},{5,9},{9,13},{2,6},{6,10},{10,14},{3,7},{... | collective-permute-start | bytes 1597448 | tf_op jit(solution)/shard_map/ppermute | solution.py:407
  145.4 32.2 %collective-permute-start.26 = (bf16[2,1024,64]{1,2,0:T(8,128)(2,1)}, bf16[2,1024,64]{1,2,0:T(8,128)(2,1)}, u32[]{:S(2)}, u32[]{:S(2)}) collective-permute-start(bf16[2,1024,64]{1,2,0:T(8,128)(2,1)} %param.38), channel_id=1, source_target_pairs={{0,4},{4,8},{8,12},{12,0},{1,5},{5,9},{9,13},{13,1},{2,6},{6,10},{... | collective-permute-start | bytes 786440 | tf_op jit(solution)/shard_map/ppermute | solution.py:257
  180.1 15.6 %collective-permute-start.31 = (f32[128,64]{0,1:T(8,128)S(1)}, f32[128,64]{0,1:T(8,128)S(1)}, u32[]{:S(2)}, u32[]{:S(2)}) collective-permute-start(f32[128,64]{0,1:T(8,128)S(1)} %add_add_fusion), channel_id=1, source_target_pairs={{0,3},{1,0},{2,1},{3,2},{4,7},{5,4},{6,5},{7,6},{8,11},{9,8},{10,9... | collective-permute-start | bytes 98312 | tf_op jit(solution)/shard_map/ppermute | solution.py:260
  180.1 15.6 %collective-permute-start.29 = (f32[128,64]{0,1:T(8,128)S(1)}, f32[128,64]{0,1:T(8,128)S(1)}, u32[]{:S(2)}, u32[]{:S(2)}) collective-permute-start(f32[128,64]{0,1:T(8,128)S(1)} %add_add_fusion), channel_id=1, source_target_pairs={{0,1},{1,2},{2,3},{3,0},{4,5},{5,6},{6,7},{7,4},{8,9},{9,10},{10,1... | collective-permute-start | bytes 98312 | tf_op jit(solution)/shard_map/ppermute | solution.py:260
  180.6 15.1 %collective-permute-start.30 = (f32[128,64]{0,1:T(8,128)S(1)}, f32[128,64]{0,1:T(8,128)S(1)}, u32[]{:S(2)}, u32[]{:S(2)}) collective-permute-start(f32[128,64]{0,1:T(8,128)S(1)} %add_add_fusion), channel_id=1, source_target_pairs={{0,2},{1,3},{2,0},{3,1},{4,6},{5,7},{6,4},{7,5},{8,10},{9,11},{10,... | collective-permute-start | bytes 98312 | tf_op jit(solution)/shard_map/ppermute | solution.py:260
  181.3 44.1 %collective-permute-start.35 = (bf16[2,64,1280]{2,1,0:T(8,128)(2,1)}, bf16[2,64,1280]{2,1,0:T(8,128)(2,1)}, u32[]{:S(2)}, u32[]{:S(2)}) collective-permute-start(bf16[2,64,1280]{2,1,0:T(8,128)(2,1)} %param.39), channel_id=1, source_target_pairs={{0,0},{1,4},{2,8},{3,12},{4,1},{5,5},{6,9},{7,13},{8,2},{9,6},{10,... | collective-permute-start | bytes 983048 | tf_op jit(solution)/shard_map/ppermute | solution.py:265
  194.6 20.3 %collective-permute-start.23 = (bf16[128,1024]{1,0:T(8,128)(2,1)S(1)}, bf16[128,1024]{1,0:T(8,128)(2,1)}, u32[]{:S(2)}, u32[]{:S(2)}) collective-permute-start(bf16[128,1024]{1,0:T(8,128)(2,1)S(1)} %multiply_convert_fusion.1), channel_id=1, source_target_pairs={{0,12},{4,0},{8,4},{12,8},{1,13},{5,1},{9,5},{13,9},{2,14},{6,2},{... | collective-permute-start | bytes 786440 | tf_op jit(solution)/shard_map/ppermute | solution.py:257
  197.3 12.5 %collective-permute-start.33 = (bf16[128,64]{0,1:T(8,128)(2,1)S(1)}, bf16[128,64]{0,1:T(8,128)(2,1)S(1)}, u32[]{:S(2)}, u32[]{:S(2)}) collective-permute-start(bf16[128,64]{0,1:T(8,128)(2,1)S(1)} %add_convert_fusion.1), channel_id=1, source_target_pairs={{0,8},{4,12},{8,0},{12,4},{1,9},{5,13},{9,1},{13,5},{2,10},{6,14},... | collective-permute-start | bytes 49160 | tf_op jit(solution)/shard_map/ppermute | solution.py:257
  198.2 16.6 %collective-permute-start.34 = (bf16[128,64]{0,1:T(8,128)(2,1)S(1)}, bf16[128,64]{0,1:T(8,128)(2,1)S(1)}, u32[]{:S(2)}, u32[]{:S(2)}) collective-permute-start(bf16[128,64]{0,1:T(8,128)(2,1)S(1)} %add_convert_fusion.1), channel_id=1, source_target_pairs={{0,4},{4,8},{8,12},{12,0},{1,5},{5,9},{9,13},{13,1},{2,6},{6,10},{... | collective-permute-start | bytes 49160 | tf_op jit(solution)/shard_map/ppermute | solution.py:257
  203.3 15.5 %collective-permute-start.24 = (bf16[128,1024]{1,0:T(8,128)(2,1)S(1)}, bf16[128,1024]{1,0:T(8,128)(2,1)S(1)}, u32[]{:S(2)}, u32[]{:S(2)}) collective-permute-start(bf16[128,1024]{1,0:T(8,128)(2,1)S(1)} %multiply_convert_fusion.1), channel_id=1, source_target_pairs={{0,8},{4,12},{8,0},{12,4},{1,9},{5,13},{9,1},{13,5},{2,10},{6,14},... | collective-permute-start | bytes 786440 | tf_op jit(solution)/shard_map/ppermute | solution.py:257
  209.9 12.6 %collective-permute-start.25 = (bf16[128,1024]{1,0:T(8,128)(2,1)S(1)}, bf16[128,1024]{1,0:T(8,128)(2,1)S(1)}, u32[]{:S(2)}, u32[]{:S(2)}) collective-permute-start(bf16[128,1024]{1,0:T(8,128)(2,1)S(1)} %multiply_convert_fusion.1), channel_id=1, source_target_pairs={{0,4},{4,8},{8,12},{12,0},{1,5},{5,9},{9,13},{13,1},{2,6},{6,10},{... | collective-permute-start | bytes 786440 | tf_op jit(solution)/shard_map/ppermute | solution.py:257
  229.4 14.3 %collective-permute-start.38 = (bf16[128,1280]{1,0:T(8,128)(2,1)}, bf16[128,1280]{1,0:T(8,128)(2,1)S(1)}, u32[]{:S(2)}, u32[]{:S(2)}) collective-permute-start(bf16[128,1280]{1,0:T(8,128)(2,1)} %get-tuple-element.17), channel_id=1, source_target_pairs={{0,3},{1,0},{2,1},{3,2},{4,7},{5,4},{6,5},{7,6},{8,11},{9,8},{10,9... | collective-permute-start | bytes 983048 | tf_op jit(solution)/shard_map/ppermute | solution.py:260
  236.2 17.1 %collective-permute-start.37 = (bf16[128,1280]{1,0:T(8,128)(2,1)}, bf16[128,1280]{1,0:T(8,128)(2,1)}, u32[]{:S(2)}, u32[]{:S(2)}) collective-permute-start(bf16[128,1280]{1,0:T(8,128)(2,1)} %get-tuple-element.18), channel_id=1, source_target_pairs={{0,2},{1,3},{2,0},{3,1},{4,6},{5,7},{6,4},{7,5},{8,10},{9,11},{10,... | collective-permute-start | bytes 983048 | tf_op jit(solution)/shard_map/ppermute | solution.py:260
  237.7 15.7 %collective-permute-start.36 = (bf16[128,1280]{1,0:T(8,128)(2,1)S(1)}, bf16[128,1280]{1,0:T(8,128)(2,1)}, u32[]{:S(2)}, u32[]{:S(2)}) collective-permute-start(bf16[128,1280]{1,0:T(8,128)(2,1)S(1)} %get-tuple-element.16), channel_id=1, source_target_pairs={{0,1},{1,2},{2,3},{3,0},{4,5},{5,6},{6,7},{7,4},{8,9},{9,10},{10,1... | collective-permute-start | bytes 983048 | tf_op jit(solution)/shard_map/ppermute | solution.py:260
  254.8 19.3 %collective-permute-start.39 = (bf16[128,1280]{1,0:T(8,128)(2,1)S(1)}, bf16[128,1280]{1,0:T(8,128)(2,1)S(1)}, u32[]{:S(2)}, u32[]{:S(2)}) collective-permute-start(bf16[128,1280]{1,0:T(8,128)(2,1)S(1)} %add_convert_fusion), channel_id=1, source_target_pairs={{0,0},{1,4},{2,8},{3,12},{4,1},{5,5},{6,9},{7,13},{8,2},{9,6},{10,... | collective-permute-start | bytes 983048 | tf_op jit(solution)/shard_map/ppermute | solution.py:265
  (40 other events, 738.7 us)

commit v11 on v9

--- a/solution.py
+++ b/solution.py
@@ -334,14 +334,14 @@
     segment = segment_of(positions, request_ends)
     previous = segment_of(jnp.reshape(start_pos - 1, (1,)), request_ends)[0]
 
-    tokens_t = transposed(tokens)
+    tokens_t, down_in_local = lax.optimization_barrier((transposed(tokens), adapter_down_input))
     stream_rows = in_order(
         [tokens_t] + [moved(tokens_t, s, "lane") for s in range(1, side)], lane
     )
     local_owned = lax.dynamic_slice_in_dim(slot_of_position, start_pos, length, 0)
     down_pick = jnp.zeros((length, rank_value), jnp.float32)
     for s in range(side):
-        piece = adapter_down_input if s == 0 else moved(adapter_down_input, s, "ctx")
+        piece = down_in_local if s == 0 else moved(down_in_local, s, "ctx")
         first = ((here - s) % side) * bank_entries
         every = jnp.einsum("pf,efr->per", tokens, piece, preferred_element_type=jnp.float32)
         chosen = local_owned[:, None] == first + jnp.arange(bank_entries, dtype=jnp.int32)[None, :]

time: 275 us -> 271 us (0.985)
  waiting for transfers between devices: 128 us -> 143 us
  starting transfers between devices: 81.5 us -> 71.4 us
  other arithmetic: 21.7 us -> 15.8 us
    ppermute x12, waiting for transfers between devices: 49.8 us -> 64.8 us  [moved(): return lax.ppermute(block, 'ctx', pairs)]
    ppermute x4, waiting for transfers between devices: 19.3 us -> 29.2 us  [moved(): return lax.ppermute(block, ('ctx', 'tp', 'dp'), pairs)]
    ppermute x15, waiting for transfers between devices: 35 us -> 25.5 us  [moved(): return lax.ppermute(block, ('tp', 'dp'), pairs)]
    unnamed x5 -> x1, matrix products: 7.48 us -> 1.8 us
    ppermute x15, starting transfers between devices: 23.9 us -> 18.6 us  [moved(): return lax.ppermute(block, ('tp', 'dp'), pairs)]
    ppermute x12, starting transfers between devices: 33.3 us -> 28.8 us  [moved(): return lax.ppermute(block, 'ctx', pairs)]
    dot_general x0 -> x4, matrix products: none -> 4.11 us  [square_body(): jnp.einsum('pf,efr->per', tokens, piece, preferred_element_type=jnp.float32)]
    unnamed x81 -> x61, local copies, waits for them, and re-layouts: 7.28 us -> 7.59 us
  transfers between devices with their start and end apart: 35 -> 35, of which waited for: 21 -> 20; matrix products, arithmetic and copies ran while one was open for 14% -> 12% of each run, Pallas kernels for 0% -> 0%
where the time goes in v11:
time: 271 us; the launch traced here: 270 us
  waiting for transfers between devices  143 us (53%)
  starting transfers between devices  71.4 us (26%)
  local copies, waits for them, and re-layouts  21.3 us (8%)
  matrix products  16.3 us (6%)
  other arithmetic  15.8 us (6%)
    ppermute x12, waiting for transfers between devices, moved(): return lax.ppermute(block, 'ctx', pairs)  64.8 us
    ppermute x4, waiting for transfers between devices, moved(): return lax.ppermute(block, ('ctx', 'tp', 'dp'), pairs)  29.2 us
    ppermute x12, starting transfers between devices, moved(): return lax.ppermute(block, 'ctx', pairs)  28.8 us
    ppermute x15, waiting for transfers between devices, moved(): return lax.ppermute(block, ('tp', 'dp'), pairs)  25.5 us
    ppermute x3, waiting for transfers between devices, square_body(): both_in = lax.ppermute(state_and_decay, 'ctx', pairs).astype(jnp.float32)  23.2 us
    ppermute x15, starting transfers between devices, moved(): return lax.ppermute(block, ('tp', 'dp'), pairs)  18.6 us
    ppermute x4, starting transfers between devices, moved(): return lax.ppermute(block, ('ctx', 'tp', 'dp'), pairs)  11.7 us
    ppermute x3, starting transfers between devices, square_body(): both_in = lax.ppermute(state_and_decay, 'ctx', pairs).astype(jnp.float32)  10.4 us
  transfers between devices with their start and end apart: 35, of which 20 were waited for; matrix products, arithmetic and copies ran while one was open for 12% of the time, Pallas kernels for 0%

profile of v11, /device:TPU:2, one launch (start us, length us, event | category | flops | bytes accessed | tf_op | source)
XLA Modules:
  0.0 269.8 jit_solution(6581052493845907020)
XLA Ops:
  0.0 4.7 %collective-permute-start = (bf16[128,1280]{1,0:T(8,128)(2,1)}, bf16[128,1280]{1,0:T(8,128)(2,1)S(1)}, u32[]{:S(2)}, u32[]{:S(2)}) collective-permute-start(bf16[128,1280]{1,0:T(8,128)(2,1)} %param.19), channel_id=1, source_target_pairs={{0,0},{1,4},{2,8},{3,12},{4,1},{5,5},{6,9},{7,13},{8,2},{9,6},{10,... | collective-permute-start | bytes 983048 | tf_op jit(solution)/shard_map/ppermute | solution.py:265
  11.3 10.0 %collective-permute-done = bf16[128,1280]{1,0:T(8,128)(2,1)S(1)} collective-permute-done((bf16[128,1280]{1,0:T(8,128)(2,1)}, bf16[128,1280]{1,0:T(8,128)(2,1)S(1)}, u32[]{:S(2)}, u32[]{:S(2)}) %collective-permute-start) | collective-permute-done | bytes 327712 | tf_op jit(solution)/shard_map/ppermute | solution.py:265
  22.1 3.4 %collective-permute-start.5 = (bf16[2,1280,64]{1,2,0:T(8,128)(2,1)}, bf16[2,1280,64]{1,2,0:T(8,128)(2,1)}, u32[]{:S(2)}, u32[]{:S(2)}) collective-permute-start(bf16[2,1280,64]{1,2,0:T(8,128)(2,1)} %param.33), channel_id=1, source_target_pairs={{0,8},{4,12},{8,0},{12,4},{1,9},{5,13},{9,1},{13,5},{2,10},{6,14},... | collective-permute-start | bytes 983048 | tf_op jit(solution)/shard_map/ppermute | solution.py:257
  27.5 2.6 collective-permute-start.1
  33.4 20.8 %collective-permute-done.5 = bf16[2,1280,64]{1,2,0:T(8,128)(2,1)} collective-permute-done((bf16[2,1280,64]{1,2,0:T(8,128)(2,1)}, bf16[2,1280,64]{1,2,0:T(8,128)(2,1)}, u32[]{:S(2)}, u32[]{:S(2)}) %collective-permute-start.5) | collective-permute-done | bytes 327712 | tf_op jit(solution)/shard_map/ppermute | solution.py:257
  61.9 2.0 collective-permute-start.12
  69.4 1.9 collective-permute-start.15
  72.1 6.8 %collective-permute-done.15 = bf16[128,1168]{0,1:T(8,128)(2,1)S(1)} collective-permute-done((bf16[128,1168]{0,1:T(8,128)(2,1)S(1)}, bf16[128,1168]{0,1:T(8,128)(2,1)S(1)}, u32[]{:S(2)}, u32[]{:S(2)}) %collective-permute-start.15) | collective-permute-done | bytes 299040 | tf_op jit(solution)/shard_map/ppermute | solution.py:257
  79.0 17.8 %collective-permute-done.14 = bf16[128,1168]{0,1:T(8,128)(2,1)S(1)} collective-permute-done((bf16[128,1168]{0,1:T(8,128)(2,1)S(1)}, bf16[128,1168]{0,1:T(8,128)(2,1)S(1)}, u32[]{:S(2)}, u32[]{:S(2)}) %collective-permute-start.14) | collective-permute-done | bytes 299040 | tf_op jit(solution)/shard_map/ppermute | solution.py:257
  103.3 3.3 %divide_multiply_fusion = f32[128,1152]{0,1:T(8,128)S(1)} fusion(f32[128,1152]{0,1:T(8,128)} %slice.129, f32[3,1152]{0,1:T(8,128)S(1)} %copy.112, f32[128]{0:T(128)S(1)} %get-tuple-element.35, f32[1152]{0:T(1024)S(1)} %get-tuple-element.10, f32[128]{0:T(128)S(1)} %get-tuple-element.36, f32[1152]{0:T(1024)S(1)} %get-tuple-element.11, ...), kind=kLoop, calls=%fused_computation.61 | loop fusion | flops 2654208 | bytes 1213952 | tf_op jit(solution)/shard_map/jit(silu)/mul | solution.py:388
  108.8 2.4 collective-permute-done.18
  114.6 6.8 %collective-permute-start.21 = (bf16[16,65,256]{2,0,1:T(8,128)(2,1)}, bf16[16,65,256]{2,0,1:T(8,128)(2,1)}, u32[]{:S(2)}, u32[]{:S(2)}) collective-permute-start(bf16[16,65,256]{2,0,1:T(8,128)(2,1)} %copy.118), channel_id=1, source_target_pairs={{0,8},{4,12},{1,9},{5,13},{2,10},{6,14},{3,11},{7,15},{16,24},{20,... | collective-permute-start | bytes 1597448 | tf_op jit(solution)/shard_map/ppermute | solution.py:407
  121.4 2.1 collective-permute-start.22
  126.0 2.2 convolution_bitcast_fusion
  128.2 5.2 %collective-permute-done.21 = bf16[16,65,256]{2,0,1:T(8,128)(2,1)} collective-permute-done((bf16[16,65,256]{2,0,1:T(8,128)(2,1)}, bf16[16,65,256]{2,0,1:T(8,128)(2,1)}, u32[]{:S(2)}, u32[]{:S(2)}) %collective-permute-start.21) | collective-permute-done | bytes 532512 | tf_op jit(solution)/shard_map/ppermute | solution.py:407
  134.6 10.3 %collective-permute-done.22 = bf16[16,65,256]{2,0,1:T(8,128)(2,1)} collective-permute-done((bf16[16,65,256]{2,0,1:T(8,128)(2,1)}, bf16[16,65,256]{2,0,1:T(8,128)(2,1)}, u32[]{:S(2)}, u32[]{:S(2)}) %collective-permute-start.22) | collective-permute-done | bytes 532512 | tf_op jit(solution)/shard_map/ppermute | solution.py:407
  146.3 7.7 %collective-permute-done.20 = bf16[16,65,256]{2,0,1:T(8,128)(2,1)S(1)} collective-permute-done((bf16[16,65,256]{2,0,1:T(8,128)(2,1)}, bf16[16,65,256]{2,0,1:T(8,128)(2,1)S(1)}, u32[]{:S(2)}, u32[]{:S(2)}) %collective-permute-start.20) | collective-permute-done | bytes 532512 | tf_op jit(solution)/shard_map/ppermute | solution.py:407
  157.5 7.0 %collective-permute-start.23 = (bf16[128,1024]{0,1:T(8,128)(2,1)}, bf16[128,1024]{0,1:T(8,128)(2,1)S(1)}, u32[]{:S(2)}, u32[]{:S(2)}) collective-permute-start(bf16[128,1024]{0,1:T(8,128)(2,1)} %fusion.34), channel_id=1, source_target_pairs={{0,12},{4,0},{8,4},{12,8},{1,13},{5,1},{9,5},{13,9},{2,14},{6,2},{... | collective-permute-start | bytes 786440 | tf_op jit(solution)/shard_map/ppermute | solution.py:257
  164.5 11.8 %collective-permute-start.24 = (bf16[128,1024]{0,1:T(8,128)(2,1)}, bf16[128,1024]{0,1:T(8,128)(2,1)}, u32[]{:S(2)}, u32[]{:S(2)}) collective-permute-start(bf16[128,1024]{0,1:T(8,128)(2,1)} %fusion.34), channel_id=1, source_target_pairs={{0,8},{4,12},{8,0},{12,4},{1,9},{5,13},{9,1},{13,5},{2,10},{6,14},... | collective-permute-start | bytes 786440 | tf_op jit(solution)/shard_map/ppermute | solution.py:257
  176.3 2.6 collective-permute-start.30
  180.3 15.3 %collective-permute-done.24 = bf16[128,1024]{0,1:T(8,128)(2,1)} collective-permute-done((bf16[128,1024]{0,1:T(8,128)(2,1)}, bf16[128,1024]{0,1:T(8,128)(2,1)}, u32[]{:S(2)}, u32[]{:S(2)}) %collective-permute-start.24) | collective-permute-done | bytes 262176 | tf_op jit(solution)/shard_map/ppermute | solution.py:257
  199.1 2.3 copy.123
  203.2 3.6 %collective-permute-start.28 = (f32[512,64]{0,1:T(8,128)S(1)}, f32[512,64]{0,1:T(8,128)S(1)}, u32[]{:S(2)}, u32[]{:S(2)}) collective-permute-start(f32[512,64]{0,1:T(8,128)S(1)} %multiply_reduce_fusion.1), channel_id=1, source_target_pairs={{0,3},{1,0},{2,1},{3,2},{4,7},{5,4},{6,5},{7,6},{8,11},{9,8},{10,9... | collective-permute-start | bytes 393224 | tf_op jit(solution)/shard_map/ppermute | solution.py:260
  206.8 8.7 %collective-permute-start.27 = (f32[512,64]{0,1:T(8,128)S(1)}, f32[512,64]{0,1:T(8,128)S(1)}, u32[]{:S(2)}, u32[]{:S(2)}) collective-permute-start(f32[512,64]{0,1:T(8,128)S(1)} %multiply_reduce_fusion.1), channel_id=1, source_target_pairs={{0,2},{1,3},{2,0},{3,1},{4,6},{5,7},{6,4},{7,5},{8,10},{9,11},{10,... | collective-permute-start | bytes 393224 | tf_op jit(solution)/shard_map/ppermute | solution.py:260
  215.6 3.5 %collective-permute-done.26 = f32[512,64]{0,1:T(8,128)S(1)} collective-permute-done((f32[512,64]{0,1:T(8,128)S(1)}, f32[512,64]{0,1:T(8,128)S(1)}, u32[]{:S(2)}, u32[]{:S(2)}) %collective-permute-start.26) | collective-permute-done | bytes 131104 | tf_op jit(solution)/shard_map/ppermute | solution.py:260
  219.0 3.0 %collective-permute-done.27 = f32[512,64]{0,1:T(8,128)S(1)} collective-permute-done((f32[512,64]{0,1:T(8,128)S(1)}, f32[512,64]{0,1:T(8,128)S(1)}, u32[]{:S(2)}, u32[]{:S(2)}) %collective-permute-start.27) | collective-permute-done | bytes 131104 | tf_op jit(solution)/shard_map/ppermute | solution.py:260
  222.0 1.9 collective-permute-start.29
  225.5 6.6 %collective-permute-done.29 = f32[512,64]{0,1:T(8,128)S(1)} collective-permute-done((f32[512,64]{0,1:T(8,128)S(1)}, f32[512,64]{0,1:T(8,128)S(1)}, u32[]{:S(2)}, u32[]{:S(2)}) %collective-permute-start.29) | collective-permute-done | bytes 131104 | tf_op jit(solution)/shard_map/ppermute | solution.py:265
  236.7 7.8 %collective-permute-done.33 = bf16[128,1280]{1,0:T(8,128)(2,1)S(1)} collective-permute-done((bf16[128,1280]{1,0:T(8,128)(2,1)}, bf16[128,1280]{1,0:T(8,128)(2,1)S(1)}, u32[]{:S(2)}, u32[]{:S(2)}) %collective-permute-start.33) | collective-permute-done | bytes 327712 | tf_op jit(solution)/shard_map/ppermute | solution.py:260
  244.5 7.1 %collective-permute-done.32 = bf16[128,1280]{1,0:T(8,128)(2,1)} collective-permute-done((bf16[128,1280]{1,0:T(8,128)(2,1)}, bf16[128,1280]{1,0:T(8,128)(2,1)}, u32[]{:S(2)}, u32[]{:S(2)}) %collective-permute-start.32) | collective-permute-done | bytes 327712 | tf_op jit(solution)/shard_map/ppermute | solution.py:260
  254.0 2.4 collective-permute-start.34
  256.4 12.6 %collective-permute-done.34 = bf16[128,1280]{1,0:T(8,128)(2,1)S(1)} collective-permute-done((bf16[128,1280]{1,0:T(8,128)(2,1)S(1)}, bf16[128,1280]{1,0:T(8,128)(2,1)S(1)}, u32[]{:S(2)}, u32[]{:S(2)}) %collective-permute-start.34) | collective-permute-done | bytes 327712 | tf_op jit(solution)/shard_map/ppermute | solution.py:265
  (192 shorter events, 61.3 us)
Async XLA Ops:
  0.0 21.3 %collective-permute-start = (bf16[128,1280]{1,0:T(8,128)(2,1)}, bf16[128,1280]{1,0:T(8,128)(2,1)S(1)}, u32[]{:S(2)}, u32[]{:S(2)}) collective-permute-start(bf16[128,1280]{1,0:T(8,128)(2,1)} %param.19), channel_id=1, source_target_pairs={{0,0},{1,4},{2,8},{3,12},{4,1},{5,5},{6,9},{7,13},{8,2},{9,6},{10,... | collective-permute-start | bytes 983048 | tf_op jit(solution)/shard_map/ppermute | solution.py:265
  21.3 10.7 %collective-permute-start.6 = (bf16[2,1280,64]{1,2,0:T(8,128)(2,1)}, bf16[2,1280,64]{1,2,0:T(8,128)(2,1)}, u32[]{:S(2)}, u32[]{:S(2)}) collective-permute-start(bf16[2,1280,64]{1,2,0:T(8,128)(2,1)} %param.33), channel_id=1, source_target_pairs={{0,12},{4,0},{8,4},{12,8},{1,13},{5,1},{9,5},{13,9},{2,14},{6,2},{... | collective-permute-start | bytes 983048 | tf_op jit(solution)/shard_map/ppermute | solution.py:257
  22.1 32.2 %collective-permute-start.5 = (bf16[2,1280,64]{1,2,0:T(8,128)(2,1)}, bf16[2,1280,64]{1,2,0:T(8,128)(2,1)}, u32[]{:S(2)}, u32[]{:S(2)}) collective-permute-start(bf16[2,1280,64]{1,2,0:T(8,128)(2,1)} %param.33), channel_id=1, source_target_pairs={{0,8},{4,12},{8,0},{12,4},{1,9},{5,13},{9,1},{13,5},{2,10},{6,14},... | collective-permute-start | bytes 983048 | tf_op jit(solution)/shard_map/ppermute | solution.py:257
  27.5 28.8 %collective-permute-start.1 = (bf16[128,1280]{1,0:T(8,128)(2,1)S(1)}, bf16[128,1280]{1,0:T(8,128)(2,1)S(1)}, u32[]{:S(2)}, u32[]{:S(2)}) collective-permute-start(bf16[128,1280]{1,0:T(8,128)(2,1)S(1)} %collective-permute-done), channel_id=1, source_target_pairs={{0,3},{1,0},{2,1},{3,2},{4,7},{5,4},{6,5},{7,6},{8,11},{9,8},{10,9... | collective-permute-start | bytes 983048 | tf_op jit(solution)/shard_map/ppermute | solution.py:260
  30.1 27.0 %collective-permute-start.2 = (bf16[128,1280]{1,0:T(8,128)(2,1)S(1)}, bf16[128,1280]{1,0:T(8,128)(2,1)S(1)}, u32[]{:S(2)}, u32[]{:S(2)}) collective-permute-start(bf16[128,1280]{1,0:T(8,128)(2,1)S(1)} %collective-permute-done), channel_id=1, source_target_pairs={{0,2},{1,3},{2,0},{3,1},{4,6},{5,7},{6,4},{7,5},{8,10},{9,11},{10,... | collective-permute-start | bytes 983048 | tf_op jit(solution)/shard_map/ppermute | solution.py:260
  30.1 25.3 %collective-permute-start.4 = (bf16[2,1280,64]{1,2,0:T(8,128)(2,1)}, bf16[2,1280,64]{1,2,0:T(8,128)(2,1)S(1)}, u32[]{:S(2)}, u32[]{:S(2)}) collective-permute-start(bf16[2,1280,64]{1,2,0:T(8,128)(2,1)} %param.33), channel_id=1, source_target_pairs={{0,4},{4,8},{8,12},{12,0},{1,5},{5,9},{9,13},{13,1},{2,6},{6,10},{... | collective-permute-start | bytes 983048 | tf_op jit(solution)/shard_map/ppermute | solution.py:257
  32.0 25.2 %collective-permute-start.3 = (bf16[128,1280]{1,0:T(8,128)(2,1)S(1)}, bf16[128,1280]{1,0:T(8,128)(2,1)S(1)}, u32[]{:S(2)}, u32[]{:S(2)}) collective-permute-start(bf16[128,1280]{1,0:T(8,128)(2,1)S(1)} %collective-permute-done), channel_id=1, source_target_pairs={{0,1},{1,2},{2,3},{3,0},{4,5},{5,6},{6,7},{7,4},{8,9},{9,10},{10,1... | collective-permute-start | bytes 983048 | tf_op jit(solution)/shard_map/ppermute | solution.py:260
  55.7 5.6 %collective-permute-start.9 = (f32[128,64]{0,1:T(8,128)S(1)}, f32[128,64]{0,1:T(8,128)S(1)}, u32[]{:S(2)}, u32[]{:S(2)}) collective-permute-start(f32[128,64]{0,1:T(8,128)S(1)} %add_add_fusion.1), channel_id=1, source_target_pairs={{0,3},{1,0},{2,1},{3,2},{4,7},{5,4},{6,5},{7,6},{8,11},{9,8},{10,9... | collective-permute-start | bytes 98312 | tf_op jit(solution)/shard_map/ppermute | solution.py:260
  55.8 5.5 %collective-permute-start.7 = (f32[128,64]{0,1:T(8,128)S(1)}, f32[128,64]{0,1:T(8,128)S(1)}, u32[]{:S(2)}, u32[]{:S(2)}) collective-permute-start(f32[128,64]{0,1:T(8,128)S(1)} %add_add_fusion.1), channel_id=1, source_target_pairs={{0,1},{1,2},{2,3},{3,0},{4,5},{5,6},{6,7},{7,4},{8,9},{9,10},{10,1... | collective-permute-start | bytes 98312 | tf_op jit(solution)/shard_map/ppermute | solution.py:260
  56.3 5.0 %collective-permute-start.8 = (f32[128,64]{0,1:T(8,128)S(1)}, f32[128,64]{0,1:T(8,128)S(1)}, u32[]{:S(2)}, u32[]{:S(2)}) collective-permute-start(f32[128,64]{0,1:T(8,128)S(1)} %add_add_fusion.1), channel_id=1, source_target_pairs={{0,2},{1,3},{2,0},{3,1},{4,6},{5,7},{6,4},{7,5},{8,10},{9,11},{10,... | collective-permute-start | bytes 98312 | tf_op jit(solution)/shard_map/ppermute | solution.py:260
  61.3 3.8 %collective-permute-start.10 = (bf16[128,64]{0,1:T(8,128)(2,1)S(1)}, bf16[128,64]{0,1:T(8,128)(2,1)S(1)}, u32[]{:S(2)}, u32[]{:S(2)}) collective-permute-start(bf16[128,64]{0,1:T(8,128)(2,1)S(1)} %add_convert_fusion.1), channel_id=1, source_target_pairs={{0,12},{4,0},{8,4},{12,8},{1,13},{5,1},{9,5},{13,9},{2,14},{6,2},{... | collective-permute-start | bytes 49160 | tf_op jit(solution)/shard_map/ppermute | solution.py:257
  61.9 4.7 %collective-permute-start.11 = (bf16[128,64]{0,1:T(8,128)(2,1)S(1)}, bf16[128,64]{0,1:T(8,128)(2,1)S(1)}, u32[]{:S(2)}, u32[]{:S(2)}) collective-permute-start(bf16[128,64]{0,1:T(8,128)(2,1)S(1)} %add_convert_fusion.1), channel_id=1, source_target_pairs={{0,8},{4,12},{8,0},{12,4},{1,9},{5,13},{9,1},{13,5},{2,10},{6,14},... | collective-permute-start | bytes 49160 | tf_op jit(solution)/shard_map/ppermute | solution.py:257
  61.9 6.3 %collective-permute-start.12 = (bf16[128,64]{0,1:T(8,128)(2,1)S(1)}, bf16[128,64]{0,1:T(8,128)(2,1)S(1)}, u32[]{:S(2)}, u32[]{:S(2)}) collective-permute-start(bf16[128,64]{0,1:T(8,128)(2,1)S(1)} %add_convert_fusion.1), channel_id=1, source_target_pairs={{0,4},{4,8},{8,12},{12,0},{1,5},{5,9},{9,13},{13,1},{2,6},{6,10},{... | collective-permute-start | bytes 49160 | tf_op jit(solution)/shard_map/ppermute | solution.py:257
  69.4 9.5 %collective-permute-start.15 = (bf16[128,1168]{0,1:T(8,128)(2,1)S(1)}, bf16[128,1168]{0,1:T(8,128)(2,1)S(1)}, u32[]{:S(2)}, u32[]{:S(2)}) collective-permute-start(bf16[128,1168]{0,1:T(8,128)(2,1)S(1)} %get-tuple-element.23), channel_id=1, source_target_pairs={{0,12},{4,0},{8,4},{12,8},{1,13},{5,1},{9,5},{13,9},{2,14},{6,2},{... | collective-permute-start | bytes 897032 | tf_op jit(solution)/shard_map/ppermute | solution.py:257
  71.4 25.3 %collective-permute-start.14 = (bf16[128,1168]{0,1:T(8,128)(2,1)S(1)}, bf16[128,1168]{0,1:T(8,128)(2,1)S(1)}, u32[]{:S(2)}, u32[]{:S(2)}) collective-permute-start(bf16[128,1168]{0,1:T(8,128)(2,1)S(1)} %get-tuple-element.24), channel_id=1, source_target_pairs={{0,8},{4,12},{8,0},{12,4},{1,9},{5,13},{9,1},{13,5},{2,10},{6,14},... | collective-permute-start | bytes 897032 | tf_op jit(solution)/shard_map/ppermute | solution.py:257
  71.4 25.3 %collective-permute-start.13 = (bf16[128,1168]{0,1:T(8,128)(2,1)S(1)}, bf16[128,1168]{0,1:T(8,128)(2,1)S(1)}, u32[]{:S(2)}, u32[]{:S(2)}) collective-permute-start(bf16[128,1168]{0,1:T(8,128)(2,1)S(1)} %get-tuple-element.22), channel_id=1, source_target_pairs={{0,4},{4,8},{8,12},{12,0},{1,5},{5,9},{9,13},{13,1},{2,6},{6,10},{... | collective-permute-start | bytes 897032 | tf_op jit(solution)/shard_map/ppermute | solution.py:257
  107.3 4.0 %collective-permute-start.18 = (bf16[128,128]{0,1:T(8,128)(2,1)S(1)}, bf16[128,128]{0,1:T(8,128)(2,1)S(1)}, u32[]{:S(2)}, u32[]{:S(2)}) collective-permute-start(bf16[128,128]{0,1:T(8,128)(2,1)S(1)} %slice.244), channel_id=1, source_target_pairs={{0,2},{1,3},{2,0},{3,1},{4,6},{5,7},{6,4},{7,5},{8,10},{9,11},{10,... | collective-permute-start | bytes 98312 | tf_op jit(solution)/shard_map/ppermute | solution.py:260
  114.6 18.9 %collective-permute-start.21 = (bf16[16,65,256]{2,0,1:T(8,128)(2,1)}, bf16[16,65,256]{2,0,1:T(8,128)(2,1)}, u32[]{:S(2)}, u32[]{:S(2)}) collective-permute-start(bf16[16,65,256]{2,0,1:T(8,128)(2,1)} %copy.118), channel_id=1, source_target_pairs={{0,8},{4,12},{1,9},{5,13},{2,10},{6,14},{3,11},{7,15},{16,24},{20,... | collective-permute-start | bytes 1597448 | tf_op jit(solution)/shard_map/ppermute | solution.py:407
  121.4 23.5 %collective-permute-start.22 = (bf16[16,65,256]{2,0,1:T(8,128)(2,1)}, bf16[16,65,256]{2,0,1:T(8,128)(2,1)}, u32[]{:S(2)}, u32[]{:S(2)}) collective-permute-start(bf16[16,65,256]{2,0,1:T(8,128)(2,1)} %copy.118), channel_id=1, source_target_pairs={{0,12},{1,13},{2,14},{3,15},{16,28},{17,29},{18,30},{19,31}} | collective-permute-start | bytes 1597448 | tf_op jit(solution)/shard_map/ppermute | solution.py:407
  124.3 29.7 %collective-permute-start.20 = (bf16[16,65,256]{2,0,1:T(8,128)(2,1)}, bf16[16,65,256]{2,0,1:T(8,128)(2,1)S(1)}, u32[]{:S(2)}, u32[]{:S(2)}) collective-permute-start(bf16[16,65,256]{2,0,1:T(8,128)(2,1)} %copy.118), channel_id=1, source_target_pairs={{0,4},{4,8},{8,12},{1,5},{5,9},{9,13},{2,6},{6,10},{10,14},{3,7},{... | collective-permute-start | bytes 1597448 | tf_op jit(solution)/shard_map/ppermute | solution.py:407
  157.5 22.8 %collective-permute-start.23 = (bf16[128,1024]{0,1:T(8,128)(2,1)}, bf16[128,1024]{0,1:T(8,128)(2,1)S(1)}, u32[]{:S(2)}, u32[]{:S(2)}) collective-permute-start(bf16[128,1024]{0,1:T(8,128)(2,1)} %fusion.34), channel_id=1, source_target_pairs={{0,12},{4,0},{8,4},{12,8},{1,13},{5,1},{9,5},{13,9},{2,14},{6,2},{... | collective-permute-start | bytes 786440 | tf_op jit(solution)/shard_map/ppermute | solution.py:257
  164.5 31.1 %collective-permute-start.24 = (bf16[128,1024]{0,1:T(8,128)(2,1)}, bf16[128,1024]{0,1:T(8,128)(2,1)}, u32[]{:S(2)}, u32[]{:S(2)}) collective-permute-start(bf16[128,1024]{0,1:T(8,128)(2,1)} %fusion.34), channel_id=1, source_target_pairs={{0,8},{4,12},{8,0},{12,4},{1,9},{5,13},{9,1},{13,5},{2,10},{6,14},... | collective-permute-start | bytes 786440 | tf_op jit(solution)/shard_map/ppermute | solution.py:257
  176.3 55.9 %collective-permute-start.30 = (bf16[2,64,1280]{2,1,0:T(8,128)(2,1)}, bf16[2,64,1280]{2,1,0:T(8,128)(2,1)}, u32[]{:S(2)}, u32[]{:S(2)}) collective-permute-start(bf16[2,64,1280]{2,1,0:T(8,128)(2,1)} %param.37), channel_id=1, source_target_pairs={{0,0},{1,4},{2,8},{3,12},{4,1},{5,5},{6,9},{7,13},{8,2},{9,6},{10,... | collective-permute-start | bytes 983048 | tf_op jit(solution)/shard_map/ppermute | solution.py:265
  178.9 17.7 %collective-permute-start.25 = (bf16[128,1024]{0,1:T(8,128)(2,1)}, bf16[128,1024]{0,1:T(8,128)(2,1)S(1)}, u32[]{:S(2)}, u32[]{:S(2)}) collective-permute-start(bf16[128,1024]{0,1:T(8,128)(2,1)} %fusion.34), channel_id=1, source_target_pairs={{0,4},{4,8},{8,12},{12,0},{1,5},{5,9},{9,13},{13,1},{2,6},{6,10},{... | collective-permute-start | bytes 786440 | tf_op jit(solution)/shard_map/ppermute | solution.py:257
  203.2 12.4 %collective-permute-start.28 = (f32[512,64]{0,1:T(8,128)S(1)}, f32[512,64]{0,1:T(8,128)S(1)}, u32[]{:S(2)}, u32[]{:S(2)}) collective-permute-start(f32[512,64]{0,1:T(8,128)S(1)} %multiply_reduce_fusion.1), channel_id=1, source_target_pairs={{0,3},{1,0},{2,1},{3,2},{4,7},{5,4},{6,5},{7,6},{8,11},{9,8},{10,9... | collective-permute-start | bytes 393224 | tf_op jit(solution)/shard_map/ppermute | solution.py:260
  206.8 12.2 %collective-permute-start.26 = (f32[512,64]{0,1:T(8,128)S(1)}, f32[512,64]{0,1:T(8,128)S(1)}, u32[]{:S(2)}, u32[]{:S(2)}) collective-permute-start(f32[512,64]{0,1:T(8,128)S(1)} %multiply_reduce_fusion.1), channel_id=1, source_target_pairs={{0,1},{1,2},{2,3},{3,0},{4,5},{5,6},{6,7},{7,4},{8,9},{9,10},{10,1... | collective-permute-start | bytes 393224 | tf_op jit(solution)/shard_map/ppermute | solution.py:260
  206.8 15.2 %collective-permute-start.27 = (f32[512,64]{0,1:T(8,128)S(1)}, f32[512,64]{0,1:T(8,128)S(1)}, u32[]{:S(2)}, u32[]{:S(2)}) collective-permute-start(f32[512,64]{0,1:T(8,128)S(1)} %multiply_reduce_fusion.1), channel_id=1, source_target_pairs={{0,2},{1,3},{2,0},{3,1},{4,6},{5,7},{6,4},{7,5},{8,10},{9,11},{10,... | collective-permute-start | bytes 393224 | tf_op jit(solution)/shard_map/ppermute | solution.py:260
  222.0 10.1 %collective-permute-start.29 = (f32[512,64]{0,1:T(8,128)S(1)}, f32[512,64]{0,1:T(8,128)S(1)}, u32[]{:S(2)}, u32[]{:S(2)}) collective-permute-start(f32[512,64]{0,1:T(8,128)S(1)} %add_add_fusion), channel_id=1, source_target_pairs={{0,0},{1,4},{2,8},{3,12},{4,1},{5,5},{6,9},{7,13},{8,2},{9,6},{10,... | collective-permute-start | bytes 393224 | tf_op jit(solution)/shard_map/ppermute | solution.py:265
  236.1 8.4 %collective-permute-start.33 = (bf16[128,1280]{1,0:T(8,128)(2,1)}, bf16[128,1280]{1,0:T(8,128)(2,1)S(1)}, u32[]{:S(2)}, u32[]{:S(2)}) collective-permute-start(bf16[128,1280]{1,0:T(8,128)(2,1)} %get-tuple-element.20), channel_id=1, source_target_pairs={{0,3},{1,0},{2,1},{3,2},{4,7},{5,4},{6,5},{7,6},{8,11},{9,8},{10,9... | collective-permute-start | bytes 983048 | tf_op jit(solution)/shard_map/ppermute | solution.py:260
  236.1 15.5 %collective-permute-start.32 = (bf16[128,1280]{1,0:T(8,128)(2,1)}, bf16[128,1280]{1,0:T(8,128)(2,1)}, u32[]{:S(2)}, u32[]{:S(2)}) collective-permute-start(bf16[128,1280]{1,0:T(8,128)(2,1)} %get-tuple-element.21), channel_id=1, source_target_pairs={{0,2},{1,3},{2,0},{3,1},{4,6},{5,7},{6,4},{7,5},{8,10},{9,11},{10,... | collective-permute-start | bytes 983048 | tf_op jit(solution)/shard_map/ppermute | solution.py:260
  236.7 15.9 %collective-permute-start.31 = (bf16[128,1280]{1,0:T(8,128)(2,1)S(1)}, bf16[128,1280]{1,0:T(8,128)(2,1)}, u32[]{:S(2)}, u32[]{:S(2)}) collective-permute-start(bf16[128,1280]{1,0:T(8,128)(2,1)S(1)} %get-tuple-element.19), channel_id=1, source_target_pairs={{0,1},{1,2},{2,3},{3,0},{4,5},{5,6},{6,7},{7,4},{8,9},{9,10},{10,1... | collective-permute-start | bytes 983048 | tf_op jit(solution)/shard_map/ppermute | solution.py:260
  254.0 15.1 %collective-permute-start.34 = (bf16[128,1280]{1,0:T(8,128)(2,1)S(1)}, bf16[128,1280]{1,0:T(8,128)(2,1)S(1)}, u32[]{:S(2)}, u32[]{:S(2)}) collective-permute-start(bf16[128,1280]{1,0:T(8,128)(2,1)S(1)} %add_convert_fusion), channel_id=1, source_target_pairs={{0,0},{1,4},{2,8},{3,12},{4,1},{5,5},{6,9},{7,13},{8,2},{9,6},{10,... | collective-permute-start | bytes 983048 | tf_op jit(solution)/shard_map/ppermute | solution.py:265
  (19 other events, 400.0 us)

commit v12 on v11

--- a/solution.py
+++ b/solution.py
@@ -352,7 +352,6 @@
     rank_hidden = in_order(
         [rank_local] + [moved(rank_local, s, "ctx") for s in range(1, side)], here
     )
-    up_out_t = transposed(adapter_up_output)
     hidden_wide = owned_rows(rank_hidden, owned_here)
     xchan_part = jnp.dot(
         stream_rows, xchan_input_weight, preferred_element_type=jnp.float32
@@ -372,6 +371,8 @@
     for s in range(1, side):
         sent = block_rows(projected, (here + s) % side, length).astype(jnp.bfloat16)
         summed = summed + moved(sent, s, "ctx").astype(jnp.float32)
+    summed, up_out_local = lax.optimization_barrier((summed, adapter_up_output))
+    up_out_t = transposed(up_out_local)
     values = summed[:, : channels + bc_width]
     step_raw = summed[:, channels + bc_width :]
 

time: 271 us -> 268 us (0.989)
  starting transfers between devices: 71.4 us -> 62 us
  waiting for transfers between devices: 143 us -> 151 us
    ppermute x15, starting transfers between devices: 18.6 us -> 8 us  [moved(): return lax.ppermute(block, ('tp', 'dp'), pairs)]
    ppermute x4, waiting for transfers between devices: 29.2 us -> 38.4 us  [moved(): return lax.ppermute(block, ('ctx', 'tp', 'dp'), pairs)]
    ppermute x15, waiting for transfers between devices: 25.5 us -> 22.3 us  [moved(): return lax.ppermute(block, ('tp', 'dp'), pairs)]
    unnamed x61 -> x63, local copies, waits for them, and re-layouts: 7.59 us -> 7.59 us
  transfers between devices with their start and end apart: 35 -> 35, of which waited for: 20 -> 20; matrix products, arithmetic and copies ran while one was open for 12% -> 10% of each run, Pallas kernels for 0% -> 0%
where the time goes in v12:
time: 268 us; the launch traced here: 267 us
  waiting for transfers between devices  151 us (56%)
  starting transfers between devices  62 us (23%)
  local copies, waits for them, and re-layouts  21.4 us (8%)
  other arithmetic  15.9 us (6%)
  matrix products  15.3 us (6%)
    ppermute x12, waiting for transfers between devices, moved(): return lax.ppermute(block, 'ctx', pairs)  66.9 us
    ppermute x4, waiting for transfers between devices, moved(): return lax.ppermute(block, ('ctx', 'tp', 'dp'), pairs)  38.4 us
    ppermute x12, starting transfers between devices, moved(): return lax.ppermute(block, 'ctx', pairs)  29.5 us
    ppermute x3, waiting for transfers between devices, square_body(): both_in = lax.ppermute(state_and_decay, 'ctx', pairs).astype(jnp.float32)  23.1 us
    ppermute x15, waiting for transfers between devices, moved(): return lax.ppermute(block, ('tp', 'dp'), pairs)  22.3 us
    ppermute x4, starting transfers between devices, moved(): return lax.ppermute(block, ('ctx', 'tp', 'dp'), pairs)  12.2 us
    ppermute x3, starting transfers between devices, square_body(): both_in = lax.ppermute(state_and_decay, 'ctx', pairs).astype(jnp.float32)  10.4 us
    ppermute x15, starting transfers between devices, moved(): return lax.ppermute(block, ('tp', 'dp'), pairs)  8 us
  transfers between devices with their start and end apart: 35, of which 20 were waited for; matrix products, arithmetic and copies ran while one was open for 10% of the time, Pallas kernels for 0%

profile of v12, /device:TPU:2, one launch (start us, length us, event | category | flops | bytes accessed | tf_op | source)
XLA Modules:
  0.0 267.5 jit_solution(7310955798750909998)
XLA Ops:
  0.0 4.7 %collective-permute-start = (bf16[128,1280]{1,0:T(8,128)(2,1)}, bf16[128,1280]{1,0:T(8,128)(2,1)S(1)}, u32[]{:S(2)}, u32[]{:S(2)}) collective-permute-start(bf16[128,1280]{1,0:T(8,128)(2,1)} %param.19), channel_id=1, source_target_pairs={{0,0},{1,4},{2,8},{3,12},{4,1},{5,5},{6,9},{7,13},{8,2},{9,6},{10,... | collective-permute-start | bytes 983048 | tf_op jit(solution)/shard_map/ppermute | solution.py:265
  11.4 9.9 %collective-permute-done = bf16[128,1280]{1,0:T(8,128)(2,1)S(1)} collective-permute-done((bf16[128,1280]{1,0:T(8,128)(2,1)}, bf16[128,1280]{1,0:T(8,128)(2,1)S(1)}, u32[]{:S(2)}, u32[]{:S(2)}) %collective-permute-start) | collective-permute-done | bytes 327712 | tf_op jit(solution)/shard_map/ppermute | solution.py:265
  22.1 3.4 %collective-permute-start.5 = (bf16[2,1280,64]{1,2,0:T(8,128)(2,1)}, bf16[2,1280,64]{1,2,0:T(8,128)(2,1)}, u32[]{:S(2)}, u32[]{:S(2)}) collective-permute-start(bf16[2,1280,64]{1,2,0:T(8,128)(2,1)} %param.33), channel_id=1, source_target_pairs={{0,8},{4,12},{8,0},{12,4},{1,9},{5,13},{9,1},{13,5},{2,10},{6,14},... | collective-permute-start | bytes 983048 | tf_op jit(solution)/shard_map/ppermute | solution.py:257
  27.5 2.6 collective-permute-start.1
  33.4 20.8 %collective-permute-done.5 = bf16[2,1280,64]{1,2,0:T(8,128)(2,1)} collective-permute-done((bf16[2,1280,64]{1,2,0:T(8,128)(2,1)}, bf16[2,1280,64]{1,2,0:T(8,128)(2,1)}, u32[]{:S(2)}, u32[]{:S(2)}) %collective-permute-start.5) | collective-permute-done | bytes 327712 | tf_op jit(solution)/shard_map/ppermute | solution.py:257
  61.9 2.0 collective-permute-start.12
  69.4 1.9 collective-permute-start.15
  72.1 6.8 %collective-permute-done.15 = bf16[128,1168]{0,1:T(8,128)(2,1)S(1)} collective-permute-done((bf16[128,1168]{0,1:T(8,128)(2,1)S(1)}, bf16[128,1168]{0,1:T(8,128)(2,1)S(1)}, u32[]{:S(2)}, u32[]{:S(2)}) %collective-permute-start.15) | collective-permute-done | bytes 299040 | tf_op jit(solution)/shard_map/ppermute | solution.py:257
  79.0 17.8 %collective-permute-done.14 = bf16[128,1168]{0,1:T(8,128)(2,1)S(1)} collective-permute-done((bf16[128,1168]{0,1:T(8,128)(2,1)S(1)}, bf16[128,1168]{0,1:T(8,128)(2,1)S(1)}, u32[]{:S(2)}, u32[]{:S(2)}) %collective-permute-start.14) | collective-permute-done | bytes 299040 | tf_op jit(solution)/shard_map/ppermute | solution.py:257
  99.6 1.9 collective-permute-start.16
  103.3 3.3 %divide_multiply_fusion = f32[128,1152]{0,1:T(8,128)S(1)} fusion(f32[128,1152]{0,1:T(8,128)} %slice.97, f32[3,1152]{0,1:T(8,128)S(1)} %copy.112, f32[128]{0:T(128)S(1)} %get-tuple-element.39, f32[1152]{0:T(1024)S(1)} %get-tuple-element.14, f32[128]{0:T(128)S(1)} %get-tuple-element.40, f32[1152]{0:T(1024)S(1)} %get-tuple-element.15, ...), kind=kLoop, calls=%fused_computation.61 | loop fusion | flops 2654208 | bytes 1213952 | tf_op jit(solution)/shard_map/jit(silu)/mul | solution.py:389
  108.8 2.4 collective-permute-done.18
  114.5 6.8 %collective-permute-start.21 = (bf16[16,65,256]{2,0,1:T(8,128)(2,1)}, bf16[16,65,256]{2,0,1:T(8,128)(2,1)}, u32[]{:S(2)}, u32[]{:S(2)}) collective-permute-start(bf16[16,65,256]{2,0,1:T(8,128)(2,1)} %copy.118), channel_id=1, source_target_pairs={{0,8},{4,12},{1,9},{5,13},{2,10},{6,14},{3,11},{7,15},{16,24},{20,... | collective-permute-start | bytes 1597448 | tf_op jit(solution)/shard_map/ppermute | solution.py:408
  121.3 2.1 collective-permute-start.22
  126.0 2.2 convolution_bitcast_fusion
  128.2 5.2 %collective-permute-done.21 = bf16[16,65,256]{2,0,1:T(8,128)(2,1)} collective-permute-done((bf16[16,65,256]{2,0,1:T(8,128)(2,1)}, bf16[16,65,256]{2,0,1:T(8,128)(2,1)}, u32[]{:S(2)}, u32[]{:S(2)}) %collective-permute-start.21) | collective-permute-done | bytes 532512 | tf_op jit(solution)/shard_map/ppermute | solution.py:408
  134.6 10.3 %collective-permute-done.22 = bf16[16,65,256]{2,0,1:T(8,128)(2,1)} collective-permute-done((bf16[16,65,256]{2,0,1:T(8,128)(2,1)}, bf16[16,65,256]{2,0,1:T(8,128)(2,1)}, u32[]{:S(2)}, u32[]{:S(2)}) %collective-permute-start.22) | collective-permute-done | bytes 532512 | tf_op jit(solution)/shard_map/ppermute | solution.py:408
  146.3 7.7 %collective-permute-done.20 = bf16[16,65,256]{2,0,1:T(8,128)(2,1)S(1)} collective-permute-done((bf16[16,65,256]{2,0,1:T(8,128)(2,1)}, bf16[16,65,256]{2,0,1:T(8,128)(2,1)S(1)}, u32[]{:S(2)}, u32[]{:S(2)}) %collective-permute-start.20) | collective-permute-done | bytes 532512 | tf_op jit(solution)/shard_map/ppermute | solution.py:408
  157.4 7.0 %collective-permute-start.23 = (bf16[128,1024]{0,1:T(8,128)(2,1)}, bf16[128,1024]{0,1:T(8,128)(2,1)S(1)}, u32[]{:S(2)}, u32[]{:S(2)}) collective-permute-start(bf16[128,1024]{0,1:T(8,128)(2,1)} %fusion.34), channel_id=1, source_target_pairs={{0,12},{4,0},{8,4},{12,8},{1,13},{5,1},{9,5},{13,9},{2,14},{6,2},{... | collective-permute-start | bytes 786440 | tf_op jit(solution)/shard_map/ppermute | solution.py:257
  164.4 11.8 %collective-permute-start.24 = (bf16[128,1024]{0,1:T(8,128)(2,1)}, bf16[128,1024]{0,1:T(8,128)(2,1)}, u32[]{:S(2)}, u32[]{:S(2)}) collective-permute-start(bf16[128,1024]{0,1:T(8,128)(2,1)} %fusion.34), channel_id=1, source_target_pairs={{0,8},{4,12},{8,0},{12,4},{1,9},{5,13},{9,1},{13,5},{2,10},{6,14},... | collective-permute-start | bytes 786440 | tf_op jit(solution)/shard_map/ppermute | solution.py:257
  176.2 2.0 collective-permute-start.25
  180.0 15.5 %collective-permute-done.24 = bf16[128,1024]{0,1:T(8,128)(2,1)} collective-permute-done((bf16[128,1024]{0,1:T(8,128)(2,1)}, bf16[128,1024]{0,1:T(8,128)(2,1)}, u32[]{:S(2)}, u32[]{:S(2)}) %collective-permute-start.24) | collective-permute-done | bytes 262176 | tf_op jit(solution)/shard_map/ppermute | solution.py:257
  199.0 2.3 copy.123
  205.0 1.9 collective-permute-start.30
  206.9 2.1 collective-permute-done.26
  209.1 2.3 collective-permute-done.27
  211.4 1.9 collective-permute-start.29
  214.9 13.0 %collective-permute-done.29 = f32[512,64]{0,1:T(8,128)S(1)} collective-permute-done((f32[512,64]{0,1:T(8,128)S(1)}, f32[512,64]{0,1:T(8,128)S(1)}, u32[]{:S(2)}, u32[]{:S(2)}) %collective-permute-start.29) | collective-permute-done | bytes 131104 | tf_op jit(solution)/shard_map/ppermute | solution.py:265
  231.4 7.9 %collective-permute-done.33 = bf16[128,1280]{1,0:T(8,128)(2,1)S(1)} collective-permute-done((bf16[128,1280]{1,0:T(8,128)(2,1)}, bf16[128,1280]{1,0:T(8,128)(2,1)S(1)}, u32[]{:S(2)}, u32[]{:S(2)}) %collective-permute-start.33) | collective-permute-done | bytes 327712 | tf_op jit(solution)/shard_map/ppermute | solution.py:260
  239.3 6.8 %collective-permute-done.32 = bf16[128,1280]{1,0:T(8,128)(2,1)} collective-permute-done((bf16[128,1280]{1,0:T(8,128)(2,1)}, bf16[128,1280]{1,0:T(8,128)(2,1)}, u32[]{:S(2)}, u32[]{:S(2)}) %collective-permute-start.32) | collective-permute-done | bytes 327712 | tf_op jit(solution)/shard_map/ppermute | solution.py:260
  247.6 3.7 %collective-permute-start.34 = (bf16[128,1280]{1,0:T(8,128)(2,1)S(1)}, bf16[128,1280]{1,0:T(8,128)(2,1)S(1)}, u32[]{:S(2)}, u32[]{:S(2)}) collective-permute-start(bf16[128,1280]{1,0:T(8,128)(2,1)S(1)} %add_convert_fusion), channel_id=1, source_target_pairs={{0,0},{1,4},{2,8},{3,12},{4,1},{5,5},{6,9},{7,13},{8,2},{9,6},{10,... | collective-permute-start | bytes 983048 | tf_op jit(solution)/shard_map/ppermute | solution.py:265
  251.2 15.6 %collective-permute-done.34 = bf16[128,1280]{1,0:T(8,128)(2,1)S(1)} collective-permute-done((bf16[128,1280]{1,0:T(8,128)(2,1)S(1)}, bf16[128,1280]{1,0:T(8,128)(2,1)S(1)}, u32[]{:S(2)}, u32[]{:S(2)}) %collective-permute-start.34) | collective-permute-done | bytes 327712 | tf_op jit(solution)/shard_map/ppermute | solution.py:265
  (194 shorter events, 59.6 us)
Async XLA Ops:
  0.0 21.3 %collective-permute-start = (bf16[128,1280]{1,0:T(8,128)(2,1)}, bf16[128,1280]{1,0:T(8,128)(2,1)S(1)}, u32[]{:S(2)}, u32[]{:S(2)}) collective-permute-start(bf16[128,1280]{1,0:T(8,128)(2,1)} %param.19), channel_id=1, source_target_pairs={{0,0},{1,4},{2,8},{3,12},{4,1},{5,5},{6,9},{7,13},{8,2},{9,6},{10,... | collective-permute-start | bytes 983048 | tf_op jit(solution)/shard_map/ppermute | solution.py:265
  21.3 10.7 %collective-permute-start.6 = (bf16[2,1280,64]{1,2,0:T(8,128)(2,1)}, bf16[2,1280,64]{1,2,0:T(8,128)(2,1)}, u32[]{:S(2)}, u32[]{:S(2)}) collective-permute-start(bf16[2,1280,64]{1,2,0:T(8,128)(2,1)} %param.33), channel_id=1, source_target_pairs={{0,12},{4,0},{8,4},{12,8},{1,13},{5,1},{9,5},{13,9},{2,14},{6,2},{... | collective-permute-start | bytes 983048 | tf_op jit(solution)/shard_map/ppermute | solution.py:257
  22.1 32.2 %collective-permute-start.5 = (bf16[2,1280,64]{1,2,0:T(8,128)(2,1)}, bf16[2,1280,64]{1,2,0:T(8,128)(2,1)}, u32[]{:S(2)}, u32[]{:S(2)}) collective-permute-start(bf16[2,1280,64]{1,2,0:T(8,128)(2,1)} %param.33), channel_id=1, source_target_pairs={{0,8},{4,12},{8,0},{12,4},{1,9},{5,13},{9,1},{13,5},{2,10},{6,14},... | collective-permute-start | bytes 983048 | tf_op jit(solution)/shard_map/ppermute | solution.py:257
  27.5 28.8 %collective-permute-start.1 = (bf16[128,1280]{1,0:T(8,128)(2,1)S(1)}, bf16[128,1280]{1,0:T(8,128)(2,1)S(1)}, u32[]{:S(2)}, u32[]{:S(2)}) collective-permute-start(bf16[128,1280]{1,0:T(8,128)(2,1)S(1)} %collective-permute-done), channel_id=1, source_target_pairs={{0,3},{1,0},{2,1},{3,2},{4,7},{5,4},{6,5},{7,6},{8,11},{9,8},{10,9... | collective-permute-start | bytes 983048 | tf_op jit(solution)/shard_map/ppermute | solution.py:260
  30.1 27.0 %collective-permute-start.2 = (bf16[128,1280]{1,0:T(8,128)(2,1)S(1)}, bf16[128,1280]{1,0:T(8,128)(2,1)S(1)}, u32[]{:S(2)}, u32[]{:S(2)}) collective-permute-start(bf16[128,1280]{1,0:T(8,128)(2,1)S(1)} %collective-permute-done), channel_id=1, source_target_pairs={{0,2},{1,3},{2,0},{3,1},{4,6},{5,7},{6,4},{7,5},{8,10},{9,11},{10,... | collective-permute-start | bytes 983048 | tf_op jit(solution)/shard_map/ppermute | solution.py:260
  30.1 25.3 %collective-permute-start.4 = (bf16[2,1280,64]{1,2,0:T(8,128)(2,1)}, bf16[2,1280,64]{1,2,0:T(8,128)(2,1)S(1)}, u32[]{:S(2)}, u32[]{:S(2)}) collective-permute-start(bf16[2,1280,64]{1,2,0:T(8,128)(2,1)} %param.33), channel_id=1, source_target_pairs={{0,4},{4,8},{8,12},{12,0},{1,5},{5,9},{9,13},{13,1},{2,6},{6,10},{... | collective-permute-start | bytes 983048 | tf_op jit(solution)/shard_map/ppermute | solution.py:257
  32.0 25.2 %collective-permute-start.3 = (bf16[128,1280]{1,0:T(8,128)(2,1)S(1)}, bf16[128,1280]{1,0:T(8,128)(2,1)S(1)}, u32[]{:S(2)}, u32[]{:S(2)}) collective-permute-start(bf16[128,1280]{1,0:T(8,128)(2,1)S(1)} %collective-permute-done), channel_id=1, source_target_pairs={{0,1},{1,2},{2,3},{3,0},{4,5},{5,6},{6,7},{7,4},{8,9},{9,10},{10,1... | collective-permute-start | bytes 983048 | tf_op jit(solution)/shard_map/ppermute | solution.py:260
  55.7 5.6 %collective-permute-start.9 = (f32[128,64]{0,1:T(8,128)S(1)}, f32[128,64]{0,1:T(8,128)S(1)}, u32[]{:S(2)}, u32[]{:S(2)}) collective-permute-start(f32[128,64]{0,1:T(8,128)S(1)} %add_add_fusion.1), channel_id=1, source_target_pairs={{0,3},{1,0},{2,1},{3,2},{4,7},{5,4},{6,5},{7,6},{8,11},{9,8},{10,9... | collective-permute-start | bytes 98312 | tf_op jit(solution)/shard_map/ppermute | solution.py:260
  55.8 5.5 %collective-permute-start.7 = (f32[128,64]{0,1:T(8,128)S(1)}, f32[128,64]{0,1:T(8,128)S(1)}, u32[]{:S(2)}, u32[]{:S(2)}) collective-permute-start(f32[128,64]{0,1:T(8,128)S(1)} %add_add_fusion.1), channel_id=1, source_target_pairs={{0,1},{1,2},{2,3},{3,0},{4,5},{5,6},{6,7},{7,4},{8,9},{9,10},{10,1... | collective-permute-start | bytes 98312 | tf_op jit(solution)/shard_map/ppermute | solution.py:260
  56.3 5.0 %collective-permute-start.8 = (f32[128,64]{0,1:T(8,128)S(1)}, f32[128,64]{0,1:T(8,128)S(1)}, u32[]{:S(2)}, u32[]{:S(2)}) collective-permute-start(f32[128,64]{0,1:T(8,128)S(1)} %add_add_fusion.1), channel_id=1, source_target_pairs={{0,2},{1,3},{2,0},{3,1},{4,6},{5,7},{6,4},{7,5},{8,10},{9,11},{10,... | collective-permute-start | bytes 98312 | tf_op jit(solution)/shard_map/ppermute | solution.py:260
  61.3 3.8 %collective-permute-start.10 = (bf16[128,64]{0,1:T(8,128)(2,1)S(1)}, bf16[128,64]{0,1:T(8,128)(2,1)S(1)}, u32[]{:S(2)}, u32[]{:S(2)}) collective-permute-start(bf16[128,64]{0,1:T(8,128)(2,1)S(1)} %add_convert_fusion.1), channel_id=1, source_target_pairs={{0,12},{4,0},{8,4},{12,8},{1,13},{5,1},{9,5},{13,9},{2,14},{6,2},{... | collective-permute-start | bytes 49160 | tf_op jit(solution)/shard_map/ppermute | solution.py:257
  61.9 4.7 %collective-permute-start.11 = (bf16[128,64]{0,1:T(8,128)(2,1)S(1)}, bf16[128,64]{0,1:T(8,128)(2,1)S(1)}, u32[]{:S(2)}, u32[]{:S(2)}) collective-permute-start(bf16[128,64]{0,1:T(8,128)(2,1)S(1)} %add_convert_fusion.1), channel_id=1, source_target_pairs={{0,8},{4,12},{8,0},{12,4},{1,9},{5,13},{9,1},{13,5},{2,10},{6,14},... | collective-permute-start | bytes 49160 | tf_op jit(solution)/shard_map/ppermute | solution.py:257
  61.9 6.3 %collective-permute-start.12 = (bf16[128,64]{0,1:T(8,128)(2,1)S(1)}, bf16[128,64]{0,1:T(8,128)(2,1)S(1)}, u32[]{:S(2)}, u32[]{:S(2)}) collective-permute-start(bf16[128,64]{0,1:T(8,128)(2,1)S(1)} %add_convert_fusion.1), channel_id=1, source_target_pairs={{0,4},{4,8},{8,12},{12,0},{1,5},{5,9},{9,13},{13,1},{2,6},{6,10},{... | collective-permute-start | bytes 49160 | tf_op jit(solution)/shard_map/ppermute | solution.py:257
  69.4 9.5 %collective-permute-start.15 = (bf16[128,1168]{0,1:T(8,128)(2,1)S(1)}, bf16[128,1168]{0,1:T(8,128)(2,1)S(1)}, u32[]{:S(2)}, u32[]{:S(2)}) collective-permute-start(bf16[128,1168]{0,1:T(8,128)(2,1)S(1)} %get-tuple-element.27), channel_id=1, source_target_pairs={{0,12},{4,0},{8,4},{12,8},{1,13},{5,1},{9,5},{13,9},{2,14},{6,2},{... | collective-permute-start | bytes 897032 | tf_op jit(solution)/shard_map/ppermute | solution.py:257
  71.4 25.3 %collective-permute-start.14 = (bf16[128,1168]{0,1:T(8,128)(2,1)S(1)}, bf16[128,1168]{0,1:T(8,128)(2,1)S(1)}, u32[]{:S(2)}, u32[]{:S(2)}) collective-permute-start(bf16[128,1168]{0,1:T(8,128)(2,1)S(1)} %get-tuple-element.28), channel_id=1, source_target_pairs={{0,8},{4,12},{8,0},{12,4},{1,9},{5,13},{9,1},{13,5},{2,10},{6,14},... | collective-permute-start | bytes 897032 | tf_op jit(solution)/shard_map/ppermute | solution.py:257
  71.4 25.3 %collective-permute-start.13 = (bf16[128,1168]{0,1:T(8,128)(2,1)S(1)}, bf16[128,1168]{0,1:T(8,128)(2,1)S(1)}, u32[]{:S(2)}, u32[]{:S(2)}) collective-permute-start(bf16[128,1168]{0,1:T(8,128)(2,1)S(1)} %get-tuple-element.26), channel_id=1, source_target_pairs={{0,4},{4,8},{8,12},{12,0},{1,5},{5,9},{9,13},{13,1},{2,6},{6,10},{... | collective-permute-start | bytes 897032 | tf_op jit(solution)/shard_map/ppermute | solution.py:257
  107.2 4.0 %collective-permute-start.18 = (bf16[128,128]{0,1:T(8,128)(2,1)S(1)}, bf16[128,128]{0,1:T(8,128)(2,1)S(1)}, u32[]{:S(2)}, u32[]{:S(2)}) collective-permute-start(bf16[128,128]{0,1:T(8,128)(2,1)S(1)} %slice.239), channel_id=1, source_target_pairs={{0,2},{1,3},{2,0},{3,1},{4,6},{5,7},{6,4},{7,5},{8,10},{9,11},{10,... | collective-permute-start | bytes 98312 | tf_op jit(solution)/shard_map/ppermute | solution.py:260
  114.5 18.9 %collective-permute-start.21 = (bf16[16,65,256]{2,0,1:T(8,128)(2,1)}, bf16[16,65,256]{2,0,1:T(8,128)(2,1)}, u32[]{:S(2)}, u32[]{:S(2)}) collective-permute-start(bf16[16,65,256]{2,0,1:T(8,128)(2,1)} %copy.118), channel_id=1, source_target_pairs={{0,8},{4,12},{1,9},{5,13},{2,10},{6,14},{3,11},{7,15},{16,24},{20,... | collective-permute-start | bytes 1597448 | tf_op jit(solution)/shard_map/ppermute | solution.py:408
  121.3 23.5 %collective-permute-start.22 = (bf16[16,65,256]{2,0,1:T(8,128)(2,1)}, bf16[16,65,256]{2,0,1:T(8,128)(2,1)}, u32[]{:S(2)}, u32[]{:S(2)}) collective-permute-start(bf16[16,65,256]{2,0,1:T(8,128)(2,1)} %copy.118), channel_id=1, source_target_pairs={{0,12},{1,13},{2,14},{3,15},{16,28},{17,29},{18,30},{19,31}} | collective-permute-start | bytes 1597448 | tf_op jit(solution)/shard_map/ppermute | solution.py:408
  124.3 29.7 %collective-permute-start.20 = (bf16[16,65,256]{2,0,1:T(8,128)(2,1)}, bf16[16,65,256]{2,0,1:T(8,128)(2,1)S(1)}, u32[]{:S(2)}, u32[]{:S(2)}) collective-permute-start(bf16[16,65,256]{2,0,1:T(8,128)(2,1)} %copy.118), channel_id=1, source_target_pairs={{0,4},{4,8},{8,12},{1,5},{5,9},{9,13},{2,6},{6,10},{10,14},{3,7},{... | collective-permute-start | bytes 1597448 | tf_op jit(solution)/shard_map/ppermute | solution.py:408
  157.4 22.6 %collective-permute-start.23 = (bf16[128,1024]{0,1:T(8,128)(2,1)}, bf16[128,1024]{0,1:T(8,128)(2,1)S(1)}, u32[]{:S(2)}, u32[]{:S(2)}) collective-permute-start(bf16[128,1024]{0,1:T(8,128)(2,1)} %fusion.34), channel_id=1, source_target_pairs={{0,12},{4,0},{8,4},{12,8},{1,13},{5,1},{9,5},{13,9},{2,14},{6,2},{... | collective-permute-start | bytes 786440 | tf_op jit(solution)/shard_map/ppermute | solution.py:257
  164.4 31.1 %collective-permute-start.24 = (bf16[128,1024]{0,1:T(8,128)(2,1)}, bf16[128,1024]{0,1:T(8,128)(2,1)}, u32[]{:S(2)}, u32[]{:S(2)}) collective-permute-start(bf16[128,1024]{0,1:T(8,128)(2,1)} %fusion.34), channel_id=1, source_target_pairs={{0,8},{4,12},{8,0},{12,4},{1,9},{5,13},{9,1},{13,5},{2,10},{6,14},... | collective-permute-start | bytes 786440 | tf_op jit(solution)/shard_map/ppermute | solution.py:257
  176.2 20.3 %collective-permute-start.25 = (bf16[128,1024]{0,1:T(8,128)(2,1)}, bf16[128,1024]{0,1:T(8,128)(2,1)S(1)}, u32[]{:S(2)}, u32[]{:S(2)}) collective-permute-start(bf16[128,1024]{0,1:T(8,128)(2,1)} %fusion.34), channel_id=1, source_target_pairs={{0,4},{4,8},{8,12},{12,0},{1,5},{5,9},{9,13},{13,1},{2,6},{6,10},{... | collective-permute-start | bytes 786440 | tf_op jit(solution)/shard_map/ppermute | solution.py:257
  203.2 3.8 %collective-permute-start.28 = (f32[512,64]{0,1:T(8,128)S(1)}, f32[512,64]{0,1:T(8,128)S(1)}, u32[]{:S(2)}, u32[]{:S(2)}) collective-permute-start(f32[512,64]{0,1:T(8,128)S(1)} %multiply_reduce_fusion.1), channel_id=1, source_target_pairs={{0,3},{1,0},{2,1},{3,2},{4,7},{5,4},{6,5},{7,6},{8,11},{9,8},{10,9... | collective-permute-start | bytes 393224 | tf_op jit(solution)/shard_map/ppermute | solution.py:260
  203.2 5.8 %collective-permute-start.26 = (f32[512,64]{0,1:T(8,128)S(1)}, f32[512,64]{0,1:T(8,128)S(1)}, u32[]{:S(2)}, u32[]{:S(2)}) collective-permute-start(f32[512,64]{0,1:T(8,128)S(1)} %multiply_reduce_fusion.1), channel_id=1, source_target_pairs={{0,1},{1,2},{2,3},{3,0},{4,5},{5,6},{6,7},{7,4},{8,9},{9,10},{10,1... | collective-permute-start | bytes 393224 | tf_op jit(solution)/shard_map/ppermute | solution.py:260
  203.7 7.7 %collective-permute-start.27 = (f32[512,64]{0,1:T(8,128)S(1)}, f32[512,64]{0,1:T(8,128)S(1)}, u32[]{:S(2)}, u32[]{:S(2)}) collective-permute-start(f32[512,64]{0,1:T(8,128)S(1)} %multiply_reduce_fusion.1), channel_id=1, source_target_pairs={{0,2},{1,3},{2,0},{3,1},{4,6},{5,7},{6,4},{7,5},{8,10},{9,11},{10,... | collective-permute-start | bytes 393224 | tf_op jit(solution)/shard_map/ppermute | solution.py:260
  205.0 22.9 %collective-permute-start.30 = (bf16[2,64,1280]{2,1,0:T(8,128)(2,1)S(1)}, bf16[2,64,1280]{2,1,0:T(8,128)(2,1)S(1)}, u32[]{:S(2)}, u32[]{:S(2)}) collective-permute-start(bf16[2,64,1280]{2,1,0:T(8,128)(2,1)S(1)} %copy-done.16), channel_id=1, source_target_pairs={{0,0},{1,4},{2,8},{3,12},{4,1},{5,5},{6,9},{7,13},{8,2},{9,6},{10,... | collective-permute-start | bytes 983048 | tf_op jit(solution)/shard_map/ppermute | solution.py:265
  211.4 16.4 %collective-permute-start.29 = (f32[512,64]{0,1:T(8,128)S(1)}, f32[512,64]{0,1:T(8,128)S(1)}, u32[]{:S(2)}, u32[]{:S(2)}) collective-permute-start(f32[512,64]{0,1:T(8,128)S(1)} %add_add_fusion), channel_id=1, source_target_pairs={{0,0},{1,4},{2,8},{3,12},{4,1},{5,5},{6,9},{7,13},{8,2},{9,6},{10,... | collective-permute-start | bytes 393224 | tf_op jit(solution)/shard_map/ppermute | solution.py:265
  230.8 8.4 %collective-permute-start.33 = (bf16[128,1280]{1,0:T(8,128)(2,1)}, bf16[128,1280]{1,0:T(8,128)(2,1)S(1)}, u32[]{:S(2)}, u32[]{:S(2)}) collective-permute-start(bf16[128,1280]{1,0:T(8,128)(2,1)} %get-tuple-element.24), channel_id=1, source_target_pairs={{0,3},{1,0},{2,1},{3,2},{4,7},{5,4},{6,5},{7,6},{8,11},{9,8},{10,9... | collective-permute-start | bytes 983048 | tf_op jit(solution)/shard_map/ppermute | solution.py:260
  230.9 15.3 %collective-permute-start.32 = (bf16[128,1280]{1,0:T(8,128)(2,1)}, bf16[128,1280]{1,0:T(8,128)(2,1)}, u32[]{:S(2)}, u32[]{:S(2)}) collective-permute-start(bf16[128,1280]{1,0:T(8,128)(2,1)} %get-tuple-element.25), channel_id=1, source_target_pairs={{0,2},{1,3},{2,0},{3,1},{4,6},{5,7},{6,4},{7,5},{8,10},{9,11},{10,... | collective-permute-start | bytes 983048 | tf_op jit(solution)/shard_map/ppermute | solution.py:260
  230.9 15.3 %collective-permute-start.31 = (bf16[128,1280]{1,0:T(8,128)(2,1)S(1)}, bf16[128,1280]{1,0:T(8,128)(2,1)}, u32[]{:S(2)}, u32[]{:S(2)}) collective-permute-start(bf16[128,1280]{1,0:T(8,128)(2,1)S(1)} %get-tuple-element.23), channel_id=1, source_target_pairs={{0,1},{1,2},{2,3},{3,0},{4,5},{5,6},{6,7},{7,4},{8,9},{9,10},{10,1... | collective-permute-start | bytes 983048 | tf_op jit(solution)/shard_map/ppermute | solution.py:260
  247.6 19.2 %collective-permute-start.34 = (bf16[128,1280]{1,0:T(8,128)(2,1)S(1)}, bf16[128,1280]{1,0:T(8,128)(2,1)S(1)}, u32[]{:S(2)}, u32[]{:S(2)}) collective-permute-start(bf16[128,1280]{1,0:T(8,128)(2,1)S(1)} %add_convert_fusion), channel_id=1, source_target_pairs={{0,0},{1,4},{2,8},{3,12},{4,1},{5,5},{6,9},{7,13},{8,2},{9,6},{10,... | collective-permute-start | bytes 983048 | tf_op jit(solution)/shard_map/ppermute | solution.py:265
  (20 other events, 384.8 us)

commit v13 on v12

--- a/solution.py
+++ b/solution.py
@@ -402,11 +402,25 @@
 
     decay_row = jnp.broadcast_to(carry_decay[:, None, None], (head_count, 1, local_state.shape[2]))
     state_and_decay = jnp.concatenate([decay_row, local_state], axis=1).astype(jnp.bfloat16)
-    entering = jnp.zeros_like(local_state)
-    for s in range(side - 1, 0, -1):
-        pairs = [(a, a + s) for a in range(side - s)]
-        both_in = lax.ppermute(state_and_decay, "ctx", pairs).astype(jnp.float32)
-        entering = both_in[:, :1, :1] * entering + both_in[:, 1:]
+    if side <= 4:
+        prior = lax.ppermute(
+            state_and_decay, "ctx", [(a, a + 1) for a in range(side - 1)]
+        ).astype(jnp.float32)
+        pair_decay = prior[:, :1, :1] * carry_decay[:, None, None]
+        pair_state = carry_decay[:, None, None] * prior[:, 1:] + local_state
+        pair = jnp.concatenate(
+            [jnp.broadcast_to(pair_decay, decay_row.shape), pair_state], axis=1
+        ).astype(jnp.bfloat16)
+        entering = prior[:, 1:]
+        if side > 2:
+            far = lax.ppermute(pair, "ctx", [(a, a + 2) for a in range(side - 2)])
+            entering = prior[:, :1, :1] * far[:, 1:].astype(jnp.float32) + entering
+    else:
+        entering = jnp.zeros_like(local_state)
+        for s in range(side - 1, 0, -1):
+            pairs = [(a, a + s) for a in range(side - s)]
+            both_in = lax.ppermute(state_and_decay, "ctx", pairs).astype(jnp.float32)
+            entering = both_in[:, :1, :1] * entering + both_in[:, 1:]
     entered = (
         jnp.einsum("tn,hdn->thd", c_proj.astype(jnp.float32), entering, precision=FULL_PRECISION)
         * enter_weight[:, :, None]

time: 268 us -> 261 us (0.974)
  waiting for transfers between devices: 151 us -> 146 us
  other arithmetic: 15.9 us -> 12.4 us
    ppermute x3 -> x2, waiting for transfers between devices: 23.1 us -> 15.8 us  [the longest x1 9.32 us: square_body(): lax.ppermute(state_and_decay, 'ctx', [(a, a + 1) for a in range(side - 1)])]
    ppermute x12, starting transfers between devices: 29.5 us -> 24 us  [moved(): return lax.ppermute(block, 'ctx', pairs)]
    ppermute x4, starting transfers between devices: 12.2 us -> 16 us  [moved(): return lax.ppermute(block, ('ctx', 'tp', 'dp'), pairs)]
    ppermute x4, waiting for transfers between devices: 38.4 us -> 41.5 us  [moved(): return lax.ppermute(block, ('ctx', 'tp', 'dp'), pairs)]
    ppermute x3 -> x2, starting transfers between devices: 10.4 us -> 11.5 us  [the longest x1 6.34 us: square_body(): far = lax.ppermute(pair, 'ctx', [(a, a + 2) for a in range(side - 2)])]
    unnamed x63 -> x61, local copies, waits for them, and re-layouts: 7.59 us -> 7 us
  transfers between devices with their start and end apart: 35 -> 34, of which waited for: 20 -> 18; matrix products, arithmetic and copies ran while one was open for 10% -> 8% of each run, Pallas kernels for 0% -> 0%
where the time goes in v13:
time: 261 us; the launch traced here: 260 us
  waiting for transfers between devices  146 us (56%)
  starting transfers between devices  61.7 us (24%)
  local copies, waits for them, and re-layouts  20.4 us (8%)
  matrix products  17.2 us (7%)
  other arithmetic  12.4 us (5%)
    ppermute x12, waiting for transfers between devices, moved(): return lax.ppermute(block, 'ctx', pairs)  68.8 us
    ppermute x4, waiting for transfers between devices, moved(): return lax.ppermute(block, ('ctx', 'tp', 'dp'), pairs)  41.5 us
    ppermute x12, starting transfers between devices, moved(): return lax.ppermute(block, 'ctx', pairs)  24 us
    ppermute x15, waiting for transfers between devices, moved(): return lax.ppermute(block, ('tp', 'dp'), pairs)  20.3 us
    ppermute x4, starting transfers between devices, moved(): return lax.ppermute(block, ('ctx', 'tp', 'dp'), pairs)  16 us
    ppermute x1, waiting for transfers between devices, square_body(): lax.ppermute(state_and_decay, 'ctx', [(a, a + 1) for a in range(side - 1)])  9.32 us
    ppermute x15, starting transfers between devices, moved(): return lax.ppermute(block, ('tp', 'dp'), pairs)  8.38 us
    unnamed x61, local copies, waits for them, and re-layouts  7 us
  transfers between devices with their start and end apart: 34, of which 18 were waited for; matrix products, arithmetic and copies ran while one was open for 8% of the time, Pallas kernels for 0%

profile of v13, /device:TPU:2, one launch (start us, length us, event | category | flops | bytes accessed | tf_op | source)
XLA Modules:
  0.0 260.4 jit_solution(1324558066834023190)
XLA Ops:
  0.0 4.7 %collective-permute-start = (bf16[128,1280]{1,0:T(8,128)(2,1)}, bf16[128,1280]{1,0:T(8,128)(2,1)S(1)}, u32[]{:S(2)}, u32[]{:S(2)}) collective-permute-start(bf16[128,1280]{1,0:T(8,128)(2,1)} %param.19), channel_id=1, source_target_pairs={{0,0},{1,4},{2,8},{3,12},{4,1},{5,5},{6,9},{7,13},{8,2},{9,6},{10,... | collective-permute-start | bytes 983048 | tf_op jit(solution)/shard_map/ppermute | solution.py:265
  9.6 11.8 %collective-permute-done = bf16[128,1280]{1,0:T(8,128)(2,1)S(1)} collective-permute-done((bf16[128,1280]{1,0:T(8,128)(2,1)}, bf16[128,1280]{1,0:T(8,128)(2,1)S(1)}, u32[]{:S(2)}, u32[]{:S(2)}) %collective-permute-start) | collective-permute-done | bytes 327712 | tf_op jit(solution)/shard_map/ppermute | solution.py:265
  22.1 3.4 %collective-permute-start.5 = (bf16[2,1280,64]{1,2,0:T(8,128)(2,1)}, bf16[2,1280,64]{1,2,0:T(8,128)(2,1)}, u32[]{:S(2)}, u32[]{:S(2)}) collective-permute-start(bf16[2,1280,64]{1,2,0:T(8,128)(2,1)} %param.33), channel_id=1, source_target_pairs={{0,8},{4,12},{8,0},{12,4},{1,9},{5,13},{9,1},{13,5},{2,10},{6,14},... | collective-permute-start | bytes 983048 | tf_op jit(solution)/shard_map/ppermute | solution.py:257
  28.1 2.7 %collective-permute-start.1 = (bf16[128,1280]{1,0:T(8,128)(2,1)S(1)}, bf16[128,1280]{1,0:T(8,128)(2,1)S(1)}, u32[]{:S(2)}, u32[]{:S(2)}) collective-permute-start(bf16[128,1280]{1,0:T(8,128)(2,1)S(1)} %collective-permute-done), channel_id=1, source_target_pairs={{0,3},{1,0},{2,1},{3,2},{4,7},{5,4},{6,5},{7,6},{8,11},{9,8},{10,9... | collective-permute-start | bytes 983048 | tf_op jit(solution)/shard_map/ppermute | solution.py:260
  34.1 20.1 %collective-permute-done.5 = bf16[2,1280,64]{1,2,0:T(8,128)(2,1)} collective-permute-done((bf16[2,1280,64]{1,2,0:T(8,128)(2,1)}, bf16[2,1280,64]{1,2,0:T(8,128)(2,1)}, u32[]{:S(2)}, u32[]{:S(2)}) %collective-permute-start.5) | collective-permute-done | bytes 327712 | tf_op jit(solution)/shard_map/ppermute | solution.py:257
  61.9 2.0 collective-permute-start.12
  66.5 1.6 collective-permute-done.12
  69.4 1.9 collective-permute-start.15
  72.8 6.2 %collective-permute-done.15 = bf16[128,1168]{0,1:T(8,128)(2,1)S(1)} collective-permute-done((bf16[128,1168]{0,1:T(8,128)(2,1)S(1)}, bf16[128,1168]{0,1:T(8,128)(2,1)S(1)}, u32[]{:S(2)}, u32[]{:S(2)}) %collective-permute-start.15) | collective-permute-done | bytes 299040 | tf_op jit(solution)/shard_map/ppermute | solution.py:257
  79.0 17.8 %collective-permute-done.14 = bf16[128,1168]{0,1:T(8,128)(2,1)S(1)} collective-permute-done((bf16[128,1168]{0,1:T(8,128)(2,1)S(1)}, bf16[128,1168]{0,1:T(8,128)(2,1)S(1)}, u32[]{:S(2)}, u32[]{:S(2)}) %collective-permute-start.14) | collective-permute-done | bytes 299040 | tf_op jit(solution)/shard_map/ppermute | solution.py:257
  99.1 1.9 collective-permute-start.16
  102.7 3.3 %divide_multiply_fusion = f32[128,1152]{0,1:T(8,128)S(1)} fusion(f32[128,1152]{0,1:T(8,128)} %slice.90, f32[3,1152]{0,1:T(8,128)S(1)} %copy.118, f32[128]{0:T(128)S(1)} %get-tuple-element.43, f32[1152]{0:T(1024)S(1)} %get-tuple-element.14, f32[128]{0:T(128)S(1)} %get-tuple-element.44, f32[1152]{0:T(1024)S(1)} %get-tuple-element.15, ...), kind=kLoop, calls=%fused_computation.61 | loop fusion | flops 2654208 | bytes 1213952 | tf_op jit(solution)/shard_map/jit(silu)/mul | solution.py:389
  107.7 2.4 collective-permute-done.18
  113.8 5.2 %collective-permute-start.20 = (bf16[16,65,256]{2,0,1:T(8,128)(2,1)}, bf16[16,65,256]{2,0,1:T(8,128)(2,1)}, u32[]{:S(2)}, u32[]{:S(2)}) collective-permute-start(bf16[16,65,256]{2,0,1:T(8,128)(2,1)} %copy.124), channel_id=1, source_target_pairs={{0,4},{4,8},{8,12},{1,5},{5,9},{9,13},{2,6},{6,10},{10,14},{3,7},{... | collective-permute-start | bytes 1597448 | tf_op jit(solution)/shard_map/ppermute | solution.py:406
  119.4 9.3 %collective-permute-done.20 = bf16[16,65,256]{2,0,1:T(8,128)(2,1)} collective-permute-done((bf16[16,65,256]{2,0,1:T(8,128)(2,1)}, bf16[16,65,256]{2,0,1:T(8,128)(2,1)}, u32[]{:S(2)}, u32[]{:S(2)}) %collective-permute-start.20) | collective-permute-done | bytes 532512 | tf_op jit(solution)/shard_map/ppermute | solution.py:406
  130.8 6.3 %collective-permute-start.21 = (bf16[16,65,256]{2,0,1:T(8,128)(2,1)S(1)}, bf16[16,65,256]{2,0,1:T(8,128)(2,1)S(1)}, u32[]{:S(2)}, u32[]{:S(2)}) collective-permute-start(bf16[16,65,256]{2,0,1:T(8,128)(2,1)S(1)} %copy.127), channel_id=1, source_target_pairs={{0,8},{4,12},{1,9},{5,13},{2,10},{6,14},{3,11},{7,15},{16,24},{20,... | collective-permute-start | bytes 1597448 | tf_op jit(solution)/shard_map/ppermute | solution.py:416
  137.3 2.2 convolution_bitcast_fusion
  139.7 6.5 %collective-permute-done.21 = bf16[16,65,256]{2,0,1:T(8,128)(2,1)S(1)} collective-permute-done((bf16[16,65,256]{2,0,1:T(8,128)(2,1)S(1)}, bf16[16,65,256]{2,0,1:T(8,128)(2,1)S(1)}, u32[]{:S(2)}, u32[]{:S(2)}) %collective-permute-start.21) | collective-permute-done | bytes 532512 | tf_op jit(solution)/shard_map/ppermute | solution.py:416
  146.3 2.1 multiply_reduce_fusion
  149.3 14.8 %collective-permute-start.22 = (bf16[128,1024]{0,1:T(8,128)(2,1)}, bf16[128,1024]{0,1:T(8,128)(2,1)S(1)}, u32[]{:S(2)}, u32[]{:S(2)}) collective-permute-start(bf16[128,1024]{0,1:T(8,128)(2,1)} %fusion.36), channel_id=1, source_target_pairs={{0,12},{4,0},{8,4},{12,8},{1,13},{5,1},{9,5},{13,9},{2,14},{6,2},{... | collective-permute-start | bytes 786440 | tf_op jit(solution)/shard_map/ppermute | solution.py:257
  164.6 6.6 %collective-permute-done.22 = bf16[128,1024]{0,1:T(8,128)(2,1)S(1)} collective-permute-done((bf16[128,1024]{0,1:T(8,128)(2,1)}, bf16[128,1024]{0,1:T(8,128)(2,1)S(1)}, u32[]{:S(2)}, u32[]{:S(2)}) %collective-permute-start.22) | collective-permute-done | bytes 262176 | tf_op jit(solution)/shard_map/ppermute | solution.py:257
  171.2 13.9 %collective-permute-done.23 = bf16[128,1024]{0,1:T(8,128)(2,1)} collective-permute-done((bf16[128,1024]{0,1:T(8,128)(2,1)}, bf16[128,1024]{0,1:T(8,128)(2,1)}, u32[]{:S(2)}, u32[]{:S(2)}) %collective-permute-start.23) | collective-permute-done | bytes 262176 | tf_op jit(solution)/shard_map/ppermute | solution.py:257
  188.6 2.3 copy.130
  190.9 1.8 fusion.77
  194.9 4.1 %collective-permute-start.29 = (bf16[2,64,1280]{2,1,0:T(8,128)(2,1)S(1)}, bf16[2,64,1280]{2,1,0:T(8,128)(2,1)S(1)}, u32[]{:S(2)}, u32[]{:S(2)}) collective-permute-start(bf16[2,64,1280]{2,1,0:T(8,128)(2,1)S(1)} %copy-done.15), channel_id=1, source_target_pairs={{0,0},{1,4},{2,8},{3,12},{4,1},{5,5},{6,9},{7,13},{8,2},{9,6},{10,... | collective-permute-start | bytes 983048 | tf_op jit(solution)/shard_map/ppermute | solution.py:265
  199.0 2.4 collective-permute-done.26
  201.5 3.6 %collective-permute-start.28 = (f32[512,64]{0,1:T(8,128)S(1)}, f32[512,64]{0,1:T(8,128)S(1)}, u32[]{:S(2)}, u32[]{:S(2)}) collective-permute-start(f32[512,64]{0,1:T(8,128)S(1)} %add_add_fusion), channel_id=1, source_target_pairs={{0,0},{1,4},{2,8},{3,12},{4,1},{5,5},{6,9},{7,13},{8,2},{9,6},{10,... | collective-permute-start | bytes 393224 | tf_op jit(solution)/shard_map/ppermute | solution.py:265
  206.7 14.0 %collective-permute-done.28 = f32[512,64]{0,1:T(8,128)S(1)} collective-permute-done((f32[512,64]{0,1:T(8,128)S(1)}, f32[512,64]{0,1:T(8,128)S(1)}, u32[]{:S(2)}, u32[]{:S(2)}) %collective-permute-start.28) | collective-permute-done | bytes 131104 | tf_op jit(solution)/shard_map/ppermute | solution.py:265
  224.2 7.9 %collective-permute-done.32 = bf16[128,1280]{1,0:T(8,128)(2,1)S(1)} collective-permute-done((bf16[128,1280]{1,0:T(8,128)(2,1)}, bf16[128,1280]{1,0:T(8,128)(2,1)S(1)}, u32[]{:S(2)}, u32[]{:S(2)}) %collective-permute-start.32) | collective-permute-done | bytes 327712 | tf_op jit(solution)/shard_map/ppermute | solution.py:260
  232.1 6.8 %collective-permute-done.31 = bf16[128,1280]{1,0:T(8,128)(2,1)} collective-permute-done((bf16[128,1280]{1,0:T(8,128)(2,1)}, bf16[128,1280]{1,0:T(8,128)(2,1)}, u32[]{:S(2)}, u32[]{:S(2)}) %collective-permute-start.31) | collective-permute-done | bytes 327712 | tf_op jit(solution)/shard_map/ppermute | solution.py:260
  240.4 3.5 %collective-permute-start.33 = (bf16[128,1280]{1,0:T(8,128)(2,1)S(1)}, bf16[128,1280]{1,0:T(8,128)(2,1)S(1)}, u32[]{:S(2)}, u32[]{:S(2)}) collective-permute-start(bf16[128,1280]{1,0:T(8,128)(2,1)S(1)} %add_convert_fusion.1), channel_id=1, source_target_pairs={{0,0},{1,4},{2,8},{3,12},{4,1},{5,5},{6,9},{7,13},{8,2},{9,6},{10,... | collective-permute-start | bytes 983048 | tf_op jit(solution)/shard_map/ppermute | solution.py:265
  243.9 15.7 %collective-permute-done.33 = bf16[128,1280]{1,0:T(8,128)(2,1)S(1)} collective-permute-done((bf16[128,1280]{1,0:T(8,128)(2,1)S(1)}, bf16[128,1280]{1,0:T(8,128)(2,1)S(1)}, u32[]{:S(2)}, u32[]{:S(2)}) %collective-permute-start.33) | collective-permute-done | bytes 327712 | tf_op jit(solution)/shard_map/ppermute | solution.py:265
  (192 shorter events, 49.2 us)
Async XLA Ops:
  0.0 21.3 %collective-permute-start = (bf16[128,1280]{1,0:T(8,128)(2,1)}, bf16[128,1280]{1,0:T(8,128)(2,1)S(1)}, u32[]{:S(2)}, u32[]{:S(2)}) collective-permute-start(bf16[128,1280]{1,0:T(8,128)(2,1)} %param.19), channel_id=1, source_target_pairs={{0,0},{1,4},{2,8},{3,12},{4,1},{5,5},{6,9},{7,13},{8,2},{9,6},{10,... | collective-permute-start | bytes 983048 | tf_op jit(solution)/shard_map/ppermute | solution.py:265
  21.3 11.3 %collective-permute-start.6 = (bf16[2,1280,64]{1,2,0:T(8,128)(2,1)}, bf16[2,1280,64]{1,2,0:T(8,128)(2,1)}, u32[]{:S(2)}, u32[]{:S(2)}) collective-permute-start(bf16[2,1280,64]{1,2,0:T(8,128)(2,1)} %param.33), channel_id=1, source_target_pairs={{0,12},{4,0},{8,4},{12,8},{1,13},{5,1},{9,5},{13,9},{2,14},{6,2},{... | collective-permute-start | bytes 983048 | tf_op jit(solution)/shard_map/ppermute | solution.py:257
  22.1 32.2 %collective-permute-start.5 = (bf16[2,1280,64]{1,2,0:T(8,128)(2,1)}, bf16[2,1280,64]{1,2,0:T(8,128)(2,1)}, u32[]{:S(2)}, u32[]{:S(2)}) collective-permute-start(bf16[2,1280,64]{1,2,0:T(8,128)(2,1)} %param.33), channel_id=1, source_target_pairs={{0,8},{4,12},{8,0},{12,4},{1,9},{5,13},{9,1},{13,5},{2,10},{6,14},... | collective-permute-start | bytes 983048 | tf_op jit(solution)/shard_map/ppermute | solution.py:257
  28.1 28.2 %collective-permute-start.1 = (bf16[128,1280]{1,0:T(8,128)(2,1)S(1)}, bf16[128,1280]{1,0:T(8,128)(2,1)S(1)}, u32[]{:S(2)}, u32[]{:S(2)}) collective-permute-start(bf16[128,1280]{1,0:T(8,128)(2,1)S(1)} %collective-permute-done), channel_id=1, source_target_pairs={{0,3},{1,0},{2,1},{3,2},{4,7},{5,4},{6,5},{7,6},{8,11},{9,8},{10,9... | collective-permute-start | bytes 983048 | tf_op jit(solution)/shard_map/ppermute | solution.py:260
  30.8 26.4 %collective-permute-start.2 = (bf16[128,1280]{1,0:T(8,128)(2,1)S(1)}, bf16[128,1280]{1,0:T(8,128)(2,1)S(1)}, u32[]{:S(2)}, u32[]{:S(2)}) collective-permute-start(bf16[128,1280]{1,0:T(8,128)(2,1)S(1)} %collective-permute-done), channel_id=1, source_target_pairs={{0,2},{1,3},{2,0},{3,1},{4,6},{5,7},{6,4},{7,5},{8,10},{9,11},{10,... | collective-permute-start | bytes 983048 | tf_op jit(solution)/shard_map/ppermute | solution.py:260
  30.8 24.7 %collective-permute-start.4 = (bf16[2,1280,64]{1,2,0:T(8,128)(2,1)}, bf16[2,1280,64]{1,2,0:T(8,128)(2,1)S(1)}, u32[]{:S(2)}, u32[]{:S(2)}) collective-permute-start(bf16[2,1280,64]{1,2,0:T(8,128)(2,1)} %param.33), channel_id=1, source_target_pairs={{0,4},{4,8},{8,12},{12,0},{1,5},{5,9},{9,13},{13,1},{2,6},{6,10},{... | collective-permute-start | bytes 983048 | tf_op jit(solution)/shard_map/ppermute | solution.py:257
  32.7 24.5 %collective-permute-start.3 = (bf16[128,1280]{1,0:T(8,128)(2,1)S(1)}, bf16[128,1280]{1,0:T(8,128)(2,1)S(1)}, u32[]{:S(2)}, u32[]{:S(2)}) collective-permute-start(bf16[128,1280]{1,0:T(8,128)(2,1)S(1)} %collective-permute-done), channel_id=1, source_target_pairs={{0,1},{1,2},{2,3},{3,0},{4,5},{5,6},{6,7},{7,4},{8,9},{9,10},{10,1... | collective-permute-start | bytes 983048 | tf_op jit(solution)/shard_map/ppermute | solution.py:260
  55.7 5.6 %collective-permute-start.9 = (f32[128,64]{0,1:T(8,128)S(1)}, f32[128,64]{0,1:T(8,128)S(1)}, u32[]{:S(2)}, u32[]{:S(2)}) collective-permute-start(f32[128,64]{0,1:T(8,128)S(1)} %add_add_fusion.1), channel_id=1, source_target_pairs={{0,3},{1,0},{2,1},{3,2},{4,7},{5,4},{6,5},{7,6},{8,11},{9,8},{10,9... | collective-permute-start | bytes 98312 | tf_op jit(solution)/shard_map/ppermute | solution.py:260
  55.8 5.5 %collective-permute-start.7 = (f32[128,64]{0,1:T(8,128)S(1)}, f32[128,64]{0,1:T(8,128)S(1)}, u32[]{:S(2)}, u32[]{:S(2)}) collective-permute-start(f32[128,64]{0,1:T(8,128)S(1)} %add_add_fusion.1), channel_id=1, source_target_pairs={{0,1},{1,2},{2,3},{3,0},{4,5},{5,6},{6,7},{7,4},{8,9},{9,10},{10,1... | collective-permute-start | bytes 98312 | tf_op jit(solution)/shard_map/ppermute | solution.py:260
  56.3 5.0 %collective-permute-start.8 = (f32[128,64]{0,1:T(8,128)S(1)}, f32[128,64]{0,1:T(8,128)S(1)}, u32[]{:S(2)}, u32[]{:S(2)}) collective-permute-start(f32[128,64]{0,1:T(8,128)S(1)} %add_add_fusion.1), channel_id=1, source_target_pairs={{0,2},{1,3},{2,0},{3,1},{4,6},{5,7},{6,4},{7,5},{8,10},{9,11},{10,... | collective-permute-start | bytes 98312 | tf_op jit(solution)/shard_map/ppermute | solution.py:260
  61.3 3.8 %collective-permute-start.10 = (bf16[128,64]{0,1:T(8,128)(2,1)S(1)}, bf16[128,64]{0,1:T(8,128)(2,1)S(1)}, u32[]{:S(2)}, u32[]{:S(2)}) collective-permute-start(bf16[128,64]{0,1:T(8,128)(2,1)S(1)} %add_convert_fusion.2), channel_id=1, source_target_pairs={{0,12},{4,0},{8,4},{12,8},{1,13},{5,1},{9,5},{13,9},{2,14},{6,2},{... | collective-permute-start | bytes 49160 | tf_op jit(solution)/shard_map/ppermute | solution.py:257
  61.9 4.7 %collective-permute-start.11 = (bf16[128,64]{0,1:T(8,128)(2,1)S(1)}, bf16[128,64]{0,1:T(8,128)(2,1)S(1)}, u32[]{:S(2)}, u32[]{:S(2)}) collective-permute-start(bf16[128,64]{0,1:T(8,128)(2,1)S(1)} %add_convert_fusion.2), channel_id=1, source_target_pairs={{0,8},{4,12},{8,0},{12,4},{1,9},{5,13},{9,1},{13,5},{2,10},{6,14},... | collective-permute-start | bytes 49160 | tf_op jit(solution)/shard_map/ppermute | solution.py:257
  61.9 6.3 %collective-permute-start.12 = (bf16[128,64]{0,1:T(8,128)(2,1)S(1)}, bf16[128,64]{0,1:T(8,128)(2,1)S(1)}, u32[]{:S(2)}, u32[]{:S(2)}) collective-permute-start(bf16[128,64]{0,1:T(8,128)(2,1)S(1)} %add_convert_fusion.2), channel_id=1, source_target_pairs={{0,4},{4,8},{8,12},{12,0},{1,5},{5,9},{9,13},{13,1},{2,6},{6,10},{... | collective-permute-start | bytes 49160 | tf_op jit(solution)/shard_map/ppermute | solution.py:257
  69.4 9.5 %collective-permute-start.15 = (bf16[128,1168]{0,1:T(8,128)(2,1)S(1)}, bf16[128,1168]{0,1:T(8,128)(2,1)S(1)}, u32[]{:S(2)}, u32[]{:S(2)}) collective-permute-start(bf16[128,1168]{0,1:T(8,128)(2,1)S(1)} %get-tuple-element.29), channel_id=1, source_target_pairs={{0,12},{4,0},{8,4},{12,8},{1,13},{5,1},{9,5},{13,9},{2,14},{6,2},{... | collective-permute-start | bytes 897032 | tf_op jit(solution)/shard_map/ppermute | solution.py:257
  71.4 25.3 %collective-permute-start.14 = (bf16[128,1168]{0,1:T(8,128)(2,1)S(1)}, bf16[128,1168]{0,1:T(8,128)(2,1)S(1)}, u32[]{:S(2)}, u32[]{:S(2)}) collective-permute-start(bf16[128,1168]{0,1:T(8,128)(2,1)S(1)} %get-tuple-element.30), channel_id=1, source_target_pairs={{0,8},{4,12},{8,0},{12,4},{1,9},{5,13},{9,1},{13,5},{2,10},{6,14},... | collective-permute-start | bytes 897032 | tf_op jit(solution)/shard_map/ppermute | solution.py:257
  71.4 25.3 %collective-permute-start.13 = (bf16[128,1168]{0,1:T(8,128)(2,1)S(1)}, bf16[128,1168]{0,1:T(8,128)(2,1)S(1)}, u32[]{:S(2)}, u32[]{:S(2)}) collective-permute-start(bf16[128,1168]{0,1:T(8,128)(2,1)S(1)} %get-tuple-element.28), channel_id=1, source_target_pairs={{0,4},{4,8},{8,12},{12,0},{1,5},{5,9},{9,13},{13,1},{2,6},{6,10},{... | collective-permute-start | bytes 897032 | tf_op jit(solution)/shard_map/ppermute | solution.py:257
  106.2 4.0 %collective-permute-start.18 = (bf16[128,128]{0,1:T(8,128)(2,1)S(1)}, bf16[128,128]{0,1:T(8,128)(2,1)S(1)}, u32[]{:S(2)}, u32[]{:S(2)}) collective-permute-start(bf16[128,128]{0,1:T(8,128)(2,1)S(1)} %slice.218), channel_id=1, source_target_pairs={{0,2},{1,3},{2,0},{3,1},{4,6},{5,7},{6,4},{7,5},{8,10},{9,11},{10,... | collective-permute-start | bytes 98312 | tf_op jit(solution)/shard_map/ppermute | solution.py:260
  107.5 3.3 %collective-permute-start.19 = (bf16[128,128]{0,1:T(8,128)(2,1)S(1)}, bf16[128,128]{0,1:T(8,128)(2,1)S(1)}, u32[]{:S(2)}, u32[]{:S(2)}) collective-permute-start(bf16[128,128]{0,1:T(8,128)(2,1)S(1)} %slice.218), channel_id=1, source_target_pairs={{0,1},{1,2},{2,3},{3,0},{4,5},{5,6},{6,7},{7,4},{8,9},{9,10},{10,1... | collective-permute-start | bytes 98312 | tf_op jit(solution)/shard_map/ppermute | solution.py:260
  113.8 14.9 %collective-permute-start.20 = (bf16[16,65,256]{2,0,1:T(8,128)(2,1)}, bf16[16,65,256]{2,0,1:T(8,128)(2,1)}, u32[]{:S(2)}, u32[]{:S(2)}) collective-permute-start(bf16[16,65,256]{2,0,1:T(8,128)(2,1)} %copy.124), channel_id=1, source_target_pairs={{0,4},{4,8},{8,12},{1,5},{5,9},{9,13},{2,6},{6,10},{10,14},{3,7},{... | collective-permute-start | bytes 1597448 | tf_op jit(solution)/shard_map/ppermute | solution.py:406
  130.8 15.4 %collective-permute-start.21 = (bf16[16,65,256]{2,0,1:T(8,128)(2,1)S(1)}, bf16[16,65,256]{2,0,1:T(8,128)(2,1)S(1)}, u32[]{:S(2)}, u32[]{:S(2)}) collective-permute-start(bf16[16,65,256]{2,0,1:T(8,128)(2,1)S(1)} %copy.127), channel_id=1, source_target_pairs={{0,8},{4,12},{1,9},{5,13},{2,10},{6,14},{3,11},{7,15},{16,24},{20,... | collective-permute-start | bytes 1597448 | tf_op jit(solution)/shard_map/ppermute | solution.py:416
  149.3 21.9 %collective-permute-start.22 = (bf16[128,1024]{0,1:T(8,128)(2,1)}, bf16[128,1024]{0,1:T(8,128)(2,1)S(1)}, u32[]{:S(2)}, u32[]{:S(2)}) collective-permute-start(bf16[128,1024]{0,1:T(8,128)(2,1)} %fusion.36), channel_id=1, source_target_pairs={{0,12},{4,0},{8,4},{12,8},{1,13},{5,1},{9,5},{13,9},{2,14},{6,2},{... | collective-permute-start | bytes 786440 | tf_op jit(solution)/shard_map/ppermute | solution.py:257
  164.0 21.1 %collective-permute-start.23 = (bf16[128,1024]{0,1:T(8,128)(2,1)}, bf16[128,1024]{0,1:T(8,128)(2,1)}, u32[]{:S(2)}, u32[]{:S(2)}) collective-permute-start(bf16[128,1024]{0,1:T(8,128)(2,1)} %fusion.36), channel_id=1, source_target_pairs={{0,8},{4,12},{8,0},{12,4},{1,9},{5,13},{9,1},{13,5},{2,10},{6,14},... | collective-permute-start | bytes 786440 | tf_op jit(solution)/shard_map/ppermute | solution.py:257
  164.0 22.0 %collective-permute-start.24 = (bf16[128,1024]{0,1:T(8,128)(2,1)}, bf16[128,1024]{0,1:T(8,128)(2,1)S(1)}, u32[]{:S(2)}, u32[]{:S(2)}) collective-permute-start(bf16[128,1024]{0,1:T(8,128)(2,1)} %fusion.36), channel_id=1, source_target_pairs={{0,4},{4,8},{8,12},{12,0},{1,5},{5,9},{9,13},{13,1},{2,6},{6,10},{... | collective-permute-start | bytes 786440 | tf_op jit(solution)/shard_map/ppermute | solution.py:257
  192.7 6.3 %collective-permute-start.27 = (f32[512,64]{0,1:T(8,128)S(1)}, f32[512,64]{0,1:T(8,128)S(1)}, u32[]{:S(2)}, u32[]{:S(2)}) collective-permute-start(f32[512,64]{0,1:T(8,128)S(1)} %multiply_reduce_fusion.1), channel_id=1, source_target_pairs={{0,3},{1,0},{2,1},{3,2},{4,7},{5,4},{6,5},{7,6},{8,11},{9,8},{10,9... | collective-permute-start | bytes 393224 | tf_op jit(solution)/shard_map/ppermute | solution.py:260
  192.8 6.2 %collective-permute-start.25 = (f32[512,64]{0,1:T(8,128)S(1)}, f32[512,64]{0,1:T(8,128)S(1)}, u32[]{:S(2)}, u32[]{:S(2)}) collective-permute-start(f32[512,64]{0,1:T(8,128)S(1)} %multiply_reduce_fusion.1), channel_id=1, source_target_pairs={{0,1},{1,2},{2,3},{3,0},{4,5},{5,6},{6,7},{7,4},{8,9},{9,10},{10,1... | collective-permute-start | bytes 393224 | tf_op jit(solution)/shard_map/ppermute | solution.py:260
  193.3 8.2 %collective-permute-start.26 = (f32[512,64]{0,1:T(8,128)S(1)}, f32[512,64]{0,1:T(8,128)S(1)}, u32[]{:S(2)}, u32[]{:S(2)}) collective-permute-start(f32[512,64]{0,1:T(8,128)S(1)} %multiply_reduce_fusion.1), channel_id=1, source_target_pairs={{0,2},{1,3},{2,0},{3,1},{4,6},{5,7},{6,4},{7,5},{8,10},{9,11},{10,... | collective-permute-start | bytes 393224 | tf_op jit(solution)/shard_map/ppermute | solution.py:260
  194.9 25.8 %collective-permute-start.29 = (bf16[2,64,1280]{2,1,0:T(8,128)(2,1)S(1)}, bf16[2,64,1280]{2,1,0:T(8,128)(2,1)S(1)}, u32[]{:S(2)}, u32[]{:S(2)}) collective-permute-start(bf16[2,64,1280]{2,1,0:T(8,128)(2,1)S(1)} %copy-done.15), channel_id=1, source_target_pairs={{0,0},{1,4},{2,8},{3,12},{4,1},{5,5},{6,9},{7,13},{8,2},{9,6},{10,... | collective-permute-start | bytes 983048 | tf_op jit(solution)/shard_map/ppermute | solution.py:265
  201.5 19.2 %collective-permute-start.28 = (f32[512,64]{0,1:T(8,128)S(1)}, f32[512,64]{0,1:T(8,128)S(1)}, u32[]{:S(2)}, u32[]{:S(2)}) collective-permute-start(f32[512,64]{0,1:T(8,128)S(1)} %add_add_fusion), channel_id=1, source_target_pairs={{0,0},{1,4},{2,8},{3,12},{4,1},{5,5},{6,9},{7,13},{8,2},{9,6},{10,... | collective-permute-start | bytes 393224 | tf_op jit(solution)/shard_map/ppermute | solution.py:265
  223.7 8.4 %collective-permute-start.32 = (bf16[128,1280]{1,0:T(8,128)(2,1)}, bf16[128,1280]{1,0:T(8,128)(2,1)S(1)}, u32[]{:S(2)}, u32[]{:S(2)}) collective-permute-start(bf16[128,1280]{1,0:T(8,128)(2,1)} %get-tuple-element.26), channel_id=1, source_target_pairs={{0,3},{1,0},{2,1},{3,2},{4,7},{5,4},{6,5},{7,6},{8,11},{9,8},{10,9... | collective-permute-start | bytes 983048 | tf_op jit(solution)/shard_map/ppermute | solution.py:260
  223.7 15.3 %collective-permute-start.31 = (bf16[128,1280]{1,0:T(8,128)(2,1)}, bf16[128,1280]{1,0:T(8,128)(2,1)}, u32[]{:S(2)}, u32[]{:S(2)}) collective-permute-start(bf16[128,1280]{1,0:T(8,128)(2,1)} %get-tuple-element.27), channel_id=1, source_target_pairs={{0,2},{1,3},{2,0},{3,1},{4,6},{5,7},{6,4},{7,5},{8,10},{9,11},{10,... | collective-permute-start | bytes 983048 | tf_op jit(solution)/shard_map/ppermute | solution.py:260
  223.7 15.3 %collective-permute-start.30 = (bf16[128,1280]{1,0:T(8,128)(2,1)S(1)}, bf16[128,1280]{1,0:T(8,128)(2,1)}, u32[]{:S(2)}, u32[]{:S(2)}) collective-permute-start(bf16[128,1280]{1,0:T(8,128)(2,1)S(1)} %get-tuple-element.25), channel_id=1, source_target_pairs={{0,1},{1,2},{2,3},{3,0},{4,5},{5,6},{6,7},{7,4},{8,9},{9,10},{10,1... | collective-permute-start | bytes 983048 | tf_op jit(solution)/shard_map/ppermute | solution.py:260
  240.4 19.3 %collective-permute-start.33 = (bf16[128,1280]{1,0:T(8,128)(2,1)S(1)}, bf16[128,1280]{1,0:T(8,128)(2,1)S(1)}, u32[]{:S(2)}, u32[]{:S(2)}) collective-permute-start(bf16[128,1280]{1,0:T(8,128)(2,1)S(1)} %add_convert_fusion.1), channel_id=1, source_target_pairs={{0,0},{1,4},{2,8},{3,12},{4,1},{5,5},{6,9},{7,13},{8,2},{9,6},{10,... | collective-permute-start | bytes 983048 | tf_op jit(solution)/shard_map/ppermute | solution.py:265
  (18 other events, 408.5 us)

commit v14 on v13

--- a/solution.py
+++ b/solution.py
@@ -450,10 +450,29 @@
         preferred_element_type=jnp.float32,
     )
     out_part = base_part + adapter_part
-    mixed_t = block_rows(out_part, lane, length)
-    for s in range(1, side):
-        sent = block_rows(out_part, (lane + s) % side, length).astype(jnp.bfloat16)
-        mixed_t = mixed_t + moved(sent, s, "lane").astype(jnp.float32)
+    if lax.axis_size("tp") == 2 and lax.axis_size("dp") == 2:
+        core = lax.axis_index("dp")
+        chip = lax.axis_index("tp")
+        blocks = out_part.reshape(side, length, -1)
+
+        def pick(index):
+            return lax.dynamic_index_in_dim(blocks, index, 0, keepdims=False)
+
+        swapped = lax.ppermute(
+            jnp.stack([pick(1 - core), pick(3 - core)]).astype(jnp.bfloat16),
+            "dp",
+            [(0, 1), (1, 0)],
+        ).astype(jnp.float32)
+        near = pick(core) + swapped[0]
+        far = pick(2 + core) + swapped[1]
+        mixed_t = jnp.where(chip == 0, near, far)
+        crossing = jnp.where(chip == 0, far, near).astype(jnp.bfloat16)
+        mixed_t = mixed_t + lax.ppermute(crossing, "tp", [(0, 1), (1, 0)]).astype(jnp.float32)
+    else:
+        mixed_t = block_rows(out_part, lane, length)
+        for s in range(1, side):
+            sent = block_rows(out_part, (lane + s) % side, length).astype(jnp.bfloat16)
+            mixed_t = mixed_t + moved(sent, s, "lane").astype(jnp.float32)
     return transposed(mixed_t.astype(jnp.bfloat16))
 
 

time: 261 us -> 258 us (0.989)
    ppermute x15 -> x12, waiting for transfers between devices: 20.3 us -> 5.56 us  [moved(): return lax.ppermute(block, ('tp', 'dp'), pairs)]
    ppermute x0 -> x2, waiting for transfers between devices: none -> 11.9 us  [the longest x1 9.74 us: square_body(): lax.ppermute(crossing, 'tp', [(0, 1), (1, 0)]).astype(jnp.float32)]
    convert_element_type x0 -> x2, other arithmetic: none -> 2.64 us  [the longest x1 1.47 us: square_body(): crossing = jnp.where(chip == 0, far, near).astype(jnp.bfloat16)]
    ppermute x15 -> x12, starting transfers between devices: 8.38 us -> 7.87 us  [moved(): return lax.ppermute(block, ('tp', 'dp'), pairs)]
    unnamed x61 -> x63, local copies, waits for them, and re-layouts: 7 us -> 7.01 us
  transfers between devices with their start and end apart: 34 -> 33, of which waited for: 18 -> 18; matrix products, arithmetic and copies ran while one was open for 8% -> 8% of each run, Pallas kernels for 0% -> 0%
where the time goes in v14:
time: 258 us
  waiting for transfers between devices  145 us (56%)
  starting transfers between devices  59.7 us (23%)
  local copies, waits for them, and re-layouts  19.5 us (8%)
  matrix products  17.2 us (7%)
  other arithmetic  13.9 us (5%)
    ppermute x12, waiting for transfers between devices, moved(): return lax.ppermute(block, 'ctx', pairs)  68.8 us
    ppermute x4, waiting for transfers between devices, moved(): return lax.ppermute(block, ('ctx', 'tp', 'dp'), pairs)  42.9 us
    ppermute x12, starting transfers between devices, moved(): return lax.ppermute(block, 'ctx', pairs)  24 us
    ppermute x4, starting transfers between devices, moved(): return lax.ppermute(block, ('ctx', 'tp', 'dp'), pairs)  14.3 us
    ppermute x1, waiting for transfers between devices, square_body(): lax.ppermute(crossing, 'tp', [(0, 1), (1, 0)]).astype(jnp.float32)  9.74 us
    ppermute x1, waiting for transfers between devices, square_body(): lax.ppermute(state_and_decay, 'ctx', [(a, a + 1) for a in range(side - 1)])  9.32 us
    ppermute x12, starting transfers between devices, moved(): return lax.ppermute(block, ('tp', 'dp'), pairs)  7.87 us
    unnamed x63, local copies, waits for them, and re-layouts  7.01 us
  transfers between devices with their start and end apart: 33, of which 18 were waited for; matrix products, arithmetic and copies ran while one was open for 8% of the time, Pallas kernels for 0%

profile of v14, /device:TPU:2, one launch (start us, length us, event | category | flops | bytes accessed | tf_op | source)
XLA Modules:
  0.0 257.6 jit_solution(11425896726298716091)
XLA Ops:
  0.0 4.7 %collective-permute-start = (bf16[128,1280]{1,0:T(8,128)(2,1)}, bf16[128,1280]{1,0:T(8,128)(2,1)S(1)}, u32[]{:S(2)}, u32[]{:S(2)}) collective-permute-start(bf16[128,1280]{1,0:T(8,128)(2,1)} %param.19), channel_id=1, source_target_pairs={{0,0},{1,4},{2,8},{3,12},{4,1},{5,5},{6,9},{7,13},{8,2},{9,6},{10,... | collective-permute-start | bytes 983048 | tf_op jit(solution)/shard_map/ppermute | solution.py:265
  9.6 11.8 %collective-permute-done = bf16[128,1280]{1,0:T(8,128)(2,1)S(1)} collective-permute-done((bf16[128,1280]{1,0:T(8,128)(2,1)}, bf16[128,1280]{1,0:T(8,128)(2,1)S(1)}, u32[]{:S(2)}, u32[]{:S(2)}) %collective-permute-start) | collective-permute-done | bytes 327712 | tf_op jit(solution)/shard_map/ppermute | solution.py:265
  22.1 3.4 %collective-permute-start.5 = (bf16[2,1280,64]{1,2,0:T(8,128)(2,1)}, bf16[2,1280,64]{1,2,0:T(8,128)(2,1)}, u32[]{:S(2)}, u32[]{:S(2)}) collective-permute-start(bf16[2,1280,64]{1,2,0:T(8,128)(2,1)} %param.33), channel_id=1, source_target_pairs={{0,8},{4,12},{8,0},{12,4},{1,9},{5,13},{9,1},{13,5},{2,10},{6,14},... | collective-permute-start | bytes 983048 | tf_op jit(solution)/shard_map/ppermute | solution.py:257
  28.1 2.7 %collective-permute-start.1 = (bf16[128,1280]{1,0:T(8,128)(2,1)S(1)}, bf16[128,1280]{1,0:T(8,128)(2,1)S(1)}, u32[]{:S(2)}, u32[]{:S(2)}) collective-permute-start(bf16[128,1280]{1,0:T(8,128)(2,1)S(1)} %collective-permute-done), channel_id=1, source_target_pairs={{0,3},{1,0},{2,1},{3,2},{4,7},{5,4},{6,5},{7,6},{8,11},{9,8},{10,9... | collective-permute-start | bytes 983048 | tf_op jit(solution)/shard_map/ppermute | solution.py:260
  34.1 20.1 %collective-permute-done.5 = bf16[2,1280,64]{1,2,0:T(8,128)(2,1)} collective-permute-done((bf16[2,1280,64]{1,2,0:T(8,128)(2,1)}, bf16[2,1280,64]{1,2,0:T(8,128)(2,1)}, u32[]{:S(2)}, u32[]{:S(2)}) %collective-permute-start.5) | collective-permute-done | bytes 327712 | tf_op jit(solution)/shard_map/ppermute | solution.py:257
  61.9 2.0 collective-permute-start.12
  66.5 1.6 collective-permute-done.12
  69.4 1.9 collective-permute-start.15
  72.8 6.2 %collective-permute-done.15 = bf16[128,1168]{0,1:T(8,128)(2,1)S(1)} collective-permute-done((bf16[128,1168]{0,1:T(8,128)(2,1)S(1)}, bf16[128,1168]{0,1:T(8,128)(2,1)S(1)}, u32[]{:S(2)}, u32[]{:S(2)}) %collective-permute-start.15) | collective-permute-done | bytes 299040 | tf_op jit(solution)/shard_map/ppermute | solution.py:257
  79.0 17.8 %collective-permute-done.14 = bf16[128,1168]{0,1:T(8,128)(2,1)S(1)} collective-permute-done((bf16[128,1168]{0,1:T(8,128)(2,1)S(1)}, bf16[128,1168]{0,1:T(8,128)(2,1)S(1)}, u32[]{:S(2)}, u32[]{:S(2)}) %collective-permute-start.14) | collective-permute-done | bytes 299040 | tf_op jit(solution)/shard_map/ppermute | solution.py:257
  99.1 1.9 collective-permute-start.16
  102.7 3.3 %divide_multiply_fusion = f32[128,1152]{0,1:T(8,128)S(1)} fusion(f32[128,1152]{0,1:T(8,128)} %slice.96, f32[3,1152]{0,1:T(8,128)S(1)} %copy.118, f32[128]{0:T(128)S(1)} %get-tuple-element.42, f32[1152]{0:T(1024)S(1)} %get-tuple-element.14, f32[128]{0:T(128)S(1)} %get-tuple-element.43, f32[1152]{0:T(1024)S(1)} %get-tuple-element.15, ...), kind=kLoop, calls=%fused_computation.65 | loop fusion | flops 2654208 | bytes 1213952 | tf_op jit(solution)/shard_map/jit(silu)/mul | solution.py:389
  107.7 2.4 collective-permute-done.18
  113.8 5.2 %collective-permute-start.20 = (bf16[16,65,256]{2,0,1:T(8,128)(2,1)}, bf16[16,65,256]{2,0,1:T(8,128)(2,1)}, u32[]{:S(2)}, u32[]{:S(2)}) collective-permute-start(bf16[16,65,256]{2,0,1:T(8,128)(2,1)} %copy.124), channel_id=1, source_target_pairs={{0,4},{4,8},{8,12},{1,5},{5,9},{9,13},{2,6},{6,10},{10,14},{3,7},{... | collective-permute-start | bytes 1597448 | tf_op jit(solution)/shard_map/ppermute | solution.py:406
  119.4 9.3 %collective-permute-done.20 = bf16[16,65,256]{2,0,1:T(8,128)(2,1)} collective-permute-done((bf16[16,65,256]{2,0,1:T(8,128)(2,1)}, bf16[16,65,256]{2,0,1:T(8,128)(2,1)}, u32[]{:S(2)}, u32[]{:S(2)}) %collective-permute-start.20) | collective-permute-done | bytes 532512 | tf_op jit(solution)/shard_map/ppermute | solution.py:406
  130.8 6.3 %collective-permute-start.21 = (bf16[16,65,256]{2,0,1:T(8,128)(2,1)S(1)}, bf16[16,65,256]{2,0,1:T(8,128)(2,1)S(1)}, u32[]{:S(2)}, u32[]{:S(2)}) collective-permute-start(bf16[16,65,256]{2,0,1:T(8,128)(2,1)S(1)} %copy.127), channel_id=1, source_target_pairs={{0,8},{4,12},{1,9},{5,13},{2,10},{6,14},{3,11},{7,15},{16,24},{20,... | collective-permute-start | bytes 1597448 | tf_op jit(solution)/shard_map/ppermute | solution.py:416
  137.3 2.2 convolution_bitcast_fusion
  139.7 6.5 %collective-permute-done.21 = bf16[16,65,256]{2,0,1:T(8,128)(2,1)S(1)} collective-permute-done((bf16[16,65,256]{2,0,1:T(8,128)(2,1)S(1)}, bf16[16,65,256]{2,0,1:T(8,128)(2,1)S(1)}, u32[]{:S(2)}, u32[]{:S(2)}) %collective-permute-start.21) | collective-permute-done | bytes 532512 | tf_op jit(solution)/shard_map/ppermute | solution.py:416
  146.3 2.1 multiply_reduce_fusion
  149.3 14.8 %collective-permute-start.22 = (bf16[128,1024]{0,1:T(8,128)(2,1)}, bf16[128,1024]{0,1:T(8,128)(2,1)S(1)}, u32[]{:S(2)}, u32[]{:S(2)}) collective-permute-start(bf16[128,1024]{0,1:T(8,128)(2,1)} %fusion.37), channel_id=1, source_target_pairs={{0,12},{4,0},{8,4},{12,8},{1,13},{5,1},{9,5},{13,9},{2,14},{6,2},{... | collective-permute-start | bytes 786440 | tf_op jit(solution)/shard_map/ppermute | solution.py:257
  164.6 6.6 %collective-permute-done.22 = bf16[128,1024]{0,1:T(8,128)(2,1)S(1)} collective-permute-done((bf16[128,1024]{0,1:T(8,128)(2,1)}, bf16[128,1024]{0,1:T(8,128)(2,1)S(1)}, u32[]{:S(2)}, u32[]{:S(2)}) %collective-permute-start.22) | collective-permute-done | bytes 262176 | tf_op jit(solution)/shard_map/ppermute | solution.py:257
  171.2 13.9 %collective-permute-done.23 = bf16[128,1024]{0,1:T(8,128)(2,1)} collective-permute-done((bf16[128,1024]{0,1:T(8,128)(2,1)}, bf16[128,1024]{0,1:T(8,128)(2,1)}, u32[]{:S(2)}, u32[]{:S(2)}) %collective-permute-start.23) | collective-permute-done | bytes 262176 | tf_op jit(solution)/shard_map/ppermute | solution.py:257
  188.6 2.3 copy.130
  190.9 1.8 fusion.79
  194.9 4.1 %collective-permute-start.29 = (bf16[2,64,1280]{2,1,0:T(8,128)(2,1)S(1)}, bf16[2,64,1280]{2,1,0:T(8,128)(2,1)S(1)}, u32[]{:S(2)}, u32[]{:S(2)}) collective-permute-start(bf16[2,64,1280]{2,1,0:T(8,128)(2,1)S(1)} %copy-done.16), channel_id=1, source_target_pairs={{0,0},{1,4},{2,8},{3,12},{4,1},{5,5},{6,9},{7,13},{8,2},{9,6},{10,... | collective-permute-start | bytes 983048 | tf_op jit(solution)/shard_map/ppermute | solution.py:265
  199.0 2.4 collective-permute-done.26
  201.5 3.6 %collective-permute-start.28 = (f32[512,64]{0,1:T(8,128)S(1)}, f32[512,64]{0,1:T(8,128)S(1)}, u32[]{:S(2)}, u32[]{:S(2)}) collective-permute-start(f32[512,64]{0,1:T(8,128)S(1)} %add_add_fusion), channel_id=1, source_target_pairs={{0,0},{1,4},{2,8},{3,12},{4,1},{5,5},{6,9},{7,13},{8,2},{9,6},{10,... | collective-permute-start | bytes 393224 | tf_op jit(solution)/shard_map/ppermute | solution.py:265
  206.7 13.9 %collective-permute-done.28 = f32[512,64]{0,1:T(8,128)S(1)} collective-permute-done((f32[512,64]{0,1:T(8,128)S(1)}, f32[512,64]{0,1:T(8,128)S(1)}, u32[]{:S(2)}, u32[]{:S(2)}) %collective-permute-start.28) | collective-permute-done | bytes 131104 | tf_op jit(solution)/shard_map/ppermute | solution.py:265
  222.9 2.2 collective-permute-done.30
  227.8 9.7 %collective-permute-done.31 = bf16[128,1280]{1,0:T(8,128)(2,1)S(1)} collective-permute-done((bf16[128,1280]{1,0:T(8,128)(2,1)S(1)}, bf16[128,1280]{1,0:T(8,128)(2,1)S(1)}, u32[]{:S(2)}, u32[]{:S(2)}) %collective-permute-start.31) | collective-permute-done | bytes 327712 | tf_op jit(solution)/shard_map/ppermute | solution.py:470
  237.7 1.9 collective-permute-start.32
  239.6 17.3 %collective-permute-done.32 = bf16[128,1280]{1,0:T(8,128)(2,1)S(1)} collective-permute-done((bf16[128,1280]{1,0:T(8,128)(2,1)S(1)}, bf16[128,1280]{1,0:T(8,128)(2,1)S(1)}, u32[]{:S(2)}, u32[]{:S(2)}) %collective-permute-start.32) | collective-permute-done | bytes 327712 | tf_op jit(solution)/shard_map/ppermute | solution.py:265
  (195 shorter events, 49.4 us)
Async XLA Ops:
  0.0 21.3 %collective-permute-start = (bf16[128,1280]{1,0:T(8,128)(2,1)}, bf16[128,1280]{1,0:T(8,128)(2,1)S(1)}, u32[]{:S(2)}, u32[]{:S(2)}) collective-permute-start(bf16[128,1280]{1,0:T(8,128)(2,1)} %param.19), channel_id=1, source_target_pairs={{0,0},{1,4},{2,8},{3,12},{4,1},{5,5},{6,9},{7,13},{8,2},{9,6},{10,... | collective-permute-start | bytes 983048 | tf_op jit(solution)/shard_map/ppermute | solution.py:265
  21.3 11.3 %collective-permute-start.6 = (bf16[2,1280,64]{1,2,0:T(8,128)(2,1)}, bf16[2,1280,64]{1,2,0:T(8,128)(2,1)}, u32[]{:S(2)}, u32[]{:S(2)}) collective-permute-start(bf16[2,1280,64]{1,2,0:T(8,128)(2,1)} %param.33), channel_id=1, source_target_pairs={{0,12},{4,0},{8,4},{12,8},{1,13},{5,1},{9,5},{13,9},{2,14},{6,2},{... | collective-permute-start | bytes 983048 | tf_op jit(solution)/shard_map/ppermute | solution.py:257
  22.1 32.2 %collective-permute-start.5 = (bf16[2,1280,64]{1,2,0:T(8,128)(2,1)}, bf16[2,1280,64]{1,2,0:T(8,128)(2,1)}, u32[]{:S(2)}, u32[]{:S(2)}) collective-permute-start(bf16[2,1280,64]{1,2,0:T(8,128)(2,1)} %param.33), channel_id=1, source_target_pairs={{0,8},{4,12},{8,0},{12,4},{1,9},{5,13},{9,1},{13,5},{2,10},{6,14},... | collective-permute-start | bytes 983048 | tf_op jit(solution)/shard_map/ppermute | solution.py:257
  28.1 28.2 %collective-permute-start.1 = (bf16[128,1280]{1,0:T(8,128)(2,1)S(1)}, bf16[128,1280]{1,0:T(8,128)(2,1)S(1)}, u32[]{:S(2)}, u32[]{:S(2)}) collective-permute-start(bf16[128,1280]{1,0:T(8,128)(2,1)S(1)} %collective-permute-done), channel_id=1, source_target_pairs={{0,3},{1,0},{2,1},{3,2},{4,7},{5,4},{6,5},{7,6},{8,11},{9,8},{10,9... | collective-permute-start | bytes 983048 | tf_op jit(solution)/shard_map/ppermute | solution.py:260
  30.8 26.4 %collective-permute-start.2 = (bf16[128,1280]{1,0:T(8,128)(2,1)S(1)}, bf16[128,1280]{1,0:T(8,128)(2,1)S(1)}, u32[]{:S(2)}, u32[]{:S(2)}) collective-permute-start(bf16[128,1280]{1,0:T(8,128)(2,1)S(1)} %collective-permute-done), channel_id=1, source_target_pairs={{0,2},{1,3},{2,0},{3,1},{4,6},{5,7},{6,4},{7,5},{8,10},{9,11},{10,... | collective-permute-start | bytes 983048 | tf_op jit(solution)/shard_map/ppermute | solution.py:260
  30.8 24.7 %collective-permute-start.4 = (bf16[2,1280,64]{1,2,0:T(8,128)(2,1)}, bf16[2,1280,64]{1,2,0:T(8,128)(2,1)S(1)}, u32[]{:S(2)}, u32[]{:S(2)}) collective-permute-start(bf16[2,1280,64]{1,2,0:T(8,128)(2,1)} %param.33), channel_id=1, source_target_pairs={{0,4},{4,8},{8,12},{12,0},{1,5},{5,9},{9,13},{13,1},{2,6},{6,10},{... | collective-permute-start | bytes 983048 | tf_op jit(solution)/shard_map/ppermute | solution.py:257
  32.7 24.5 %collective-permute-start.3 = (bf16[128,1280]{1,0:T(8,128)(2,1)S(1)}, bf16[128,1280]{1,0:T(8,128)(2,1)S(1)}, u32[]{:S(2)}, u32[]{:S(2)}) collective-permute-start(bf16[128,1280]{1,0:T(8,128)(2,1)S(1)} %collective-permute-done), channel_id=1, source_target_pairs={{0,1},{1,2},{2,3},{3,0},{4,5},{5,6},{6,7},{7,4},{8,9},{9,10},{10,1... | collective-permute-start | bytes 983048 | tf_op jit(solution)/shard_map/ppermute | solution.py:260
  55.7 5.6 %collective-permute-start.9 = (f32[128,64]{0,1:T(8,128)S(1)}, f32[128,64]{0,1:T(8,128)S(1)}, u32[]{:S(2)}, u32[]{:S(2)}) collective-permute-start(f32[128,64]{0,1:T(8,128)S(1)} %add_add_fusion.1), channel_id=1, source_target_pairs={{0,3},{1,0},{2,1},{3,2},{4,7},{5,4},{6,5},{7,6},{8,11},{9,8},{10,9... | collective-permute-start | bytes 98312 | tf_op jit(solution)/shard_map/ppermute | solution.py:260
  55.8 5.5 %collective-permute-start.7 = (f32[128,64]{0,1:T(8,128)S(1)}, f32[128,64]{0,1:T(8,128)S(1)}, u32[]{:S(2)}, u32[]{:S(2)}) collective-permute-start(f32[128,64]{0,1:T(8,128)S(1)} %add_add_fusion.1), channel_id=1, source_target_pairs={{0,1},{1,2},{2,3},{3,0},{4,5},{5,6},{6,7},{7,4},{8,9},{9,10},{10,1... | collective-permute-start | bytes 98312 | tf_op jit(solution)/shard_map/ppermute | solution.py:260
  56.3 5.0 %collective-permute-start.8 = (f32[128,64]{0,1:T(8,128)S(1)}, f32[128,64]{0,1:T(8,128)S(1)}, u32[]{:S(2)}, u32[]{:S(2)}) collective-permute-start(f32[128,64]{0,1:T(8,128)S(1)} %add_add_fusion.1), channel_id=1, source_target_pairs={{0,2},{1,3},{2,0},{3,1},{4,6},{5,7},{6,4},{7,5},{8,10},{9,11},{10,... | collective-permute-start | bytes 98312 | tf_op jit(solution)/shard_map/ppermute | solution.py:260
  61.3 3.8 %collective-permute-start.10 = (bf16[128,64]{0,1:T(8,128)(2,1)S(1)}, bf16[128,64]{0,1:T(8,128)(2,1)S(1)}, u32[]{:S(2)}, u32[]{:S(2)}) collective-permute-start(bf16[128,64]{0,1:T(8,128)(2,1)S(1)} %add_convert_fusion.1), channel_id=1, source_target_pairs={{0,12},{4,0},{8,4},{12,8},{1,13},{5,1},{9,5},{13,9},{2,14},{6,2},{... | collective-permute-start | bytes 49160 | tf_op jit(solution)/shard_map/ppermute | solution.py:257
  61.9 4.7 %collective-permute-start.11 = (bf16[128,64]{0,1:T(8,128)(2,1)S(1)}, bf16[128,64]{0,1:T(8,128)(2,1)S(1)}, u32[]{:S(2)}, u32[]{:S(2)}) collective-permute-start(bf16[128,64]{0,1:T(8,128)(2,1)S(1)} %add_convert_fusion.1), channel_id=1, source_target_pairs={{0,8},{4,12},{8,0},{12,4},{1,9},{5,13},{9,1},{13,5},{2,10},{6,14},... | collective-permute-start | bytes 49160 | tf_op jit(solution)/shard_map/ppermute | solution.py:257
  61.9 6.3 %collective-permute-start.12 = (bf16[128,64]{0,1:T(8,128)(2,1)S(1)}, bf16[128,64]{0,1:T(8,128)(2,1)S(1)}, u32[]{:S(2)}, u32[]{:S(2)}) collective-permute-start(bf16[128,64]{0,1:T(8,128)(2,1)S(1)} %add_convert_fusion.1), channel_id=1, source_target_pairs={{0,4},{4,8},{8,12},{12,0},{1,5},{5,9},{9,13},{13,1},{2,6},{6,10},{... | collective-permute-start | bytes 49160 | tf_op jit(solution)/shard_map/ppermute | solution.py:257
  69.4 9.5 %collective-permute-start.15 = (bf16[128,1168]{0,1:T(8,128)(2,1)S(1)}, bf16[128,1168]{0,1:T(8,128)(2,1)S(1)}, u32[]{:S(2)}, u32[]{:S(2)}) collective-permute-start(bf16[128,1168]{0,1:T(8,128)(2,1)S(1)} %get-tuple-element.28), channel_id=1, source_target_pairs={{0,12},{4,0},{8,4},{12,8},{1,13},{5,1},{9,5},{13,9},{2,14},{6,2},{... | collective-permute-start | bytes 897032 | tf_op jit(solution)/shard_map/ppermute | solution.py:257
  71.4 25.3 %collective-permute-start.14 = (bf16[128,1168]{0,1:T(8,128)(2,1)S(1)}, bf16[128,1168]{0,1:T(8,128)(2,1)S(1)}, u32[]{:S(2)}, u32[]{:S(2)}) collective-permute-start(bf16[128,1168]{0,1:T(8,128)(2,1)S(1)} %get-tuple-element.29), channel_id=1, source_target_pairs={{0,8},{4,12},{8,0},{12,4},{1,9},{5,13},{9,1},{13,5},{2,10},{6,14},... | collective-permute-start | bytes 897032 | tf_op jit(solution)/shard_map/ppermute | solution.py:257
  71.4 25.3 %collective-permute-start.13 = (bf16[128,1168]{0,1:T(8,128)(2,1)S(1)}, bf16[128,1168]{0,1:T(8,128)(2,1)S(1)}, u32[]{:S(2)}, u32[]{:S(2)}) collective-permute-start(bf16[128,1168]{0,1:T(8,128)(2,1)S(1)} %get-tuple-element.27), channel_id=1, source_target_pairs={{0,4},{4,8},{8,12},{12,0},{1,5},{5,9},{9,13},{13,1},{2,6},{6,10},{... | collective-permute-start | bytes 897032 | tf_op jit(solution)/shard_map/ppermute | solution.py:257
  99.1 3.3 %collective-permute-start.16 = (f32[3,1152]{1,0:T(4,128)S(1)}, f32[3,1152]{1,0:T(4,128)S(1)}, u32[]{:S(2)}, u32[]{:S(2)}) collective-permute-start(f32[3,1152]{1,0:T(4,128)S(1)} %copy.117), channel_id=1, source_target_pairs={{0,4},{4,8},{8,12},{1,5},{5,9},{9,13},{2,6},{6,10},{10,14},{3,7},{... | collective-permute-start | bytes 41480 | tf_op jit(solution)/shard_map/ppermute | solution.py:18
  106.2 4.0 %collective-permute-start.18 = (bf16[128,128]{0,1:T(8,128)(2,1)S(1)}, bf16[128,128]{0,1:T(8,128)(2,1)S(1)}, u32[]{:S(2)}, u32[]{:S(2)}) collective-permute-start(bf16[128,128]{0,1:T(8,128)(2,1)S(1)} %slice.238), channel_id=1, source_target_pairs={{0,2},{1,3},{2,0},{3,1},{4,6},{5,7},{6,4},{7,5},{8,10},{9,11},{10,... | collective-permute-start | bytes 98312 | tf_op jit(solution)/shard_map/ppermute | solution.py:260
  107.5 3.3 %collective-permute-start.19 = (bf16[128,128]{0,1:T(8,128)(2,1)S(1)}, bf16[128,128]{0,1:T(8,128)(2,1)S(1)}, u32[]{:S(2)}, u32[]{:S(2)}) collective-permute-start(bf16[128,128]{0,1:T(8,128)(2,1)S(1)} %slice.238), channel_id=1, source_target_pairs={{0,1},{1,2},{2,3},{3,0},{4,5},{5,6},{6,7},{7,4},{8,9},{9,10},{10,1... | collective-permute-start | bytes 98312 | tf_op jit(solution)/shard_map/ppermute | solution.py:260
  113.8 14.9 %collective-permute-start.20 = (bf16[16,65,256]{2,0,1:T(8,128)(2,1)}, bf16[16,65,256]{2,0,1:T(8,128)(2,1)}, u32[]{:S(2)}, u32[]{:S(2)}) collective-permute-start(bf16[16,65,256]{2,0,1:T(8,128)(2,1)} %copy.124), channel_id=1, source_target_pairs={{0,4},{4,8},{8,12},{1,5},{5,9},{9,13},{2,6},{6,10},{10,14},{3,7},{... | collective-permute-start | bytes 1597448 | tf_op jit(solution)/shard_map/ppermute | solution.py:406
  130.8 15.4 %collective-permute-start.21 = (bf16[16,65,256]{2,0,1:T(8,128)(2,1)S(1)}, bf16[16,65,256]{2,0,1:T(8,128)(2,1)S(1)}, u32[]{:S(2)}, u32[]{:S(2)}) collective-permute-start(bf16[16,65,256]{2,0,1:T(8,128)(2,1)S(1)} %copy.127), channel_id=1, source_target_pairs={{0,8},{4,12},{1,9},{5,13},{2,10},{6,14},{3,11},{7,15},{16,24},{20,... | collective-permute-start | bytes 1597448 | tf_op jit(solution)/shard_map/ppermute | solution.py:416
  149.3 21.9 %collective-permute-start.22 = (bf16[128,1024]{0,1:T(8,128)(2,1)}, bf16[128,1024]{0,1:T(8,128)(2,1)S(1)}, u32[]{:S(2)}, u32[]{:S(2)}) collective-permute-start(bf16[128,1024]{0,1:T(8,128)(2,1)} %fusion.37), channel_id=1, source_target_pairs={{0,12},{4,0},{8,4},{12,8},{1,13},{5,1},{9,5},{13,9},{2,14},{6,2},{... | collective-permute-start | bytes 786440 | tf_op jit(solution)/shard_map/ppermute | solution.py:257
  164.0 21.1 %collective-permute-start.23 = (bf16[128,1024]{0,1:T(8,128)(2,1)}, bf16[128,1024]{0,1:T(8,128)(2,1)}, u32[]{:S(2)}, u32[]{:S(2)}) collective-permute-start(bf16[128,1024]{0,1:T(8,128)(2,1)} %fusion.37), channel_id=1, source_target_pairs={{0,8},{4,12},{8,0},{12,4},{1,9},{5,13},{9,1},{13,5},{2,10},{6,14},... | collective-permute-start | bytes 786440 | tf_op jit(solution)/shard_map/ppermute | solution.py:257
  164.0 22.0 %collective-permute-start.24 = (bf16[128,1024]{0,1:T(8,128)(2,1)}, bf16[128,1024]{0,1:T(8,128)(2,1)S(1)}, u32[]{:S(2)}, u32[]{:S(2)}) collective-permute-start(bf16[128,1024]{0,1:T(8,128)(2,1)} %fusion.37), channel_id=1, source_target_pairs={{0,4},{4,8},{8,12},{12,0},{1,5},{5,9},{9,13},{13,1},{2,6},{6,10},{... | collective-permute-start | bytes 786440 | tf_op jit(solution)/shard_map/ppermute | solution.py:257
  192.7 6.3 %collective-permute-start.27 = (f32[512,64]{0,1:T(8,128)S(1)}, f32[512,64]{0,1:T(8,128)S(1)}, u32[]{:S(2)}, u32[]{:S(2)}) collective-permute-start(f32[512,64]{0,1:T(8,128)S(1)} %multiply_reduce_fusion.1), channel_id=1, source_target_pairs={{0,3},{1,0},{2,1},{3,2},{4,7},{5,4},{6,5},{7,6},{8,11},{9,8},{10,9... | collective-permute-start | bytes 393224 | tf_op jit(solution)/shard_map/ppermute | solution.py:260
  192.8 6.2 %collective-permute-start.25 = (f32[512,64]{0,1:T(8,128)S(1)}, f32[512,64]{0,1:T(8,128)S(1)}, u32[]{:S(2)}, u32[]{:S(2)}) collective-permute-start(f32[512,64]{0,1:T(8,128)S(1)} %multiply_reduce_fusion.1), channel_id=1, source_target_pairs={{0,1},{1,2},{2,3},{3,0},{4,5},{5,6},{6,7},{7,4},{8,9},{9,10},{10,1... | collective-permute-start | bytes 393224 | tf_op jit(solution)/shard_map/ppermute | solution.py:260
  193.3 8.2 %collective-permute-start.26 = (f32[512,64]{0,1:T(8,128)S(1)}, f32[512,64]{0,1:T(8,128)S(1)}, u32[]{:S(2)}, u32[]{:S(2)}) collective-permute-start(f32[512,64]{0,1:T(8,128)S(1)} %multiply_reduce_fusion.1), channel_id=1, source_target_pairs={{0,2},{1,3},{2,0},{3,1},{4,6},{5,7},{6,4},{7,5},{8,10},{9,11},{10,... | collective-permute-start | bytes 393224 | tf_op jit(solution)/shard_map/ppermute | solution.py:260
  194.9 25.7 %collective-permute-start.29 = (bf16[2,64,1280]{2,1,0:T(8,128)(2,1)S(1)}, bf16[2,64,1280]{2,1,0:T(8,128)(2,1)S(1)}, u32[]{:S(2)}, u32[]{:S(2)}) collective-permute-start(bf16[2,64,1280]{2,1,0:T(8,128)(2,1)S(1)} %copy-done.16), channel_id=1, source_target_pairs={{0,0},{1,4},{2,8},{3,12},{4,1},{5,5},{6,9},{7,13},{8,2},{9,6},{10,... | collective-permute-start | bytes 983048 | tf_op jit(solution)/shard_map/ppermute | solution.py:265
  201.5 19.0 %collective-permute-start.28 = (f32[512,64]{0,1:T(8,128)S(1)}, f32[512,64]{0,1:T(8,128)S(1)}, u32[]{:S(2)}, u32[]{:S(2)}) collective-permute-start(f32[512,64]{0,1:T(8,128)S(1)} %add_add_fusion), channel_id=1, source_target_pairs={{0,0},{1,4},{2,8},{3,12},{4,1},{5,5},{6,9},{7,13},{8,2},{9,6},{10,... | collective-permute-start | bytes 393224 | tf_op jit(solution)/shard_map/ppermute | solution.py:265
  222.8 2.3 collective-permute-start.30
  227.7 9.8 %collective-permute-start.31 = (bf16[128,1280]{1,0:T(8,128)(2,1)S(1)}, bf16[128,1280]{1,0:T(8,128)(2,1)S(1)}, u32[]{:S(2)}, u32[]{:S(2)}) collective-permute-start(bf16[128,1280]{1,0:T(8,128)(2,1)S(1)} %fusion.47), channel_id=1, source_target_pairs={{0,2},{2,0},{1,3},{3,1},{4,6},{6,4},{5,7},{7,5},{8,10},{10,8},{9,1... | collective-permute-start | bytes 983048 | tf_op jit(solution)/shard_map/ppermute | solution.py:470
  237.7 19.2 %collective-permute-start.32 = (bf16[128,1280]{1,0:T(8,128)(2,1)S(1)}, bf16[128,1280]{1,0:T(8,128)(2,1)S(1)}, u32[]{:S(2)}, u32[]{:S(2)}) collective-permute-start(bf16[128,1280]{1,0:T(8,128)(2,1)S(1)} %fusion.21), channel_id=1, source_target_pairs={{0,0},{1,4},{2,8},{3,12},{4,1},{5,5},{6,9},{7,13},{8,2},{9,6},{10,... | collective-permute-start | bytes 983048 | tf_op jit(solution)/shard_map/ppermute | solution.py:265
  (18 other events, 419.8 us)

commit v15 on v14

--- a/solution.py
+++ b/solution.py
@@ -285,6 +285,32 @@
     )
 
 
+def lane_pair():
+    return lax.axis_size("tp") == 2 and lax.axis_size("dp") == 2
+
+
+def lane_sum(part):
+    if lane_pair():
+        part = part + lax.ppermute(part, "dp", [(0, 1), (1, 0)])
+        return part + lax.ppermute(part, "tp", [(0, 1), (1, 0)])
+    side = lax.axis_size("ctx")
+    return part + sum(moved(part, s, "lane") for s in range(1, side))
+
+
+def lane_rows(piece):
+    if lane_pair():
+        other = lax.ppermute(piece, "dp", [(0, 1), (1, 0)])
+        first = lax.axis_index("dp") == 0
+        pair = jnp.where(first, jnp.concatenate([piece, other]), jnp.concatenate([other, piece]))
+        other = lax.ppermute(pair, "tp", [(0, 1), (1, 0)])
+        first = lax.axis_index("tp") == 0
+        return jnp.where(first, jnp.concatenate([pair, other]), jnp.concatenate([other, pair]))
+    side = lax.axis_size("ctx")
+    return in_order(
+        [piece] + [moved(piece, s, "lane") for s in range(1, side)], lax.axis_index(("tp", "dp"))
+    )
+
+
 def square_body(
     tokens,
     lengths,
@@ -335,9 +361,7 @@
     previous = segment_of(jnp.reshape(start_pos - 1, (1,)), request_ends)[0]
 
     tokens_t, down_in_local = lax.optimization_barrier((transposed(tokens), adapter_down_input))
-    stream_rows = in_order(
-        [tokens_t] + [moved(tokens_t, s, "lane") for s in range(1, side)], lane
-    )
+    stream_rows = lane_rows(tokens_t)
     local_owned = lax.dynamic_slice_in_dim(slot_of_position, start_pos, length, 0)
     down_pick = jnp.zeros((length, rank_value), jnp.float32)
     for s in range(side):
@@ -346,9 +370,7 @@
         every = jnp.einsum("pf,efr->per", tokens, piece, preferred_element_type=jnp.float32)
         chosen = local_owned[:, None] == first + jnp.arange(bank_entries, dtype=jnp.int32)[None, :]
         down_pick = down_pick + jnp.sum(every * chosen[:, :, None].astype(jnp.float32), axis=1)
-    rank_local = (
-        down_pick + sum(moved(down_pick, s, "lane") for s in range(1, side))
-    ).astype(jnp.bfloat16)
+    rank_local = lane_sum(down_pick).astype(jnp.bfloat16)
     rank_hidden = in_order(
         [rank_local] + [moved(rank_local, s, "ctx") for s in range(1, side)], here
     )
@@ -389,8 +411,7 @@
     act = jax.nn.silu(convolved)
     x_heads = act[:, :channels].reshape(length, head_count, -1)
     bc_local = act[:, channels:].astype(jnp.bfloat16)
-    bc_pieces = [bc_local] + [moved(bc_local, s, "lane") for s in range(1, side)]
-    bc_all = jnp.transpose(in_order([piece.T for piece in bc_pieces], lane))
+    bc_all = jnp.transpose(lane_rows(bc_local.T))
     state_width = bc_all.shape[1] // 2
     b_proj = bc_all[:, :state_width]
     c_proj = bc_all[:, state_width:]
@@ -438,9 +459,7 @@
         "pc,ecr->per", normed_stream, adapter_down_output, preferred_element_type=jnp.float32
     )
     out_down_pick = jnp.sum(out_down_part * owned_here[:, :, None].astype(jnp.float32), axis=1)
-    rank_hidden_output = transposed(
-        out_down_pick + sum(moved(out_down_pick, s, "lane") for s in range(1, side))
-    )
+    rank_hidden_output = transposed(lane_sum(out_down_pick))
     base_part = jnp.dot(
         normed_stream, output_weight, preferred_element_type=jnp.float32
     ).astype(jnp.bfloat16).astype(jnp.float32)

time: 258 us -> 267 us (1.035)
  starting transfers between devices: 59.7 us -> 63.8 us
  other arithmetic: 13.9 us -> 17.2 us
  waiting for transfers between devices: 145 us -> 148 us
    ppermute x12 -> x8, waiting for transfers between devices: 5.56 us -> 13 us  [the longest x2 9.34 us: lane_rows(): other = lax.ppermute(pair, 'tp', [(0, 1), (1, 0)])]
    ppermute x1, starting transfers between devices: 1.86 us -> 8.37 us  [passed_along(): return lax.ppermute(shard, axis, pairs)]
    ppermute x12, waiting for transfers between devices: 68.8 us -> 62.4 us  [moved(): return lax.ppermute(block, 'ctx', pairs)]
    unnamed x63 -> x51, local copies, waits for them, and re-layouts: 7.01 us -> 3.15 us
    ppermute x12 -> x8, starting transfers between devices: 7.87 us -> 4.71 us  [the longest x2 3.36 us: lane_rows(): other = lax.ppermute(pair, 'tp', [(0, 1), (1, 0)])]
  transfers between devices with their start and end apart: 33 -> 29, of which waited for: 18 -> 23; matrix products, arithmetic and copies ran while one was open for 8% -> 9% of each run, Pallas kernels for 0% -> 0%
where the time goes in v15:
time: 267 us; the launch traced here: 266 us
  waiting for transfers between devices  148 us (55%)
  starting transfers between devices  63.8 us (24%)
  local copies, waits for them, and re-layouts  17.7 us (7%)
  other arithmetic  17.2 us (6%)
  matrix products  17.1 us (6%)
    ppermute x12, waiting for transfers between devices, moved(): return lax.ppermute(block, 'ctx', pairs)  62.4 us
    ppermute x4, waiting for transfers between devices, moved(): return lax.ppermute(block, ('ctx', 'tp', 'dp'), pairs)  42.7 us
    ppermute x12, starting transfers between devices, moved(): return lax.ppermute(block, 'ctx', pairs)  24.3 us
    ppermute x4, starting transfers between devices, moved(): return lax.ppermute(block, ('ctx', 'tp', 'dp'), pairs)  17 us
    ppermute x1, waiting for transfers between devices, square_body(): lax.ppermute(state_and_decay, 'ctx', [(a, a + 1) for a in range(side - 1)])  10.3 us
    ppermute x1, waiting for transfers between devices, square_body(): lax.ppermute(crossing, 'tp', [(0, 1), (1, 0)]).astype(jnp.float32)  9.74 us
    ppermute x2, waiting for transfers between devices, lane_rows(): other = lax.ppermute(pair, 'tp', [(0, 1), (1, 0)])  9.34 us
    ppermute x1, starting transfers between devices, passed_along(): return lax.ppermute(shard, axis, pairs)  8.37 us
  transfers between devices with their start and end apart: 29, of which 23 were waited for; matrix products, arithmetic and copies ran while one was open for 9% of the time, Pallas kernels for 0%

profile of v15, /device:TPU:2, one launch (start us, length us, event | category | flops | bytes accessed | tf_op | source)
XLA Modules:
  0.0 266.1 jit_solution(14396952752943910613)
XLA Ops:
  0.0 4.7 %collective-permute-start = (bf16[128,1280]{1,0:T(8,128)(2,1)}, bf16[128,1280]{1,0:T(8,128)(2,1)S(1)}, u32[]{:S(2)}, u32[]{:S(2)}) collective-permute-start(bf16[128,1280]{1,0:T(8,128)(2,1)} %param.19), channel_id=1, source_target_pairs={{0,0},{1,4},{2,8},{3,12},{4,1},{5,5},{6,9},{7,13},{8,2},{9,6},{10,... | collective-permute-start | bytes 983048 | tf_op jit(solution)/shard_map/ppermute | solution.py:265
  9.6 11.8 %collective-permute-done = bf16[128,1280]{1,0:T(8,128)(2,1)S(1)} collective-permute-done((bf16[128,1280]{1,0:T(8,128)(2,1)}, bf16[128,1280]{1,0:T(8,128)(2,1)S(1)}, u32[]{:S(2)}, u32[]{:S(2)}) %collective-permute-start) | collective-permute-done | bytes 327712 | tf_op jit(solution)/shard_map/ppermute | solution.py:265
  21.9 2.0 collective-permute-start.3
  27.3 9.6 %collective-permute-done.5 = bf16[2,1280,64]{1,2,0:T(8,128)(2,1)S(1)} collective-permute-done((bf16[2,1280,64]{1,2,0:T(8,128)(2,1)}, bf16[2,1280,64]{1,2,0:T(8,128)(2,1)S(1)}, u32[]{:S(2)}, u32[]{:S(2)}) %collective-permute-start.5) | collective-permute-done | bytes 327712 | tf_op jit(solution)/shard_map/ppermute | solution.py:257
  38.4 12.5 %collective-permute-done.4 = bf16[2,1280,64]{1,2,0:T(8,128)(2,1)S(1)} collective-permute-done((bf16[2,1280,64]{1,2,0:T(8,128)(2,1)}, bf16[2,1280,64]{1,2,0:T(8,128)(2,1)S(1)}, u32[]{:S(2)}, u32[]{:S(2)}) %collective-permute-start.4) | collective-permute-done | bytes 327712 | tf_op jit(solution)/shard_map/ppermute | solution.py:257
  61.9 2.7 %collective-permute-done.9 = bf16[128,64]{0,1:T(8,128)(2,1)S(1)} collective-permute-done((bf16[128,64]{0,1:T(8,128)(2,1)S(1)}, bf16[128,64]{0,1:T(8,128)(2,1)S(1)}, u32[]{:S(2)}, u32[]{:S(2)}) %collective-permute-start.9) | collective-permute-done | bytes 16416 | tf_op jit(solution)/shard_map/ppermute | solution.py:257
  67.8 7.0 %collective-permute-done.2 = bf16[256,1280]{1,0:T(8,128)(2,1)S(1)} collective-permute-done((bf16[256,1280]{1,0:T(8,128)(2,1)S(1)}, bf16[256,1280]{1,0:T(8,128)(2,1)S(1)}, u32[]{:S(2)}, u32[]{:S(2)}) %collective-permute-start.2) | collective-permute-done | bytes 655392 | tf_op jit(solution)/shard_map/ppermute | solution.py:305
  78.9 2.8 %collective-permute-start.13 = (bf16[128,1168]{0,1:T(8,128)(2,1)S(1)}, bf16[128,1168]{0,1:T(8,128)(2,1)S(1)}, u32[]{:S(2)}, u32[]{:S(2)}) collective-permute-start(bf16[128,1168]{0,1:T(8,128)(2,1)S(1)} %get-tuple-element.28), channel_id=1, source_target_pairs={{0,12},{4,0},{8,4},{12,8},{1,13},{5,1},{9,5},{13,9},{2,14},{6,2},{... | collective-permute-start | bytes 897032 | tf_op jit(solution)/shard_map/ppermute | solution.py:257
  83.4 6.4 %collective-permute-done.11 = bf16[128,1168]{0,1:T(8,128)(2,1)S(1)} collective-permute-done((bf16[128,1168]{0,1:T(8,128)(2,1)S(1)}, bf16[128,1168]{0,1:T(8,128)(2,1)S(1)}, u32[]{:S(2)}, u32[]{:S(2)}) %collective-permute-start.11) | collective-permute-done | bytes 299040 | tf_op jit(solution)/shard_map/ppermute | solution.py:257
  89.8 10.0 %collective-permute-done.12 = bf16[128,1168]{0,1:T(8,128)(2,1)S(1)} collective-permute-done((bf16[128,1168]{0,1:T(8,128)(2,1)S(1)}, bf16[128,1168]{0,1:T(8,128)(2,1)S(1)}, u32[]{:S(2)}, u32[]{:S(2)}) %collective-permute-start.12) | collective-permute-done | bytes 299040 | tf_op jit(solution)/shard_map/ppermute | solution.py:257
  102.4 8.4 %collective-permute-start.14 = (f32[3,1152]{1,0:T(4,128)S(1)}, f32[3,1152]{1,0:T(4,128)S(1)}, u32[]{:S(2)}, u32[]{:S(2)}) collective-permute-start(f32[3,1152]{1,0:T(4,128)S(1)} %copy.110), channel_id=1, source_target_pairs={{0,4},{4,8},{8,12},{1,5},{5,9},{9,13},{2,6},{6,10},{10,14},{3,7},{... | collective-permute-start | bytes 41480 | tf_op jit(solution)/shard_map/ppermute | solution.py:18
  113.3 4.0 %divide_multiply_fusion = f32[128,1152]{0,1:T(8,128)S(1)} fusion(f32[128,1152]{0,1:T(8,128)} %slice.96, f32[3,1152]{0,1:T(8,128)} %copy.111, f32[128]{0:T(128)S(1)} %get-tuple-element.42, f32[1152]{0:T(1024)S(1)} %get-tuple-element.14, f32[128]{0:T(128)S(1)} %get-tuple-element.43, f32[1152]{0:T(1024)S(1)} %get-tuple-element.15, ...), kind=kLoop, calls=%fused_computation.67 | loop fusion | flops 2654208 | bytes 1213952 | tf_op jit(solution)/shard_map/jit(silu)/mul | solution.py:411
  118.6 2.4 collective-permute-start.16
  121.0 2.4 collective-permute-done.16
  126.2 5.0 %collective-permute-start.17 = (bf16[16,65,256]{2,0,1:T(8,128)(2,1)}, bf16[16,65,256]{2,0,1:T(8,128)(2,1)}, u32[]{:S(2)}, u32[]{:S(2)}) collective-permute-start(bf16[16,65,256]{2,0,1:T(8,128)(2,1)} %copy.117), channel_id=1, source_target_pairs={{0,4},{4,8},{8,12},{1,5},{5,9},{9,13},{2,6},{6,10},{10,14},{3,7},{... | collective-permute-start | bytes 1597448 | tf_op jit(solution)/shard_map/ppermute | solution.py:427
  131.6 10.3 %collective-permute-done.17 = bf16[16,65,256]{2,0,1:T(8,128)(2,1)} collective-permute-done((bf16[16,65,256]{2,0,1:T(8,128)(2,1)}, bf16[16,65,256]{2,0,1:T(8,128)(2,1)}, u32[]{:S(2)}, u32[]{:S(2)}) %collective-permute-start.17) | collective-permute-done | bytes 532512 | tf_op jit(solution)/shard_map/ppermute | solution.py:427
  143.9 4.3 %collective-permute-start.18 = (bf16[16,65,256]{2,0,1:T(8,128)(2,1)S(1)}, bf16[16,65,256]{2,0,1:T(8,128)(2,1)S(1)}, u32[]{:S(2)}, u32[]{:S(2)}) collective-permute-start(bf16[16,65,256]{2,0,1:T(8,128)(2,1)S(1)} %copy.120), channel_id=1, source_target_pairs={{0,8},{4,12},{1,9},{5,13},{2,10},{6,14},{3,11},{7,15},{16,24},{20,... | collective-permute-start | bytes 1597448 | tf_op jit(solution)/shard_map/ppermute | solution.py:437
  148.5 2.2 convolution_bitcast_fusion
  150.9 7.8 %collective-permute-done.18 = bf16[16,65,256]{2,0,1:T(8,128)(2,1)S(1)} collective-permute-done((bf16[16,65,256]{2,0,1:T(8,128)(2,1)S(1)}, bf16[16,65,256]{2,0,1:T(8,128)(2,1)S(1)}, u32[]{:S(2)}, u32[]{:S(2)}) %collective-permute-start.18) | collective-permute-done | bytes 532512 | tf_op jit(solution)/shard_map/ppermute | solution.py:437
  160.0 14.3 %collective-permute-start.19 = (bf16[128,1024]{0,1:T(8,128)(2,1)S(1)}, bf16[128,1024]{0,1:T(8,128)(2,1)S(1)}, u32[]{:S(2)}, u32[]{:S(2)}) collective-permute-start(bf16[128,1024]{0,1:T(8,128)(2,1)S(1)} %fusion.37), channel_id=1, source_target_pairs={{0,12},{4,0},{8,4},{12,8},{1,13},{5,1},{9,5},{13,9},{2,14},{6,2},{... | collective-permute-start | bytes 786440 | tf_op jit(solution)/shard_map/ppermute | solution.py:257
  175.0 6.2 %collective-permute-done.19 = bf16[128,1024]{0,1:T(8,128)(2,1)S(1)} collective-permute-done((bf16[128,1024]{0,1:T(8,128)(2,1)S(1)}, bf16[128,1024]{0,1:T(8,128)(2,1)S(1)}, u32[]{:S(2)}, u32[]{:S(2)}) %collective-permute-start.19) | collective-permute-done | bytes 262176 | tf_op jit(solution)/shard_map/ppermute | solution.py:257
  181.2 13.4 %collective-permute-done.20 = bf16[128,1024]{0,1:T(8,128)(2,1)S(1)} collective-permute-done((bf16[128,1024]{0,1:T(8,128)(2,1)S(1)}, bf16[128,1024]{0,1:T(8,128)(2,1)S(1)}, u32[]{:S(2)}, u32[]{:S(2)}) %collective-permute-start.20) | collective-permute-done | bytes 262176 | tf_op jit(solution)/shard_map/ppermute | solution.py:257
  196.2 2.3 copy.124
  198.5 1.7 fusion.81
  202.3 6.2 %collective-permute-start.25 = (bf16[2,64,1280]{2,1,0:T(8,128)(2,1)S(1)}, bf16[2,64,1280]{2,1,0:T(8,128)(2,1)S(1)}, u32[]{:S(2)}, u32[]{:S(2)}) collective-permute-start(bf16[2,64,1280]{2,1,0:T(8,128)(2,1)S(1)} %copy-done.16), channel_id=1, source_target_pairs={{0,0},{1,4},{2,8},{3,12},{4,1},{5,5},{6,9},{7,13},{8,2},{9,6},{10,... | collective-permute-start | bytes 983048 | tf_op jit(solution)/shard_map/ppermute | solution.py:265
  208.6 4.1 %collective-permute-start.24 = (f32[512,64]{0,1:T(8,128)S(1)}, f32[512,64]{0,1:T(8,128)S(1)}, u32[]{:S(2)}, u32[]{:S(2)}) collective-permute-start(f32[512,64]{0,1:T(8,128)S(1)} %add.340), channel_id=1, source_target_pairs={{0,0},{1,4},{2,8},{3,12},{4,1},{5,5},{6,9},{7,13},{8,2},{9,6},{10,... | collective-permute-start | bytes 393224 | tf_op jit(solution)/shard_map/ppermute | solution.py:265
  212.7 2.7 %fusion = f32[512,1280]{1,0:T(8,128)S(1)} fusion(bf16[512,1024]{1,0:T(8,128)(2,1)} %bitcast.141, bf16[1024,1280]{1,0:T(8,128)(2,1)S(1)} %copy-done), kind=kOutput, calls=%fused_computation.3 | convolution fusion | flops 1343488000 | bytes 6291456 | tf_op jit(solution)/shard_map/dot_general | solution.py:463
  215.4 13.5 %collective-permute-done.24 = f32[512,64]{0,1:T(8,128)S(1)} collective-permute-done((f32[512,64]{0,1:T(8,128)S(1)}, f32[512,64]{0,1:T(8,128)S(1)}, u32[]{:S(2)}, u32[]{:S(2)}) %collective-permute-start.24) | collective-permute-done | bytes 131104 | tf_op jit(solution)/shard_map/ppermute | solution.py:265
  231.2 2.2 collective-permute-done.26
  236.1 9.7 %collective-permute-done.27 = bf16[128,1280]{1,0:T(8,128)(2,1)S(1)} collective-permute-done((bf16[128,1280]{1,0:T(8,128)(2,1)S(1)}, bf16[128,1280]{1,0:T(8,128)(2,1)S(1)}, u32[]{:S(2)}, u32[]{:S(2)}) %collective-permute-start.27) | collective-permute-done | bytes 327712 | tf_op jit(solution)/shard_map/ppermute | solution.py:489
  246.0 1.9 collective-permute-start.28
  248.0 17.4 %collective-permute-done.28 = bf16[128,1280]{1,0:T(8,128)(2,1)S(1)} collective-permute-done((bf16[128,1280]{1,0:T(8,128)(2,1)S(1)}, bf16[128,1280]{1,0:T(8,128)(2,1)S(1)}, u32[]{:S(2)}, u32[]{:S(2)}) %collective-permute-start.28) | collective-permute-done | bytes 327712 | tf_op jit(solution)/shard_map/ppermute | solution.py:265
  (175 shorter events, 52.0 us)
Async XLA Ops:
  0.0 212.7 %copy-start = (bf16[1024,1280]{1,0:T(8,128)(2,1)S(1)}, bf16[1024,1280]{1,0:T(8,128)(2,1)}, u32[]{:S(2)}) copy-start(bf16[1024,1280]{1,0:T(8,128)(2,1)} %param.32) | copy-start | bytes 7864324
  0.0 21.3 %collective-permute-start = (bf16[128,1280]{1,0:T(8,128)(2,1)}, bf16[128,1280]{1,0:T(8,128)(2,1)S(1)}, u32[]{:S(2)}, u32[]{:S(2)}) collective-permute-start(bf16[128,1280]{1,0:T(8,128)(2,1)} %param.19), channel_id=1, source_target_pairs={{0,0},{1,4},{2,8},{3,12},{4,1},{5,5},{6,9},{7,13},{8,2},{9,6},{10,... | collective-permute-start | bytes 983048 | tf_op jit(solution)/shard_map/ppermute | solution.py:265
  9.4 41.9 %copy-start.8 = (f32[4,1024]{1,0:T(4,128)S(1)}, f32[4,1024]{1,0:T(4,128)}, u32[]{:S(2)}) copy-start(f32[4,1024]{1,0:T(4,128)} %param.26) | copy-start | bytes 49156
  9.4 43.7 %copy-start.11 = (f32[4,128]{1,0:T(4,128)S(1)}, f32[4,128]{1,0:T(4,128)}, u32[]{:S(2)}) copy-start(f32[4,128]{1,0:T(4,128)} %param.27) | copy-start | bytes 6148
  21.3 15.5 %collective-permute-start.5 = (bf16[2,1280,64]{1,2,0:T(8,128)(2,1)}, bf16[2,1280,64]{1,2,0:T(8,128)(2,1)S(1)}, u32[]{:S(2)}, u32[]{:S(2)}) collective-permute-start(bf16[2,1280,64]{1,2,0:T(8,128)(2,1)} %param.33), channel_id=1, source_target_pairs={{0,12},{4,0},{8,4},{12,8},{1,13},{5,1},{9,5},{13,9},{2,14},{6,2},{... | collective-permute-start | bytes 983048 | tf_op jit(solution)/shard_map/ppermute | solution.py:257
  21.9 16.2 %collective-permute-start.3 = (bf16[2,1280,64]{1,2,0:T(8,128)(2,1)}, bf16[2,1280,64]{1,2,0:T(8,128)(2,1)S(1)}, u32[]{:S(2)}, u32[]{:S(2)}) collective-permute-start(bf16[2,1280,64]{1,2,0:T(8,128)(2,1)} %param.33), channel_id=1, source_target_pairs={{0,4},{4,8},{8,12},{12,0},{1,5},{5,9},{9,13},{13,1},{2,6},{6,10},{... | collective-permute-start | bytes 983048 | tf_op jit(solution)/shard_map/ppermute | solution.py:257
  24.6 26.3 %collective-permute-start.4 = (bf16[2,1280,64]{1,2,0:T(8,128)(2,1)}, bf16[2,1280,64]{1,2,0:T(8,128)(2,1)S(1)}, u32[]{:S(2)}, u32[]{:S(2)}) collective-permute-start(bf16[2,1280,64]{1,2,0:T(8,128)(2,1)} %param.33), channel_id=1, source_target_pairs={{0,8},{4,12},{8,0},{12,4},{1,9},{5,13},{9,1},{13,5},{2,10},{6,14},... | collective-permute-start | bytes 983048 | tf_op jit(solution)/shard_map/ppermute | solution.py:257
  51.2 1.3 collective-permute-start.6
  51.9 7.0 %collective-permute-start.1 = (bf16[128,1280]{1,0:T(8,128)(2,1)S(1)}, bf16[128,1280]{1,0:T(8,128)(2,1)S(1)}, u32[]{:S(2)}, u32[]{:S(2)}) collective-permute-start(bf16[128,1280]{1,0:T(8,128)(2,1)S(1)} %collective-permute-done), channel_id=1, source_target_pairs={{0,1},{1,0},{2,3},{3,2},{4,5},{5,4},{6,7},{7,6},{8,9},{9,8},{10,11... | collective-permute-start | bytes 983048 | tf_op jit(solution)/shard_map/ppermute | solution.py:302
  53.1 4.2 %collective-permute-start.7 = (f32[128,64]{0,1:T(8,128)}, f32[128,64]{0,1:T(8,128)}, u32[]{:S(2)}, u32[]{:S(2)}) collective-permute-start(f32[128,64]{0,1:T(8,128)} %add.303), channel_id=1, source_target_pairs={{0,2},{2,0},{1,3},{3,1},{4,6},{6,4},{5,7},{7,5},{8,10},{10,8},{9,1... | collective-permute-start | bytes 98312 | tf_op jit(solution)/shard_map/ppermute | solution.py:295
  58.1 3.8 %collective-permute-start.8 = (bf16[128,64]{0,1:T(8,128)(2,1)S(1)}, bf16[128,64]{0,1:T(8,128)(2,1)S(1)}, u32[]{:S(2)}, u32[]{:S(2)}) collective-permute-start(bf16[128,64]{0,1:T(8,128)(2,1)S(1)} %add_convert_fusion.1), channel_id=1, source_target_pairs={{0,12},{4,0},{8,4},{12,8},{1,13},{5,1},{9,5},{13,9},{2,14},{6,2},{... | collective-permute-start | bytes 49160 | tf_op jit(solution)/shard_map/ppermute | solution.py:257
  59.0 15.8 %collective-permute-start.2 = (bf16[256,1280]{1,0:T(8,128)(2,1)S(1)}, bf16[256,1280]{1,0:T(8,128)(2,1)S(1)}, u32[]{:S(2)}, u32[]{:S(2)}) collective-permute-start(bf16[256,1280]{1,0:T(8,128)(2,1)S(1)} %maximum_select_fusion.1), channel_id=1, source_target_pairs={{0,2},{2,0},{1,3},{3,1},{4,6},{6,4},{5,7},{7,5},{8,10},{10,8},{9,1... | collective-permute-start | bytes 1966088 | tf_op jit(solution)/shard_map/ppermute | solution.py:305
  59.9 4.6 %collective-permute-start.9 = (bf16[128,64]{0,1:T(8,128)(2,1)S(1)}, bf16[128,64]{0,1:T(8,128)(2,1)S(1)}, u32[]{:S(2)}, u32[]{:S(2)}) collective-permute-start(bf16[128,64]{0,1:T(8,128)(2,1)S(1)} %add_convert_fusion.1), channel_id=1, source_target_pairs={{0,8},{4,12},{8,0},{12,4},{1,9},{5,13},{9,1},{13,5},{2,10},{6,14},... | collective-permute-start | bytes 49160 | tf_op jit(solution)/shard_map/ppermute | solution.py:257
  59.9 5.6 %collective-permute-start.10 = (bf16[128,64]{0,1:T(8,128)(2,1)S(1)}, bf16[128,64]{0,1:T(8,128)(2,1)S(1)}, u32[]{:S(2)}, u32[]{:S(2)}) collective-permute-start(bf16[128,64]{0,1:T(8,128)(2,1)S(1)} %add_convert_fusion.1), channel_id=1, source_target_pairs={{0,4},{4,8},{8,12},{12,0},{1,5},{5,9},{9,13},{13,1},{2,6},{6,10},{... | collective-permute-start | bytes 49160 | tf_op jit(solution)/shard_map/ppermute | solution.py:257
  77.9 12.0 %collective-permute-start.11 = (bf16[128,1168]{0,1:T(8,128)(2,1)S(1)}, bf16[128,1168]{0,1:T(8,128)(2,1)S(1)}, u32[]{:S(2)}, u32[]{:S(2)}) collective-permute-start(bf16[128,1168]{0,1:T(8,128)(2,1)S(1)} %get-tuple-element.27), channel_id=1, source_target_pairs={{0,4},{4,8},{8,12},{12,0},{1,5},{5,9},{9,13},{13,1},{2,6},{6,10},{... | collective-permute-start | bytes 897032 | tf_op jit(solution)/shard_map/ppermute | solution.py:257
  78.9 21.0 %collective-permute-start.12 = (bf16[128,1168]{0,1:T(8,128)(2,1)S(1)}, bf16[128,1168]{0,1:T(8,128)(2,1)S(1)}, u32[]{:S(2)}, u32[]{:S(2)}) collective-permute-start(bf16[128,1168]{0,1:T(8,128)(2,1)S(1)} %get-tuple-element.29), channel_id=1, source_target_pairs={{0,8},{4,12},{8,0},{12,4},{1,9},{5,13},{9,1},{13,5},{2,10},{6,14},... | collective-permute-start | bytes 897032 | tf_op jit(solution)/shard_map/ppermute | solution.py:257
  78.9 21.0 %collective-permute-start.13 = (bf16[128,1168]{0,1:T(8,128)(2,1)S(1)}, bf16[128,1168]{0,1:T(8,128)(2,1)S(1)}, u32[]{:S(2)}, u32[]{:S(2)}) collective-permute-start(bf16[128,1168]{0,1:T(8,128)(2,1)S(1)} %get-tuple-element.28), channel_id=1, source_target_pairs={{0,12},{4,0},{8,4},{12,8},{1,13},{5,1},{9,5},{13,9},{2,14},{6,2},{... | collective-permute-start | bytes 897032 | tf_op jit(solution)/shard_map/ppermute | solution.py:257
  102.4 9.8 %collective-permute-start.14 = (f32[3,1152]{1,0:T(4,128)S(1)}, f32[3,1152]{1,0:T(4,128)S(1)}, u32[]{:S(2)}, u32[]{:S(2)}) collective-permute-start(f32[3,1152]{1,0:T(4,128)S(1)} %copy.110), channel_id=1, source_target_pairs={{0,4},{4,8},{8,12},{1,5},{5,9},{9,13},{2,6},{6,10},{10,14},{3,7},{... | collective-permute-start | bytes 41480 | tf_op jit(solution)/shard_map/ppermute | solution.py:18
  117.3 1.3 collective-permute-start.15
  118.6 4.8 %collective-permute-start.16 = (bf16[256,128]{1,0:T(8,128)(2,1)S(1)}, bf16[256,128]{1,0:T(8,128)(2,1)S(1)}, u32[]{:S(2)}, u32[]{:S(2)}) collective-permute-start(bf16[256,128]{1,0:T(8,128)(2,1)S(1)} %maximum_select_fusion.3), channel_id=1, source_target_pairs={{0,2},{2,0},{1,3},{3,1},{4,6},{6,4},{5,7},{7,5},{8,10},{10,8},{9,1... | collective-permute-start | bytes 196616 | tf_op jit(solution)/shard_map/ppermute | solution.py:305
  126.2 15.7 %collective-permute-start.17 = (bf16[16,65,256]{2,0,1:T(8,128)(2,1)}, bf16[16,65,256]{2,0,1:T(8,128)(2,1)}, u32[]{:S(2)}, u32[]{:S(2)}) collective-permute-start(bf16[16,65,256]{2,0,1:T(8,128)(2,1)} %copy.117), channel_id=1, source_target_pairs={{0,4},{4,8},{8,12},{1,5},{5,9},{9,13},{2,6},{6,10},{10,14},{3,7},{... | collective-permute-start | bytes 1597448 | tf_op jit(solution)/shard_map/ppermute | solution.py:427
  143.9 14.7 %collective-permute-start.18 = (bf16[16,65,256]{2,0,1:T(8,128)(2,1)S(1)}, bf16[16,65,256]{2,0,1:T(8,128)(2,1)S(1)}, u32[]{:S(2)}, u32[]{:S(2)}) collective-permute-start(bf16[16,65,256]{2,0,1:T(8,128)(2,1)S(1)} %copy.120), channel_id=1, source_target_pairs={{0,8},{4,12},{1,9},{5,13},{2,10},{6,14},{3,11},{7,15},{16,24},{20,... | collective-permute-start | bytes 1597448 | tf_op jit(solution)/shard_map/ppermute | solution.py:437
  160.0 21.1 %collective-permute-start.19 = (bf16[128,1024]{0,1:T(8,128)(2,1)S(1)}, bf16[128,1024]{0,1:T(8,128)(2,1)S(1)}, u32[]{:S(2)}, u32[]{:S(2)}) collective-permute-start(bf16[128,1024]{0,1:T(8,128)(2,1)S(1)} %fusion.37), channel_id=1, source_target_pairs={{0,12},{4,0},{8,4},{12,8},{1,13},{5,1},{9,5},{13,9},{2,14},{6,2},{... | collective-permute-start | bytes 786440 | tf_op jit(solution)/shard_map/ppermute | solution.py:257
  174.3 20.2 %collective-permute-start.20 = (bf16[128,1024]{0,1:T(8,128)(2,1)S(1)}, bf16[128,1024]{0,1:T(8,128)(2,1)S(1)}, u32[]{:S(2)}, u32[]{:S(2)}) collective-permute-start(bf16[128,1024]{0,1:T(8,128)(2,1)S(1)} %fusion.37), channel_id=1, source_target_pairs={{0,8},{4,12},{8,0},{12,4},{1,9},{5,13},{9,1},{13,5},{2,10},{6,14},... | collective-permute-start | bytes 786440 | tf_op jit(solution)/shard_map/ppermute | solution.py:257
  174.3 20.3 %collective-permute-start.21 = (bf16[128,1024]{0,1:T(8,128)(2,1)S(1)}, bf16[128,1024]{0,1:T(8,128)(2,1)S(1)}, u32[]{:S(2)}, u32[]{:S(2)}) collective-permute-start(bf16[128,1024]{0,1:T(8,128)(2,1)S(1)} %fusion.37), channel_id=1, source_target_pairs={{0,4},{4,8},{8,12},{12,0},{1,5},{5,9},{9,13},{13,1},{2,6},{6,10},{... | collective-permute-start | bytes 786440 | tf_op jit(solution)/shard_map/ppermute | solution.py:257
  200.2 1.4 collective-permute-start.22
  201.6 6.9 %collective-permute-start.23 = (f32[512,64]{0,1:T(8,128)S(1)}, f32[512,64]{0,1:T(8,128)S(1)}, u32[]{:S(2)}, u32[]{:S(2)}) collective-permute-start(f32[512,64]{0,1:T(8,128)S(1)} %add.339), channel_id=1, source_target_pairs={{0,2},{2,0},{1,3},{3,1},{4,6},{6,4},{5,7},{7,5},{8,10},{10,8},{9,1... | collective-permute-start | bytes 393224 | tf_op jit(solution)/shard_map/ppermute | solution.py:295
  202.3 26.6 %collective-permute-start.25 = (bf16[2,64,1280]{2,1,0:T(8,128)(2,1)S(1)}, bf16[2,64,1280]{2,1,0:T(8,128)(2,1)S(1)}, u32[]{:S(2)}, u32[]{:S(2)}) collective-permute-start(bf16[2,64,1280]{2,1,0:T(8,128)(2,1)S(1)} %copy-done.16), channel_id=1, source_target_pairs={{0,0},{1,4},{2,8},{3,12},{4,1},{5,5},{6,9},{7,13},{8,2},{9,6},{10,... | collective-permute-start | bytes 983048 | tf_op jit(solution)/shard_map/ppermute | solution.py:265
  208.6 20.3 %collective-permute-start.24 = (f32[512,64]{0,1:T(8,128)S(1)}, f32[512,64]{0,1:T(8,128)S(1)}, u32[]{:S(2)}, u32[]{:S(2)}) collective-permute-start(f32[512,64]{0,1:T(8,128)S(1)} %add.340), channel_id=1, source_target_pairs={{0,0},{1,4},{2,8},{3,12},{4,1},{5,5},{6,9},{7,13},{8,2},{9,6},{10,... | collective-permute-start | bytes 393224 | tf_op jit(solution)/shard_map/ppermute | solution.py:265
  231.1 2.3 collective-permute-start.26
  236.1 9.8 %collective-permute-start.27 = (bf16[128,1280]{1,0:T(8,128)(2,1)S(1)}, bf16[128,1280]{1,0:T(8,128)(2,1)S(1)}, u32[]{:S(2)}, u32[]{:S(2)}) collective-permute-start(bf16[128,1280]{1,0:T(8,128)(2,1)S(1)} %fusion.47), channel_id=1, source_target_pairs={{0,2},{2,0},{1,3},{3,1},{4,6},{6,4},{5,7},{7,5},{8,10},{10,8},{9,1... | collective-permute-start | bytes 983048 | tf_op jit(solution)/shard_map/ppermute | solution.py:489
  246.0 19.4 %collective-permute-start.28 = (bf16[128,1280]{1,0:T(8,128)(2,1)S(1)}, bf16[128,1280]{1,0:T(8,128)(2,1)S(1)}, u32[]{:S(2)}, u32[]{:S(2)}) collective-permute-start(bf16[128,1280]{1,0:T(8,128)(2,1)S(1)} %fusion.21), channel_id=1, source_target_pairs={{0,0},{1,4},{2,8},{3,12},{4,1},{5,5},{6,9},{7,13},{8,2},{9,6},{10,... | collective-permute-start | bytes 983048 | tf_op jit(solution)/shard_map/ppermute | solution.py:265
  (15 other events, 228.0 us)

commit v16 on v14

--- a/solution.py
+++ b/solution.py
@@ -438,9 +438,12 @@
         "pc,ecr->per", normed_stream, adapter_down_output, preferred_element_type=jnp.float32
     )
     out_down_pick = jnp.sum(out_down_part * owned_here[:, :, None].astype(jnp.float32), axis=1)
-    rank_hidden_output = transposed(
-        out_down_pick + sum(moved(out_down_pick, s, "lane") for s in range(1, side))
-    )
+    if lax.axis_size("tp") == 2 and lax.axis_size("dp") == 2:
+        summed_pick = out_down_pick + lax.ppermute(out_down_pick, "dp", [(0, 1), (1, 0)])
+        summed_pick = summed_pick + lax.ppermute(summed_pick, "tp", [(0, 1), (1, 0)])
+    else:
+        summed_pick = out_down_pick + sum(moved(out_down_pick, s, "lane") for s in range(1, side))
+    rank_hidden_output = transposed(summed_pick)
     base_part = jnp.dot(
         normed_stream, output_weight, preferred_element_type=jnp.float32
     ).astype(jnp.bfloat16).astype(jnp.float32)

time: 258 us -> 256 us (level)
    ppermute x4, starting transfers between devices: 14.3 us -> 17 us  [moved(): return lax.ppermute(block, ('ctx', 'tp', 'dp'), pairs)]
    ppermute x12 -> x9, waiting for transfers between devices: 5.56 us -> 3.13 us  [moved(): return lax.ppermute(block, ('tp', 'dp'), pairs)]
    ppermute x12 -> x9, starting transfers between devices: 7.87 us -> 5.72 us  [moved(): return lax.ppermute(block, ('tp', 'dp'), pairs)]
    unnamed x63 -> x59, local copies, waits for them, and re-layouts: 7.01 us -> 5.05 us
  transfers between devices with their start and end apart: 33 -> 32, of which waited for: 18 -> 18; matrix products, arithmetic and copies ran while one was open for 8% -> 9% of each run, Pallas kernels for 0% -> 0%
where the time goes in v16:
time: 256 us; the launch traced here: 255 us
  waiting for transfers between devices  143 us (56%)
  starting transfers between devices  62 us (24%)
  local copies, waits for them, and re-layouts  17.6 us (7%)
  matrix products  17.3 us (7%)
  other arithmetic  13.1 us (5%)
    ppermute x12, waiting for transfers between devices, moved(): return lax.ppermute(block, 'ctx', pairs)  68.4 us
    ppermute x4, waiting for transfers between devices, moved(): return lax.ppermute(block, ('ctx', 'tp', 'dp'), pairs)  42.4 us
    ppermute x12, starting transfers between devices, moved(): return lax.ppermute(block, 'ctx', pairs)  24.1 us
    ppermute x4, starting transfers between devices, moved(): return lax.ppermute(block, ('ctx', 'tp', 'dp'), pairs)  17 us
    ppermute x1, waiting for transfers between devices, square_body(): lax.ppermute(crossing, 'tp', [(0, 1), (1, 0)]).astype(jnp.float32)  9.74 us
    ppermute x1, waiting for transfers between devices, square_body(): lax.ppermute(state_and_decay, 'ctx', [(a, a + 1) for a in range(side - 1)])  9.32 us
    ppermute x1, waiting for transfers between devices, square_body(): far = lax.ppermute(pair, 'ctx', [(a, a + 2) for a in range(side - 2)])  6.49 us
    ppermute x1, starting transfers between devices, square_body(): far = lax.ppermute(pair, 'ctx', [(a, a + 2) for a in range(side - 2)])  6.33 us
  transfers between devices with their start and end apart: 32, of which 18 were waited for; matrix products, arithmetic and copies ran while one was open for 9% of the time, Pallas kernels for 0%

profile of v16, /device:TPU:2, one launch (start us, length us, event | category | flops | bytes accessed | tf_op | source)
XLA Modules:
  0.0 255.3 jit_solution(329128032210852830)
XLA Ops:
  0.0 4.7 %collective-permute-start = (bf16[128,1280]{1,0:T(8,128)(2,1)}, bf16[128,1280]{1,0:T(8,128)(2,1)S(1)}, u32[]{:S(2)}, u32[]{:S(2)}) collective-permute-start(bf16[128,1280]{1,0:T(8,128)(2,1)} %param.19), channel_id=1, source_target_pairs={{0,0},{1,4},{2,8},{3,12},{4,1},{5,5},{6,9},{7,13},{8,2},{9,6},{10,... | collective-permute-start | bytes 983048 | tf_op jit(solution)/shard_map/ppermute | solution.py:265
  9.6 11.8 %collective-permute-done = bf16[128,1280]{1,0:T(8,128)(2,1)S(1)} collective-permute-done((bf16[128,1280]{1,0:T(8,128)(2,1)}, bf16[128,1280]{1,0:T(8,128)(2,1)S(1)}, u32[]{:S(2)}, u32[]{:S(2)}) %collective-permute-start) | collective-permute-done | bytes 327712 | tf_op jit(solution)/shard_map/ppermute | solution.py:265
  22.1 3.4 %collective-permute-start.5 = (bf16[2,1280,64]{1,2,0:T(8,128)(2,1)}, bf16[2,1280,64]{1,2,0:T(8,128)(2,1)}, u32[]{:S(2)}, u32[]{:S(2)}) collective-permute-start(bf16[2,1280,64]{1,2,0:T(8,128)(2,1)} %param.33), channel_id=1, source_target_pairs={{0,8},{4,12},{8,0},{12,4},{1,9},{5,13},{9,1},{13,5},{2,10},{6,14},... | collective-permute-start | bytes 983048 | tf_op jit(solution)/shard_map/ppermute | solution.py:257
  28.1 2.7 %collective-permute-start.1 = (bf16[128,1280]{1,0:T(8,128)(2,1)S(1)}, bf16[128,1280]{1,0:T(8,128)(2,1)S(1)}, u32[]{:S(2)}, u32[]{:S(2)}) collective-permute-start(bf16[128,1280]{1,0:T(8,128)(2,1)S(1)} %collective-permute-done), channel_id=1, source_target_pairs={{0,3},{1,0},{2,1},{3,2},{4,7},{5,4},{6,5},{7,6},{8,11},{9,8},{10,9... | collective-permute-start | bytes 983048 | tf_op jit(solution)/shard_map/ppermute | solution.py:260
  34.1 20.1 %collective-permute-done.5 = bf16[2,1280,64]{1,2,0:T(8,128)(2,1)} collective-permute-done((bf16[2,1280,64]{1,2,0:T(8,128)(2,1)}, bf16[2,1280,64]{1,2,0:T(8,128)(2,1)}, u32[]{:S(2)}, u32[]{:S(2)}) %collective-permute-start.5) | collective-permute-done | bytes 327712 | tf_op jit(solution)/shard_map/ppermute | solution.py:257
  61.9 2.0 collective-permute-start.12
  66.5 1.6 collective-permute-done.12
  69.4 1.9 collective-permute-start.15
  72.8 6.2 %collective-permute-done.15 = bf16[128,1168]{0,1:T(8,128)(2,1)S(1)} collective-permute-done((bf16[128,1168]{0,1:T(8,128)(2,1)S(1)}, bf16[128,1168]{0,1:T(8,128)(2,1)S(1)}, u32[]{:S(2)}, u32[]{:S(2)}) %collective-permute-start.15) | collective-permute-done | bytes 299040 | tf_op jit(solution)/shard_map/ppermute | solution.py:257
  79.0 17.8 %collective-permute-done.14 = bf16[128,1168]{0,1:T(8,128)(2,1)S(1)} collective-permute-done((bf16[128,1168]{0,1:T(8,128)(2,1)S(1)}, bf16[128,1168]{0,1:T(8,128)(2,1)S(1)}, u32[]{:S(2)}, u32[]{:S(2)}) %collective-permute-start.14) | collective-permute-done | bytes 299040 | tf_op jit(solution)/shard_map/ppermute | solution.py:257
  99.2 1.9 collective-permute-start.16
  102.7 3.3 %divide_multiply_fusion = f32[128,1152]{0,1:T(8,128)S(1)} fusion(f32[128,1152]{0,1:T(8,128)} %slice.96, f32[3,1152]{0,1:T(8,128)S(1)} %copy.118, f32[128]{0:T(128)S(1)} %get-tuple-element.42, f32[1152]{0:T(1024)S(1)} %get-tuple-element.14, f32[128]{0:T(128)S(1)} %get-tuple-element.43, f32[1152]{0:T(1024)S(1)} %get-tuple-element.15, ...), kind=kLoop, calls=%fused_computation.65 | loop fusion | flops 2654208 | bytes 1213952 | tf_op jit(solution)/shard_map/jit(silu)/mul | solution.py:389
  107.7 2.4 collective-permute-done.18
  113.8 5.2 %collective-permute-start.20 = (bf16[16,65,256]{2,0,1:T(8,128)(2,1)}, bf16[16,65,256]{2,0,1:T(8,128)(2,1)}, u32[]{:S(2)}, u32[]{:S(2)}) collective-permute-start(bf16[16,65,256]{2,0,1:T(8,128)(2,1)} %copy.124), channel_id=1, source_target_pairs={{0,4},{4,8},{8,12},{1,5},{5,9},{9,13},{2,6},{6,10},{10,14},{3,7},{... | collective-permute-start | bytes 1597448 | tf_op jit(solution)/shard_map/ppermute | solution.py:406
  119.3 9.3 %collective-permute-done.20 = bf16[16,65,256]{2,0,1:T(8,128)(2,1)} collective-permute-done((bf16[16,65,256]{2,0,1:T(8,128)(2,1)}, bf16[16,65,256]{2,0,1:T(8,128)(2,1)}, u32[]{:S(2)}, u32[]{:S(2)}) %collective-permute-start.20) | collective-permute-done | bytes 532512 | tf_op jit(solution)/shard_map/ppermute | solution.py:406
  130.7 6.3 %collective-permute-start.21 = (bf16[16,65,256]{2,0,1:T(8,128)(2,1)S(1)}, bf16[16,65,256]{2,0,1:T(8,128)(2,1)S(1)}, u32[]{:S(2)}, u32[]{:S(2)}) collective-permute-start(bf16[16,65,256]{2,0,1:T(8,128)(2,1)S(1)} %copy.127), channel_id=1, source_target_pairs={{0,8},{4,12},{1,9},{5,13},{2,10},{6,14},{3,11},{7,15},{16,24},{20,... | collective-permute-start | bytes 1597448 | tf_op jit(solution)/shard_map/ppermute | solution.py:416
  137.2 2.3 convolution_bitcast_fusion
  139.7 6.5 %collective-permute-done.21 = bf16[16,65,256]{2,0,1:T(8,128)(2,1)S(1)} collective-permute-done((bf16[16,65,256]{2,0,1:T(8,128)(2,1)S(1)}, bf16[16,65,256]{2,0,1:T(8,128)(2,1)S(1)}, u32[]{:S(2)}, u32[]{:S(2)}) %collective-permute-start.21) | collective-permute-done | bytes 532512 | tf_op jit(solution)/shard_map/ppermute | solution.py:416
  147.5 14.8 %collective-permute-start.22 = (bf16[128,1024]{0,1:T(8,128)(2,1)S(1)}, bf16[128,1024]{0,1:T(8,128)(2,1)S(1)}, u32[]{:S(2)}, u32[]{:S(2)}) collective-permute-start(bf16[128,1024]{0,1:T(8,128)(2,1)S(1)} %fusion.37), channel_id=1, source_target_pairs={{0,12},{4,0},{8,4},{12,8},{1,13},{5,1},{9,5},{13,9},{2,14},{6,2},{... | collective-permute-start | bytes 786440 | tf_op jit(solution)/shard_map/ppermute | solution.py:257
  162.9 6.2 %collective-permute-done.22 = bf16[128,1024]{0,1:T(8,128)(2,1)S(1)} collective-permute-done((bf16[128,1024]{0,1:T(8,128)(2,1)S(1)}, bf16[128,1024]{0,1:T(8,128)(2,1)S(1)}, u32[]{:S(2)}, u32[]{:S(2)}) %collective-permute-start.22) | collective-permute-done | bytes 262176 | tf_op jit(solution)/shard_map/ppermute | solution.py:257
  169.1 13.9 %collective-permute-done.23 = bf16[128,1024]{0,1:T(8,128)(2,1)S(1)} collective-permute-done((bf16[128,1024]{0,1:T(8,128)(2,1)S(1)}, bf16[128,1024]{0,1:T(8,128)(2,1)S(1)}, u32[]{:S(2)}, u32[]{:S(2)}) %collective-permute-start.23) | collective-permute-done | bytes 262176 | tf_op jit(solution)/shard_map/ppermute | solution.py:257
  184.6 2.3 copy.130
  186.9 1.7 fusion.79
  190.1 1.7 collective-permute-start.26
  191.8 5.2 %collective-permute-start.28 = (bf16[2,64,1280]{2,1,0:T(8,128)(2,1)S(1)}, bf16[2,64,1280]{2,1,0:T(8,128)(2,1)S(1)}, u32[]{:S(2)}, u32[]{:S(2)}) collective-permute-start(bf16[2,64,1280]{2,1,0:T(8,128)(2,1)S(1)} %copy-done.14), channel_id=1, source_target_pairs={{0,0},{1,4},{2,8},{3,12},{4,1},{5,5},{6,9},{7,13},{8,2},{9,6},{10,... | collective-permute-start | bytes 983048 | tf_op jit(solution)/shard_map/ppermute | solution.py:265
  197.1 5.1 %collective-permute-start.27 = (f32[512,64]{0,1:T(8,128)S(1)}, f32[512,64]{0,1:T(8,128)S(1)}, u32[]{:S(2)}, u32[]{:S(2)}) collective-permute-start(f32[512,64]{0,1:T(8,128)S(1)} %add.365), channel_id=1, source_target_pairs={{0,0},{1,4},{2,8},{3,12},{4,1},{5,5},{6,9},{7,13},{8,2},{9,6},{10,... | collective-permute-start | bytes 393224 | tf_op jit(solution)/shard_map/ppermute | solution.py:265
  202.2 2.7 %fusion = f32[512,1280]{1,0:T(8,128)S(1)} fusion(bf16[512,1024]{1,0:T(8,128)(2,1)} %bitcast.178, bf16[1024,1280]{1,0:T(8,128)(2,1)S(1)} %copy-done), kind=kOutput, calls=%fused_computation.3 | convolution fusion | flops 1343488000 | bytes 6291456 | tf_op jit(solution)/shard_map/dot_general | solution.py:447
  204.9 13.3 %collective-permute-done.27 = f32[512,64]{0,1:T(8,128)S(1)} collective-permute-done((f32[512,64]{0,1:T(8,128)S(1)}, f32[512,64]{0,1:T(8,128)S(1)}, u32[]{:S(2)}, u32[]{:S(2)}) %collective-permute-start.27) | collective-permute-done | bytes 131104 | tf_op jit(solution)/shard_map/ppermute | solution.py:265
  220.5 2.2 collective-permute-done.29
  225.4 9.7 %collective-permute-done.30 = bf16[128,1280]{1,0:T(8,128)(2,1)S(1)} collective-permute-done((bf16[128,1280]{1,0:T(8,128)(2,1)S(1)}, bf16[128,1280]{1,0:T(8,128)(2,1)S(1)}, u32[]{:S(2)}, u32[]{:S(2)}) %collective-permute-start.30) | collective-permute-done | bytes 327712 | tf_op jit(solution)/shard_map/ppermute | solution.py:473
  235.3 1.9 collective-permute-start.31
  237.3 17.3 %collective-permute-done.31 = bf16[128,1280]{1,0:T(8,128)(2,1)S(1)} collective-permute-done((bf16[128,1280]{1,0:T(8,128)(2,1)S(1)}, bf16[128,1280]{1,0:T(8,128)(2,1)S(1)}, u32[]{:S(2)}, u32[]{:S(2)}) %collective-permute-start.31) | collective-permute-done | bytes 327712 | tf_op jit(solution)/shard_map/ppermute | solution.py:265
  (190 shorter events, 45.6 us)
Async XLA Ops:
  0.0 21.3 %collective-permute-start = (bf16[128,1280]{1,0:T(8,128)(2,1)}, bf16[128,1280]{1,0:T(8,128)(2,1)S(1)}, u32[]{:S(2)}, u32[]{:S(2)}) collective-permute-start(bf16[128,1280]{1,0:T(8,128)(2,1)} %param.19), channel_id=1, source_target_pairs={{0,0},{1,4},{2,8},{3,12},{4,1},{5,5},{6,9},{7,13},{8,2},{9,6},{10,... | collective-permute-start | bytes 983048 | tf_op jit(solution)/shard_map/ppermute | solution.py:265
  21.3 11.3 %collective-permute-start.6 = (bf16[2,1280,64]{1,2,0:T(8,128)(2,1)}, bf16[2,1280,64]{1,2,0:T(8,128)(2,1)}, u32[]{:S(2)}, u32[]{:S(2)}) collective-permute-start(bf16[2,1280,64]{1,2,0:T(8,128)(2,1)} %param.33), channel_id=1, source_target_pairs={{0,12},{4,0},{8,4},{12,8},{1,13},{5,1},{9,5},{13,9},{2,14},{6,2},{... | collective-permute-start | bytes 983048 | tf_op jit(solution)/shard_map/ppermute | solution.py:257
  22.1 32.2 %collective-permute-start.5 = (bf16[2,1280,64]{1,2,0:T(8,128)(2,1)}, bf16[2,1280,64]{1,2,0:T(8,128)(2,1)}, u32[]{:S(2)}, u32[]{:S(2)}) collective-permute-start(bf16[2,1280,64]{1,2,0:T(8,128)(2,1)} %param.33), channel_id=1, source_target_pairs={{0,8},{4,12},{8,0},{12,4},{1,9},{5,13},{9,1},{13,5},{2,10},{6,14},... | collective-permute-start | bytes 983048 | tf_op jit(solution)/shard_map/ppermute | solution.py:257
  28.1 28.2 %collective-permute-start.1 = (bf16[128,1280]{1,0:T(8,128)(2,1)S(1)}, bf16[128,1280]{1,0:T(8,128)(2,1)S(1)}, u32[]{:S(2)}, u32[]{:S(2)}) collective-permute-start(bf16[128,1280]{1,0:T(8,128)(2,1)S(1)} %collective-permute-done), channel_id=1, source_target_pairs={{0,3},{1,0},{2,1},{3,2},{4,7},{5,4},{6,5},{7,6},{8,11},{9,8},{10,9... | collective-permute-start | bytes 983048 | tf_op jit(solution)/shard_map/ppermute | solution.py:260
  30.8 26.4 %collective-permute-start.2 = (bf16[128,1280]{1,0:T(8,128)(2,1)S(1)}, bf16[128,1280]{1,0:T(8,128)(2,1)S(1)}, u32[]{:S(2)}, u32[]{:S(2)}) collective-permute-start(bf16[128,1280]{1,0:T(8,128)(2,1)S(1)} %collective-permute-done), channel_id=1, source_target_pairs={{0,2},{1,3},{2,0},{3,1},{4,6},{5,7},{6,4},{7,5},{8,10},{9,11},{10,... | collective-permute-start | bytes 983048 | tf_op jit(solution)/shard_map/ppermute | solution.py:260
  30.8 24.7 %collective-permute-start.4 = (bf16[2,1280,64]{1,2,0:T(8,128)(2,1)}, bf16[2,1280,64]{1,2,0:T(8,128)(2,1)S(1)}, u32[]{:S(2)}, u32[]{:S(2)}) collective-permute-start(bf16[2,1280,64]{1,2,0:T(8,128)(2,1)} %param.33), channel_id=1, source_target_pairs={{0,4},{4,8},{8,12},{12,0},{1,5},{5,9},{9,13},{13,1},{2,6},{6,10},{... | collective-permute-start | bytes 983048 | tf_op jit(solution)/shard_map/ppermute | solution.py:257
  32.7 24.5 %collective-permute-start.3 = (bf16[128,1280]{1,0:T(8,128)(2,1)S(1)}, bf16[128,1280]{1,0:T(8,128)(2,1)S(1)}, u32[]{:S(2)}, u32[]{:S(2)}) collective-permute-start(bf16[128,1280]{1,0:T(8,128)(2,1)S(1)} %collective-permute-done), channel_id=1, source_target_pairs={{0,1},{1,2},{2,3},{3,0},{4,5},{5,6},{6,7},{7,4},{8,9},{9,10},{10,1... | collective-permute-start | bytes 983048 | tf_op jit(solution)/shard_map/ppermute | solution.py:260
  55.7 5.6 %collective-permute-start.9 = (f32[128,64]{0,1:T(8,128)S(1)}, f32[128,64]{0,1:T(8,128)S(1)}, u32[]{:S(2)}, u32[]{:S(2)}) collective-permute-start(f32[128,64]{0,1:T(8,128)S(1)} %add_add_fusion), channel_id=1, source_target_pairs={{0,3},{1,0},{2,1},{3,2},{4,7},{5,4},{6,5},{7,6},{8,11},{9,8},{10,9... | collective-permute-start | bytes 98312 | tf_op jit(solution)/shard_map/ppermute | solution.py:260
  55.8 5.5 %collective-permute-start.7 = (f32[128,64]{0,1:T(8,128)S(1)}, f32[128,64]{0,1:T(8,128)S(1)}, u32[]{:S(2)}, u32[]{:S(2)}) collective-permute-start(f32[128,64]{0,1:T(8,128)S(1)} %add_add_fusion), channel_id=1, source_target_pairs={{0,1},{1,2},{2,3},{3,0},{4,5},{5,6},{6,7},{7,4},{8,9},{9,10},{10,1... | collective-permute-start | bytes 98312 | tf_op jit(solution)/shard_map/ppermute | solution.py:260
  56.3 5.0 %collective-permute-start.8 = (f32[128,64]{0,1:T(8,128)S(1)}, f32[128,64]{0,1:T(8,128)S(1)}, u32[]{:S(2)}, u32[]{:S(2)}) collective-permute-start(f32[128,64]{0,1:T(8,128)S(1)} %add_add_fusion), channel_id=1, source_target_pairs={{0,2},{1,3},{2,0},{3,1},{4,6},{5,7},{6,4},{7,5},{8,10},{9,11},{10,... | collective-permute-start | bytes 98312 | tf_op jit(solution)/shard_map/ppermute | solution.py:260
  61.3 3.8 %collective-permute-start.10 = (bf16[128,64]{0,1:T(8,128)(2,1)S(1)}, bf16[128,64]{0,1:T(8,128)(2,1)S(1)}, u32[]{:S(2)}, u32[]{:S(2)}) collective-permute-start(bf16[128,64]{0,1:T(8,128)(2,1)S(1)} %add_convert_fusion.1), channel_id=1, source_target_pairs={{0,12},{4,0},{8,4},{12,8},{1,13},{5,1},{9,5},{13,9},{2,14},{6,2},{... | collective-permute-start | bytes 49160 | tf_op jit(solution)/shard_map/ppermute | solution.py:257
  61.9 4.7 %collective-permute-start.11 = (bf16[128,64]{0,1:T(8,128)(2,1)S(1)}, bf16[128,64]{0,1:T(8,128)(2,1)S(1)}, u32[]{:S(2)}, u32[]{:S(2)}) collective-permute-start(bf16[128,64]{0,1:T(8,128)(2,1)S(1)} %add_convert_fusion.1), channel_id=1, source_target_pairs={{0,8},{4,12},{8,0},{12,4},{1,9},{5,13},{9,1},{13,5},{2,10},{6,14},... | collective-permute-start | bytes 49160 | tf_op jit(solution)/shard_map/ppermute | solution.py:257
  61.9 6.3 %collective-permute-start.12 = (bf16[128,64]{0,1:T(8,128)(2,1)S(1)}, bf16[128,64]{0,1:T(8,128)(2,1)S(1)}, u32[]{:S(2)}, u32[]{:S(2)}) collective-permute-start(bf16[128,64]{0,1:T(8,128)(2,1)S(1)} %add_convert_fusion.1), channel_id=1, source_target_pairs={{0,4},{4,8},{8,12},{12,0},{1,5},{5,9},{9,13},{13,1},{2,6},{6,10},{... | collective-permute-start | bytes 49160 | tf_op jit(solution)/shard_map/ppermute | solution.py:257
  69.4 9.5 %collective-permute-start.15 = (bf16[128,1168]{0,1:T(8,128)(2,1)S(1)}, bf16[128,1168]{0,1:T(8,128)(2,1)S(1)}, u32[]{:S(2)}, u32[]{:S(2)}) collective-permute-start(bf16[128,1168]{0,1:T(8,128)(2,1)S(1)} %get-tuple-element.28), channel_id=1, source_target_pairs={{0,12},{4,0},{8,4},{12,8},{1,13},{5,1},{9,5},{13,9},{2,14},{6,2},{... | collective-permute-start | bytes 897032 | tf_op jit(solution)/shard_map/ppermute | solution.py:257
  71.4 25.3 %collective-permute-start.14 = (bf16[128,1168]{0,1:T(8,128)(2,1)S(1)}, bf16[128,1168]{0,1:T(8,128)(2,1)S(1)}, u32[]{:S(2)}, u32[]{:S(2)}) collective-permute-start(bf16[128,1168]{0,1:T(8,128)(2,1)S(1)} %get-tuple-element.29), channel_id=1, source_target_pairs={{0,8},{4,12},{8,0},{12,4},{1,9},{5,13},{9,1},{13,5},{2,10},{6,14},... | collective-permute-start | bytes 897032 | tf_op jit(solution)/shard_map/ppermute | solution.py:257
  71.4 25.3 %collective-permute-start.13 = (bf16[128,1168]{0,1:T(8,128)(2,1)S(1)}, bf16[128,1168]{0,1:T(8,128)(2,1)S(1)}, u32[]{:S(2)}, u32[]{:S(2)}) collective-permute-start(bf16[128,1168]{0,1:T(8,128)(2,1)S(1)} %get-tuple-element.27), channel_id=1, source_target_pairs={{0,4},{4,8},{8,12},{12,0},{1,5},{5,9},{9,13},{13,1},{2,6},{6,10},{... | collective-permute-start | bytes 897032 | tf_op jit(solution)/shard_map/ppermute | solution.py:257
  99.2 3.3 %collective-permute-start.16 = (f32[3,1152]{1,0:T(4,128)S(1)}, f32[3,1152]{1,0:T(4,128)S(1)}, u32[]{:S(2)}, u32[]{:S(2)}) collective-permute-start(f32[3,1152]{1,0:T(4,128)S(1)} %copy.117), channel_id=1, source_target_pairs={{0,4},{4,8},{8,12},{1,5},{5,9},{9,13},{2,6},{6,10},{10,14},{3,7},{... | collective-permute-start | bytes 41480 | tf_op jit(solution)/shard_map/ppermute | solution.py:18
  106.0 1.7 collective-permute-start.17
  106.1 4.0 %collective-permute-start.18 = (bf16[128,128]{0,1:T(8,128)(2,1)S(1)}, bf16[128,128]{0,1:T(8,128)(2,1)S(1)}, u32[]{:S(2)}, u32[]{:S(2)}) collective-permute-start(bf16[128,128]{0,1:T(8,128)(2,1)S(1)} %slice.238), channel_id=1, source_target_pairs={{0,2},{1,3},{2,0},{3,1},{4,6},{5,7},{6,4},{7,5},{8,10},{9,11},{10,... | collective-permute-start | bytes 98312 | tf_op jit(solution)/shard_map/ppermute | solution.py:260
  107.4 3.3 %collective-permute-start.19 = (bf16[128,128]{0,1:T(8,128)(2,1)S(1)}, bf16[128,128]{0,1:T(8,128)(2,1)S(1)}, u32[]{:S(2)}, u32[]{:S(2)}) collective-permute-start(bf16[128,128]{0,1:T(8,128)(2,1)S(1)} %slice.238), channel_id=1, source_target_pairs={{0,1},{1,2},{2,3},{3,0},{4,5},{5,6},{6,7},{7,4},{8,9},{9,10},{10,1... | collective-permute-start | bytes 98312 | tf_op jit(solution)/shard_map/ppermute | solution.py:260
  113.8 14.9 %collective-permute-start.20 = (bf16[16,65,256]{2,0,1:T(8,128)(2,1)}, bf16[16,65,256]{2,0,1:T(8,128)(2,1)}, u32[]{:S(2)}, u32[]{:S(2)}) collective-permute-start(bf16[16,65,256]{2,0,1:T(8,128)(2,1)} %copy.124), channel_id=1, source_target_pairs={{0,4},{4,8},{8,12},{1,5},{5,9},{9,13},{2,6},{6,10},{10,14},{3,7},{... | collective-permute-start | bytes 1597448 | tf_op jit(solution)/shard_map/ppermute | solution.py:406
  130.7 15.4 %collective-permute-start.21 = (bf16[16,65,256]{2,0,1:T(8,128)(2,1)S(1)}, bf16[16,65,256]{2,0,1:T(8,128)(2,1)S(1)}, u32[]{:S(2)}, u32[]{:S(2)}) collective-permute-start(bf16[16,65,256]{2,0,1:T(8,128)(2,1)S(1)} %copy.127), channel_id=1, source_target_pairs={{0,8},{4,12},{1,9},{5,13},{2,10},{6,14},{3,11},{7,15},{16,24},{20,... | collective-permute-start | bytes 1597448 | tf_op jit(solution)/shard_map/ppermute | solution.py:416
  147.5 21.6 %collective-permute-start.22 = (bf16[128,1024]{0,1:T(8,128)(2,1)S(1)}, bf16[128,1024]{0,1:T(8,128)(2,1)S(1)}, u32[]{:S(2)}, u32[]{:S(2)}) collective-permute-start(bf16[128,1024]{0,1:T(8,128)(2,1)S(1)} %fusion.37), channel_id=1, source_target_pairs={{0,12},{4,0},{8,4},{12,8},{1,13},{5,1},{9,5},{13,9},{2,14},{6,2},{... | collective-permute-start | bytes 786440 | tf_op jit(solution)/shard_map/ppermute | solution.py:257
  162.3 20.7 %collective-permute-start.23 = (bf16[128,1024]{0,1:T(8,128)(2,1)S(1)}, bf16[128,1024]{0,1:T(8,128)(2,1)S(1)}, u32[]{:S(2)}, u32[]{:S(2)}) collective-permute-start(bf16[128,1024]{0,1:T(8,128)(2,1)S(1)} %fusion.37), channel_id=1, source_target_pairs={{0,8},{4,12},{8,0},{12,4},{1,9},{5,13},{9,1},{13,5},{2,10},{6,14},... | collective-permute-start | bytes 786440 | tf_op jit(solution)/shard_map/ppermute | solution.py:257
  162.3 20.8 %collective-permute-start.24 = (bf16[128,1024]{0,1:T(8,128)(2,1)S(1)}, bf16[128,1024]{0,1:T(8,128)(2,1)S(1)}, u32[]{:S(2)}, u32[]{:S(2)}) collective-permute-start(bf16[128,1024]{0,1:T(8,128)(2,1)S(1)} %fusion.37), channel_id=1, source_target_pairs={{0,4},{4,8},{8,12},{12,0},{1,5},{5,9},{9,13},{13,1},{2,6},{6,10},{... | collective-permute-start | bytes 786440 | tf_op jit(solution)/shard_map/ppermute | solution.py:257
  188.7 1.4 collective-permute-start.25
  190.1 6.9 %collective-permute-start.26 = (f32[512,64]{0,1:T(8,128)S(1)}, f32[512,64]{0,1:T(8,128)S(1)}, u32[]{:S(2)}, u32[]{:S(2)}) collective-permute-start(f32[512,64]{0,1:T(8,128)S(1)} %add.364), channel_id=1, source_target_pairs={{0,2},{2,0},{1,3},{3,1},{4,6},{6,4},{5,7},{7,5},{8,10},{10,8},{9,1... | collective-permute-start | bytes 393224 | tf_op jit(solution)/shard_map/ppermute | solution.py:443
  191.8 26.4 %collective-permute-start.28 = (bf16[2,64,1280]{2,1,0:T(8,128)(2,1)S(1)}, bf16[2,64,1280]{2,1,0:T(8,128)(2,1)S(1)}, u32[]{:S(2)}, u32[]{:S(2)}) collective-permute-start(bf16[2,64,1280]{2,1,0:T(8,128)(2,1)S(1)} %copy-done.14), channel_id=1, source_target_pairs={{0,0},{1,4},{2,8},{3,12},{4,1},{5,5},{6,9},{7,13},{8,2},{9,6},{10,... | collective-permute-start | bytes 983048 | tf_op jit(solution)/shard_map/ppermute | solution.py:265
  197.1 21.1 %collective-permute-start.27 = (f32[512,64]{0,1:T(8,128)S(1)}, f32[512,64]{0,1:T(8,128)S(1)}, u32[]{:S(2)}, u32[]{:S(2)}) collective-permute-start(f32[512,64]{0,1:T(8,128)S(1)} %add.365), channel_id=1, source_target_pairs={{0,0},{1,4},{2,8},{3,12},{4,1},{5,5},{6,9},{7,13},{8,2},{9,6},{10,... | collective-permute-start | bytes 393224 | tf_op jit(solution)/shard_map/ppermute | solution.py:265
  220.4 2.3 collective-permute-start.29
  225.3 9.8 %collective-permute-start.30 = (bf16[128,1280]{1,0:T(8,128)(2,1)S(1)}, bf16[128,1280]{1,0:T(8,128)(2,1)S(1)}, u32[]{:S(2)}, u32[]{:S(2)}) collective-permute-start(bf16[128,1280]{1,0:T(8,128)(2,1)S(1)} %fusion.47), channel_id=1, source_target_pairs={{0,2},{2,0},{1,3},{3,1},{4,6},{6,4},{5,7},{7,5},{8,10},{10,8},{9,1... | collective-permute-start | bytes 983048 | tf_op jit(solution)/shard_map/ppermute | solution.py:473
  235.3 19.2 %collective-permute-start.31 = (bf16[128,1280]{1,0:T(8,128)(2,1)S(1)}, bf16[128,1280]{1,0:T(8,128)(2,1)S(1)}, u32[]{:S(2)}, u32[]{:S(2)}) collective-permute-start(bf16[128,1280]{1,0:T(8,128)(2,1)S(1)} %fusion.21), channel_id=1, source_target_pairs={{0,0},{1,4},{2,8},{3,12},{4,1},{5,5},{6,9},{7,13},{8,2},{9,6},{10,... | collective-permute-start | bytes 983048 | tf_op jit(solution)/shard_map/ppermute | solution.py:265
  (15 other events, 369.6 us)

commit v17 on v16

--- a/solution.py
+++ b/solution.py
@@ -346,9 +346,12 @@
         every = jnp.einsum("pf,efr->per", tokens, piece, preferred_element_type=jnp.float32)
         chosen = local_owned[:, None] == first + jnp.arange(bank_entries, dtype=jnp.int32)[None, :]
         down_pick = down_pick + jnp.sum(every * chosen[:, :, None].astype(jnp.float32), axis=1)
-    rank_local = (
-        down_pick + sum(moved(down_pick, s, "lane") for s in range(1, side))
-    ).astype(jnp.bfloat16)
+    if lax.axis_size("tp") == 2 and lax.axis_size("dp") == 2:
+        down_pick = down_pick + lax.ppermute(down_pick, "dp", [(0, 1), (1, 0)])
+        rank_local = down_pick + lax.ppermute(down_pick, "tp", [(0, 1), (1, 0)])
+    else:
+        rank_local = down_pick + sum(moved(down_pick, s, "lane") for s in range(1, side))
+    rank_local = rank_local.astype(jnp.bfloat16)
     rank_hidden = in_order(
         [rank_local] + [moved(rank_local, s, "ctx") for s in range(1, side)], here
     )

time: 256 us -> 254 us (level)
  waiting for transfers between devices: 143 us -> 146 us
    ppermute x9 -> x6, waiting for transfers between devices: 3.13 us -> 14.1 us  [moved(): return lax.ppermute(block, ('tp', 'dp'), pairs)]
    ppermute x12, waiting for transfers between devices: 68.4 us -> 61.7 us  [moved(): return lax.ppermute(block, 'ctx', pairs)]
    ppermute x9 -> x6, starting transfers between devices: 5.72 us -> 2.38 us  [moved(): return lax.ppermute(block, ('tp', 'dp'), pairs)]
    ppermute x4, waiting for transfers between devices: 42.4 us -> 39 us  [moved(): return lax.ppermute(block, ('ctx', 'tp', 'dp'), pairs)]
  transfers between devices with their start and end apart: 32 -> 31, of which waited for: 18 -> 21; matrix products, arithmetic and copies ran while one was open for 9% -> 8% of each run, Pallas kernels for 0% -> 0%
where the time goes in v17:
time: 254 us
  waiting for transfers between devices  146 us (57%)
  starting transfers between devices  60 us (24%)
  local copies, waits for them, and re-layouts  16.8 us (7%)
  matrix products  15.3 us (6%)
  other arithmetic  13.1 us (5%)
    ppermute x12, waiting for transfers between devices, moved(): return lax.ppermute(block, 'ctx', pairs)  61.7 us
    ppermute x4, waiting for transfers between devices, moved(): return lax.ppermute(block, ('ctx', 'tp', 'dp'), pairs)  39 us
    ppermute x12, starting transfers between devices, moved(): return lax.ppermute(block, 'ctx', pairs)  23.4 us
    ppermute x4, starting transfers between devices, moved(): return lax.ppermute(block, ('ctx', 'tp', 'dp'), pairs)  16.9 us
    ppermute x6, waiting for transfers between devices, moved(): return lax.ppermute(block, ('tp', 'dp'), pairs)  14.1 us
    ppermute x1, waiting for transfers between devices, square_body(): lax.ppermute(crossing, 'tp', [(0, 1), (1, 0)]).astype(jnp.float32)  9.74 us
    ppermute x1, waiting for transfers between devices, square_body(): lax.ppermute(state_and_decay, 'ctx', [(a, a + 1) for a in range(side - 1)])  9.55 us
    ppermute x1, waiting for transfers between devices, square_body(): far = lax.ppermute(pair, 'ctx', [(a, a + 2) for a in range(side - 2)])  6.79 us
  transfers between devices with their start and end apart: 31, of which 21 were waited for; matrix products, arithmetic and copies ran while one was open for 8% of the time, Pallas kernels for 0%

profile of v17, /device:TPU:2, one launch (start us, length us, event | category | flops | bytes accessed | tf_op | source)
XLA Modules:
  0.0 253.5 jit_solution(8467887488939448641)
XLA Ops:
  0.0 4.7 %collective-permute-start = (bf16[128,1280]{1,0:T(8,128)(2,1)}, bf16[128,1280]{1,0:T(8,128)(2,1)S(1)}, u32[]{:S(2)}, u32[]{:S(2)}) collective-permute-start(bf16[128,1280]{1,0:T(8,128)(2,1)} %param.19), channel_id=1, source_target_pairs={{0,0},{1,4},{2,8},{3,12},{4,1},{5,5},{6,9},{7,13},{8,2},{9,6},{10,... | collective-permute-start | bytes 983048 | tf_op jit(solution)/shard_map/ppermute | solution.py:265
  12.9 8.5 %collective-permute-done = bf16[128,1280]{1,0:T(8,128)(2,1)S(1)} collective-permute-done((bf16[128,1280]{1,0:T(8,128)(2,1)}, bf16[128,1280]{1,0:T(8,128)(2,1)S(1)}, u32[]{:S(2)}, u32[]{:S(2)}) %collective-permute-start) | collective-permute-done | bytes 327712 | tf_op jit(solution)/shard_map/ppermute | solution.py:265
  21.9 2.0 collective-permute-start.6
  25.3 4.2 %collective-permute-done.1 = bf16[128,1280]{1,0:T(8,128)(2,1)S(1)} collective-permute-done((bf16[128,1280]{1,0:T(8,128)(2,1)S(1)}, bf16[128,1280]{1,0:T(8,128)(2,1)S(1)}, u32[]{:S(2)}, u32[]{:S(2)}) %collective-permute-start.1) | collective-permute-done | bytes 327712 | tf_op jit(solution)/shard_map/ppermute | solution.py:260
  29.6 6.7 %collective-permute-done.2 = bf16[128,1280]{1,0:T(8,128)(2,1)S(1)} collective-permute-done((bf16[128,1280]{1,0:T(8,128)(2,1)S(1)}, bf16[128,1280]{1,0:T(8,128)(2,1)S(1)}, u32[]{:S(2)}, u32[]{:S(2)}) %collective-permute-start.2) | collective-permute-done | bytes 327712 | tf_op jit(solution)/shard_map/ppermute | solution.py:260
  36.8 15.8 %collective-permute-done.5 = bf16[2,1280,64]{1,2,0:T(8,128)(2,1)S(1)} collective-permute-done((bf16[2,1280,64]{1,2,0:T(8,128)(2,1)}, bf16[2,1280,64]{1,2,0:T(8,128)(2,1)S(1)}, u32[]{:S(2)}, u32[]{:S(2)}) %collective-permute-start.5) | collective-permute-done | bytes 327712 | tf_op jit(solution)/shard_map/ppermute | solution.py:257
  56.3 1.8 collective-permute-start.8
  62.5 2.0 collective-permute-start.11
  65.4 2.6 %collective-permute-done.11 = bf16[128,64]{0,1:T(8,128)(2,1)S(1)} collective-permute-done((bf16[128,64]{0,1:T(8,128)(2,1)S(1)}, bf16[128,64]{0,1:T(8,128)(2,1)S(1)}, u32[]{:S(2)}, u32[]{:S(2)}) %collective-permute-start.11) | collective-permute-done | bytes 16416 | tf_op jit(solution)/shard_map/ppermute | solution.py:257
  72.2 5.7 %collective-permute-done.14 = bf16[128,1168]{0,1:T(8,128)(2,1)S(1)} collective-permute-done((bf16[128,1168]{0,1:T(8,128)(2,1)S(1)}, bf16[128,1168]{0,1:T(8,128)(2,1)S(1)}, u32[]{:S(2)}, u32[]{:S(2)}) %collective-permute-start.14) | collective-permute-done | bytes 299040 | tf_op jit(solution)/shard_map/ppermute | solution.py:257
  77.9 16.6 %collective-permute-done.13 = bf16[128,1168]{0,1:T(8,128)(2,1)S(1)} collective-permute-done((bf16[128,1168]{0,1:T(8,128)(2,1)S(1)}, bf16[128,1168]{0,1:T(8,128)(2,1)S(1)}, u32[]{:S(2)}, u32[]{:S(2)}) %collective-permute-start.13) | collective-permute-done | bytes 299040 | tf_op jit(solution)/shard_map/ppermute | solution.py:257
  96.9 2.1 collective-permute-start.15
  100.7 3.3 %divide_multiply_fusion = f32[128,1152]{0,1:T(8,128)S(1)} fusion(f32[128,1152]{0,1:T(8,128)} %slice.96, f32[3,1152]{0,1:T(8,128)S(1)} %copy.118, f32[128]{0:T(128)S(1)} %get-tuple-element.42, f32[1152]{0:T(1024)S(1)} %get-tuple-element.14, f32[128]{0:T(128)S(1)} %get-tuple-element.43, f32[1152]{0:T(1024)S(1)} %get-tuple-element.15, ...), kind=kLoop, calls=%fused_computation.65 | loop fusion | flops 2654208 | bytes 1213952 | tf_op jit(solution)/shard_map/jit(silu)/mul | solution.py:392
  106.3 2.4 collective-permute-done.17
  112.1 5.2 %collective-permute-start.19 = (bf16[16,65,256]{2,0,1:T(8,128)(2,1)}, bf16[16,65,256]{2,0,1:T(8,128)(2,1)}, u32[]{:S(2)}, u32[]{:S(2)}) collective-permute-start(bf16[16,65,256]{2,0,1:T(8,128)(2,1)} %copy.124), channel_id=1, source_target_pairs={{0,4},{4,8},{8,12},{1,5},{5,9},{9,13},{2,6},{6,10},{10,14},{3,7},{... | collective-permute-start | bytes 1597448 | tf_op jit(solution)/shard_map/ppermute | solution.py:409
  117.6 9.6 %collective-permute-done.19 = bf16[16,65,256]{2,0,1:T(8,128)(2,1)} collective-permute-done((bf16[16,65,256]{2,0,1:T(8,128)(2,1)}, bf16[16,65,256]{2,0,1:T(8,128)(2,1)}, u32[]{:S(2)}, u32[]{:S(2)}) %collective-permute-start.19) | collective-permute-done | bytes 532512 | tf_op jit(solution)/shard_map/ppermute | solution.py:409
  129.2 6.4 %collective-permute-start.20 = (bf16[16,65,256]{2,0,1:T(8,128)(2,1)S(1)}, bf16[16,65,256]{2,0,1:T(8,128)(2,1)S(1)}, u32[]{:S(2)}, u32[]{:S(2)}) collective-permute-start(bf16[16,65,256]{2,0,1:T(8,128)(2,1)S(1)} %copy.127), channel_id=1, source_target_pairs={{0,8},{4,12},{1,9},{5,13},{2,10},{6,14},{3,11},{7,15},{16,24},{20,... | collective-permute-start | bytes 1597448 | tf_op jit(solution)/shard_map/ppermute | solution.py:419
  135.8 2.3 convolution_bitcast_fusion
  138.2 6.8 %collective-permute-done.20 = bf16[16,65,256]{2,0,1:T(8,128)(2,1)S(1)} collective-permute-done((bf16[16,65,256]{2,0,1:T(8,128)(2,1)S(1)}, bf16[16,65,256]{2,0,1:T(8,128)(2,1)S(1)}, u32[]{:S(2)}, u32[]{:S(2)}) %collective-permute-start.20) | collective-permute-done | bytes 532512 | tf_op jit(solution)/shard_map/ppermute | solution.py:419
  146.4 14.8 %collective-permute-start.21 = (bf16[128,1024]{0,1:T(8,128)(2,1)S(1)}, bf16[128,1024]{0,1:T(8,128)(2,1)S(1)}, u32[]{:S(2)}, u32[]{:S(2)}) collective-permute-start(bf16[128,1024]{0,1:T(8,128)(2,1)S(1)} %fusion.37), channel_id=1, source_target_pairs={{0,12},{4,0},{8,4},{12,8},{1,13},{5,1},{9,5},{13,9},{2,14},{6,2},{... | collective-permute-start | bytes 786440 | tf_op jit(solution)/shard_map/ppermute | solution.py:257
  161.8 6.2 %collective-permute-done.21 = bf16[128,1024]{0,1:T(8,128)(2,1)S(1)} collective-permute-done((bf16[128,1024]{0,1:T(8,128)(2,1)S(1)}, bf16[128,1024]{0,1:T(8,128)(2,1)S(1)}, u32[]{:S(2)}, u32[]{:S(2)}) %collective-permute-start.21) | collective-permute-done | bytes 262176 | tf_op jit(solution)/shard_map/ppermute | solution.py:257
  168.0 13.9 %collective-permute-done.22 = bf16[128,1024]{0,1:T(8,128)(2,1)S(1)} collective-permute-done((bf16[128,1024]{0,1:T(8,128)(2,1)S(1)}, bf16[128,1024]{0,1:T(8,128)(2,1)S(1)}, u32[]{:S(2)}, u32[]{:S(2)}) %collective-permute-start.22) | collective-permute-done | bytes 262176 | tf_op jit(solution)/shard_map/ppermute | solution.py:257
  183.5 2.3 copy.130
  185.8 1.7 fusion.79
  190.0 5.9 %collective-permute-start.27 = (bf16[2,64,1280]{2,1,0:T(8,128)(2,1)S(1)}, bf16[2,64,1280]{2,1,0:T(8,128)(2,1)S(1)}, u32[]{:S(2)}, u32[]{:S(2)}) collective-permute-start(bf16[2,64,1280]{2,1,0:T(8,128)(2,1)S(1)} %copy-done.14), channel_id=1, source_target_pairs={{0,0},{1,4},{2,8},{3,12},{4,1},{5,5},{6,9},{7,13},{8,2},{9,6},{10,... | collective-permute-start | bytes 983048 | tf_op jit(solution)/shard_map/ppermute | solution.py:265
  195.9 4.4 %collective-permute-start.26 = (f32[512,64]{0,1:T(8,128)S(1)}, f32[512,64]{0,1:T(8,128)S(1)}, u32[]{:S(2)}, u32[]{:S(2)}) collective-permute-start(f32[512,64]{0,1:T(8,128)S(1)} %add.361), channel_id=1, source_target_pairs={{0,0},{1,4},{2,8},{3,12},{4,1},{5,5},{6,9},{7,13},{8,2},{9,6},{10,... | collective-permute-start | bytes 393224 | tf_op jit(solution)/shard_map/ppermute | solution.py:265
  200.4 2.7 %fusion = f32[512,1280]{1,0:T(8,128)S(1)} fusion(bf16[512,1024]{1,0:T(8,128)(2,1)} %bitcast.178, bf16[1024,1280]{1,0:T(8,128)(2,1)S(1)} %copy-done), kind=kOutput, calls=%fused_computation.3 | convolution fusion | flops 1343488000 | bytes 6291456 | tf_op jit(solution)/shard_map/dot_general | solution.py:450
  203.1 13.3 %collective-permute-done.26 = f32[512,64]{0,1:T(8,128)S(1)} collective-permute-done((f32[512,64]{0,1:T(8,128)S(1)}, f32[512,64]{0,1:T(8,128)S(1)}, u32[]{:S(2)}, u32[]{:S(2)}) %collective-permute-start.26) | collective-permute-done | bytes 131104 | tf_op jit(solution)/shard_map/ppermute | solution.py:265
  218.7 2.2 collective-permute-done.28
  223.7 9.7 %collective-permute-done.29 = bf16[128,1280]{1,0:T(8,128)(2,1)S(1)} collective-permute-done((bf16[128,1280]{1,0:T(8,128)(2,1)S(1)}, bf16[128,1280]{1,0:T(8,128)(2,1)S(1)}, u32[]{:S(2)}, u32[]{:S(2)}) %collective-permute-start.29) | collective-permute-done | bytes 327712 | tf_op jit(solution)/shard_map/ppermute | solution.py:476
  233.6 1.9 collective-permute-start.30
  235.5 17.3 %collective-permute-done.30 = bf16[128,1280]{1,0:T(8,128)(2,1)S(1)} collective-permute-done((bf16[128,1280]{1,0:T(8,128)(2,1)S(1)}, bf16[128,1280]{1,0:T(8,128)(2,1)S(1)}, u32[]{:S(2)}, u32[]{:S(2)}) %collective-permute-start.30) | collective-permute-done | bytes 327712 | tf_op jit(solution)/shard_map/ppermute | solution.py:265
  (189 shorter events, 46.2 us)
Async XLA Ops:
  0.0 200.4 %copy-start = (bf16[1024,1280]{1,0:T(8,128)(2,1)S(1)}, bf16[1024,1280]{1,0:T(8,128)(2,1)}, u32[]{:S(2)}) copy-start(bf16[1024,1280]{1,0:T(8,128)(2,1)} %param.32) | copy-start | bytes 7864324
  0.0 21.4 %collective-permute-start = (bf16[128,1280]{1,0:T(8,128)(2,1)}, bf16[128,1280]{1,0:T(8,128)(2,1)S(1)}, u32[]{:S(2)}, u32[]{:S(2)}) collective-permute-start(bf16[128,1280]{1,0:T(8,128)(2,1)} %param.19), channel_id=1, source_target_pairs={{0,0},{1,4},{2,8},{3,12},{4,1},{5,5},{6,9},{7,13},{8,2},{9,6},{10,... | collective-permute-start | bytes 983048 | tf_op jit(solution)/shard_map/ppermute | solution.py:265
  21.4 8.1 %collective-permute-start.1 = (bf16[128,1280]{1,0:T(8,128)(2,1)S(1)}, bf16[128,1280]{1,0:T(8,128)(2,1)S(1)}, u32[]{:S(2)}, u32[]{:S(2)}) collective-permute-start(bf16[128,1280]{1,0:T(8,128)(2,1)S(1)} %collective-permute-done), channel_id=1, source_target_pairs={{0,3},{1,0},{2,1},{3,2},{4,7},{5,4},{6,5},{7,6},{8,11},{9,8},{10,9... | collective-permute-start | bytes 983048 | tf_op jit(solution)/shard_map/ppermute | solution.py:260
  21.4 14.9 %collective-permute-start.2 = (bf16[128,1280]{1,0:T(8,128)(2,1)S(1)}, bf16[128,1280]{1,0:T(8,128)(2,1)S(1)}, u32[]{:S(2)}, u32[]{:S(2)}) collective-permute-start(bf16[128,1280]{1,0:T(8,128)(2,1)S(1)} %collective-permute-done), channel_id=1, source_target_pairs={{0,2},{1,3},{2,0},{3,1},{4,6},{5,7},{6,4},{7,5},{8,10},{9,11},{10,... | collective-permute-start | bytes 983048 | tf_op jit(solution)/shard_map/ppermute | solution.py:260
  21.5 14.9 %collective-permute-start.3 = (bf16[128,1280]{1,0:T(8,128)(2,1)S(1)}, bf16[128,1280]{1,0:T(8,128)(2,1)S(1)}, u32[]{:S(2)}, u32[]{:S(2)}) collective-permute-start(bf16[128,1280]{1,0:T(8,128)(2,1)S(1)} %collective-permute-done), channel_id=1, source_target_pairs={{0,1},{1,2},{2,3},{3,0},{4,5},{5,6},{6,7},{7,4},{8,9},{9,10},{10,1... | collective-permute-start | bytes 983048 | tf_op jit(solution)/shard_map/ppermute | solution.py:260
  21.9 14.6 %collective-permute-start.6 = (bf16[2,1280,64]{1,2,0:T(8,128)(2,1)}, bf16[2,1280,64]{1,2,0:T(8,128)(2,1)S(1)}, u32[]{:S(2)}, u32[]{:S(2)}) collective-permute-start(bf16[2,1280,64]{1,2,0:T(8,128)(2,1)} %param.33), channel_id=1, source_target_pairs={{0,12},{4,0},{8,4},{12,8},{1,13},{5,1},{9,5},{13,9},{2,14},{6,2},{... | collective-permute-start | bytes 983048 | tf_op jit(solution)/shard_map/ppermute | solution.py:257
  23.9 28.7 %collective-permute-start.5 = (bf16[2,1280,64]{1,2,0:T(8,128)(2,1)}, bf16[2,1280,64]{1,2,0:T(8,128)(2,1)S(1)}, u32[]{:S(2)}, u32[]{:S(2)}) collective-permute-start(bf16[2,1280,64]{1,2,0:T(8,128)(2,1)} %param.33), channel_id=1, source_target_pairs={{0,8},{4,12},{8,0},{12,4},{1,9},{5,13},{9,1},{13,5},{2,10},{6,14},... | collective-permute-start | bytes 983048 | tf_op jit(solution)/shard_map/ppermute | solution.py:257
  29.5 23.4 %collective-permute-start.4 = (bf16[2,1280,64]{1,2,0:T(8,128)(2,1)}, bf16[2,1280,64]{1,2,0:T(8,128)(2,1)S(1)}, u32[]{:S(2)}, u32[]{:S(2)}) collective-permute-start(bf16[2,1280,64]{1,2,0:T(8,128)(2,1)} %param.33), channel_id=1, source_target_pairs={{0,4},{4,8},{8,12},{12,0},{1,5},{5,9},{9,13},{13,1},{2,6},{6,10},{... | collective-permute-start | bytes 983048 | tf_op jit(solution)/shard_map/ppermute | solution.py:257
  53.2 3.0 %collective-permute-start.7 = (f32[128,64]{0,1:T(8,128)S(1)}, f32[128,64]{0,1:T(8,128)S(1)}, u32[]{:S(2)}, u32[]{:S(2)}) collective-permute-start(f32[128,64]{0,1:T(8,128)S(1)} %add_add_fusion), channel_id=1, source_target_pairs={{0,1},{1,0},{2,3},{3,2},{4,5},{5,4},{6,7},{7,6},{8,9},{9,8},{10,11... | collective-permute-start | bytes 98312 | tf_op jit(solution)/shard_map/ppermute | solution.py:350
  56.3 4.0 %collective-permute-start.8 = (f32[128,64]{0,1:T(8,128)S(1)}, f32[128,64]{0,1:T(8,128)S(1)}, u32[]{:S(2)}, u32[]{:S(2)}) collective-permute-start(f32[128,64]{0,1:T(8,128)S(1)} %add.324), channel_id=1, source_target_pairs={{0,2},{2,0},{1,3},{3,1},{4,6},{6,4},{5,7},{7,5},{8,10},{10,8},{9,1... | collective-permute-start | bytes 98312 | tf_op jit(solution)/shard_map/ppermute | solution.py:351
  60.3 4.2 %collective-permute-start.9 = (bf16[128,64]{0,1:T(8,128)(2,1)S(1)}, bf16[128,64]{0,1:T(8,128)(2,1)S(1)}, u32[]{:S(2)}, u32[]{:S(2)}) collective-permute-start(bf16[128,64]{0,1:T(8,128)(2,1)S(1)} %add_convert_fusion.1), channel_id=1, source_target_pairs={{0,12},{4,0},{8,4},{12,8},{1,13},{5,1},{9,5},{13,9},{2,14},{6,2},{... | collective-permute-start | bytes 49160 | tf_op jit(solution)/shard_map/ppermute | solution.py:257
  60.8 4.7 %collective-permute-start.10 = (bf16[128,64]{0,1:T(8,128)(2,1)S(1)}, bf16[128,64]{0,1:T(8,128)(2,1)S(1)}, u32[]{:S(2)}, u32[]{:S(2)}) collective-permute-start(bf16[128,64]{0,1:T(8,128)(2,1)S(1)} %add_convert_fusion.1), channel_id=1, source_target_pairs={{0,8},{4,12},{8,0},{12,4},{1,9},{5,13},{9,1},{13,5},{2,10},{6,14},... | collective-permute-start | bytes 49160 | tf_op jit(solution)/shard_map/ppermute | solution.py:257
  62.5 5.5 %collective-permute-start.11 = (bf16[128,64]{0,1:T(8,128)(2,1)S(1)}, bf16[128,64]{0,1:T(8,128)(2,1)S(1)}, u32[]{:S(2)}, u32[]{:S(2)}) collective-permute-start(bf16[128,64]{0,1:T(8,128)(2,1)S(1)} %add_convert_fusion.1), channel_id=1, source_target_pairs={{0,4},{4,8},{8,12},{12,0},{1,5},{5,9},{9,13},{13,1},{2,6},{6,10},{... | collective-permute-start | bytes 49160 | tf_op jit(solution)/shard_map/ppermute | solution.py:257
  69.3 8.5 %collective-permute-start.14 = (bf16[128,1168]{0,1:T(8,128)(2,1)S(1)}, bf16[128,1168]{0,1:T(8,128)(2,1)S(1)}, u32[]{:S(2)}, u32[]{:S(2)}) collective-permute-start(bf16[128,1168]{0,1:T(8,128)(2,1)S(1)} %get-tuple-element.28), channel_id=1, source_target_pairs={{0,12},{4,0},{8,4},{12,8},{1,13},{5,1},{9,5},{13,9},{2,14},{6,2},{... | collective-permute-start | bytes 897032 | tf_op jit(solution)/shard_map/ppermute | solution.py:257
  70.3 24.2 %collective-permute-start.13 = (bf16[128,1168]{0,1:T(8,128)(2,1)S(1)}, bf16[128,1168]{0,1:T(8,128)(2,1)S(1)}, u32[]{:S(2)}, u32[]{:S(2)}) collective-permute-start(bf16[128,1168]{0,1:T(8,128)(2,1)S(1)} %get-tuple-element.29), channel_id=1, source_target_pairs={{0,8},{4,12},{8,0},{12,4},{1,9},{5,13},{9,1},{13,5},{2,10},{6,14},... | collective-permute-start | bytes 897032 | tf_op jit(solution)/shard_map/ppermute | solution.py:257
  71.0 23.4 %collective-permute-start.12 = (bf16[128,1168]{0,1:T(8,128)(2,1)S(1)}, bf16[128,1168]{0,1:T(8,128)(2,1)S(1)}, u32[]{:S(2)}, u32[]{:S(2)}) collective-permute-start(bf16[128,1168]{0,1:T(8,128)(2,1)S(1)} %get-tuple-element.27), channel_id=1, source_target_pairs={{0,4},{4,8},{8,12},{12,0},{1,5},{5,9},{9,13},{13,1},{2,6},{6,10},{... | collective-permute-start | bytes 897032 | tf_op jit(solution)/shard_map/ppermute | solution.py:257
  96.9 3.6 %collective-permute-start.15 = (f32[3,1152]{1,0:T(4,128)S(1)}, f32[3,1152]{1,0:T(4,128)S(1)}, u32[]{:S(2)}, u32[]{:S(2)}) collective-permute-start(f32[3,1152]{1,0:T(4,128)S(1)} %copy.117), channel_id=1, source_target_pairs={{0,4},{4,8},{8,12},{1,5},{5,9},{9,13},{2,6},{6,10},{10,14},{3,7},{... | collective-permute-start | bytes 41480 | tf_op jit(solution)/shard_map/ppermute | solution.py:18
  104.0 2.3 collective-permute-start.16
  104.7 4.0 %collective-permute-start.17 = (bf16[128,128]{0,1:T(8,128)(2,1)S(1)}, bf16[128,128]{0,1:T(8,128)(2,1)S(1)}, u32[]{:S(2)}, u32[]{:S(2)}) collective-permute-start(bf16[128,128]{0,1:T(8,128)(2,1)S(1)} %slice.238), channel_id=1, source_target_pairs={{0,2},{1,3},{2,0},{3,1},{4,6},{5,7},{6,4},{7,5},{8,10},{9,11},{10,... | collective-permute-start | bytes 98312 | tf_op jit(solution)/shard_map/ppermute | solution.py:260
  105.7 3.4 %collective-permute-start.18 = (bf16[128,128]{0,1:T(8,128)(2,1)S(1)}, bf16[128,128]{0,1:T(8,128)(2,1)S(1)}, u32[]{:S(2)}, u32[]{:S(2)}) collective-permute-start(bf16[128,128]{0,1:T(8,128)(2,1)S(1)} %slice.238), channel_id=1, source_target_pairs={{0,1},{1,2},{2,3},{3,0},{4,5},{5,6},{6,7},{7,4},{8,9},{9,10},{10,1... | collective-permute-start | bytes 98312 | tf_op jit(solution)/shard_map/ppermute | solution.py:260
  112.1 15.1 %collective-permute-start.19 = (bf16[16,65,256]{2,0,1:T(8,128)(2,1)}, bf16[16,65,256]{2,0,1:T(8,128)(2,1)}, u32[]{:S(2)}, u32[]{:S(2)}) collective-permute-start(bf16[16,65,256]{2,0,1:T(8,128)(2,1)} %copy.124), channel_id=1, source_target_pairs={{0,4},{4,8},{8,12},{1,5},{5,9},{9,13},{2,6},{6,10},{10,14},{3,7},{... | collective-permute-start | bytes 1597448 | tf_op jit(solution)/shard_map/ppermute | solution.py:409
  129.2 15.8 %collective-permute-start.20 = (bf16[16,65,256]{2,0,1:T(8,128)(2,1)S(1)}, bf16[16,65,256]{2,0,1:T(8,128)(2,1)S(1)}, u32[]{:S(2)}, u32[]{:S(2)}) collective-permute-start(bf16[16,65,256]{2,0,1:T(8,128)(2,1)S(1)} %copy.127), channel_id=1, source_target_pairs={{0,8},{4,12},{1,9},{5,13},{2,10},{6,14},{3,11},{7,15},{16,24},{20,... | collective-permute-start | bytes 1597448 | tf_op jit(solution)/shard_map/ppermute | solution.py:419
  146.4 21.6 %collective-permute-start.21 = (bf16[128,1024]{0,1:T(8,128)(2,1)S(1)}, bf16[128,1024]{0,1:T(8,128)(2,1)S(1)}, u32[]{:S(2)}, u32[]{:S(2)}) collective-permute-start(bf16[128,1024]{0,1:T(8,128)(2,1)S(1)} %fusion.37), channel_id=1, source_target_pairs={{0,12},{4,0},{8,4},{12,8},{1,13},{5,1},{9,5},{13,9},{2,14},{6,2},{... | collective-permute-start | bytes 786440 | tf_op jit(solution)/shard_map/ppermute | solution.py:257
  161.2 20.7 %collective-permute-start.22 = (bf16[128,1024]{0,1:T(8,128)(2,1)S(1)}, bf16[128,1024]{0,1:T(8,128)(2,1)S(1)}, u32[]{:S(2)}, u32[]{:S(2)}) collective-permute-start(bf16[128,1024]{0,1:T(8,128)(2,1)S(1)} %fusion.37), channel_id=1, source_target_pairs={{0,8},{4,12},{8,0},{12,4},{1,9},{5,13},{9,1},{13,5},{2,10},{6,14},... | collective-permute-start | bytes 786440 | tf_op jit(solution)/shard_map/ppermute | solution.py:257
  161.2 20.8 %collective-permute-start.23 = (bf16[128,1024]{0,1:T(8,128)(2,1)S(1)}, bf16[128,1024]{0,1:T(8,128)(2,1)S(1)}, u32[]{:S(2)}, u32[]{:S(2)}) collective-permute-start(bf16[128,1024]{0,1:T(8,128)(2,1)S(1)} %fusion.37), channel_id=1, source_target_pairs={{0,4},{4,8},{8,12},{12,0},{1,5},{5,9},{9,13},{13,1},{2,6},{6,10},{... | collective-permute-start | bytes 786440 | tf_op jit(solution)/shard_map/ppermute | solution.py:257
  187.6 1.4 collective-permute-start.24
  189.0 6.9 %collective-permute-start.25 = (f32[512,64]{0,1:T(8,128)S(1)}, f32[512,64]{0,1:T(8,128)S(1)}, u32[]{:S(2)}, u32[]{:S(2)}) collective-permute-start(f32[512,64]{0,1:T(8,128)S(1)} %add.360), channel_id=1, source_target_pairs={{0,2},{2,0},{1,3},{3,1},{4,6},{6,4},{5,7},{7,5},{8,10},{10,8},{9,1... | collective-permute-start | bytes 393224 | tf_op jit(solution)/shard_map/ppermute | solution.py:446
  190.0 26.4 %collective-permute-start.27 = (bf16[2,64,1280]{2,1,0:T(8,128)(2,1)S(1)}, bf16[2,64,1280]{2,1,0:T(8,128)(2,1)S(1)}, u32[]{:S(2)}, u32[]{:S(2)}) collective-permute-start(bf16[2,64,1280]{2,1,0:T(8,128)(2,1)S(1)} %copy-done.14), channel_id=1, source_target_pairs={{0,0},{1,4},{2,8},{3,12},{4,1},{5,5},{6,9},{7,13},{8,2},{9,6},{10,... | collective-permute-start | bytes 983048 | tf_op jit(solution)/shard_map/ppermute | solution.py:265
  195.9 20.5 %collective-permute-start.26 = (f32[512,64]{0,1:T(8,128)S(1)}, f32[512,64]{0,1:T(8,128)S(1)}, u32[]{:S(2)}, u32[]{:S(2)}) collective-permute-start(f32[512,64]{0,1:T(8,128)S(1)} %add.361), channel_id=1, source_target_pairs={{0,0},{1,4},{2,8},{3,12},{4,1},{5,5},{6,9},{7,13},{8,2},{9,6},{10,... | collective-permute-start | bytes 393224 | tf_op jit(solution)/shard_map/ppermute | solution.py:265
  218.6 2.3 collective-permute-start.28
  223.6 9.8 %collective-permute-start.29 = (bf16[128,1280]{1,0:T(8,128)(2,1)S(1)}, bf16[128,1280]{1,0:T(8,128)(2,1)S(1)}, u32[]{:S(2)}, u32[]{:S(2)}) collective-permute-start(bf16[128,1280]{1,0:T(8,128)(2,1)S(1)} %fusion.47), channel_id=1, source_target_pairs={{0,2},{2,0},{1,3},{3,1},{4,6},{6,4},{5,7},{7,5},{8,10},{10,8},{9,1... | collective-permute-start | bytes 983048 | tf_op jit(solution)/shard_map/ppermute | solution.py:476
  233.6 19.2 %collective-permute-start.30 = (bf16[128,1280]{1,0:T(8,128)(2,1)S(1)}, bf16[128,1280]{1,0:T(8,128)(2,1)S(1)}, u32[]{:S(2)}, u32[]{:S(2)}) collective-permute-start(bf16[128,1280]{1,0:T(8,128)(2,1)S(1)} %fusion.21), channel_id=1, source_target_pairs={{0,0},{1,4},{2,8},{3,12},{4,1},{5,5},{6,9},{7,13},{8,2},{9,6},{10,... | collective-permute-start | bytes 983048 | tf_op jit(solution)/shard_map/ppermute | solution.py:265
  (14 other events, 135.2 us)

commit v18 on v17

--- a/solution.py
+++ b/solution.py
@@ -392,8 +392,22 @@
     act = jax.nn.silu(convolved)
     x_heads = act[:, :channels].reshape(length, head_count, -1)
     bc_local = act[:, channels:].astype(jnp.bfloat16)
-    bc_pieces = [bc_local] + [moved(bc_local, s, "lane") for s in range(1, side)]
-    bc_all = jnp.transpose(in_order([piece.T for piece in bc_pieces], lane))
+    if lax.axis_size("tp") == 2 and lax.axis_size("dp") == 2:
+        other = lax.ppermute(bc_local, "dp", [(0, 1), (1, 0)])
+        pair = jnp.where(
+            lax.axis_index("dp") == 0,
+            jnp.concatenate([bc_local, other], axis=1),
+            jnp.concatenate([other, bc_local], axis=1),
+        )
+        other = lax.ppermute(pair, "tp", [(0, 1), (1, 0)])
+        bc_all = jnp.where(
+            lax.axis_index("tp") == 0,
+            jnp.concatenate([pair, other], axis=1),
+            jnp.concatenate([other, pair], axis=1),
+        )
+    else:
+        bc_pieces = [bc_local] + [moved(bc_local, s, "lane") for s in range(1, side)]
+        bc_all = jnp.transpose(in_order([piece.T for piece in bc_pieces], lane))
     state_width = bc_all.shape[1] // 2
     b_proj = bc_all[:, :state_width]
     c_proj = bc_all[:, state_width:]

time: 254 us -> 257 us (1.012)
    ppermute x0 -> x2, waiting for transfers between devices: none -> 3.79 us  [the longest x1 2.69 us: square_body(): other = lax.ppermute(pair, 'tp', [(0, 1), (1, 0)])]
    ppermute x6 -> x3, waiting for transfers between devices: 14.1 us -> 11 us  [moved(): return lax.ppermute(block, ('tp', 'dp'), pairs)]
  transfers between devices with their start and end apart: 31 -> 30, of which waited for: 21 -> 21; matrix products, arithmetic and copies ran while one was open for 8% -> 8% of each run, Pallas kernels for 0% -> 0%
where the time goes in v18:
time: 257 us; the launch traced here: 256 us
  waiting for transfers between devices  147 us (57%)
  starting transfers between devices  60.3 us (23%)
  local copies, waits for them, and re-layouts  17.4 us (7%)
  matrix products  15.3 us (6%)
  other arithmetic  13.9 us (5%)
    ppermute x12, waiting for transfers between devices, moved(): return lax.ppermute(block, 'ctx', pairs)  61.7 us
    ppermute x4, waiting for transfers between devices, moved(): return lax.ppermute(block, ('ctx', 'tp', 'dp'), pairs)  39.1 us
    ppermute x12, starting transfers between devices, moved(): return lax.ppermute(block, 'ctx', pairs)  23.4 us
    ppermute x4, starting transfers between devices, moved(): return lax.ppermute(block, ('ctx', 'tp', 'dp'), pairs)  16.9 us
    ppermute x3, waiting for transfers between devices, moved(): return lax.ppermute(block, ('tp', 'dp'), pairs)  11 us
    ppermute x1, waiting for transfers between devices, square_body(): lax.ppermute(crossing, 'tp', [(0, 1), (1, 0)]).astype(jnp.float32)  9.74 us
    ppermute x1, waiting for transfers between devices, square_body(): lax.ppermute(state_and_decay, 'ctx', [(a, a + 1) for a in range(side - 1)])  9.66 us
    ppermute x1, waiting for transfers between devices, square_body(): far = lax.ppermute(pair, 'ctx', [(a, a + 2) for a in range(side - 2)])  6.79 us
  transfers between devices with their start and end apart: 30, of which 21 were waited for; matrix products, arithmetic and copies ran while one was open for 8% of the time, Pallas kernels for 0%

profile of v18, /device:TPU:2, one launch (start us, length us, event | category | flops | bytes accessed | tf_op | source)
XLA Modules:
  0.0 256.1 jit_solution(16411246542541448503)
XLA Ops:
  0.0 4.7 %collective-permute-start = (bf16[128,1280]{1,0:T(8,128)(2,1)}, bf16[128,1280]{1,0:T(8,128)(2,1)S(1)}, u32[]{:S(2)}, u32[]{:S(2)}) collective-permute-start(bf16[128,1280]{1,0:T(8,128)(2,1)} %param.19), channel_id=1, source_target_pairs={{0,0},{1,4},{2,8},{3,12},{4,1},{5,5},{6,9},{7,13},{8,2},{9,6},{10,... | collective-permute-start | bytes 983048 | tf_op jit(solution)/shard_map/ppermute | solution.py:265
  12.9 8.5 %collective-permute-done = bf16[128,1280]{1,0:T(8,128)(2,1)S(1)} collective-permute-done((bf16[128,1280]{1,0:T(8,128)(2,1)}, bf16[128,1280]{1,0:T(8,128)(2,1)S(1)}, u32[]{:S(2)}, u32[]{:S(2)}) %collective-permute-start) | collective-permute-done | bytes 327712 | tf_op jit(solution)/shard_map/ppermute | solution.py:265
  21.9 2.0 collective-permute-start.6
  25.3 4.2 %collective-permute-done.1 = bf16[128,1280]{1,0:T(8,128)(2,1)S(1)} collective-permute-done((bf16[128,1280]{1,0:T(8,128)(2,1)S(1)}, bf16[128,1280]{1,0:T(8,128)(2,1)S(1)}, u32[]{:S(2)}, u32[]{:S(2)}) %collective-permute-start.1) | collective-permute-done | bytes 327712 | tf_op jit(solution)/shard_map/ppermute | solution.py:260
  29.6 6.7 %collective-permute-done.2 = bf16[128,1280]{1,0:T(8,128)(2,1)S(1)} collective-permute-done((bf16[128,1280]{1,0:T(8,128)(2,1)S(1)}, bf16[128,1280]{1,0:T(8,128)(2,1)S(1)}, u32[]{:S(2)}, u32[]{:S(2)}) %collective-permute-start.2) | collective-permute-done | bytes 327712 | tf_op jit(solution)/shard_map/ppermute | solution.py:260
  36.8 15.8 %collective-permute-done.5 = bf16[2,1280,64]{1,2,0:T(8,128)(2,1)S(1)} collective-permute-done((bf16[2,1280,64]{1,2,0:T(8,128)(2,1)}, bf16[2,1280,64]{1,2,0:T(8,128)(2,1)S(1)}, u32[]{:S(2)}, u32[]{:S(2)}) %collective-permute-start.5) | collective-permute-done | bytes 327712 | tf_op jit(solution)/shard_map/ppermute | solution.py:257
  56.3 1.8 collective-permute-start.8
  62.5 2.0 collective-permute-start.11
  65.4 2.6 %collective-permute-done.11 = bf16[128,64]{0,1:T(8,128)(2,1)S(1)} collective-permute-done((bf16[128,64]{0,1:T(8,128)(2,1)S(1)}, bf16[128,64]{0,1:T(8,128)(2,1)S(1)}, u32[]{:S(2)}, u32[]{:S(2)}) %collective-permute-start.11) | collective-permute-done | bytes 16416 | tf_op jit(solution)/shard_map/ppermute | solution.py:257
  72.2 5.7 %collective-permute-done.14 = bf16[128,1168]{0,1:T(8,128)(2,1)S(1)} collective-permute-done((bf16[128,1168]{0,1:T(8,128)(2,1)S(1)}, bf16[128,1168]{0,1:T(8,128)(2,1)S(1)}, u32[]{:S(2)}, u32[]{:S(2)}) %collective-permute-start.14) | collective-permute-done | bytes 299040 | tf_op jit(solution)/shard_map/ppermute | solution.py:257
  77.9 16.6 %collective-permute-done.13 = bf16[128,1168]{0,1:T(8,128)(2,1)S(1)} collective-permute-done((bf16[128,1168]{0,1:T(8,128)(2,1)S(1)}, bf16[128,1168]{0,1:T(8,128)(2,1)S(1)}, u32[]{:S(2)}, u32[]{:S(2)}) %collective-permute-start.13) | collective-permute-done | bytes 299040 | tf_op jit(solution)/shard_map/ppermute | solution.py:257
  96.9 2.1 collective-permute-start.15
  101.5 4.0 %divide_multiply_fusion = f32[128,1152]{0,1:T(8,128)S(1)} fusion(f32[128,1152]{0,1:T(8,128)} %slice.96, f32[3,1152]{0,1:T(8,128)} %copy.111, f32[128]{0:T(128)S(1)} %get-tuple-element.42, f32[1152]{0:T(1024)S(1)} %get-tuple-element.14, f32[128]{0:T(128)S(1)} %get-tuple-element.43, f32[1152]{0:T(1024)S(1)} %get-tuple-element.15, ...), kind=kLoop, calls=%fused_computation.65 | loop fusion | flops 2654208 | bytes 1213952 | tf_op jit(solution)/shard_map/jit(silu)/mul | solution.py:392
  108.5 2.7 %collective-permute-done.17 = bf16[128,256]{0,1:T(8,128)(2,1)S(1)} collective-permute-done((bf16[128,256]{0,1:T(8,128)(2,1)S(1)}, bf16[128,256]{0,1:T(8,128)(2,1)S(1)}, u32[]{:S(2)}, u32[]{:S(2)}) %collective-permute-start.17) | collective-permute-done | bytes 65568 | tf_op jit(solution)/shard_map/ppermute | solution.py:402
  113.9 5.2 %collective-permute-start.18 = (bf16[16,65,256]{2,0,1:T(8,128)(2,1)}, bf16[16,65,256]{2,0,1:T(8,128)(2,1)}, u32[]{:S(2)}, u32[]{:S(2)}) collective-permute-start(bf16[16,65,256]{2,0,1:T(8,128)(2,1)} %copy.117), channel_id=1, source_target_pairs={{0,4},{4,8},{8,12},{1,5},{5,9},{9,13},{2,6},{6,10},{10,14},{3,7},{... | collective-permute-start | bytes 1597448 | tf_op jit(solution)/shard_map/ppermute | solution.py:423
  119.5 9.7 %collective-permute-done.18 = bf16[16,65,256]{2,0,1:T(8,128)(2,1)} collective-permute-done((bf16[16,65,256]{2,0,1:T(8,128)(2,1)}, bf16[16,65,256]{2,0,1:T(8,128)(2,1)}, u32[]{:S(2)}, u32[]{:S(2)}) %collective-permute-start.18) | collective-permute-done | bytes 532512 | tf_op jit(solution)/shard_map/ppermute | solution.py:423
  131.2 6.3 %collective-permute-start.19 = (bf16[16,65,256]{2,0,1:T(8,128)(2,1)S(1)}, bf16[16,65,256]{2,0,1:T(8,128)(2,1)S(1)}, u32[]{:S(2)}, u32[]{:S(2)}) collective-permute-start(bf16[16,65,256]{2,0,1:T(8,128)(2,1)S(1)} %copy.120), channel_id=1, source_target_pairs={{0,8},{4,12},{1,9},{5,13},{2,10},{6,14},{3,11},{7,15},{16,24},{20,... | collective-permute-start | bytes 1597448 | tf_op jit(solution)/shard_map/ppermute | solution.py:433
  137.8 2.2 convolution_bitcast_fusion
  140.2 6.8 %collective-permute-done.19 = bf16[16,65,256]{2,0,1:T(8,128)(2,1)S(1)} collective-permute-done((bf16[16,65,256]{2,0,1:T(8,128)(2,1)S(1)}, bf16[16,65,256]{2,0,1:T(8,128)(2,1)S(1)}, u32[]{:S(2)}, u32[]{:S(2)}) %collective-permute-start.19) | collective-permute-done | bytes 532512 | tf_op jit(solution)/shard_map/ppermute | solution.py:433
  148.3 14.8 %collective-permute-start.20 = (bf16[128,1024]{0,1:T(8,128)(2,1)S(1)}, bf16[128,1024]{0,1:T(8,128)(2,1)S(1)}, u32[]{:S(2)}, u32[]{:S(2)}) collective-permute-start(bf16[128,1024]{0,1:T(8,128)(2,1)S(1)} %fusion.37), channel_id=1, source_target_pairs={{0,12},{4,0},{8,4},{12,8},{1,13},{5,1},{9,5},{13,9},{2,14},{6,2},{... | collective-permute-start | bytes 786440 | tf_op jit(solution)/shard_map/ppermute | solution.py:257
  163.8 6.2 %collective-permute-done.20 = bf16[128,1024]{0,1:T(8,128)(2,1)S(1)} collective-permute-done((bf16[128,1024]{0,1:T(8,128)(2,1)S(1)}, bf16[128,1024]{0,1:T(8,128)(2,1)S(1)}, u32[]{:S(2)}, u32[]{:S(2)}) %collective-permute-start.20) | collective-permute-done | bytes 262176 | tf_op jit(solution)/shard_map/ppermute | solution.py:257
  170.0 13.9 %collective-permute-done.21 = bf16[128,1024]{0,1:T(8,128)(2,1)S(1)} collective-permute-done((bf16[128,1024]{0,1:T(8,128)(2,1)S(1)}, bf16[128,1024]{0,1:T(8,128)(2,1)S(1)}, u32[]{:S(2)}, u32[]{:S(2)}) %collective-permute-start.21) | collective-permute-done | bytes 262176 | tf_op jit(solution)/shard_map/ppermute | solution.py:257
  185.5 2.3 copy.124
  187.8 1.7 fusion.79
  192.6 5.3 %collective-permute-start.26 = (bf16[2,64,1280]{2,1,0:T(8,128)(2,1)S(1)}, bf16[2,64,1280]{2,1,0:T(8,128)(2,1)S(1)}, u32[]{:S(2)}, u32[]{:S(2)}) collective-permute-start(bf16[2,64,1280]{2,1,0:T(8,128)(2,1)S(1)} %copy-done.14), channel_id=1, source_target_pairs={{0,0},{1,4},{2,8},{3,12},{4,1},{5,5},{6,9},{7,13},{8,2},{9,6},{10,... | collective-permute-start | bytes 983048 | tf_op jit(solution)/shard_map/ppermute | solution.py:265
  197.9 5.0 %collective-permute-start.25 = (f32[512,64]{0,1:T(8,128)S(1)}, f32[512,64]{0,1:T(8,128)S(1)}, u32[]{:S(2)}, u32[]{:S(2)}) collective-permute-start(f32[512,64]{0,1:T(8,128)S(1)} %add.356), channel_id=1, source_target_pairs={{0,0},{1,4},{2,8},{3,12},{4,1},{5,5},{6,9},{7,13},{8,2},{9,6},{10,... | collective-permute-start | bytes 393224 | tf_op jit(solution)/shard_map/ppermute | solution.py:265
  203.0 2.7 %fusion = f32[512,1280]{1,0:T(8,128)S(1)} fusion(bf16[512,1024]{1,0:T(8,128)(2,1)} %bitcast.156, bf16[1024,1280]{1,0:T(8,128)(2,1)S(1)} %copy-done), kind=kOutput, calls=%fused_computation.3 | convolution fusion | flops 1343488000 | bytes 6291456 | tf_op jit(solution)/shard_map/dot_general | solution.py:464
  205.7 13.3 %collective-permute-done.25 = f32[512,64]{0,1:T(8,128)S(1)} collective-permute-done((f32[512,64]{0,1:T(8,128)S(1)}, f32[512,64]{0,1:T(8,128)S(1)}, u32[]{:S(2)}, u32[]{:S(2)}) %collective-permute-start.25) | collective-permute-done | bytes 131104 | tf_op jit(solution)/shard_map/ppermute | solution.py:265
  221.3 2.2 collective-permute-done.27
  226.2 9.7 %collective-permute-done.28 = bf16[128,1280]{1,0:T(8,128)(2,1)S(1)} collective-permute-done((bf16[128,1280]{1,0:T(8,128)(2,1)S(1)}, bf16[128,1280]{1,0:T(8,128)(2,1)S(1)}, u32[]{:S(2)}, u32[]{:S(2)}) %collective-permute-start.28) | collective-permute-done | bytes 327712 | tf_op jit(solution)/shard_map/ppermute | solution.py:490
  236.1 1.9 collective-permute-start.29
  238.1 17.3 %collective-permute-done.29 = bf16[128,1280]{1,0:T(8,128)(2,1)S(1)} collective-permute-done((bf16[128,1280]{1,0:T(8,128)(2,1)S(1)}, bf16[128,1280]{1,0:T(8,128)(2,1)S(1)}, u32[]{:S(2)}, u32[]{:S(2)}) %collective-permute-start.29) | collective-permute-done | bytes 327712 | tf_op jit(solution)/shard_map/ppermute | solution.py:265
  (179 shorter events, 47.9 us)
Async XLA Ops:
  0.0 202.9 %copy-start = (bf16[1024,1280]{1,0:T(8,128)(2,1)S(1)}, bf16[1024,1280]{1,0:T(8,128)(2,1)}, u32[]{:S(2)}) copy-start(bf16[1024,1280]{1,0:T(8,128)(2,1)} %param.32) | copy-start | bytes 7864324
  0.0 21.4 %collective-permute-start = (bf16[128,1280]{1,0:T(8,128)(2,1)}, bf16[128,1280]{1,0:T(8,128)(2,1)S(1)}, u32[]{:S(2)}, u32[]{:S(2)}) collective-permute-start(bf16[128,1280]{1,0:T(8,128)(2,1)} %param.19), channel_id=1, source_target_pairs={{0,0},{1,4},{2,8},{3,12},{4,1},{5,5},{6,9},{7,13},{8,2},{9,6},{10,... | collective-permute-start | bytes 983048 | tf_op jit(solution)/shard_map/ppermute | solution.py:265
  21.4 8.1 %collective-permute-start.1 = (bf16[128,1280]{1,0:T(8,128)(2,1)S(1)}, bf16[128,1280]{1,0:T(8,128)(2,1)S(1)}, u32[]{:S(2)}, u32[]{:S(2)}) collective-permute-start(bf16[128,1280]{1,0:T(8,128)(2,1)S(1)} %collective-permute-done), channel_id=1, source_target_pairs={{0,3},{1,0},{2,1},{3,2},{4,7},{5,4},{6,5},{7,6},{8,11},{9,8},{10,9... | collective-permute-start | bytes 983048 | tf_op jit(solution)/shard_map/ppermute | solution.py:260
  21.4 14.9 %collective-permute-start.2 = (bf16[128,1280]{1,0:T(8,128)(2,1)S(1)}, bf16[128,1280]{1,0:T(8,128)(2,1)S(1)}, u32[]{:S(2)}, u32[]{:S(2)}) collective-permute-start(bf16[128,1280]{1,0:T(8,128)(2,1)S(1)} %collective-permute-done), channel_id=1, source_target_pairs={{0,2},{1,3},{2,0},{3,1},{4,6},{5,7},{6,4},{7,5},{8,10},{9,11},{10,... | collective-permute-start | bytes 983048 | tf_op jit(solution)/shard_map/ppermute | solution.py:260
  21.5 14.9 %collective-permute-start.3 = (bf16[128,1280]{1,0:T(8,128)(2,1)S(1)}, bf16[128,1280]{1,0:T(8,128)(2,1)S(1)}, u32[]{:S(2)}, u32[]{:S(2)}) collective-permute-start(bf16[128,1280]{1,0:T(8,128)(2,1)S(1)} %collective-permute-done), channel_id=1, source_target_pairs={{0,1},{1,2},{2,3},{3,0},{4,5},{5,6},{6,7},{7,4},{8,9},{9,10},{10,1... | collective-permute-start | bytes 983048 | tf_op jit(solution)/shard_map/ppermute | solution.py:260
  21.9 14.6 %collective-permute-start.6 = (bf16[2,1280,64]{1,2,0:T(8,128)(2,1)}, bf16[2,1280,64]{1,2,0:T(8,128)(2,1)S(1)}, u32[]{:S(2)}, u32[]{:S(2)}) collective-permute-start(bf16[2,1280,64]{1,2,0:T(8,128)(2,1)} %param.33), channel_id=1, source_target_pairs={{0,12},{4,0},{8,4},{12,8},{1,13},{5,1},{9,5},{13,9},{2,14},{6,2},{... | collective-permute-start | bytes 983048 | tf_op jit(solution)/shard_map/ppermute | solution.py:257
  23.9 28.7 %collective-permute-start.5 = (bf16[2,1280,64]{1,2,0:T(8,128)(2,1)}, bf16[2,1280,64]{1,2,0:T(8,128)(2,1)S(1)}, u32[]{:S(2)}, u32[]{:S(2)}) collective-permute-start(bf16[2,1280,64]{1,2,0:T(8,128)(2,1)} %param.33), channel_id=1, source_target_pairs={{0,8},{4,12},{8,0},{12,4},{1,9},{5,13},{9,1},{13,5},{2,10},{6,14},... | collective-permute-start | bytes 983048 | tf_op jit(solution)/shard_map/ppermute | solution.py:257
  29.5 23.4 %collective-permute-start.4 = (bf16[2,1280,64]{1,2,0:T(8,128)(2,1)}, bf16[2,1280,64]{1,2,0:T(8,128)(2,1)S(1)}, u32[]{:S(2)}, u32[]{:S(2)}) collective-permute-start(bf16[2,1280,64]{1,2,0:T(8,128)(2,1)} %param.33), channel_id=1, source_target_pairs={{0,4},{4,8},{8,12},{12,0},{1,5},{5,9},{9,13},{13,1},{2,6},{6,10},{... | collective-permute-start | bytes 983048 | tf_op jit(solution)/shard_map/ppermute | solution.py:257
  53.2 3.0 %collective-permute-start.7 = (f32[128,64]{0,1:T(8,128)S(1)}, f32[128,64]{0,1:T(8,128)S(1)}, u32[]{:S(2)}, u32[]{:S(2)}) collective-permute-start(f32[128,64]{0,1:T(8,128)S(1)} %add_add_fusion), channel_id=1, source_target_pairs={{0,1},{1,0},{2,3},{3,2},{4,5},{5,4},{6,7},{7,6},{8,9},{9,8},{10,11... | collective-permute-start | bytes 98312 | tf_op jit(solution)/shard_map/ppermute | solution.py:350
  56.3 4.0 %collective-permute-start.8 = (f32[128,64]{0,1:T(8,128)S(1)}, f32[128,64]{0,1:T(8,128)S(1)}, u32[]{:S(2)}, u32[]{:S(2)}) collective-permute-start(f32[128,64]{0,1:T(8,128)S(1)} %add.319), channel_id=1, source_target_pairs={{0,2},{2,0},{1,3},{3,1},{4,6},{6,4},{5,7},{7,5},{8,10},{10,8},{9,1... | collective-permute-start | bytes 98312 | tf_op jit(solution)/shard_map/ppermute | solution.py:351
  60.3 4.2 %collective-permute-start.9 = (bf16[128,64]{0,1:T(8,128)(2,1)S(1)}, bf16[128,64]{0,1:T(8,128)(2,1)S(1)}, u32[]{:S(2)}, u32[]{:S(2)}) collective-permute-start(bf16[128,64]{0,1:T(8,128)(2,1)S(1)} %add_convert_fusion.1), channel_id=1, source_target_pairs={{0,12},{4,0},{8,4},{12,8},{1,13},{5,1},{9,5},{13,9},{2,14},{6,2},{... | collective-permute-start | bytes 49160 | tf_op jit(solution)/shard_map/ppermute | solution.py:257
  60.8 4.7 %collective-permute-start.10 = (bf16[128,64]{0,1:T(8,128)(2,1)S(1)}, bf16[128,64]{0,1:T(8,128)(2,1)S(1)}, u32[]{:S(2)}, u32[]{:S(2)}) collective-permute-start(bf16[128,64]{0,1:T(8,128)(2,1)S(1)} %add_convert_fusion.1), channel_id=1, source_target_pairs={{0,8},{4,12},{8,0},{12,4},{1,9},{5,13},{9,1},{13,5},{2,10},{6,14},... | collective-permute-start | bytes 49160 | tf_op jit(solution)/shard_map/ppermute | solution.py:257
  62.5 5.5 %collective-permute-start.11 = (bf16[128,64]{0,1:T(8,128)(2,1)S(1)}, bf16[128,64]{0,1:T(8,128)(2,1)S(1)}, u32[]{:S(2)}, u32[]{:S(2)}) collective-permute-start(bf16[128,64]{0,1:T(8,128)(2,1)S(1)} %add_convert_fusion.1), channel_id=1, source_target_pairs={{0,4},{4,8},{8,12},{12,0},{1,5},{5,9},{9,13},{13,1},{2,6},{6,10},{... | collective-permute-start | bytes 49160 | tf_op jit(solution)/shard_map/ppermute | solution.py:257
  69.3 29.7 %copy-start.11 = (f32[16]{0:T(128)S(1)}, f32[16]{0:T(128)}, u32[]{:S(2)}) copy-start(f32[16]{0:T(128)} %param.28) | copy-start | bytes 196
  69.3 8.5 %collective-permute-start.14 = (bf16[128,1168]{0,1:T(8,128)(2,1)S(1)}, bf16[128,1168]{0,1:T(8,128)(2,1)S(1)}, u32[]{:S(2)}, u32[]{:S(2)}) collective-permute-start(bf16[128,1168]{0,1:T(8,128)(2,1)S(1)} %get-tuple-element.28), channel_id=1, source_target_pairs={{0,12},{4,0},{8,4},{12,8},{1,13},{5,1},{9,5},{13,9},{2,14},{6,2},{... | collective-permute-start | bytes 897032 | tf_op jit(solution)/shard_map/ppermute | solution.py:257
  70.3 24.2 %collective-permute-start.13 = (bf16[128,1168]{0,1:T(8,128)(2,1)S(1)}, bf16[128,1168]{0,1:T(8,128)(2,1)S(1)}, u32[]{:S(2)}, u32[]{:S(2)}) collective-permute-start(bf16[128,1168]{0,1:T(8,128)(2,1)S(1)} %get-tuple-element.29), channel_id=1, source_target_pairs={{0,8},{4,12},{8,0},{12,4},{1,9},{5,13},{9,1},{13,5},{2,10},{6,14},... | collective-permute-start | bytes 897032 | tf_op jit(solution)/shard_map/ppermute | solution.py:257
  71.0 23.4 %collective-permute-start.12 = (bf16[128,1168]{0,1:T(8,128)(2,1)S(1)}, bf16[128,1168]{0,1:T(8,128)(2,1)S(1)}, u32[]{:S(2)}, u32[]{:S(2)}) collective-permute-start(bf16[128,1168]{0,1:T(8,128)(2,1)S(1)} %get-tuple-element.27), channel_id=1, source_target_pairs={{0,4},{4,8},{8,12},{12,0},{1,5},{5,9},{9,13},{13,1},{2,6},{6,10},{... | collective-permute-start | bytes 897032 | tf_op jit(solution)/shard_map/ppermute | solution.py:257
  96.9 3.6 %collective-permute-start.15 = (f32[3,1152]{1,0:T(4,128)S(1)}, f32[3,1152]{1,0:T(4,128)S(1)}, u32[]{:S(2)}, u32[]{:S(2)}) collective-permute-start(f32[3,1152]{1,0:T(4,128)S(1)} %copy.110), channel_id=1, source_target_pairs={{0,4},{4,8},{8,12},{1,5},{5,9},{9,13},{2,6},{6,10},{10,14},{3,7},{... | collective-permute-start | bytes 41480 | tf_op jit(solution)/shard_map/ppermute | solution.py:18
  105.5 1.3 collective-permute-start.16
  106.8 4.3 %collective-permute-start.17 = (bf16[128,256]{0,1:T(8,128)(2,1)S(1)}, bf16[128,256]{0,1:T(8,128)(2,1)S(1)}, u32[]{:S(2)}, u32[]{:S(2)}) collective-permute-start(bf16[128,256]{0,1:T(8,128)(2,1)S(1)} %maximum_select_fusion.1), channel_id=1, source_target_pairs={{0,2},{2,0},{1,3},{3,1},{4,6},{6,4},{5,7},{7,5},{8,10},{10,8},{9,1... | collective-permute-start | bytes 196616 | tf_op jit(solution)/shard_map/ppermute | solution.py:402
  113.9 15.2 %collective-permute-start.18 = (bf16[16,65,256]{2,0,1:T(8,128)(2,1)}, bf16[16,65,256]{2,0,1:T(8,128)(2,1)}, u32[]{:S(2)}, u32[]{:S(2)}) collective-permute-start(bf16[16,65,256]{2,0,1:T(8,128)(2,1)} %copy.117), channel_id=1, source_target_pairs={{0,4},{4,8},{8,12},{1,5},{5,9},{9,13},{2,6},{6,10},{10,14},{3,7},{... | collective-permute-start | bytes 1597448 | tf_op jit(solution)/shard_map/ppermute | solution.py:423
  131.2 15.8 %collective-permute-start.19 = (bf16[16,65,256]{2,0,1:T(8,128)(2,1)S(1)}, bf16[16,65,256]{2,0,1:T(8,128)(2,1)S(1)}, u32[]{:S(2)}, u32[]{:S(2)}) collective-permute-start(bf16[16,65,256]{2,0,1:T(8,128)(2,1)S(1)} %copy.120), channel_id=1, source_target_pairs={{0,8},{4,12},{1,9},{5,13},{2,10},{6,14},{3,11},{7,15},{16,24},{20,... | collective-permute-start | bytes 1597448 | tf_op jit(solution)/shard_map/ppermute | solution.py:433
  148.3 21.6 %collective-permute-start.20 = (bf16[128,1024]{0,1:T(8,128)(2,1)S(1)}, bf16[128,1024]{0,1:T(8,128)(2,1)S(1)}, u32[]{:S(2)}, u32[]{:S(2)}) collective-permute-start(bf16[128,1024]{0,1:T(8,128)(2,1)S(1)} %fusion.37), channel_id=1, source_target_pairs={{0,12},{4,0},{8,4},{12,8},{1,13},{5,1},{9,5},{13,9},{2,14},{6,2},{... | collective-permute-start | bytes 786440 | tf_op jit(solution)/shard_map/ppermute | solution.py:257
  163.1 20.7 %collective-permute-start.21 = (bf16[128,1024]{0,1:T(8,128)(2,1)S(1)}, bf16[128,1024]{0,1:T(8,128)(2,1)S(1)}, u32[]{:S(2)}, u32[]{:S(2)}) collective-permute-start(bf16[128,1024]{0,1:T(8,128)(2,1)S(1)} %fusion.37), channel_id=1, source_target_pairs={{0,8},{4,12},{8,0},{12,4},{1,9},{5,13},{9,1},{13,5},{2,10},{6,14},... | collective-permute-start | bytes 786440 | tf_op jit(solution)/shard_map/ppermute | solution.py:257
  163.2 20.8 %collective-permute-start.22 = (bf16[128,1024]{0,1:T(8,128)(2,1)S(1)}, bf16[128,1024]{0,1:T(8,128)(2,1)S(1)}, u32[]{:S(2)}, u32[]{:S(2)}) collective-permute-start(bf16[128,1024]{0,1:T(8,128)(2,1)S(1)} %fusion.37), channel_id=1, source_target_pairs={{0,4},{4,8},{8,12},{12,0},{1,5},{5,9},{9,13},{13,1},{2,6},{6,10},{... | collective-permute-start | bytes 786440 | tf_op jit(solution)/shard_map/ppermute | solution.py:257
  189.5 1.4 collective-permute-start.23
  191.0 6.9 %collective-permute-start.24 = (f32[512,64]{0,1:T(8,128)S(1)}, f32[512,64]{0,1:T(8,128)S(1)}, u32[]{:S(2)}, u32[]{:S(2)}) collective-permute-start(f32[512,64]{0,1:T(8,128)S(1)} %add.355), channel_id=1, source_target_pairs={{0,2},{2,0},{1,3},{3,1},{4,6},{6,4},{5,7},{7,5},{8,10},{10,8},{9,1... | collective-permute-start | bytes 393224 | tf_op jit(solution)/shard_map/ppermute | solution.py:460
  192.6 26.4 %collective-permute-start.26 = (bf16[2,64,1280]{2,1,0:T(8,128)(2,1)S(1)}, bf16[2,64,1280]{2,1,0:T(8,128)(2,1)S(1)}, u32[]{:S(2)}, u32[]{:S(2)}) collective-permute-start(bf16[2,64,1280]{2,1,0:T(8,128)(2,1)S(1)} %copy-done.14), channel_id=1, source_target_pairs={{0,0},{1,4},{2,8},{3,12},{4,1},{5,5},{6,9},{7,13},{8,2},{9,6},{10,... | collective-permute-start | bytes 983048 | tf_op jit(solution)/shard_map/ppermute | solution.py:265
  197.9 21.1 %collective-permute-start.25 = (f32[512,64]{0,1:T(8,128)S(1)}, f32[512,64]{0,1:T(8,128)S(1)}, u32[]{:S(2)}, u32[]{:S(2)}) collective-permute-start(f32[512,64]{0,1:T(8,128)S(1)} %add.356), channel_id=1, source_target_pairs={{0,0},{1,4},{2,8},{3,12},{4,1},{5,5},{6,9},{7,13},{8,2},{9,6},{10,... | collective-permute-start | bytes 393224 | tf_op jit(solution)/shard_map/ppermute | solution.py:265
  221.2 2.3 collective-permute-start.27
  226.2 9.8 %collective-permute-start.28 = (bf16[128,1280]{1,0:T(8,128)(2,1)S(1)}, bf16[128,1280]{1,0:T(8,128)(2,1)S(1)}, u32[]{:S(2)}, u32[]{:S(2)}) collective-permute-start(bf16[128,1280]{1,0:T(8,128)(2,1)S(1)} %fusion.47), channel_id=1, source_target_pairs={{0,2},{2,0},{1,3},{3,1},{4,6},{6,4},{5,7},{7,5},{8,10},{10,8},{9,1... | collective-permute-start | bytes 983048 | tf_op jit(solution)/shard_map/ppermute | solution.py:490
  236.1 19.2 %collective-permute-start.29 = (bf16[128,1280]{1,0:T(8,128)(2,1)S(1)}, bf16[128,1280]{1,0:T(8,128)(2,1)S(1)}, u32[]{:S(2)}, u32[]{:S(2)}) collective-permute-start(bf16[128,1280]{1,0:T(8,128)(2,1)S(1)} %fusion.21), channel_id=1, source_target_pairs={{0,0},{1,4},{2,8},{3,12},{4,1},{5,5},{6,9},{7,13},{8,2},{9,6},{10,... | collective-permute-start | bytes 983048 | tf_op jit(solution)/shard_map/ppermute | solution.py:265
  (13 other events, 106.2 us)
